TPU v7x, 32 devices: a whole 2x2x4 slice. The times are simulated.
32 devices in a mesh: groups: 2 (over y), tensor: 4 (over x, core), dp: 4 (over z).
Axes of the slice: x: 2, y: 2, z: 4, core: 2. Of those that a mesh axis runs over, the one named last changes fastest.
Arguments:
- tokens: bfloat16 [65536, 4096], P(('groups', 'dp'), 'tensor'), parts along dimension 0, may hold values from -6 to 6
- cotangent: bfloat16 [65536, 4096], P(('groups', 'dp'), 'tensor'), parts along dimension 0, may hold values from -6 to 6
- w_first: bfloat16 [16, 256, 256], P('tensor'), may hold values from -0.375 to 0.375
- w_second: bfloat16 [16, 256, 256], P('tensor'), may hold values from -0.375 to 0.375
Outputs:
- grad_tokens: bfloat16 [65536, 4096], P(('groups', 'dp'), 'tensor'), parts along dimension 0
- grad_first: float32 [32, 256, 256], P(('groups', 'tensor'), 'dp'), parts along dimension 0
- grad_second: float32 [32, 256, 256], P(('groups', 'tensor'), 'dp'), parts along dimension 0
There are 2 independent parts, one for each index of `groups`. A program takes and returns all parts, laid end to end along the dimension named above; an argument that names none is the same for every part. Nothing has to cross between parts.
All inputs are finite; a program needn't handle non-finite values.
Results may differ from a plain program's by a relative error of at most 0.0065.
Values may be sent and summed in bfloat16 or wider, within the bound.
No kernel may reach another device: no remote copies, remote signals or barrier semaphores. Data moves between devices by JAX's collectives and lax.ppermute only.
A program may use at most 192 MiB of HBM per device.

v0:
```python
import math

import jax
import jax.numpy as jnp
from jax import lax
from jax.sharding import PartitionSpec as P

NB = 16


def shards(tokens, cotangent, w_first, w_second):
    tok_rows = tokens.shape[0]
    blk_local = w_first.shape[0]
    blk_width = w_first.shape[1]
    sub_width = blk_width // NB
    dp_count = lax.axis_size("dp")
    grad_scale = 1.0 / math.sqrt(tok_rows * dp_count)
    inputs = tokens.reshape(tok_rows, blk_local, blk_width)
    upstream = cotangent.reshape(tok_rows, blk_local, blk_width)
    hidden = jnp.einsum("tbi,bij->bjt", inputs, w_first, preferred_element_type=jnp.float32).astype(
        jnp.bfloat16
    )
    hidden = hidden.reshape(blk_local, NB, sub_width, tok_rows)
    second_view = w_second.reshape(blk_local, sub_width, NB, blk_width)
    moved = lax.all_to_all(hidden, "tensor", split_axis=1, concat_axis=0, tiled=True)
    active = jnp.maximum(moved, jnp.zeros((), jnp.bfloat16))
    second_term = jnp.einsum("bcjt,tco->cjbo", active, upstream, preferred_element_type=jnp.float32)
    second_term = second_term.reshape(blk_local, blk_width, blk_width) * grad_scale
    backed = jnp.einsum("tco,cjbo->bcjt", upstream, second_view, preferred_element_type=jnp.float32)
    masked = jnp.where(moved > 0, backed, jnp.zeros((), jnp.float32)).astype(jnp.bfloat16)
    returned = lax.all_to_all(masked, "tensor", split_axis=0, concat_axis=1, tiled=True)
    returned = returned.reshape(blk_local, blk_width, tok_rows)
    first_term = (
        jnp.einsum("tbi,bjt->bij", inputs, returned, preferred_element_type=jnp.float32)
        * grad_scale
    )
    grad_tokens = jnp.einsum("bjt,bij->tbi", returned, w_first, preferred_element_type=jnp.float32)
    grad_tokens = grad_tokens.astype(jnp.bfloat16).reshape(tok_rows, blk_local * blk_width)
    grad_first, grad_second = (
        lax.psum_scatter(first_term, "dp", scatter_dimension=1, tiled=True),
        lax.psum_scatter(second_term, "dp", scatter_dimension=1, tiled=True),
    )
    return (grad_tokens, grad_first, grad_second)


def solution(mesh):
    return jax.shard_map(
        shards,
        mesh=mesh,
        in_specs=(
            P(("groups", "dp"), "tensor"),
            P(("groups", "dp"), "tensor"),
            P("tensor", None, None),
            P("tensor", None, None),
        ),
        out_specs=(
            P(("groups", "dp"), "tensor"),
            P(("groups", "tensor"), "dp", None),
            P(("groups", "tensor"), "dp", None),
        ),
        check_vma=False,
    )
```

profile of v0, /device:TPU:0, one launch (start us, length us, event | category | flops | bytes accessed | tf_op | source)
XLA Modules:
  0.0 638.0 jit_solution(12787721479795042683)
XLA Ops:
  7.2 0.0 copy-start
  7.2 1.0 copy-done
  8.2 20.5 %fusion.5 = bf16[4,256,8192]{2,1,0:T(8,128)(2,1)} fusion(bf16[4,256,256]{2,1,0:T(8,128)(2,1)S(1)} %copy-done, bf16[1024,4,8,256]{3,2,1,0:T(8,128)(2,1)} %bitcast.56), kind=kOutput, calls=%fused_computation.7 | convolution fusion | flops 4303355904 | bytes 34078720 | tf_op jit(solution)/shard_map/tbi,bij->bjt/dot_general | solution.py:20
  28.8 13.9 %copy.30 = bf16[4,16,16,8192]{3,2,0,1:T(8,128)(2,1)} copy(bf16[4,16,16,8192]{3,2,1,0:T(8,128)(2,1)} %bitcast.53) | data formatting | bytes 33554432 | tf_op jit(solution)/shard_map/reshape | solution.py:23
  42.6 7.0 %all-to-all-start = ((bf16[4,16,16,8192]{3,2,0,1:T(8,128)(2,1)}), bf16[4,16,16,8192]{3,2,0,1:T(8,128)(2,1)}, u32[]{:S(2)}, u32[]{:S(2)}) async-start(bf16[4,16,16,8192]{3,2,0,1:T(8,128)(2,1)} %copy.30), calls=%async_computation | async-start | bytes 33554432 | tf_op jit(solution)/shard_map/all_to_all | solution.py:25
  49.6 27.9 %reshape.39 = bf16[8192,4,256]{2,1,0:T(4,128)(2,1)} reshape(bf16[8192,1024]{1,0:T(8,128)(2,1)} %param.5) | data formatting | bytes 33554432 | tf_op jit(solution)/shard_map/reshape | solution.py:19
  77.5 155.8 %all-to-all-done = bf16[4,16,16,8192]{3,2,0,1:T(8,128)(2,1)} async-done(((bf16[4,16,16,8192]{3,2,0,1:T(8,128)(2,1)}), bf16[4,16,16,8192]{3,2,0,1:T(8,128)(2,1)}, u32[]{:S(2)}, u32[]{:S(2)}) %all-to-all-start) | async-done | bytes 16777248 | tf_op jit(solution)/shard_map/all_to_all | solution.py:25
  233.3 7.4 %broadcast_compare_fusion = pred[4,16,16,8192]{3,2,0,1:T(8,128)(4,1)S(1)} fusion(bf16[4,16,16,8192]{3,2,0,1:T(8,128)(2,1)} %all-to-all-done), kind=kLoop, calls=%fused_computation.15 | loop fusion | flops 8388608 | bytes 25165824 | tf_op jit(solution)/shard_map/gt | solution.py:30
  240.7 25.3 %copy.71 = pred[4,4,4,16,8192]{4,0,1,3,2:T(4,128)(4,1)} copy(pred[4,4,4,16,8192]{4,3,0,2,1:T(8,128)(4,1)S(1)} %bitcast.54) | data formatting | bytes 16777216 | tf_op jit(solution)/shard_map/gt | solution.py:30
  265.9 20.9 %gt.15 = pred[16,4,16,8192]{3,0,2,1:T(8,128)(4,1)} reshape(pred[4,4,4,16,8192]{4,1,0,3,2:T(4,128)(4,1)} %bitcast.55) | data formatting | bytes 16777216 | tf_op jit(solution)/shard_map/gt | solution.py:30
  286.8 24.9 %fusion = bf16[16,4,16,8192]{3,0,2,1:T(8,128)(2,1)} fusion(pred[16,4,16,8192]{3,0,2,1:T(8,128)(4,1)} %gt.15, bf16[4,16,16,256]{3,2,1,0:T(8,128)(2,1)S(1)} %bitcast.62, bf16[8192,4,256,1]{2,1,0,3:T(4,128)(2,1)} %bitcast.58), kind=kOutput, calls=%fused_computation.1 | convolution fusion | flops 4311744512 | bytes 42467328 | tf_op jit(solution)/shard_map/tco,cjbo->bcjt/dot_general | solution.py:29
  311.7 18.5 %copy.33 = bf16[16,4,16,8192]{3,2,1,0:T(8,128)(2,1)} copy(bf16[16,4,16,8192]{3,0,2,1:T(8,128)(2,1)} %fusion) | data formatting | bytes 33554432 | tf_op jit(solution)/shard_map/convert_element_type | solution.py:30
  330.1 7.1 %all-to-all-start.1 = ((bf16[16,4,16,8192]{3,2,1,0:T(8,128)(2,1)}), bf16[16,4,16,8192]{3,2,1,0:T(8,128)(2,1)}, u32[]{:S(2)}, u32[]{:S(2)}) async-start(bf16[16,4,16,8192]{3,2,1,0:T(8,128)(2,1)} %copy.33), calls=%async_computation.1 | async-start | bytes 33554432 | tf_op jit(solution)/shard_map/all_to_all | solution.py:31
  337.2 0.2 all-reduce.3.cloned.1.call-start
  337.5 8.0 %broadcast_maximum_fusion = bf16[4,16,16,8192]{3,2,0,1:T(8,128)(2,1)S(1)} fusion(bf16[4,16,16,8192]{3,2,0,1:T(8,128)(2,1)} %all-to-all-done), kind=kLoop, calls=%fused_computation.14 | loop fusion | flops 8388608 | bytes 33554432 | tf_op jit(solution)/shard_map/max | solution.py:26
  345.4 6.6 %copy.37 = bf16[4,4,4,16,8192]{4,3,0,1,2:T(8,128)(2,1)} copy(bf16[4,4,4,16,8192]{4,3,0,2,1:T(8,128)(2,1)S(1)} %bitcast.51) | data formatting | bytes 33554432 | tf_op jit(solution)/shard_map/max | solution.py:26
  352.0 168.3 %all-to-all-done.1 = bf16[16,4,16,8192]{3,2,1,0:T(8,128)(2,1)} async-done(((bf16[16,4,16,8192]{3,2,1,0:T(8,128)(2,1)}), bf16[16,4,16,8192]{3,2,1,0:T(8,128)(2,1)}, u32[]{:S(2)}, u32[]{:S(2)}) %all-to-all-start.1) | async-done | bytes 16777248 | tf_op jit(solution)/shard_map/all_to_all | solution.py:31
  520.3 13.9 %copy.34 = bf16[4,4,4,16,8192]{4,3,2,0,1:T(8,128)(2,1)} copy(bf16[4,4,4,16,8192]{4,3,2,1,0:T(8,128)(2,1)} %bitcast.6) | data formatting | bytes 33554432 | tf_op jit(solution)/shard_map/all_to_all | solution.py:31
  534.2 12.9 %fusion.22 = f32[4,256,256]{1,2,0:T(8,128)S(1)} fusion(bf16[4,256,8192]{2,1,0:T(8,128)(2,1)} %bitcast.49, bf16[1024,4,8,256]{3,2,1,0:T(8,128)(2,1)} %bitcast.57), kind=kOutput, calls=%fused_computation.19 | convolution fusion | flops 4295229440 | bytes 34603008 | tf_op jit(solution)/shard_map/tbi,bjt->bij/dot_general | solution.py:34
  547.1 1.4 copy.36
  548.5 0.0 all-reduce.3.cloned.1.call-update
  548.5 0.0 reduce-scatter.2.cloned.1.call-start
  548.6 13.1 %fusion.16 = f32[4,16,16,256]{3,1,2,0:T(8,128)S(1)} fusion(bf16[16,4,16,8192]{3,2,0,1:T(8,128)(2,1)} %bitcast.60, bf16[8192,4,256,1]{2,1,0,3:T(4,128)(2,1)} %bitcast.59), kind=kOutput, calls=%fused_computation.17 | convolution fusion | flops 4295229440 | bytes 34603008 | tf_op jit(solution)/shard_map/bcjt,tco->cjbo/dot_general | solution.py:27
  561.7 1.6 copy.39
  563.3 0.0 reduce-scatter.2.cloned.1.call-update
  563.4 0.6 dynamic-slice
  564.6 13.9 %convolution_convert_fusion = bf16[4,8192,256]{1,2,0:T(8,128)(2,1)} fusion(bf16[4,256,256]{2,1,0:T(8,128)(2,1)S(1)} %copy-done, bf16[4,256,8192]{2,1,0:T(8,128)(2,1)} %bitcast.50), kind=kOutput, calls=%fused_computation.8 | convolution fusion | flops 4303355904 | bytes 34078720 | tf_op jit(solution)/shard_map/bjt,bij->tbi/dot_general | solution.py:37
  578.5 22.5 %copy.40 = bf16[8192,1024]{1,0:T(8,128)(2,1)} copy(bf16[8192,1024]{0,1:T(8,128)(2,1)} %bitcast.52) | data formatting | bytes 33554432
  601.0 0.7 all-reduce.3.cloned.1.call-done
  601.7 1.0 constant_dynamic-slice_fusion
  602.6 0.8 copy.41
  603.4 27.8 %reduce-scatter.2.cloned.1.call-done = f32[4,64,256]{2,1,0:T(8,128)} async-done(((f32[4,256,256]{2,1,0:T(8,128)}), f32[4,64,256]{2,1,0:T(8,128)}) %reduce-scatter.2.cloned.1.call-update) | async-done | bytes 262160 | tf_op jit(solution)/shard_map/reduce_scatter | solution.py:41
  (4 shorter events, 0.0 us)
Async XLA Ops:
  7.2 1.0 copy-start
  42.6 190.6 %all-to-all-start = ((bf16[4,16,16,8192]{3,2,0,1:T(8,128)(2,1)}), bf16[4,16,16,8192]{3,2,0,1:T(8,128)(2,1)}, u32[]{:S(2)}, u32[]{:S(2)}) async-start(bf16[4,16,16,8192]{3,2,0,1:T(8,128)(2,1)} %copy.30), calls=%async_computation | async-start | bytes 33554432 | tf_op jit(solution)/shard_map/all_to_all | solution.py:25
  240.7 46.1 %copy-start.1 = (bf16[4,256,256]{2,1,0:T(8,128)(2,1)S(1)}, bf16[4,256,256]{2,1,0:T(8,128)(2,1)}, u32[]{:S(2)}) copy-start(bf16[4,256,256]{2,1,0:T(8,128)(2,1)} %param.7) | copy-start | bytes 1572868
  330.1 190.2 %all-to-all-start.1 = ((bf16[16,4,16,8192]{3,2,1,0:T(8,128)(2,1)}), bf16[16,4,16,8192]{3,2,1,0:T(8,128)(2,1)}, u32[]{:S(2)}, u32[]{:S(2)}) async-start(bf16[16,4,16,8192]{3,2,1,0:T(8,128)(2,1)} %copy.33), calls=%async_computation.1 | async-start | bytes 33554432 | tf_op jit(solution)/shard_map/all_to_all | solution.py:31
  337.2 264.4 %all-reduce.3.cloned.1.call-start = ((), (), s32[]{:S(2)}) async-start(), calls=%async_computation.4 | async-start | bytes 2097152
  548.5 82.6 %reduce-scatter.2.cloned.1.call-start = ((), (), s32[]{:S(2)}) async-start(), calls=%async_computation.3 | async-start | bytes 1310720 | tf_op jit(solution)/shard_map/reduce_scatter | solution.py:41
  548.6 14.8 %copy-start.2 = (u32[32]{0:T(128)S(1)}, u32[32]{0:T(128)}, u32[]{:S(2)}) copy-start(u32[32]{0:T(128)} %constant.8) | copy-start | bytes 388
Sparse Core Ops, SparseCore 0:
  548.6 52.9 all-reduce.2
  604.6 26.5 reduce-scatter.1
where the time goes:
time: 641 us; the launch traced here: 638 us
  waiting for transfers between devices  353 us (55%)
  local copies, waits for them, and re-layouts  156 us (24%)
  matrix products  85.4 us (13%)
  other arithmetic  15.3 us (2%)
  between operations  14.8 us (2%)
  starting transfers between devices  14.3 us (2%)
    all_to_all x1, waiting for transfers between devices, shards(): lax.all_to_all(masked, 'tensor', split_axis=0, concat_axis=1, tiled=True)  168 us
    all_to_all x1, waiting for transfers between devices, shards(): lax.all_to_all(hidden, 'tensor', split_axis=1, concat_axis=0, tiled=True)  156 us
    gt x2, local copies, waits for them, and re-layouts, shards(): moved > 0  46.1 us
    reshape x1, local copies, waits for them, and re-layouts, shards(): upstream = cotangent.reshape(tok_rows, blk_local, blk_width)  27.9 us
    reduce_scatter x1, waiting for transfers between devices, shards(): lax.psum_scatter(second_term, 'dp', scatter_dimension=1, tiled=True)  27.8 us
    unnamed x10, local copies, waits for them, and re-layouts  25.8 us
    dot_general x1, matrix products, shards(): jnp.einsum('tco,cjbo->bcjt', upstream, second_view, preferred_element_typ...  24.9 us
    dot_general x1, matrix products, shards(): jnp.einsum('tbi,bij->bjt', inputs, w_first, preferred_element_type=jnp.fl...  20.5 us
  transfers between devices with their start and end apart: 4, of which 4 were waited for; matrix products, arithmetic and copies ran while one was open for 15% of the time, Pallas kernels for 0%

commit v1 on v0

v1 whole, which is shorter than its diff:
```python
import math

import jax
import jax.numpy as jnp
from jax import lax
from jax.sharding import PartitionSpec as P

NB = 16
CHUNKS = 4


def expanded_weights(w_first, w_second, n_dev):
    blk_local, bs, _ = w_first.shape
    sub = bs // NB
    eye = jnp.eye(blk_local, dtype=jnp.bool_)
    zero = jnp.zeros((), w_first.dtype)
    w1r = w_first.reshape(blk_local, bs, n_dev, blk_local, sub)
    w1p = jnp.where(
        eye[:, None, None, None, :, None], w1r[:, :, :, :, None, :], zero
    ).reshape(blk_local * bs, blk_local * bs)
    w2r = w_second.reshape(blk_local, sub, n_dev, blk_local, bs).transpose(0, 4, 2, 3, 1)
    w2p = jnp.where(
        eye[:, None, None, :, None, None], w2r[:, :, :, None, :, :], zero
    ).reshape(blk_local * bs, blk_local * bs)
    w1t = w_first.reshape(blk_local, bs, NB, sub).transpose(2, 3, 0, 1)
    w1tp = jnp.where(
        eye[None, :, None, :, None], w1t[:, None, :, :, :], zero
    ).reshape(blk_local * bs, blk_local * bs)
    return w1p, w2p, w1tp


def shards(tokens, cotangent, w_first, w_second):
    tok_rows = tokens.shape[0]
    blk_local, bs, _ = w_first.shape
    feat = blk_local * bs
    sub = bs // NB
    n_dev = lax.axis_size("tensor")
    dp_count = lax.axis_size("dp")
    grad_scale = 1.0 / math.sqrt(tok_rows * dp_count)
    w1p, w2p, w1tp = expanded_weights(w_first, w_second, n_dev)
    step = tok_rows // CHUNKS

    gf_acc = None
    gs_acc = None
    outs = []
    for k in range(CHUNKS):
        x = tokens[k * step:(k + 1) * step]
        cot = cotangent[k * step:(k + 1) * step]
        hidden = jnp.dot(x, w1p, preferred_element_type=jnp.float32).astype(jnp.bfloat16)
        moved = lax.all_to_all(
            hidden.reshape(step, n_dev, feat // n_dev), "tensor", 1, 1, tiled=True
        ).reshape(step, feat)
        active = jnp.maximum(moved, jnp.zeros((), jnp.bfloat16))
        gs = lax.dot_general(
            active, cot, (((0,), (0,)), ((), ())), preferred_element_type=jnp.float32
        )
        backed = jnp.dot(cot, w2p, preferred_element_type=jnp.float32)
        masked = jnp.where(moved > 0, backed, 0.0).astype(jnp.bfloat16)
        returned = lax.all_to_all(
            masked.reshape(step, n_dev, feat // n_dev), "tensor", 1, 1, tiled=True
        ).reshape(step, feat)
        gt = jnp.dot(returned, w1tp, preferred_element_type=jnp.float32).astype(jnp.bfloat16)
        outs.append(gt)
        gf = lax.dot_general(
            x, returned, (((0,), (0,)), ((), ())), preferred_element_type=jnp.float32
        )
        gf_acc = gf if gf_acc is None else gf_acc + gf
        gs_acc = gs if gs_acc is None else gs_acc + gs

    grad_tokens = jnp.concatenate(outs, axis=0)
    gf5 = gf_acc.reshape(blk_local, bs, NB, blk_local, sub)
    first_term = jnp.diagonal(gf5, axis1=0, axis2=3).transpose(3, 0, 1, 2)
    first_term = first_term.reshape(blk_local, bs, bs) * grad_scale
    gs6 = gs_acc.reshape(n_dev, blk_local, blk_local, sub, blk_local, bs)
    gsd = jnp.diagonal(gs6, axis1=1, axis2=4)
    second_term = gsd.transpose(4, 2, 0, 1, 3).reshape(blk_local, bs, bs) * grad_scale
    grad_first, grad_second = (
        lax.psum_scatter(first_term, "dp", scatter_dimension=1, tiled=True),
        lax.psum_scatter(second_term, "dp", scatter_dimension=1, tiled=True),
    )
    return (grad_tokens, grad_first, grad_second)


def solution(mesh):
    return jax.shard_map(
        shards,
        mesh=mesh,
        in_specs=(
            P(("groups", "dp"), "tensor"),
            P(("groups", "dp"), "tensor"),
            P("tensor", None, None),
            P("tensor", None, None),
        ),
        out_specs=(
            P(("groups", "dp"), "tensor"),
            P(("groups", "tensor"), "dp", None),
            P(("groups", "tensor"), "dp", None),
        ),
        check_vma=False,
    )
```

time: 641 us -> 590 us (0.920)
  local copies, waits for them, and re-layouts: 156 us -> 40.9 us
  matrix products: 85.4 us -> 178 us
  waiting for transfers between devices: 353 us -> 264 us
  other arithmetic: 15.3 us -> 43.8 us
  starting transfers between devices: 14.3 us -> 40.1 us
    all_to_all x2 -> x8, waiting for transfers between devices: 324 us -> 192 us  [the longest x4 136 us: shards(): lax.all_to_all(hidden.reshape(step, n_dev, feat // n_dev), 'tensor', 1, 1...]
    dot_general x5 -> x20, matrix products: 85.4 us -> 178 us  [the longest x4 38.4 us: shards(): lax.dot_general(active, cot, (((0,), (0,)), ((), ())), preferred_element_...]
    unnamed x3 -> x2, waiting for transfers between devices: 0.72 us -> 72.2 us
    gt x2 -> x0, local copies, waits for them, and re-layouts: 46.1 us -> none  [shards(): moved > 0]
    reduce_scatter x1 -> x0, waiting for transfers between devices: 27.8 us -> none  [shards(): lax.psum_scatter(second_term, 'dp', scatter_dimension=1, tiled=True)]
    all_to_all x2 -> x8, starting transfers between devices: 14.1 us -> 39.9 us  [the longest x4 20 us: shards(): lax.all_to_all(masked.reshape(step, n_dev, feat // n_dev), 'tensor', 1, 1...]
    reshape x2 -> x5, local copies, waits for them, and re-layouts: 41.8 us -> 22.4 us  [the longest x2 10.8 us: shards(): gs6 = gs_acc.reshape(n_dev, blk_local, blk_local, sub, blk_local, bs)]
    convert_element_type x1 -> x0, local copies, waits for them, and re-layouts: 18.5 us -> none  [shards(): jnp.where(moved > 0, backed, jnp.zeros((), jnp.float32))]
  transfers between devices with their start and end apart: 4 -> 9, of which waited for: 4 -> 8; matrix products, arithmetic and copies ran while one was open for 15% -> 36% of each run, Pallas kernels for 0% -> 0%
where the time goes in v1:
time: 590 us; the launch traced here: 582 us
  waiting for transfers between devices  264 us (45%)
  matrix products  178 us (30%)
  other arithmetic  43.8 us (7%)
  local copies, waits for them, and re-layouts  40.9 us (7%)
  starting transfers between devices  40.1 us (7%)
  between operations  15.3 us (3%)
    all_to_all x4, waiting for transfers between devices, shards(): lax.all_to_all(hidden.reshape(step, n_dev, feat // n_dev), 'tensor', 1, 1...  136 us
    unnamed x2, waiting for transfers between devices  72.2 us
    all_to_all x4, waiting for transfers between devices, shards(): lax.all_to_all(masked.reshape(step, n_dev, feat // n_dev), 'tensor', 1, 1...  55.3 us
    dot_general x4, matrix products, shards(): lax.dot_general(active, cot, (((0,), (0,)), ((), ())), preferred_element_...  38.4 us
    dot_general x4, matrix products, shards(): lax.dot_general(x, returned, (((0,), (0,)), ((), ())), preferred_element_...  36.4 us
    dot_general x4, matrix products, shards(): jnp.dot(x, w1p, preferred_element_type=jnp.float32).astype(jnp.bfloat16)  36.1 us
    dot_general x4, matrix products, shards(): backed = jnp.dot(cot, w2p, preferred_element_type=jnp.float32)  33.5 us
    dot_general x4, matrix products, shards(): jnp.dot(returned, w1tp, preferred_element_type=jnp.float32)  33.3 us
  transfers between devices with their start and end apart: 9, of which 8 were waited for; matrix products, arithmetic and copies ran while one was open for 36% of the time, Pallas kernels for 0%

profile of v1, /device:TPU:0, one launch (start us, length us, event | category | flops | bytes accessed | tf_op | source)
XLA Modules:
  0.0 581.8 jit_solution(16535600350372632069)
XLA Ops:
  12.5 9.1 %convolution_convert_fusion.3 = bf16[1024,2048]{1,0:T(8,128)(2,1)} fusion(bf16[1024,1024]{0,1:T(8,128)(2,1)S(1)} %bitcast.136, bf16[8192,1024]{1,0:T(8,128)(2,1)} %param.4), kind=kOutput, calls=%fused_computation.18 | convolution fusion | flops 4297064448 | bytes 10485760 | tf_op jit(solution)/shard_map/dot_general | solution.py:49
  26.5 9.3 %convolution_convert_fusion.5 = bf16[1024,2048]{1,0:T(8,128)(2,1)} fusion(bf16[1024,1024]{0,1:T(8,128)(2,1)} %bitcast.137, bf16[8192,1024]{1,0:T(8,128)(2,1)} %param.4), kind=kOutput, calls=%fused_computation.20 | convolution fusion | flops 4297064448 | bytes 10485760 | tf_op jit(solution)/shard_map/dot_general | solution.py:49
  35.8 39.5 %all-to-all-done.4 = bf16[2048,4,256]{0,2,1:T(8,128)(2,1)} async-done(((bf16[2048,4,256]{0,2,1:T(8,128)(2,1)}), bf16[2048,4,256]{0,2,1:T(8,128)(2,1)}, u32[]{:S(2)}, u32[]{:S(2)}) %all-to-all-start.4) | async-done | bytes 4194336 | tf_op jit(solution)/shard_map/all_to_all | solution.py:50
  80.4 9.4 %convolution_convert_fusion.7 = bf16[1024,2048]{1,0:T(8,128)(2,1)} fusion(bf16[1024,1024]{0,1:T(8,128)(2,1)} %bitcast.138, bf16[8192,1024]{1,0:T(8,128)(2,1)} %param.4), kind=kOutput, calls=%fused_computation.22 | convolution fusion | flops 4297064448 | bytes 10485760 | tf_op jit(solution)/shard_map/dot_general | solution.py:49
  89.7 38.8 %all-to-all-done.2 = bf16[2048,4,256]{0,2,1:T(8,128)(2,1)} async-done(((bf16[2048,4,256]{0,2,1:T(8,128)(2,1)}), bf16[2048,4,256]{0,2,1:T(8,128)(2,1)}, u32[]{:S(2)}, u32[]{:S(2)}) %all-to-all-start.2) | async-done | bytes 4194336 | tf_op jit(solution)/shard_map/all_to_all | solution.py:50
  139.7 8.3 %convolution_convert_fusion.1 = bf16[1024,2048]{1,0:T(8,128)(2,1)} fusion(bf16[1024,1024]{0,1:T(8,128)(2,1)S(1)} %bitcast.139, bf16[8192,1024]{1,0:T(8,128)(2,1)} %param.4), kind=kOutput, calls=%fused_computation.16 | convolution fusion | flops 4297064448 | bytes 10485760 | tf_op jit(solution)/shard_map/dot_general | solution.py:49
  148.0 33.7 %all-to-all-done = bf16[2048,4,256]{0,2,1:T(8,128)(2,1)} async-done(((bf16[2048,4,256]{0,2,1:T(8,128)(2,1)}), bf16[2048,4,256]{0,2,1:T(8,128)(2,1)}, u32[]{:S(2)}, u32[]{:S(2)}) %all-to-all-start) | async-done | bytes 4194336 | tf_op jit(solution)/shard_map/all_to_all | solution.py:50
  202.4 8.3 %fusion.1 = bf16[2048,1024]{0,1:T(8,128)(2,1)} fusion(pred[2048,4,256]{0,2,1:T(32,128)(4,1)S(1)} %broadcast_compare_fusion.1, bf16[1024,1024]{0,1:T(8,128)(2,1)S(1)} %bitcast.132, bf16[8192,1024]{1,0:T(8,128)(2,1)} %param.5), kind=kOutput, calls=%fused_computation.6 | convolution fusion | flops 4299161600 | bytes 12582912 | tf_op jit(solution)/shard_map/dot_general | solution.py:57
  210.7 24.3 %all-to-all-done.6 = bf16[2048,4,256]{0,2,1:T(8,128)(2,1)} async-done(((bf16[2048,4,256]{0,2,1:T(8,128)(2,1)}), bf16[2048,4,256]{0,2,1:T(8,128)(2,1)}, u32[]{:S(2)}, u32[]{:S(2)}) %all-to-all-start.6) | async-done | bytes 4194336 | tf_op jit(solution)/shard_map/all_to_all | solution.py:50
  249.1 8.5 %fusion.2 = bf16[2048,1024]{0,1:T(8,128)(2,1)} fusion(pred[2048,4,256]{0,2,1:T(32,128)(4,1)S(1)} %broadcast_compare_fusion.2, bf16[1024,1024]{0,1:T(8,128)(2,1)S(1)} %bitcast.133, bf16[8192,1024]{1,0:T(8,128)(2,1)} %param.5), kind=kOutput, calls=%fused_computation.8 | convolution fusion | flops 4299161600 | bytes 12582912 | tf_op jit(solution)/shard_map/dot_general | solution.py:57
  257.6 8.2 %fusion.10 = f32[1024,1024]{1,0:T(8,128)} fusion(bf16[2048,1024]{0,1:T(8,128)(2,1)S(1)} %bitcast.117, bf16[8192,1024]{1,0:T(8,128)(2,1)} %param.5), kind=kOutput, calls=%fused_computation.29 | convolution fusion | flops 4294967296 | bytes 12582912 | tf_op jit(solution)/shard_map/dot_general | solution.py:54
  265.8 22.3 %all-to-all-done.5 = bf16[2048,4,256]{0,2,1:T(8,128)(2,1)} async-done(((bf16[2048,4,256]{0,2,1:T(8,128)(2,1)}), bf16[2048,4,256]{0,2,1:T(8,128)(2,1)}, u32[]{:S(2)}, u32[]{:S(2)}) %all-to-all-start.5) | async-done | bytes 4194336 | tf_op jit(solution)/shard_map/all_to_all | solution.py:59
  288.1 5.3 all-to-all-start.3
  298.0 8.4 %fusion = bf16[2048,1024]{0,1:T(8,128)(2,1)} fusion(pred[2048,4,256]{0,2,1:T(32,128)(4,1)S(1)} %copy-done.6, bf16[1024,1024]{0,1:T(8,128)(2,1)S(1)} %bitcast.134, bf16[8192,1024]{1,0:T(8,128)(2,1)} %param.5), kind=kOutput, calls=%fused_computation.4 | convolution fusion | flops 4299161600 | bytes 12582912 | tf_op jit(solution)/shard_map/dot_general | solution.py:57
  306.4 8.3 %fusion.16 = f32[1024,1024]{1,0:T(8,128)} fusion(bf16[2048,1024]{0,1:T(8,128)(2,1)S(1)} %bitcast.115, bf16[8192,1024]{1,0:T(8,128)(2,1)} %param.5), kind=kOutput, calls=%fused_computation.35 | convolution fusion | flops 4294967296 | bytes 12582912 | tf_op jit(solution)/shard_map/dot_general | solution.py:54
  314.8 8.2 %fusion.4 = f32[1024,1024]{1,0:T(8,128)} fusion(bf16[2048,1024]{0,1:T(8,128)(2,1)S(1)} %bitcast.118, bf16[8192,1024]{1,0:T(8,128)(2,1)} %param.5), kind=kOutput, calls=%fused_computation.23 | convolution fusion | flops 4294967296 | bytes 12582912 | tf_op jit(solution)/shard_map/dot_general | solution.py:54
  323.0 18.6 %all-to-all-done.3 = bf16[2048,4,256]{0,2,1:T(8,128)(2,1)} async-done(((bf16[2048,4,256]{0,2,1:T(8,128)(2,1)}), bf16[2048,4,256]{0,2,1:T(8,128)(2,1)}, u32[]{:S(2)}, u32[]{:S(2)}) %all-to-all-start.3) | async-done | bytes 4194336 | tf_op jit(solution)/shard_map/all_to_all | solution.py:59
  346.5 13.7 %add_add_fusion = f32[1024,1024]{1,0:T(8,128)} fusion(f32[1024,1024]{1,0:T(8,128)} %fusion.4, f32[1024,1024]{1,0:T(8,128)} %fusion.10, f32[1024,1024]{1,0:T(8,128)} %fusion.16, bf16[2048,1024]{0,1:T(8,128)(2,1)} %bitcast.123, bf16[8192,1024]{1,0:T(8,128)(2,1)} %param.5), kind=kOutput, calls=%fused_computation.13 | convolution fusion | flops 4298113024 | bytes 25165824 | tf_op jit(solution)/shard_map/dot_general | solution.py:54
  360.1 5.6 reshape.154
  378.8 8.4 %fusion.3 = bf16[2048,1024]{0,1:T(8,128)(2,1)} fusion(pred[2048,4,256]{0,2,1:T(32,128)(4,1)S(1)} %broadcast_compare_fusion.3, bf16[1024,1024]{0,1:T(8,128)(2,1)S(1)} %bitcast.135, bf16[8192,1024]{1,0:T(8,128)(2,1)} %param.5), kind=kOutput, calls=%fused_computation.10 | convolution fusion | flops 4299161600 | bytes 12582912 | tf_op jit(solution)/shard_map/dot_general | solution.py:57
  387.1 10.0 %fusion.13 = f32[1024,1024]{1,0:T(8,128)} fusion(bf16[2048,1024]{0,1:T(8,128)(2,1)} %bitcast.21, bf16[8192,1024]{1,0:T(8,128)(2,1)} %param.4), kind=kOutput, calls=%fused_computation.32 | convolution fusion | flops 4294967296 | bytes 12582912 | tf_op jit(solution)/shard_map/dot_general | solution.py:64
  402.4 8.5 %convolution_convert_fusion.2 = bf16[2048,1024]{1,0:T(8,128)(2,1)} fusion(bf16[2048,1024]{0,1:T(8,128)(2,1)} %bitcast.21, bf16[1024,1024]{1,0:T(8,128)(2,1)S(1)} %bitcast.129), kind=kOutput, calls=%fused_computation.17 | convolution fusion | flops 4297064448 | bytes 10485760 | tf_op jit(solution)/shard_map/dot_general | solution.py:62
  410.9 8.5 %convolution_convert_fusion.4 = bf16[2048,1024]{1,0:T(8,128)(2,1)} fusion(bf16[2048,1024]{0,1:T(8,128)(2,1)} %bitcast.15, bf16[1024,1024]{1,0:T(8,128)(2,1)S(1)} %bitcast.130), kind=kOutput, calls=%fused_computation.19 | convolution fusion | flops 4297064448 | bytes 10485760 | tf_op jit(solution)/shard_map/dot_general | solution.py:62
  419.4 8.3 %fusion.19 = f32[1024,1024]{1,0:T(8,128)} fusion(bf16[2048,1024]{0,1:T(8,128)(2,1)} %bitcast.15, bf16[8192,1024]{1,0:T(8,128)(2,1)S(1)} %bitcast.142), kind=kOutput, calls=%fused_computation.38 | convolution fusion | flops 4294967296 | bytes 12582912 | tf_op jit(solution)/shard_map/dot_general | solution.py:64
  427.7 8.2 %fusion.7 = f32[1024,1024]{1,0:T(8,128)} fusion(bf16[2048,1024]{0,1:T(8,128)(2,1)} %bitcast.27, bf16[8192,1024]{1,0:T(8,128)(2,1)S(1)} %bitcast.142), kind=kOutput, calls=%fused_computation.26 | convolution fusion | flops 4294967296 | bytes 12582912 | tf_op jit(solution)/shard_map/dot_general | solution.py:64
  435.9 14.4 %all-to-all-done.1 = bf16[2048,4,256]{0,2,1:T(8,128)(2,1)} async-done(((bf16[2048,4,256]{0,2,1:T(8,128)(2,1)}), bf16[2048,4,256]{0,2,1:T(8,128)(2,1)}, u32[]{:S(2)}, u32[]{:S(2)}) %all-to-all-start.1) | async-done | bytes 4194336 | tf_op jit(solution)/shard_map/all_to_all | solution.py:59
  450.3 8.7 %convolution_convert_fusion.6 = bf16[2048,1024]{1,0:T(8,128)(2,1)} fusion(bf16[2048,1024]{0,1:T(8,128)(2,1)} %bitcast.7, bf16[1024,1024]{1,0:T(8,128)(2,1)S(1)} %bitcast.131), kind=kOutput, calls=%fused_computation.21 | convolution fusion | flops 4297064448 | bytes 10485760 | tf_op jit(solution)/shard_map/dot_general | solution.py:62
  459.1 10.0 %add_bitcast_fusion = f32[1024,1024]{0,1:T(8,128)} fusion(f32[1024,1024]{1,0:T(8,128)S(1)} %copy-done.16, f32[1024,1024]{1,0:T(8,128)S(1)} %copy-done.14, f32[1024,1024]{1,0:T(8,128)S(1)} %copy-done.15, bf16[2048,1024]{0,1:T(8,128)(2,1)} %bitcast.7, bf16[8192,1024]{1,0:T(8,128)(2,1)} %param.4), kind=kOutput, calls=%fused_computation.14 | convolution fusion | flops 4298113024 | bytes 25165824 | tf_op jit(solution)/shard_map/dot_general | solution.py:64
  469.1 5.6 reshape.153
  483.8 7.6 %convolution_convert_fusion = bf16[2048,1024]{1,0:T(8,128)(2,1)S(1)} fusion(bf16[2048,1024]{0,1:T(8,128)(2,1)} %bitcast.27, bf16[1024,1024]{1,0:T(8,128)(2,1)} %bitcast.128), kind=kOutput, calls=%fused_computation.15 | convolution fusion | flops 4297064448 | bytes 10485760 | tf_op jit(solution)/shard_map/dot_general | solution.py:62
  491.4 8.5 %pad_maximum_fusion = bf16[8192,1024]{1,0:T(8,128)(2,1)} fusion(bf16[2048,1024]{1,0:T(8,128)(2,1)S(1)} %convolution_convert_fusion, bf16[2048,1024]{1,0:T(8,128)(2,1)S(1)} %copy-done.3, bf16[2048,1024]{1,0:T(8,128)(2,1)S(1)} %copy-done.4, bf16[2048,1024]{1,0:T(8,128)(2,1)S(1)} %copy-done.5), kind=kLoop, calls=%fused_computation.2 | loop fusion | flops 67108864 | bytes 33554432 | tf_op jit(solution)/shard_map/concatenate | solution.py:70
  500.0 72.2 %all-reduce.5.cloned.1.call-done = (f32[4,256,256]{2,0,1:T(4,128)}, f32[4,256,256]{2,0,1:T(4,128)}) async-done(((f32[4,256,256]{2,0,1:T(4,128)}, f32[4,256,256]{2,0,1:T(4,128)}), (f32[4,256,256]{2,0,1:T(4,128)}, f32[4,256,256]{2,0,1:T(4,128)})) %all-reduce.5.cloned.1.call-update) | async-done | bytes 2097168
  (86 shorter events, 99.7 us)
Async XLA Ops:
  12.5 9.1 %copy-start.11 = (bf16[128,8,4,256]{3,1,2,0:T(8,128)(2,1)}, bf16[128,8,4,256]{3,1,2,0:T(8,128)(2,1)S(1)}, u32[]{:S(2)}) copy-start(bf16[128,8,4,256]{3,1,2,0:T(8,128)(2,1)S(1)} %copy.43) | copy-start | bytes 6291460
  21.6 53.7 %all-to-all-start.4 = ((bf16[2048,4,256]{0,2,1:T(8,128)(2,1)}), bf16[2048,4,256]{0,2,1:T(8,128)(2,1)}, u32[]{:S(2)}, u32[]{:S(2)}) async-start(bf16[2048,4,256]{0,2,1:T(8,128)(2,1)} %bitcast.125), calls=%async_computation.4 | async-start | bytes 8388608 | tf_op jit(solution)/shard_map/all_to_all | solution.py:50
  75.3 53.2 %all-to-all-start.2 = ((bf16[2048,4,256]{0,2,1:T(8,128)(2,1)}), bf16[2048,4,256]{0,2,1:T(8,128)(2,1)}, u32[]{:S(2)}, u32[]{:S(2)}) async-start(bf16[2048,4,256]{0,2,1:T(8,128)(2,1)} %bitcast.124), calls=%async_computation.2 | async-start | bytes 8388608 | tf_op jit(solution)/shard_map/all_to_all | solution.py:50
  128.6 53.1 %all-to-all-start = ((bf16[2048,4,256]{0,2,1:T(8,128)(2,1)}), bf16[2048,4,256]{0,2,1:T(8,128)(2,1)}, u32[]{:S(2)}, u32[]{:S(2)}) async-start(bf16[2048,4,256]{0,2,1:T(8,128)(2,1)} %bitcast.114), calls=%async_computation | async-start | bytes 8388608 | tf_op jit(solution)/shard_map/all_to_all | solution.py:50
  135.4 3.0 copy-start.13
  135.4 4.3 copy-start.12
  181.7 53.3 %all-to-all-start.6 = ((bf16[2048,4,256]{0,2,1:T(8,128)(2,1)}), bf16[2048,4,256]{0,2,1:T(8,128)(2,1)}, u32[]{:S(2)}, u32[]{:S(2)}) async-start(bf16[2048,4,256]{0,2,1:T(8,128)(2,1)} %bitcast.121), calls=%async_computation.6 | async-start | bytes 8388608 | tf_op jit(solution)/shard_map/all_to_all | solution.py:50
  199.0 3.4 copy-start.8
  235.0 53.1 %all-to-all-start.5 = ((bf16[2048,4,256]{0,2,1:T(8,128)(2,1)}), bf16[2048,4,256]{0,2,1:T(8,128)(2,1)}, u32[]{:S(2)}, u32[]{:S(2)}) async-start(bf16[2048,4,256]{0,2,1:T(8,128)(2,1)} %bitcast.122), calls=%async_computation.5 | async-start | bytes 8388608 | tf_op jit(solution)/shard_map/all_to_all | solution.py:59
  244.3 4.7 copy-start.9
  249.1 8.5 %copy-start.1 = (bf16[2048,4,256]{0,2,1:T(8,128)(2,1)S(1)}, bf16[2048,4,256]{0,2,1:T(8,128)(2,1)}, u32[]{:S(2)}) copy-start(bf16[2048,4,256]{0,2,1:T(8,128)(2,1)} %broadcast_maximum_fusion.1) | copy-start | bytes 12582916
  288.1 53.5 %all-to-all-start.3 = ((bf16[2048,4,256]{0,2,1:T(8,128)(2,1)}), bf16[2048,4,256]{0,2,1:T(8,128)(2,1)}, u32[]{:S(2)}, u32[]{:S(2)}) async-start(bf16[2048,4,256]{0,2,1:T(8,128)(2,1)} %bitcast.120), calls=%async_computation.3 | async-start | bytes 8388608 | tf_op jit(solution)/shard_map/all_to_all | solution.py:59
  293.4 4.6 copy-start.6
  293.4 4.6 copy-start.10
  298.0 8.4 %copy-start = (bf16[2048,4,256]{0,2,1:T(8,128)(2,1)S(1)}, bf16[2048,4,256]{0,2,1:T(8,128)(2,1)}, u32[]{:S(2)}) copy-start(bf16[2048,4,256]{0,2,1:T(8,128)(2,1)} %broadcast_maximum_fusion.2) | copy-start | bytes 12582916
  306.4 8.4 %copy-start.2 = (bf16[2048,4,256]{0,2,1:T(8,128)(2,1)S(1)}, bf16[2048,4,256]{0,2,1:T(8,128)(2,1)}, u32[]{:S(2)}) copy-start(bf16[2048,4,256]{0,2,1:T(8,128)(2,1)} %broadcast_maximum_fusion) | copy-start | bytes 12582916
  341.6 55.5 %all-to-all-start.7 = ((bf16[2048,4,256]{0,2,1:T(8,128)(2,1)}), bf16[2048,4,256]{0,2,1:T(8,128)(2,1)}, u32[]{:S(2)}, u32[]{:S(2)}) async-start(bf16[2048,4,256]{0,2,1:T(8,128)(2,1)} %bitcast.116), calls=%async_computation.7 | async-start | bytes 8388608 | tf_op jit(solution)/shard_map/all_to_all | solution.py:59
  397.1 5.2 copy-start.7
  397.1 53.2 %all-to-all-start.1 = ((bf16[2048,4,256]{0,2,1:T(8,128)(2,1)}), bf16[2048,4,256]{0,2,1:T(8,128)(2,1)}, u32[]{:S(2)}, u32[]{:S(2)}) async-start(bf16[2048,4,256]{0,2,1:T(8,128)(2,1)} %bitcast.119), calls=%async_computation.1 | async-start | bytes 8388608 | tf_op jit(solution)/shard_map/all_to_all | solution.py:59
  402.1 170.0 %all-reduce.5.cloned.1.call-start = ((), (), s32[]{:S(2)}) async-start(), calls=%async_computation.8 | async-start | bytes 4194304
  402.3 17.0 %slice-start = ((s8[16777216]{0:T(1024)(128)(4,1)}), s8[4194304]{0:T(1024)(128)(4,1)S(1)}, s32[]{:S(2)}) async-start(s8[16777216]{0:T(1024)(128)(4,1)} %bitcast.141), calls=%async_computation.9 | async-start | bytes 8388608
  402.4 17.0 %slice-start.1 = ((s8[16777216]{0:T(1024)(128)(4,1)}), s8[4194304]{0:T(1024)(128)(4,1)S(1)}, s32[]{:S(2)}) async-start(s8[16777216]{0:T(1024)(128)(4,1)} %bitcast.141), calls=%async_computation.10 | async-start | bytes 8388608
  410.8 8.5 %slice-start.2 = ((s8[16777216]{0:T(1024)(128)(4,1)}), s8[4194304]{0:T(1024)(128)(4,1)S(1)}, s32[]{:S(2)}) async-start(s8[16777216]{0:T(1024)(128)(4,1)} %bitcast.141), calls=%async_computation.11 | async-start | bytes 8388608
  410.8 8.6 %slice-start.3 = ((s8[16777216]{0:T(1024)(128)(4,1)}), s8[4194304]{0:T(1024)(128)(4,1)S(1)}, s32[]{:S(2)}) async-start(s8[16777216]{0:T(1024)(128)(4,1)} %bitcast.141), calls=%async_computation.12 | async-start | bytes 8388608
  450.3 8.7 %copy-start.14 = (f32[1024,1024]{1,0:T(8,128)S(1)}, f32[1024,1024]{1,0:T(8,128)}, u32[]{:S(2)}) copy-start(f32[1024,1024]{1,0:T(8,128)} %fusion.13) | copy-start | bytes 12582916
  450.3 8.7 %copy-start.15 = (f32[1024,1024]{1,0:T(8,128)S(1)}, f32[1024,1024]{1,0:T(8,128)}, u32[]{:S(2)}) copy-start(f32[1024,1024]{1,0:T(8,128)} %fusion.19) | copy-start | bytes 12582916
  450.3 8.7 %copy-start.16 = (f32[1024,1024]{1,0:T(8,128)S(1)}, f32[1024,1024]{1,0:T(8,128)}, u32[]{:S(2)}) copy-start(f32[1024,1024]{1,0:T(8,128)} %fusion.7) | copy-start | bytes 12582916
  483.8 7.6 %copy-start.3 = (bf16[2048,1024]{1,0:T(8,128)(2,1)S(1)}, bf16[2048,1024]{1,0:T(8,128)(2,1)}, u32[]{:S(2)}) copy-start(bf16[2048,1024]{1,0:T(8,128)(2,1)} %convolution_convert_fusion.2) | copy-start | bytes 12582916
  483.8 7.6 %copy-start.4 = (bf16[2048,1024]{1,0:T(8,128)(2,1)S(1)}, bf16[2048,1024]{1,0:T(8,128)(2,1)}, u32[]{:S(2)}) copy-start(bf16[2048,1024]{1,0:T(8,128)(2,1)} %convolution_convert_fusion.4) | copy-start | bytes 12582916
  483.8 7.6 %copy-start.5 = (bf16[2048,1024]{1,0:T(8,128)(2,1)S(1)}, bf16[2048,1024]{1,0:T(8,128)(2,1)}, u32[]{:S(2)}) copy-start(bf16[2048,1024]{1,0:T(8,128)(2,1)} %convolution_convert_fusion.6) | copy-start | bytes 12582916
Sparse Core Ops, SparseCore 0:
  483.9 88.1 all-reduce.4

commit v2 on v1

v2 whole, which is shorter than its diff:
```python
import math

import jax
import jax.numpy as jnp
from jax import lax
from jax.sharding import PartitionSpec as P

NB = 16
CHUNKS = 4


def expanded_weights(w_first, w_second, n_dev, order):
    blk_local, bs, _ = w_first.shape
    sub = bs // NB
    feat = blk_local * bs
    eye = jnp.eye(blk_local, dtype=jnp.bool_)
    zero = jnp.zeros((), w_first.dtype)
    w1r = jnp.take(w_first.reshape(blk_local, bs, n_dev, blk_local, sub), order, axis=2)
    w1p = jnp.where(
        eye[:, None, None, None, :, None], w1r[:, :, :, :, None, :], zero
    ).reshape(feat, feat)
    w2r = jnp.take(w_second.reshape(blk_local, sub, n_dev, blk_local, bs), order, axis=2)
    w2r = w2r.transpose(0, 4, 2, 3, 1)
    w2p = jnp.where(
        eye[:, None, None, :, None, None], w2r[:, :, :, None, :, :], zero
    ).reshape(feat, feat)
    w1t = w1r.transpose(2, 3, 4, 0, 1)
    w1tp = jnp.where(
        eye[None, None, :, None, :, None], w1t[:, :, None, :, :, :], zero
    ).reshape(feat, feat)
    return w1p, w2p, w1tp


def exchange(pieces, n_dev):
    outs = [pieces[0]]
    for m in range(1, n_dev):
        outs.append(lax.ppermute(pieces[m], "tensor", [(i, i ^ m) for i in range(n_dev)]))
    return outs


def shards(tokens, cotangent, w_first, w_second):
    tok_rows = tokens.shape[0]
    blk_local, bs, _ = w_first.shape
    feat = blk_local * bs
    sub = bs // NB
    part = feat // lax.axis_size("tensor")
    n_dev = lax.axis_size("tensor")
    dp_count = lax.axis_size("dp")
    grad_scale = 1.0 / math.sqrt(tok_rows * dp_count)
    idx = lax.axis_index("tensor")
    order = jnp.bitwise_xor(idx, jnp.arange(n_dev, dtype=idx.dtype))
    w1p, w2p, w1tp = expanded_weights(w_first, w_second, n_dev, order)
    step = tok_rows // CHUNKS

    gf_acc = None
    gs_acc = None
    outs = []
    for k in range(CHUNKS):
        x = tokens[k * step:(k + 1) * step]
        cot = cotangent[k * step:(k + 1) * step]
        hidden = jnp.dot(x, w1p, preferred_element_type=jnp.float32).astype(jnp.bfloat16)
        backed = jnp.dot(cot, w2p, preferred_element_type=jnp.float32)
        moved = exchange([hidden[:, m * part:(m + 1) * part] for m in range(n_dev)], n_dev)
        masked = [
            jnp.where(moved[m] > 0, backed[:, m * part:(m + 1) * part], 0.0).astype(jnp.bfloat16)
            for m in range(n_dev)
        ]
        active = jnp.maximum(jnp.concatenate(moved, axis=1), jnp.zeros((), jnp.bfloat16))
        gs = lax.dot_general(
            active, cot, (((0,), (0,)), ((), ())), preferred_element_type=jnp.float32
        )
        returned = jnp.concatenate(exchange(masked, n_dev), axis=1)
        gt = jnp.dot(returned, w1tp, preferred_element_type=jnp.float32).astype(jnp.bfloat16)
        outs.append(gt)
        gf = lax.dot_general(
            x, returned, (((0,), (0,)), ((), ())), preferred_element_type=jnp.float32
        )
        gf_acc = gf if gf_acc is None else gf_acc + gf
        gs_acc = gs if gs_acc is None else gs_acc + gs

    grad_tokens = jnp.concatenate(outs, axis=0)
    gs6 = gs_acc.reshape(n_dev, blk_local, blk_local, sub, blk_local, bs)
    gsd = jnp.take(jnp.diagonal(gs6, axis1=1, axis2=4), order, axis=0)
    second_term = gsd.transpose(2, 0, 1, 4, 3).reshape(bs, blk_local, bs) * grad_scale
    grad_second = lax.psum_scatter(second_term, "dp", scatter_dimension=0, tiled=True)
    gf_acc, grad_second = lax.optimization_barrier((gf_acc, grad_second))
    gf6 = gf_acc.reshape(blk_local, bs, n_dev, blk_local, blk_local, sub)
    gfd = jnp.take(jnp.diagonal(gf6, axis1=0, axis2=4), order, axis=1)
    first_term = gfd.transpose(0, 4, 1, 2, 3).reshape(bs, blk_local, bs) * grad_scale
    grad_first = lax.psum_scatter(first_term, "dp", scatter_dimension=0, tiled=True)
    return (grad_tokens, grad_first.transpose(1, 0, 2), grad_second.transpose(1, 0, 2))


def solution(mesh):
    return jax.shard_map(
        shards,
        mesh=mesh,
        in_specs=(
            P(("groups", "dp"), "tensor"),
            P(("groups", "dp"), "tensor"),
            P("tensor", None, None),
            P("tensor", None, None),
        ),
        out_specs=(
            P(("groups", "dp"), "tensor"),
            P(("groups", "tensor"), "dp", None),
            P(("groups", "tensor"), "dp", None),
        ),
        check_vma=False,
    )
```

time: 590 us -> 517 us (0.88)
  waiting for transfers between devices: 264 us -> 239 us
  starting transfers between devices: 40.1 us -> 19.6 us
  matrix products: 178 us -> 159 us
  other arithmetic: 43.8 us -> 28.1 us
  local copies, waits for them, and re-layouts: 40.9 us -> 51.4 us
    all_to_all x8 -> x0, waiting for transfers between devices: 192 us -> none  [the longest x4 136 us: shards(): lax.all_to_all(hidden.reshape(step, n_dev, feat // n_dev), 'tensor', 1, 1...]
    ppermute x0 -> x24, waiting for transfers between devices: none -> 174 us  [exchange(): lax.ppermute(pieces[m], 'tensor', [(i, i ^ m) for i in range(n_dev)])]
    all_to_all x8 -> x0, starting transfers between devices: 39.9 us -> none  [the longest x4 20 us: shards(): lax.all_to_all(masked.reshape(step, n_dev, feat // n_dev), 'tensor', 1, 1...]
    ppermute x0 -> x24, starting transfers between devices: none -> 19.1 us  [exchange(): lax.ppermute(pieces[m], 'tensor', [(i, i ^ m) for i in range(n_dev)])]
    max x4 -> x0, other arithmetic: 18 us -> none  [shards(): active = jnp.maximum(moved, jnp.zeros((), jnp.bfloat16))]
    slice x0 -> x4, other arithmetic: none -> 15.4 us  [shards(): hidden[:, m * part:(m + 1) * part]]
    gt x4 -> x0, other arithmetic: 14.7 us -> none  [shards(): masked = jnp.where(moved > 0, backed, 0.0).astype(jnp.bfloat16)]
    dot_general x4, matrix products: 33.3 us -> 23.3 us  [shards(): jnp.dot(returned, w1tp, preferred_element_type=jnp.float32)]
  transfers between devices with their start and end apart: 9 -> 26, of which waited for: 8 -> 13; matrix products, arithmetic and copies ran while one was open for 36% -> 31% of each run, Pallas kernels for 0% -> 0%
where the time goes in v2:
time: 517 us; the launch traced here: 512 us
  waiting for transfers between devices  239 us (46%)
  matrix products  159 us (31%)
  local copies, waits for them, and re-layouts  51.4 us (10%)
  other arithmetic  28.1 us (5%)
  starting transfers between devices  19.6 us (4%)
  between operations  15.6 us (3%)
    ppermute x24, waiting for transfers between devices, exchange(): lax.ppermute(pieces[m], 'tensor', [(i, i ^ m) for i in range(n_dev)])  174 us
    unnamed x4, waiting for transfers between devices  65 us
    dot_general x4, matrix products, shards(): lax.dot_general(active, cot, (((0,), (0,)), ((), ())), preferred_element_...  41.2 us
    dot_general x4, matrix products, shards(): lax.dot_general(x, returned, (((0,), (0,)), ((), ())), preferred_element_...  36.5 us
    dot_general x4, matrix products, shards(): backed = jnp.dot(cot, w2p, preferred_element_type=jnp.float32)  29.4 us
    dot_general x4, matrix products, shards(): jnp.dot(x, w1p, preferred_element_type=jnp.float32).astype(jnp.bfloat16)  28.4 us
    dot_general x4, matrix products, shards(): jnp.dot(returned, w1tp, preferred_element_type=jnp.float32)  23.3 us
    ppermute x24, starting transfers between devices, exchange(): lax.ppermute(pieces[m], 'tensor', [(i, i ^ m) for i in range(n_dev)])  19.1 us
  transfers between devices with their start and end apart: 26, of which 13 were waited for; matrix products, arithmetic and copies ran while one was open for 31% of the time, Pallas kernels for 0%

profile of v2, /device:TPU:0, one launch (start us, length us, event | category | flops | bytes accessed | tf_op | source)
XLA Modules:
  0.0 512.5 jit_solution(13969275779868941734)
XLA Ops:
  14.5 7.2 %convert_bitcast_fusion.3 = bf16[2048,1024]{0,1:T(8,128)(2,1)S(1)} fusion(bf16[1024,1024]{0,1:T(8,128)(2,1)S(1)} %bitcast.88, bf16[8192,1024]{1,0:T(8,128)(2,1)} %param.4), kind=kOutput, calls=%fused_computation.54 | convolution fusion | flops 4297064448 | bytes 10485760 | tf_op jit(solution)/shard_map/dot_general | solution.py:61
  27.1 7.0 %convert_bitcast_fusion.2 = bf16[2048,1024]{0,1:T(8,128)(2,1)S(1)} fusion(bf16[1024,1024]{0,1:T(8,128)(2,1)S(1)} %bitcast.89, bf16[8192,1024]{1,0:T(8,128)(2,1)} %param.4), kind=kOutput, calls=%fused_computation.53 | convolution fusion | flops 4297064448 | bytes 10485760 | tf_op jit(solution)/shard_map/dot_general | solution.py:61
  37.9 7.8 %convolution_bitcast_fusion.3 = bf16[2048,1024]{0,1:T(8,128)(2,1)S(1)} fusion(bf16[1024,1024]{0,1:T(8,128)(2,1)S(1)} %bitcast.92, bf16[8192,1024]{1,0:T(8,128)(2,1)} %param.5), kind=kOutput, calls=%fused_computation.10 | convolution fusion | flops 4294967296 | bytes 10485760 | tf_op jit(solution)/shard_map/dot_general | solution.py:62
  45.7 7.1 %convolution_bitcast_fusion.2 = bf16[2048,1024]{0,1:T(8,128)(2,1)S(1)} fusion(bf16[1024,1024]{0,1:T(8,128)(2,1)S(1)} %bitcast.93, bf16[8192,1024]{1,0:T(8,128)(2,1)} %param.5), kind=kOutput, calls=%fused_computation.9 | convolution fusion | flops 4294967296 | bytes 10485760 | tf_op jit(solution)/shard_map/dot_general | solution.py:62
  52.8 7.1 %convert_bitcast_fusion.1 = bf16[2048,1024]{0,1:T(8,128)(2,1)S(1)} fusion(bf16[1024,1024]{0,1:T(8,128)(2,1)S(1)} %bitcast.90, bf16[8192,1024]{1,0:T(8,128)(2,1)} %param.4), kind=kOutput, calls=%fused_computation.52 | convolution fusion | flops 4297064448 | bytes 10485760 | tf_op jit(solution)/shard_map/dot_general | solution.py:61
  59.9 7.5 %convolution_bitcast_fusion.1 = bf16[2048,1024]{0,1:T(8,128)(2,1)S(1)} fusion(bf16[1024,1024]{0,1:T(8,128)(2,1)S(1)} %bitcast.94, bf16[8192,1024]{1,0:T(8,128)(2,1)} %param.5), kind=kOutput, calls=%fused_computation.8 | convolution fusion | flops 4294967296 | bytes 10485760 | tf_op jit(solution)/shard_map/dot_general | solution.py:62
  67.4 7.1 %convert_bitcast_fusion = bf16[2048,1024]{0,1:T(8,128)(2,1)S(1)} fusion(bf16[1024,1024]{0,1:T(8,128)(2,1)S(1)} %bitcast.91, bf16[8192,1024]{1,0:T(8,128)(2,1)} %param.4), kind=kOutput, calls=%fused_computation.51 | convolution fusion | flops 4297064448 | bytes 10485760 | tf_op jit(solution)/shard_map/dot_general | solution.py:61
  78.5 7.0 %convolution_bitcast_fusion = bf16[2048,1024]{0,1:T(8,128)(2,1)S(1)} fusion(bf16[1024,1024]{0,1:T(8,128)(2,1)S(1)} %bitcast.95, bf16[8192,1024]{1,0:T(8,128)(2,1)} %param.5), kind=kOutput, calls=%fused_computation.7 | convolution fusion | flops 4294967296 | bytes 10485760 | tf_op jit(solution)/shard_map/dot_general | solution.py:62
  92.1 10.1 %fusion = f32[1024,1024]{1,0:T(8,128)} fusion(bf16[2048,256]{0,1:T(8,128)(2,1)} %collective-permute-done.4, bf16[2048,256]{0,1:T(8,128)(2,1)} %collective-permute-done.2, bf16[2048,256]{0,1:T(8,128)(2,1)} %collective-permute-done, bf16[2048,256]{0,1:T(8,128)(2,1)} %get-tuple-element.26, bf16[8192,1024]{1,0:T(8,128)(2,1)} %param.5), kind=kOutput, calls=%fused_computation.16 | convolution fusion | flops 4315938816 | bytes 12582912 | tf_op jit(solution)/shard_map/dot_general | solution.py:69
  103.3 15.0 %collective-permute-done.8 = bf16[2048,256]{0,1:T(8,128)(2,1)} collective-permute-done((bf16[2048,256]{0,1:T(8,128)(2,1)}, bf16[2048,256]{0,1:T(8,128)(2,1)}, u32[]{:S(2)}, u32[]{:S(2)}) %collective-permute-start.8) | collective-permute-done | bytes 1048608 | tf_op jit(solution)/shard_map/ppermute | solution.py:37
  124.8 10.0 %fusion.7 = f32[1024,1024]{1,0:T(8,128)} fusion(bf16[2048,256]{0,1:T(8,128)(2,1)} %collective-permute-done.10, bf16[2048,256]{0,1:T(8,128)(2,1)} %collective-permute-done.8, bf16[2048,256]{0,1:T(8,128)(2,1)} %collective-permute-done.6, bf16[2048,256]{0,1:T(8,128)(2,1)} %get-tuple-element.21, bf16[8192,1024]{1,0:T(8,128)(2,1)} %param.5), kind=kOutput, calls=%fused_computation.24 | convolution fusion | flops 4315938816 | bytes 12582912 | tf_op jit(solution)/shard_map/dot_general | solution.py:69
  134.8 6.0 %collective-permute-done.14 = bf16[2048,256]{0,1:T(8,128)(2,1)} collective-permute-done((bf16[2048,256]{0,1:T(8,128)(2,1)}, bf16[2048,256]{0,1:T(8,128)(2,1)}, u32[]{:S(2)}, u32[]{:S(2)}) %collective-permute-start.14) | collective-permute-done | bytes 1048608 | tf_op jit(solution)/shard_map/ppermute | solution.py:37
  140.7 22.0 %collective-permute-done.16 = bf16[2048,256]{0,1:T(8,128)(2,1)S(1)} collective-permute-done((bf16[2048,256]{0,1:T(8,128)(2,1)S(1)}, bf16[2048,256]{0,1:T(8,128)(2,1)S(1)}, u32[]{:S(2)}, u32[]{:S(2)}) %collective-permute-start.16) | collective-permute-done | bytes 1048608 | tf_op jit(solution)/shard_map/ppermute | solution.py:37
  166.6 9.3 %fusion.14 = f32[1024,1024]{1,0:T(8,128)} fusion(bf16[2048,256]{0,1:T(8,128)(2,1)S(1)} %collective-permute-done.16, bf16[2048,256]{0,1:T(8,128)(2,1)} %collective-permute-done.14, bf16[2048,256]{0,1:T(8,128)(2,1)} %collective-permute-done.12, bf16[2048,256]{0,1:T(8,128)(2,1)S(1)} %get-tuple-element.31, bf16[8192,1024]{1,0:T(8,128)(2,1)} %param.5), kind=kOutput, calls=%fused_computation.32 | convolution fusion | flops 4315938816 | bytes 12582912 | tf_op jit(solution)/shard_map/dot_general | solution.py:69
  176.0 9.6 %collective-permute-done.20 = bf16[2048,256]{0,1:T(8,128)(2,1)S(1)} collective-permute-done((bf16[2048,256]{0,1:T(8,128)(2,1)S(1)}, bf16[2048,256]{0,1:T(8,128)(2,1)S(1)}, u32[]{:S(2)}, u32[]{:S(2)}) %collective-permute-start.20) | collective-permute-done | bytes 1048608 | tf_op jit(solution)/shard_map/ppermute | solution.py:37
  185.6 22.1 %collective-permute-done.22 = bf16[2048,256]{0,1:T(8,128)(2,1)S(1)} collective-permute-done((bf16[2048,256]{0,1:T(8,128)(2,1)S(1)}, bf16[2048,256]{0,1:T(8,128)(2,1)S(1)}, u32[]{:S(2)}, u32[]{:S(2)}) %collective-permute-start.22) | collective-permute-done | bytes 1048608 | tf_op jit(solution)/shard_map/ppermute | solution.py:37
  210.4 11.8 %add_add_fusion = f32[1024,1024]{1,0:T(8,128)} fusion(f32[1024,1024]{1,0:T(8,128)} %fusion.14, f32[1024,1024]{1,0:T(8,128)S(1)} %copy-done.42, f32[1024,1024]{1,0:T(8,128)} %fusion.7, bf16[8192,1024]{1,0:T(8,128)(2,1)} %param.5, bf16[2048,256]{0,1:T(8,128)(2,1)} %copy-done.21, bf16[2048,256]{0,1:T(8,128)(2,1)S(1)} %collective-permute-done.20, ...), kind=kOutput, calls=%fused_computation.49 | convolution fusion | flops 4319084544 | bytes 25165824 | tf_op jit(solution)/shard_map/dot_general | solution.py:69
  247.1 44.5 %all-reduce.5.cloned.1.call-done = f32[256,4,256]{2,1,0:T(4,128)} async-done(((f32[256,4,256]{2,1,0:T(4,128)}), f32[256,4,256]{2,1,0:T(4,128)}) %all-reduce.5.cloned.1.call-update) | async-done | bytes 1048592
  294.9 7.8 %fusion.40 = f32[1024,1024]{1,0:T(8,128)S(1)} fusion(bf16[8192,1024]{1,0:T(8,128)(2,1)} %param.4, bf16[2048,256]{0,1:T(8,128)(2,1)} %collective-permute-done.11, bf16[2048,256]{0,1:T(8,128)(2,1)} %collective-permute-done.9, bf16[2048,256]{0,1:T(8,128)(2,1)} %collective-permute-done.7, bf16[2048,256]{0,1:T(8,128)(2,1)S(1)} %copy-done.10), kind=kOutput, calls=%fused_computation.71 | convolution fusion | flops 4311744512 | bytes 12582912 | tf_op jit(solution)/shard_map/dot_general | solution.py:75
  303.6 6.3 %collective-permute-done.3 = bf16[2048,256]{0,1:T(8,128)(2,1)} collective-permute-done((bf16[2048,256]{0,1:T(8,128)(2,1)}, bf16[2048,256]{0,1:T(8,128)(2,1)}, u32[]{:S(2)}, u32[]{:S(2)}) %collective-permute-start.3) | collective-permute-done | bytes 1048608 | tf_op jit(solution)/shard_map/ppermute | solution.py:37
  309.9 21.8 %collective-permute-done.5 = bf16[2048,256]{0,1:T(8,128)(2,1)S(1)} collective-permute-done((bf16[2048,256]{0,1:T(8,128)(2,1)S(1)}, bf16[2048,256]{0,1:T(8,128)(2,1)S(1)}, u32[]{:S(2)}, u32[]{:S(2)}) %collective-permute-start.5) | collective-permute-done | bytes 1048608 | tf_op jit(solution)/shard_map/ppermute | solution.py:37
  333.2 7.5 %fusion.45 = f32[1024,1024]{1,0:T(8,128)S(1)} fusion(bf16[8192,1024]{1,0:T(8,128)(2,1)} %param.4, bf16[2048,256]{0,1:T(8,128)(2,1)S(1)} %collective-permute-done.5, bf16[2048,256]{0,1:T(8,128)(2,1)} %collective-permute-done.3, bf16[2048,256]{0,1:T(8,128)(2,1)} %collective-permute-done.1, bf16[2048,256]{0,1:T(8,128)(2,1)S(1)} %copy-done.9), kind=kOutput, calls=%fused_computation.76 | convolution fusion | flops 4311744512 | bytes 12582912 | tf_op jit(solution)/shard_map/dot_general | solution.py:75
  341.1 13.6 %collective-permute-done.15 = bf16[2048,256]{0,1:T(8,128)(2,1)S(1)} collective-permute-done((bf16[2048,256]{0,1:T(8,128)(2,1)}, bf16[2048,256]{0,1:T(8,128)(2,1)S(1)}, u32[]{:S(2)}, u32[]{:S(2)}) %collective-permute-start.15) | collective-permute-done | bytes 1048608 | tf_op jit(solution)/shard_map/ppermute | solution.py:37
  354.7 21.9 %collective-permute-done.17 = bf16[2048,256]{0,1:T(8,128)(2,1)S(1)} collective-permute-done((bf16[2048,256]{0,1:T(8,128)(2,1)S(1)}, bf16[2048,256]{0,1:T(8,128)(2,1)S(1)}, u32[]{:S(2)}, u32[]{:S(2)}) %collective-permute-start.17) | collective-permute-done | bytes 1048608 | tf_op jit(solution)/shard_map/ppermute | solution.py:37
  376.7 9.1 %fusion.35 = f32[1024,1024]{1,0:T(8,128)} fusion(bf16[8192,1024]{1,0:T(8,128)(2,1)} %param.4, bf16[2048,256]{0,1:T(8,128)(2,1)S(1)} %collective-permute-done.17, bf16[2048,256]{0,1:T(8,128)(2,1)S(1)} %collective-permute-done.15, bf16[2048,256]{0,1:T(8,128)(2,1)S(1)} %collective-permute-done.13, bf16[2048,256]{0,1:T(8,128)(2,1)S(1)} %copy-done.12), kind=kOutput, calls=%fused_computation.66 | convolution fusion | flops 4311744512 | bytes 12582912 | tf_op jit(solution)/shard_map/dot_general | solution.py:75
  385.8 13.9 %collective-permute-done.21 = bf16[2048,256]{0,1:T(8,128)(2,1)S(1)} collective-permute-done((bf16[2048,256]{0,1:T(8,128)(2,1)S(1)}, bf16[2048,256]{0,1:T(8,128)(2,1)S(1)}, u32[]{:S(2)}, u32[]{:S(2)}) %collective-permute-start.21) | collective-permute-done | bytes 1048608 | tf_op jit(solution)/shard_map/ppermute | solution.py:37
  399.7 21.9 %collective-permute-done.23 = bf16[2048,256]{0,1:T(8,128)(2,1)S(1)} collective-permute-done((bf16[2048,256]{0,1:T(8,128)(2,1)S(1)}, bf16[2048,256]{0,1:T(8,128)(2,1)S(1)}, u32[]{:S(2)}, u32[]{:S(2)}) %collective-permute-start.23) | collective-permute-done | bytes 1048608 | tf_op jit(solution)/shard_map/ppermute | solution.py:37
  422.6 12.1 %add_bitcast_fusion = f32[1024,1024]{0,1:T(8,128)} fusion(f32[1024,1024]{1,0:T(8,128)} %fusion.35, f32[1024,1024]{1,0:T(8,128)S(1)} %fusion.45, f32[1024,1024]{1,0:T(8,128)S(1)} %fusion.40, bf16[8192,1024]{1,0:T(8,128)(2,1)} %param.4, bf16[2048,256]{0,1:T(8,128)(2,1)S(1)} %collective-permute-done.23, bf16[2048,256]{0,1:T(8,128)(2,1)S(1)} %collective-permute-done.21, ...), kind=kOutput, calls=%fused_computation.50 | convolution fusion | flops 4314890240 | bytes 25165824 | tf_op jit(solution)/shard_map/dot_general | solution.py:75
  451.2 6.8 %convolution_convert_fusion.3 = bf16[2048,1024]{1,0:T(8,128)(2,1)S(1)} fusion(bf16[1024,1024]{1,0:T(8,128)(2,1)S(1)} %bitcast.84, bf16[2048,256]{0,1:T(8,128)(2,1)} %copy-done.28, bf16[2048,256]{0,1:T(8,128)(2,1)} %collective-permute-done.3, bf16[2048,256]{0,1:T(8,128)(2,1)} %collective-permute-done.1, bf16[2048,256]{0,1:T(8,128)(2,1)} %get-tuple-element.27), kind=kOutput, calls=%fused_computation.58 | convolution fusion | flops 4313841664 | bytes 10485760 | tf_op jit(solution)/shard_map/dot_general | solution.py:73
  458.1 6.6 %convolution_convert_fusion.2 = bf16[2048,1024]{1,0:T(8,128)(2,1)S(1)} fusion(bf16[1024,1024]{1,0:T(8,128)(2,1)S(1)} %bitcast.85, bf16[2048,256]{0,1:T(8,128)(2,1)} %collective-permute-done.11, bf16[2048,256]{0,1:T(8,128)(2,1)} %collective-permute-done.9, bf16[2048,256]{0,1:T(8,128)(2,1)} %collective-permute-done.7, bf16[2048,256]{0,1:T(8,128)(2,1)S(1)} %copy-done.11), kind=kOutput, calls=%fused_computation.57 | convolution fusion | flops 4313841664 | bytes 10485760 | tf_op jit(solution)/shard_map/dot_general | solution.py:73
  474.7 8.6 %pad_maximum_fusion = bf16[8192,1024]{1,0:T(8,128)(2,1)} fusion(bf16[2048,1024]{1,0:T(8,128)(2,1)S(1)} %convolution_convert_fusion, bf16[2048,1024]{1,0:T(8,128)(2,1)S(1)} %convolution_convert_fusion.1, bf16[2048,1024]{1,0:T(8,128)(2,1)S(1)} %convolution_convert_fusion.2, bf16[2048,1024]{1,0:T(8,128)(2,1)S(1)} %convolution_convert_fusion.3), kind=kLoop, calls=%fused_computation.6 | loop fusion | flops 67108864 | bytes 33554432 | tf_op jit(solution)/shard_map/concatenate | solution.py:81
  483.3 20.4 %all-reduce.7.cloned.1.call-done = f32[256,4,256]{2,1,0:T(4,128)} async-done(((f32[256,4,256]{2,1,0:T(4,128)}), f32[256,4,256]{2,1,0:T(4,128)}) %all-reduce.7.cloned.1.call-update) | async-done | bytes 1048592
  (175 shorter events, 100.3 us)
Async XLA Ops:
  7.2 284.5 %all-reduce.5.cloned.1.call-start = ((), (), s32[]{:S(2)}) async-start(), calls=%async_computation | async-start | bytes 2097152
  23.6 62.0 %collective-permute-start = (bf16[2048,256]{0,1:T(8,128)(2,1)}, bf16[2048,256]{0,1:T(8,128)(2,1)}, u32[]{:S(2)}, u32[]{:S(2)}) collective-permute-start(bf16[2048,256]{0,1:T(8,128)(2,1)} %get-tuple-element.36), channel_id=1, source_target_pairs={{0,4},{4,0},{8,12},{12,8},{1,5},{5,1},{9,13},{13,9},{2,6},{6,2},{1... | collective-permute-start | bytes 3145736 | tf_op jit(solution)/shard_map/ppermute | solution.py:37
  24.0 62.5 %collective-permute-start.2 = (bf16[2048,256]{0,1:T(8,128)(2,1)}, bf16[2048,256]{0,1:T(8,128)(2,1)}, u32[]{:S(2)}, u32[]{:S(2)}) collective-permute-start(bf16[2048,256]{0,1:T(8,128)(2,1)} %get-tuple-element.38), channel_id=1, source_target_pairs={{0,8},{4,12},{8,0},{12,4},{1,9},{5,13},{9,1},{13,5},{2,10},{6,14},... | collective-permute-start | bytes 3145736 | tf_op jit(solution)/shard_map/ppermute | solution.py:37
  26.5 60.2 %collective-permute-start.4 = (bf16[2048,256]{0,1:T(8,128)(2,1)}, bf16[2048,256]{0,1:T(8,128)(2,1)}, u32[]{:S(2)}, u32[]{:S(2)}) collective-permute-start(bf16[2048,256]{0,1:T(8,128)(2,1)} %get-tuple-element.37), channel_id=1, source_target_pairs={{0,12},{4,8},{8,4},{12,0},{1,13},{5,9},{9,5},{13,1},{2,14},{6,10},... | collective-permute-start | bytes 3145736 | tf_op jit(solution)/shard_map/ppermute | solution.py:37
  36.0 66.2 %collective-permute-start.10 = (bf16[2048,256]{0,1:T(8,128)(2,1)}, bf16[2048,256]{0,1:T(8,128)(2,1)}, u32[]{:S(2)}, u32[]{:S(2)}) collective-permute-start(bf16[2048,256]{0,1:T(8,128)(2,1)} %get-tuple-element.40), channel_id=1, source_target_pairs={{0,12},{4,8},{8,4},{12,0},{1,13},{5,9},{9,5},{13,1},{2,14},{6,10},... | collective-permute-start | bytes 3145736 | tf_op jit(solution)/shard_map/ppermute | solution.py:37
  37.2 65.6 %collective-permute-start.6 = (bf16[2048,256]{0,1:T(8,128)(2,1)}, bf16[2048,256]{0,1:T(8,128)(2,1)}, u32[]{:S(2)}, u32[]{:S(2)}) collective-permute-start(bf16[2048,256]{0,1:T(8,128)(2,1)} %get-tuple-element.39), channel_id=1, source_target_pairs={{0,4},{4,0},{8,12},{12,8},{1,5},{5,1},{9,13},{13,9},{2,6},{6,2},{1... | collective-permute-start | bytes 3145736 | tf_op jit(solution)/shard_map/ppermute | solution.py:37
  85.6 32.7 %collective-permute-start.8 = (bf16[2048,256]{0,1:T(8,128)(2,1)}, bf16[2048,256]{0,1:T(8,128)(2,1)}, u32[]{:S(2)}, u32[]{:S(2)}) collective-permute-start(bf16[2048,256]{0,1:T(8,128)(2,1)} %get-tuple-element.41), channel_id=1, source_target_pairs={{0,8},{4,12},{8,0},{12,4},{1,9},{5,13},{9,1},{13,5},{2,10},{6,14},... | collective-permute-start | bytes 3145736 | tf_op jit(solution)/shard_map/ppermute | solution.py:37
  86.5 48.2 %collective-permute-start.12 = (bf16[2048,256]{0,1:T(8,128)(2,1)}, bf16[2048,256]{0,1:T(8,128)(2,1)}, u32[]{:S(2)}, u32[]{:S(2)}) collective-permute-start(bf16[2048,256]{0,1:T(8,128)(2,1)} %get-tuple-element.42), channel_id=1, source_target_pairs={{0,4},{4,0},{8,12},{12,8},{1,5},{5,1},{9,13},{13,9},{2,6},{6,2},{1... | collective-permute-start | bytes 3145736 | tf_op jit(solution)/shard_map/ppermute | solution.py:37
  86.8 54.0 %collective-permute-start.14 = (bf16[2048,256]{0,1:T(8,128)(2,1)}, bf16[2048,256]{0,1:T(8,128)(2,1)}, u32[]{:S(2)}, u32[]{:S(2)}) collective-permute-start(bf16[2048,256]{0,1:T(8,128)(2,1)} %get-tuple-element.44), channel_id=1, source_target_pairs={{0,8},{4,12},{8,0},{12,4},{1,9},{5,13},{9,1},{13,5},{2,10},{6,14},... | collective-permute-start | bytes 3145736 | tf_op jit(solution)/shard_map/ppermute | solution.py:37
  102.1 60.6 %collective-permute-start.16 = (bf16[2048,256]{0,1:T(8,128)(2,1)S(1)}, bf16[2048,256]{0,1:T(8,128)(2,1)S(1)}, u32[]{:S(2)}, u32[]{:S(2)}) collective-permute-start(bf16[2048,256]{0,1:T(8,128)(2,1)S(1)} %copy-done.8), channel_id=1, source_target_pairs={{0,12},{4,8},{8,4},{12,0},{1,13},{5,9},{9,5},{13,1},{2,14},{6,10},... | collective-permute-start | bytes 3145736 | tf_op jit(solution)/shard_map/ppermute | solution.py:37
  102.8 73.2 %collective-permute-start.18 = (bf16[2048,256]{0,1:T(8,128)(2,1)S(1)}, bf16[2048,256]{0,1:T(8,128)(2,1)S(1)}, u32[]{:S(2)}, u32[]{:S(2)}) collective-permute-start(bf16[2048,256]{0,1:T(8,128)(2,1)S(1)} %copy-done.7), channel_id=1, source_target_pairs={{0,4},{4,0},{8,12},{12,8},{1,5},{5,1},{9,13},{13,9},{2,6},{6,2},{1... | collective-permute-start | bytes 3145736 | tf_op jit(solution)/shard_map/ppermute | solution.py:37
  118.3 67.3 %collective-permute-start.20 = (bf16[2048,256]{0,1:T(8,128)(2,1)S(1)}, bf16[2048,256]{0,1:T(8,128)(2,1)S(1)}, u32[]{:S(2)}, u32[]{:S(2)}) collective-permute-start(bf16[2048,256]{0,1:T(8,128)(2,1)S(1)} %copy-done.6), channel_id=1, source_target_pairs={{0,8},{4,12},{8,0},{12,4},{1,9},{5,13},{9,1},{13,5},{2,10},{6,14},... | collective-permute-start | bytes 3145736 | tf_op jit(solution)/shard_map/ppermute | solution.py:37
  134.8 72.9 %collective-permute-start.22 = (bf16[2048,256]{0,1:T(8,128)(2,1)S(1)}, bf16[2048,256]{0,1:T(8,128)(2,1)S(1)}, u32[]{:S(2)}, u32[]{:S(2)}) collective-permute-start(bf16[2048,256]{0,1:T(8,128)(2,1)S(1)} %get-tuple-element.46), channel_id=1, source_target_pairs={{0,12},{4,8},{8,4},{12,0},{1,13},{5,9},{9,5},{13,1},{2,14},{6,10},... | collective-permute-start | bytes 3145736 | tf_op jit(solution)/shard_map/ppermute | solution.py:37
  238.4 265.3 %all-reduce.7.cloned.1.call-start = ((), (), s32[]{:S(2)}) async-start(), calls=%async_computation.1 | async-start | bytes 2097152
  238.8 53.8 %collective-permute-start.11 = (bf16[2048,256]{0,1:T(8,128)(2,1)}, bf16[2048,256]{0,1:T(8,128)(2,1)}, u32[]{:S(2)}, u32[]{:S(2)}) collective-permute-start(bf16[2048,256]{0,1:T(8,128)(2,1)} %get-tuple-element.23), channel_id=1, source_target_pairs={{0,12},{4,8},{8,4},{12,0},{1,13},{5,9},{9,5},{13,1},{2,14},{6,10},... | collective-permute-start | bytes 3145736 | tf_op jit(solution)/shard_map/ppermute | solution.py:37
  240.3 53.6 %collective-permute-start.7 = (bf16[2048,256]{0,1:T(8,128)(2,1)}, bf16[2048,256]{0,1:T(8,128)(2,1)}, u32[]{:S(2)}, u32[]{:S(2)}) collective-permute-start(bf16[2048,256]{0,1:T(8,128)(2,1)} %get-tuple-element.25), channel_id=1, source_target_pairs={{0,4},{4,0},{8,12},{12,8},{1,5},{5,1},{9,13},{13,9},{2,6},{6,2},{1... | collective-permute-start | bytes 3145736 | tf_op jit(solution)/shard_map/ppermute | solution.py:37
  240.5 53.8 %collective-permute-start.9 = (bf16[2048,256]{0,1:T(8,128)(2,1)}, bf16[2048,256]{0,1:T(8,128)(2,1)}, u32[]{:S(2)}, u32[]{:S(2)}) collective-permute-start(bf16[2048,256]{0,1:T(8,128)(2,1)} %get-tuple-element.24), channel_id=1, source_target_pairs={{0,8},{4,12},{8,0},{12,4},{1,9},{5,13},{9,1},{13,5},{2,10},{6,14},... | collective-permute-start | bytes 3145736 | tf_op jit(solution)/shard_map/ppermute | solution.py:37
  241.2 51.5 %copy-start.14 = (bf16[2048,256]{0,1:T(8,128)(2,1)S(1)}, bf16[2048,256]{0,1:T(8,128)(2,1)}, u32[]{:S(2)}) copy-start(bf16[2048,256]{0,1:T(8,128)(2,1)} %get-tuple-element.28) | copy-start | bytes 3145732
  241.2 53.7 %copy-start.10 = (bf16[2048,256]{0,1:T(8,128)(2,1)S(1)}, bf16[2048,256]{0,1:T(8,128)(2,1)}, u32[]{:S(2)}) copy-start(bf16[2048,256]{0,1:T(8,128)(2,1)} %get-tuple-element.22) | copy-start | bytes 3145732
  245.5 57.2 %collective-permute-start.1 = (bf16[2048,256]{0,1:T(8,128)(2,1)}, bf16[2048,256]{0,1:T(8,128)(2,1)}, u32[]{:S(2)}, u32[]{:S(2)}) collective-permute-start(bf16[2048,256]{0,1:T(8,128)(2,1)} %get-tuple-element.30), channel_id=1, source_target_pairs={{0,4},{4,0},{8,12},{12,8},{1,5},{5,1},{9,13},{13,9},{2,6},{6,2},{1... | collective-permute-start | bytes 3145736 | tf_op jit(solution)/shard_map/ppermute | solution.py:37
  245.5 64.4 %collective-permute-start.3 = (bf16[2048,256]{0,1:T(8,128)(2,1)}, bf16[2048,256]{0,1:T(8,128)(2,1)}, u32[]{:S(2)}, u32[]{:S(2)}) collective-permute-start(bf16[2048,256]{0,1:T(8,128)(2,1)} %get-tuple-element.29), channel_id=1, source_target_pairs={{0,8},{4,12},{8,0},{12,4},{1,9},{5,13},{9,1},{13,5},{2,10},{6,14},... | collective-permute-start | bytes 3145736 | tf_op jit(solution)/shard_map/ppermute | solution.py:37
  292.7 39.1 %collective-permute-start.5 = (bf16[2048,256]{0,1:T(8,128)(2,1)S(1)}, bf16[2048,256]{0,1:T(8,128)(2,1)S(1)}, u32[]{:S(2)}, u32[]{:S(2)}) collective-permute-start(bf16[2048,256]{0,1:T(8,128)(2,1)S(1)} %copy-done.14), channel_id=1, source_target_pairs={{0,12},{4,8},{8,4},{12,0},{1,13},{5,9},{9,5},{13,1},{2,14},{6,10},... | collective-permute-start | bytes 3145736 | tf_op jit(solution)/shard_map/ppermute | solution.py:37
  293.8 46.9 %collective-permute-start.13 = (bf16[2048,256]{0,1:T(8,128)(2,1)}, bf16[2048,256]{0,1:T(8,128)(2,1)S(1)}, u32[]{:S(2)}, u32[]{:S(2)}) collective-permute-start(bf16[2048,256]{0,1:T(8,128)(2,1)} %get-tuple-element.35), channel_id=1, source_target_pairs={{0,4},{4,0},{8,12},{12,8},{1,5},{5,1},{9,13},{13,9},{2,6},{6,2},{1... | collective-permute-start | bytes 3145736 | tf_op jit(solution)/shard_map/ppermute | solution.py:37
  294.3 60.4 %collective-permute-start.15 = (bf16[2048,256]{0,1:T(8,128)(2,1)}, bf16[2048,256]{0,1:T(8,128)(2,1)S(1)}, u32[]{:S(2)}, u32[]{:S(2)}) collective-permute-start(bf16[2048,256]{0,1:T(8,128)(2,1)} %get-tuple-element.34), channel_id=1, source_target_pairs={{0,8},{4,12},{8,0},{12,4},{1,9},{5,13},{9,1},{13,5},{2,10},{6,14},... | collective-permute-start | bytes 3145736 | tf_op jit(solution)/shard_map/ppermute | solution.py:37
  294.9 38.3 %copy-start.9 = (bf16[2048,256]{0,1:T(8,128)(2,1)S(1)}, bf16[2048,256]{0,1:T(8,128)(2,1)}, u32[]{:S(2)}) copy-start(bf16[2048,256]{0,1:T(8,128)(2,1)} %get-tuple-element.27) | copy-start | bytes 3145732
  302.7 74.0 %collective-permute-start.17 = (bf16[2048,256]{0,1:T(8,128)(2,1)S(1)}, bf16[2048,256]{0,1:T(8,128)(2,1)S(1)}, u32[]{:S(2)}, u32[]{:S(2)}) collective-permute-start(bf16[2048,256]{0,1:T(8,128)(2,1)S(1)} %copy-done.17), channel_id=1, source_target_pairs={{0,12},{4,8},{8,4},{12,0},{1,13},{5,9},{9,5},{13,1},{2,14},{6,10},... | collective-permute-start | bytes 3145736 | tf_op jit(solution)/shard_map/ppermute | solution.py:37
  309.9 75.9 %collective-permute-start.19 = (bf16[2048,256]{0,1:T(8,128)(2,1)S(1)}, bf16[2048,256]{0,1:T(8,128)(2,1)S(1)}, u32[]{:S(2)}, u32[]{:S(2)}) collective-permute-start(bf16[2048,256]{0,1:T(8,128)(2,1)S(1)} %copy-done.20), channel_id=1, source_target_pairs={{0,4},{4,0},{8,12},{12,8},{1,5},{5,1},{9,13},{13,9},{2,6},{6,2},{1... | collective-permute-start | bytes 3145736 | tf_op jit(solution)/shard_map/ppermute | solution.py:37
  331.7 68.0 %collective-permute-start.21 = (bf16[2048,256]{0,1:T(8,128)(2,1)S(1)}, bf16[2048,256]{0,1:T(8,128)(2,1)S(1)}, u32[]{:S(2)}, u32[]{:S(2)}) collective-permute-start(bf16[2048,256]{0,1:T(8,128)(2,1)S(1)} %copy-done.19), channel_id=1, source_target_pairs={{0,8},{4,12},{8,0},{12,4},{1,9},{5,13},{9,1},{13,5},{2,10},{6,14},... | collective-permute-start | bytes 3145736 | tf_op jit(solution)/shard_map/ppermute | solution.py:37
  333.2 43.4 %copy-start.12 = (bf16[2048,256]{0,1:T(8,128)(2,1)S(1)}, bf16[2048,256]{0,1:T(8,128)(2,1)}, u32[]{:S(2)}) copy-start(bf16[2048,256]{0,1:T(8,128)(2,1)} %get-tuple-element.32) | copy-start | bytes 3145732
  340.7 45.1 %copy-start.29 = (bf16[2048,256]{0,1:T(8,128)(2,1)}, bf16[2048,256]{0,1:T(8,128)(2,1)S(1)}, u32[]{:S(2)}) copy-start(bf16[2048,256]{0,1:T(8,128)(2,1)S(1)} %collective-permute-done.13) | copy-start | bytes 3145732
  340.7 80.9 %collective-permute-start.23 = (bf16[2048,256]{0,1:T(8,128)(2,1)S(1)}, bf16[2048,256]{0,1:T(8,128)(2,1)S(1)}, u32[]{:S(2)}, u32[]{:S(2)}) collective-permute-start(bf16[2048,256]{0,1:T(8,128)(2,1)S(1)} %copy-done.18), channel_id=1, source_target_pairs={{0,12},{4,8},{8,4},{12,0},{1,13},{5,9},{9,5},{13,1},{2,14},{6,10},... | collective-permute-start | bytes 3145736 | tf_op jit(solution)/shard_map/ppermute | solution.py:37
  376.7 45.9 %copy-start.15 = (bf16[2048,256]{0,1:T(8,128)(2,1)S(1)}, bf16[2048,256]{0,1:T(8,128)(2,1)}, u32[]{:S(2)}) copy-start(bf16[2048,256]{0,1:T(8,128)(2,1)} %get-tuple-element.17) | copy-start | bytes 3145732
  (37 other events, 378.9 us)
Sparse Core Ops, SparseCore 0:
  238.5 53.1 all-reduce.4
  450.6 53.0 all-reduce.6

commit v3 on v2

--- a/solution.py
+++ b/solution.py
@@ -43,8 +43,8 @@
     blk_local, bs, _ = w_first.shape
     feat = blk_local * bs
     sub = bs // NB
-    part = feat // lax.axis_size("tensor")
     n_dev = lax.axis_size("tensor")
+    part = feat // n_dev
     dp_count = lax.axis_size("dp")
     grad_scale = 1.0 / math.sqrt(tok_rows * dp_count)
     idx = lax.axis_index("tensor")
@@ -52,43 +52,68 @@
     w1p, w2p, w1tp = expanded_weights(w_first, w_second, n_dev, order)
     step = tok_rows // CHUNKS
 
-    gf_acc = None
-    gs_acc = None
+    def rows(a, k):
+        return a[k * step:(k + 1) * step]
+
+    def forward(k):
+        hidden = jnp.dot(rows(tokens, k), w1p, preferred_element_type=jnp.float32)
+        hidden = hidden.astype(jnp.bfloat16)
+        backed = jnp.dot(rows(cotangent, k), w2p, preferred_element_type=jnp.float32)
+        return [hidden[:, m * part:(m + 1) * part] for m in range(n_dev)], backed
+
+    def add(acc, val):
+        return val if acc is None else acc + val
+
+    pieces, backed = forward(0)
+    moved = exchange(pieces, n_dev)
+    gf_acc = gs_acc = None
     outs = []
+    returned_prev = None
     for k in range(CHUNKS):
-        x = tokens[k * step:(k + 1) * step]
-        cot = cotangent[k * step:(k + 1) * step]
-        hidden = jnp.dot(x, w1p, preferred_element_type=jnp.float32).astype(jnp.bfloat16)
-        backed = jnp.dot(cot, w2p, preferred_element_type=jnp.float32)
-        moved = exchange([hidden[:, m * part:(m + 1) * part] for m in range(n_dev)], n_dev)
         masked = [
             jnp.where(moved[m] > 0, backed[:, m * part:(m + 1) * part], 0.0).astype(jnp.bfloat16)
             for m in range(n_dev)
         ]
         active = jnp.maximum(jnp.concatenate(moved, axis=1), jnp.zeros((), jnp.bfloat16))
-        gs = lax.dot_general(
-            active, cot, (((0,), (0,)), ((), ())), preferred_element_type=jnp.float32
+        gs_k = lax.dot_general(
+            active, rows(cotangent, k), (((0,), (0,)), ((), ())), preferred_element_type=jnp.float32
         )
-        returned = jnp.concatenate(exchange(masked, n_dev), axis=1)
-        gt = jnp.dot(returned, w1tp, preferred_element_type=jnp.float32).astype(jnp.bfloat16)
-        outs.append(gt)
-        gf = lax.dot_general(
-            x, returned, (((0,), (0,)), ((), ())), preferred_element_type=jnp.float32
-        )
-        gf_acc = gf if gf_acc is None else gf_acc + gf
-        gs_acc = gs if gs_acc is None else gs_acc + gs
-
-    grad_tokens = jnp.concatenate(outs, axis=0)
+        if k + 1 < CHUNKS:
+            pieces, backed = forward(k + 1)
+            tied = (masked, pieces, backed, gs_acc, gf_acc, outs)
+            masked, pieces, backed, gs_acc, gf_acc, outs = lax.optimization_barrier(tied)
+            moved = exchange(pieces, n_dev)
+        gs_acc = add(gs_acc, gs_k)
+        if returned_prev is not None:
+            gt, gf = backward(returned_prev, tokens, k - 1, w1tp, step, n_dev, blk_local, sub)
+            outs = outs + [gt]
+            gf_acc = add(gf_acc, gf)
+        returned_prev = jnp.concatenate(exchange(masked, n_dev), axis=1)
     gs6 = gs_acc.reshape(n_dev, blk_local, blk_local, sub, blk_local, bs)
     gsd = jnp.take(jnp.diagonal(gs6, axis1=1, axis2=4), order, axis=0)
     second_term = gsd.transpose(2, 0, 1, 4, 3).reshape(bs, blk_local, bs) * grad_scale
     grad_second = lax.psum_scatter(second_term, "dp", scatter_dimension=0, tiled=True)
-    gf_acc, grad_second = lax.optimization_barrier((gf_acc, grad_second))
-    gf6 = gf_acc.reshape(blk_local, bs, n_dev, blk_local, blk_local, sub)
-    gfd = jnp.take(jnp.diagonal(gf6, axis1=0, axis2=4), order, axis=1)
-    first_term = gfd.transpose(0, 4, 1, 2, 3).reshape(bs, blk_local, bs) * grad_scale
+    returned_prev, grad_second = lax.optimization_barrier((returned_prev, grad_second))
+    gt, gf = backward(returned_prev, tokens, CHUNKS - 1, w1tp, step, n_dev, blk_local, sub)
+    outs = outs + [gt]
+    gf_acc = add(gf_acc, gf)
+
+    grad_tokens = jnp.concatenate(outs, axis=0)
+    first_term = jnp.take(gf_acc, order, axis=2).reshape(bs, blk_local, bs) * grad_scale
     grad_first = lax.psum_scatter(first_term, "dp", scatter_dimension=0, tiled=True)
     return (grad_tokens, grad_first.transpose(1, 0, 2), grad_second.transpose(1, 0, 2))
+
+
+def backward(returned, tokens, k, w1tp, step, n_dev, blk_local, sub):
+    x = tokens[k * step:(k + 1) * step]
+    gt = jnp.dot(returned, w1tp, preferred_element_type=jnp.float32).astype(jnp.bfloat16)
+    gf = jnp.einsum(
+        "tmcbq,tbi->ibmcq",
+        returned.reshape(step, n_dev, blk_local, blk_local, sub),
+        x.reshape(step, blk_local, -1),
+        preferred_element_type=jnp.float32,
+    )
+    return gt, gf
 
 
 def solution(mesh):

time: 517 us -> 553 us (1.070)
  local copies, waits for them, and re-layouts: 51.4 us -> 96.3 us
  matrix products: 159 us -> 133 us
  other arithmetic: 28.1 us -> 37.5 us
    unnamed x93 -> x101, local copies, waits for them, and re-layouts: 7.98 us -> 58.2 us
    dot_general x20, matrix products: 159 us -> 133 us  [the longest x4 35.7 us: forward(): jnp.dot(rows(cotangent, k), w2p, preferred_element_type=jnp.float32)]
    convert_element_type x0 -> x3, other arithmetic: none -> 12.5 us  [shards(): jnp.where(moved[m] > 0, backed[:, m * part:(m + 1) * part], 0.0)]
    slice x4 -> x1, other arithmetic: 15.4 us -> 4.59 us  [forward(): return ([hidden[:, m * part:(m + 1) * part] for m in range(n_dev)], backed)]
    reshape x2 -> x0, local copies, waits for them, and re-layouts: 10.5 us -> none  [shards(): gf6 = gf_acc.reshape(blk_local, bs, n_dev, blk_local, blk_local, sub)]
    unnamed x4, waiting for transfers between devices: 65 us -> 71.1 us
  transfers between devices with their start and end apart: 26 -> 26, of which waited for: 13 -> 11; matrix products, arithmetic and copies ran while one was open for 31% -> 41% of each run, Pallas kernels for 0% -> 0%
where the time goes in v3:
time: 553 us; the launch traced here: 544 us
  waiting for transfers between devices  240 us (43%)
  matrix products  133 us (24%)
  local copies, waits for them, and re-layouts  96.3 us (17%)
  other arithmetic  37.5 us (7%)
  starting transfers between devices  20.9 us (4%)
  between operations  15.6 us (3%)
    ppermute x24, waiting for transfers between devices, exchange(): lax.ppermute(pieces[m], 'tensor', [(i, i ^ m) for i in range(n_dev)])  169 us
    unnamed x4, waiting for transfers between devices  71.1 us
    unnamed x101, local copies, waits for them, and re-layouts  58.2 us
    dot_general x4, matrix products, forward(): jnp.dot(rows(cotangent, k), w2p, preferred_element_type=jnp.float32)  35.7 us
    dot_general x4, matrix products, shards(): lax.dot_general(active, rows(cotangent, k), (((0,), (0,)), ((), ())), pre...  32.3 us
    dot_general x4, matrix products, forward(): hidden = jnp.dot(rows(tokens, k), w1p, preferred_element_type=jnp.float32)  28.2 us
    dot_general x4, matrix products, backward(): jnp.dot(returned, w1tp, preferred_element_type=jnp.float32)  27.8 us
    ppermute x24, starting transfers between devices, exchange(): lax.ppermute(pieces[m], 'tensor', [(i, i ^ m) for i in range(n_dev)])  20.8 us
  transfers between devices with their start and end apart: 26, of which 11 were waited for; matrix products, arithmetic and copies ran while one was open for 41% of the time, Pallas kernels for 0%

profile of v3, /device:TPU:0, one launch (start us, length us, event | category | flops | bytes accessed | tf_op | source)
XLA Modules:
  0.0 543.7 jit_solution(15687418837493945028)
XLA Ops:
  13.7 7.5 %convert_bitcast_fusion.3 = bf16[2048,1024]{0,1:T(8,128)(2,1)S(1)} fusion(bf16[1024,1024]{0,1:T(8,128)(2,1)S(1)} %bitcast.132, bf16[8192,1024]{1,0:T(8,128)(2,1)} %param.4), kind=kOutput, calls=%fused_computation.56 | convolution fusion | flops 4297064448 | bytes 10485760 | tf_op jit(solution)/shard_map/dot_general | solution.py:59
  26.2 6.1 %convert_bitcast_fusion.2 = bf16[2048,1024]{0,1:T(8,128)(2,1)} fusion(bf16[1024,1024]{0,1:T(8,128)(2,1)S(1)} %bitcast.133, bf16[8192,1024]{1,0:T(8,128)(2,1)S(1)} %bitcast.114), kind=kOutput, calls=%fused_computation.55 | convolution fusion | flops 4297064448 | bytes 10485760 | tf_op jit(solution)/shard_map/dot_general | solution.py:59
  32.8 9.1 %convolution_bitcast_fusion.3 = bf16[2048,1024]{0,1:T(8,128)(2,1)} fusion(bf16[1024,1024]{0,1:T(8,128)(2,1)S(1)} %bitcast.128, bf16[8192,1024]{1,0:T(8,128)(2,1)} %param.5), kind=kOutput, calls=%fused_computation.9 | convolution fusion | flops 4294967296 | bytes 10485760 | tf_op jit(solution)/shard_map/dot_general | solution.py:61
  41.9 8.4 %convolution_bitcast_fusion.2 = bf16[2048,1024]{0,1:T(8,128)(2,1)} fusion(bf16[1024,1024]{0,1:T(8,128)(2,1)S(1)} %bitcast.129, bf16[8192,1024]{1,0:T(8,128)(2,1)} %param.5), kind=kOutput, calls=%fused_computation.8 | convolution fusion | flops 4294967296 | bytes 10485760 | tf_op jit(solution)/shard_map/dot_general | solution.py:61
  56.5 8.6 %convolution_bitcast_fusion.1 = bf16[2048,1024]{0,1:T(8,128)(2,1)} fusion(bf16[1024,1024]{0,1:T(8,128)(2,1)S(1)} %bitcast.130, bf16[8192,1024]{1,0:T(8,128)(2,1)} %param.5), kind=kOutput, calls=%fused_computation.7 | convolution fusion | flops 4294967296 | bytes 10485760 | tf_op jit(solution)/shard_map/dot_general | solution.py:61
  71.4 8.4 %convert_bitcast_fusion = bf16[2048,1024]{0,1:T(8,128)(2,1)} fusion(bf16[1024,1024]{0,1:T(8,128)(2,1)S(1)} %bitcast.135, bf16[8192,1024]{1,0:T(8,128)(2,1)} %param.4), kind=kOutput, calls=%fused_computation.53 | convolution fusion | flops 4297064448 | bytes 10485760 | tf_op jit(solution)/shard_map/dot_general | solution.py:59
  84.9 6.5 %copy.93 = bf16[2048,1024]{0,1:T(8,128)(2,1)} copy(bf16[2048,1024]{1,0:T(8,128)(2,1)} %get-tuple-element.78) | data formatting | bytes 8388608
  94.3 6.5 %copy.92 = bf16[2048,1024]{0,1:T(8,128)(2,1)} copy(bf16[2048,1024]{1,0:T(8,128)(2,1)} %get-tuple-element.80) | data formatting | bytes 8388608
  104.8 6.5 %copy.95 = bf16[2048,1024]{0,1:T(8,128)(2,1)} copy(bf16[2048,1024]{1,0:T(8,128)(2,1)} %get-tuple-element.81) | data formatting | bytes 8388608
  111.2 6.6 %copy.94 = bf16[2048,1024]{0,1:T(8,128)(2,1)} copy(bf16[2048,1024]{1,0:T(8,128)(2,1)} %get-tuple-element.79) | data formatting | bytes 8388608
  119.7 9.5 %convolution_bitcast_fusion = bf16[2048,1024]{0,1:T(8,128)(2,1)} fusion(bf16[1024,1024]{0,1:T(8,128)(2,1)} %bitcast.131, bf16[8192,1024]{1,0:T(8,128)(2,1)} %param.5), kind=kOutput, calls=%fused_computation.6 | convolution fusion | flops 4294967296 | bytes 10485760 | tf_op jit(solution)/shard_map/dot_general | solution.py:61
  138.1 7.8 %fusion = f32[1024,1024]{1,0:T(8,128)S(1)} fusion(bf16[2048,256]{0,1:T(8,128)(2,1)} %collective-permute-done.2, bf16[2048,256]{0,1:T(8,128)(2,1)} %collective-permute-done.1, bf16[2048,256]{0,1:T(8,128)(2,1)} %collective-permute-done, bf16[2048,256]{0,1:T(8,128)(2,1)S(1)} %get-tuple-element.94, bf16[8192,1024]{1,0:T(8,128)(2,1)} %param.5), kind=kOutput, calls=%fused_computation.11 | convolution fusion | flops 4315938816 | bytes 12582912 | tf_op jit(solution)/shard_map/dot_general | solution.py:78
  147.0 13.1 %collective-permute-done.4 = bf16[2048,256]{0,1:T(8,128)(2,1)S(1)} collective-permute-done((bf16[2048,256]{0,1:T(8,128)(2,1)S(1)}, bf16[2048,256]{0,1:T(8,128)(2,1)S(1)}, u32[]{:S(2)}, u32[]{:S(2)}) %collective-permute-start.4) | collective-permute-done | bytes 1048608 | tf_op jit(solution)/shard_map/ppermute | solution.py:37
  160.0 21.9 %collective-permute-done.5 = bf16[2048,256]{0,1:T(8,128)(2,1)S(1)} collective-permute-done((bf16[2048,256]{0,1:T(8,128)(2,1)S(1)}, bf16[2048,256]{0,1:T(8,128)(2,1)S(1)}, u32[]{:S(2)}, u32[]{:S(2)}) %collective-permute-start.5) | collective-permute-done | bytes 1048608 | tf_op jit(solution)/shard_map/ppermute | solution.py:37
  188.3 16.6 %collective-permute-done.10 = bf16[2048,256]{0,1:T(8,128)(2,1)S(1)} collective-permute-done((bf16[2048,256]{0,1:T(8,128)(2,1)S(1)}, bf16[2048,256]{0,1:T(8,128)(2,1)S(1)}, u32[]{:S(2)}, u32[]{:S(2)}) %collective-permute-start.10) | collective-permute-done | bytes 1048608 | tf_op jit(solution)/shard_map/ppermute | solution.py:37
  208.0 6.8 %fusion.7 = f32[1024,1024]{1,0:T(8,128)S(1)} fusion(bf16[2048,256]{0,1:T(8,128)(2,1)S(1)} %collective-permute-done.5, bf16[2048,256]{0,1:T(8,128)(2,1)S(1)} %collective-permute-done.4, bf16[2048,256]{0,1:T(8,128)(2,1)S(1)} %collective-permute-done.3, bf16[2048,256]{0,1:T(8,128)(2,1)S(1)} %get-tuple-element.36, bf16[8192,1024]{1,0:T(8,128)(2,1)} %param.5), kind=kOutput, calls=%fused_computation.19 | convolution fusion | flops 4315938816 | bytes 12582912 | tf_op jit(solution)/shard_map/dot_general | solution.py:78
  214.8 12.2 %collective-permute-done.11 = bf16[2048,256]{0,1:T(8,128)(2,1)} collective-permute-done((bf16[2048,256]{0,1:T(8,128)(2,1)}, bf16[2048,256]{0,1:T(8,128)(2,1)}, u32[]{:S(2)}, u32[]{:S(2)}) %collective-permute-start.11) | collective-permute-done | bytes 1048608 | tf_op jit(solution)/shard_map/ppermute | solution.py:37
  231.3 8.7 %convolution_convert_fusion.3 = bf16[2048,1024]{1,0:T(8,128)(2,1)} fusion(bf16[2048,1024]{0,1:T(8,128)(2,1)} %constant_dynamic-update-slice_fusion, bf16[1024,1024]{1,0:T(8,128)(2,1)S(1)} %bitcast.124), kind=kOutput, calls=%fused_computation.60 | convolution fusion | flops 4297064448 | bytes 10485760 | tf_op jit(solution)/shard_map/dot_general | solution.py:109
  244.8 27.6 %collective-permute-done.7 = bf16[2048,256]{0,1:T(8,128)(2,1)S(1)} collective-permute-done((bf16[2048,256]{0,1:T(8,128)(2,1)}, bf16[2048,256]{0,1:T(8,128)(2,1)S(1)}, u32[]{:S(2)}, u32[]{:S(2)}) %collective-permute-start.7) | collective-permute-done | bytes 1048608 | tf_op jit(solution)/shard_map/ppermute | solution.py:37
  272.4 22.0 %collective-permute-done.8 = bf16[2048,256]{0,1:T(8,128)(2,1)S(1)} collective-permute-done((bf16[2048,256]{0,1:T(8,128)(2,1)}, bf16[2048,256]{0,1:T(8,128)(2,1)S(1)}, u32[]{:S(2)}, u32[]{:S(2)}) %collective-permute-start.8) | collective-permute-done | bytes 1048608 | tf_op jit(solution)/shard_map/ppermute | solution.py:37
  304.9 11.9 %collective-permute-done.14 = bf16[2048,256]{0,1:T(8,128)(2,1)S(1)} collective-permute-done((bf16[2048,256]{0,1:T(8,128)(2,1)S(1)}, bf16[2048,256]{0,1:T(8,128)(2,1)S(1)}, u32[]{:S(2)}, u32[]{:S(2)}) %collective-permute-start.14) | collective-permute-done | bytes 1048608 | tf_op jit(solution)/shard_map/ppermute | solution.py:37
  324.4 8.9 %fusion.14 = f32[1024,1024]{1,0:T(8,128)} fusion(bf16[2048,256]{0,1:T(8,128)(2,1)S(1)} %copy-done.20, bf16[2048,256]{0,1:T(8,128)(2,1)S(1)} %collective-permute-done.7, bf16[2048,256]{0,1:T(8,128)(2,1)S(1)} %collective-permute-done.6, bf16[2048,256]{0,1:T(8,128)(2,1)S(1)} %get-tuple-element.41, bf16[8192,1024]{1,0:T(8,128)(2,1)} %param.5), kind=kOutput, calls=%fused_computation.28 | convolution fusion | flops 4315938816 | bytes 12582912 | tf_op jit(solution)/shard_map/dot_general | solution.py:78
  334.4 6.4 %convolution_convert_fusion.2 = bf16[2048,1024]{1,0:T(8,128)(2,1)} fusion(bf16[2048,1024]{0,1:T(8,128)(2,1)S(1)} %copy-done.30, bf16[1024,1024]{1,0:T(8,128)(2,1)S(1)} %bitcast.125), kind=kOutput, calls=%fused_computation.59 | convolution fusion | flops 4297064448 | bytes 10485760 | tf_op jit(solution)/shard_map/dot_general | solution.py:109
  340.9 21.4 %collective-permute-done.20 = bf16[2048,256]{0,1:T(8,128)(2,1)S(1)} collective-permute-done((bf16[2048,256]{0,1:T(8,128)(2,1)S(1)}, bf16[2048,256]{0,1:T(8,128)(2,1)S(1)}, u32[]{:S(2)}, u32[]{:S(2)}) %collective-permute-start.20) | collective-permute-done | bytes 1048608 | tf_op jit(solution)/shard_map/ppermute | solution.py:37
  362.3 21.9 %collective-permute-done.22 = bf16[2048,256]{0,1:T(8,128)(2,1)S(1)} collective-permute-done((bf16[2048,256]{0,1:T(8,128)(2,1)S(1)}, bf16[2048,256]{0,1:T(8,128)(2,1)S(1)}, u32[]{:S(2)}, u32[]{:S(2)}) %collective-permute-start.22) | collective-permute-done | bytes 1048608 | tf_op jit(solution)/shard_map/ppermute | solution.py:37
  385.2 8.8 %add_add_fusion = f32[1024,1024]{1,0:T(8,128)} fusion(f32[1024,1024]{1,0:T(8,128)S(1)} %add.49, f32[1024,1024]{1,0:T(8,128)S(1)} %copy-done.35, bf16[8192,1024]{1,0:T(8,128)(2,1)} %param.5, bf16[2048,256]{0,1:T(8,128)(2,1)S(1)} %collective-permute-done.22, bf16[2048,256]{0,1:T(8,128)(2,1)S(1)} %collective-permute-done.20, ...), kind=kOutput, calls=%fused_computation.52 | convolution fusion | flops 4318035968 | bytes 20971520 | tf_op jit(solution)/shard_map/dot_general | solution.py:78
  410.5 6.4 %select_convert_fusion.3 = (bf16[2048,256]{0,1:T(8,128)(2,1)S(1)}, bf16[2048,256]{0,1:T(8,128)(2,1)}, bf16[2048,256]{0,1:T(8,128)(2,1)}, bf16[2048,256]{0,1:T(8,128)(2,1)}) fusion(bf16[2048,1024]{0,1:T(8,128)(2,1)} %convolution_bitcast_fusion, bf16[2048,256]{0,1:T(8,128)(2,1)S(1)} %get-tuple-element.60, bf16[2048,256]{0,1:T(8,128)(2,1)} %copy-done.22, ...), kind=kLoop, calls=%fused_computation.80 | loop fusion | flops 6815744 | bytes 12582912 | tf_op jit(solution)/shard_map/convert_element_type | solution.py:74
  425.5 6.5 %convolution_convert_fusion.1 = bf16[2048,1024]{1,0:T(8,128)(2,1)} fusion(bf16[2048,1024]{0,1:T(8,128)(2,1)S(1)} %constant_dynamic-update-slice_fusion.8, bf16[1024,1024]{1,0:T(8,128)(2,1)S(1)} %bitcast.126), kind=kOutput, calls=%fused_computation.58 | convolution fusion | flops 4297064448 | bytes 10485760 | tf_op jit(solution)/shard_map/dot_general | solution.py:109
  432.1 32.4 %all-reduce.5.cloned.1.call-done = f32[256,4,256]{2,1,0:T(4,128)} async-done(((f32[256,4,256]{2,1,0:T(4,128)}), f32[256,4,256]{2,1,0:T(4,128)}) %all-reduce.5.cloned.1.call-update) | async-done | bytes 1048592
  467.6 6.2 %convolution_convert_fusion = bf16[2048,1024]{1,0:T(8,128)(2,1)} fusion(bf16[2048,1024]{0,1:T(8,128)(2,1)S(1)} %pad_maximum_fusion.1, bf16[1024,1024]{1,0:T(8,128)(2,1)S(1)} %bitcast.127), kind=kOutput, calls=%fused_computation.57 | convolution fusion | flops 4297064448 | bytes 10485760 | tf_op jit(solution)/shard_map/dot_general | solution.py:109
  482.4 13.8 %pad_maximum_fusion = bf16[8192,1024]{1,0:T(8,128)(2,1)} fusion(bf16[2048,1024]{1,0:T(8,128)(2,1)} %convolution_convert_fusion, bf16[2048,1024]{1,0:T(8,128)(2,1)} %convolution_convert_fusion.1, bf16[2048,1024]{1,0:T(8,128)(2,1)} %convolution_convert_fusion.2, bf16[2048,1024]{1,0:T(8,128)(2,1)} %convolution_convert_fusion.3), kind=kLoop, calls=%fused_computation.5 | loop fusion | flops 67108864 | bytes 33554432 | tf_op jit(solution)/shard_map/concatenate | solution.py:101
  496.2 38.7 %all-reduce.7.cloned.1.call-done = f32[256,4,256]{2,1,0:T(4,128)} async-done(((f32[256,4,256]{2,1,0:T(4,128)}), f32[256,4,256]{2,1,0:T(4,128)}) %all-reduce.7.cloned.1.call-update) | async-done | bytes 1048592
  (188 shorter events, 124.3 us)
Async XLA Ops:
  7.2 457.4 %all-reduce.5.cloned.1.call-start = ((), (), s32[]{:S(2)}) async-start(), calls=%async_computation | async-start | bytes 2097152
  23.0 106.2 %collective-permute-start = (bf16[2048,256]{0,1:T(8,128)(2,1)}, bf16[2048,256]{0,1:T(8,128)(2,1)}, u32[]{:S(2)}, u32[]{:S(2)}) collective-permute-start(bf16[2048,256]{0,1:T(8,128)(2,1)} %get-tuple-element.113), channel_id=1, source_target_pairs={{0,4},{4,0},{8,12},{12,8},{1,5},{5,1},{9,13},{13,9},{2,6},{6,2},{1... | collective-permute-start | bytes 3145736 | tf_op jit(solution)/shard_map/ppermute | solution.py:37
  23.5 105.8 %collective-permute-start.1 = (bf16[2048,256]{0,1:T(8,128)(2,1)}, bf16[2048,256]{0,1:T(8,128)(2,1)}, u32[]{:S(2)}, u32[]{:S(2)}) collective-permute-start(bf16[2048,256]{0,1:T(8,128)(2,1)} %get-tuple-element.112), channel_id=1, source_target_pairs={{0,8},{4,12},{8,0},{12,4},{1,9},{5,13},{9,1},{13,5},{2,10},{6,14},... | collective-permute-start | bytes 3145736 | tf_op jit(solution)/shard_map/ppermute | solution.py:37
  26.0 103.3 %collective-permute-start.2 = (bf16[2048,256]{0,1:T(8,128)(2,1)}, bf16[2048,256]{0,1:T(8,128)(2,1)}, u32[]{:S(2)}, u32[]{:S(2)}) collective-permute-start(bf16[2048,256]{0,1:T(8,128)(2,1)} %get-tuple-element.111), channel_id=1, source_target_pairs={{0,12},{4,8},{8,4},{12,0},{1,13},{5,9},{9,5},{13,1},{2,14},{6,10},... | collective-permute-start | bytes 3145736 | tf_op jit(solution)/shard_map/ppermute | solution.py:37
  133.9 13.0 %collective-permute-start.3 = (bf16[2048,256]{0,1:T(8,128)(2,1)S(1)}, bf16[2048,256]{0,1:T(8,128)(2,1)S(1)}, u32[]{:S(2)}, u32[]{:S(2)}) collective-permute-start(bf16[2048,256]{0,1:T(8,128)(2,1)S(1)} %copy-done.28), channel_id=1, source_target_pairs={{0,4},{4,0},{8,12},{12,8},{1,5},{5,1},{9,13},{13,9},{2,6},{6,2},{1... | collective-permute-start | bytes 3145736 | tf_op jit(solution)/shard_map/ppermute | solution.py:37
  134.1 26.0 %collective-permute-start.4 = (bf16[2048,256]{0,1:T(8,128)(2,1)S(1)}, bf16[2048,256]{0,1:T(8,128)(2,1)S(1)}, u32[]{:S(2)}, u32[]{:S(2)}) collective-permute-start(bf16[2048,256]{0,1:T(8,128)(2,1)S(1)} %copy-done.27), channel_id=1, source_target_pairs={{0,8},{4,12},{8,0},{12,4},{1,9},{5,13},{9,1},{13,5},{2,10},{6,14},... | collective-permute-start | bytes 3145736 | tf_op jit(solution)/shard_map/ppermute | solution.py:37
  136.0 46.0 %collective-permute-start.5 = (bf16[2048,256]{0,1:T(8,128)(2,1)S(1)}, bf16[2048,256]{0,1:T(8,128)(2,1)S(1)}, u32[]{:S(2)}, u32[]{:S(2)}) collective-permute-start(bf16[2048,256]{0,1:T(8,128)(2,1)S(1)} %copy-done.26), channel_id=1, source_target_pairs={{0,12},{4,8},{8,4},{12,0},{1,13},{5,9},{9,5},{13,1},{2,14},{6,10},... | collective-permute-start | bytes 3145736 | tf_op jit(solution)/shard_map/ppermute | solution.py:37
  136.0 51.3 %collective-permute-start.9 = (bf16[2048,256]{0,1:T(8,128)(2,1)S(1)}, bf16[2048,256]{0,1:T(8,128)(2,1)S(1)}, u32[]{:S(2)}, u32[]{:S(2)}) collective-permute-start(bf16[2048,256]{0,1:T(8,128)(2,1)S(1)} %get-tuple-element.48), channel_id=1, source_target_pairs={{0,4},{4,0},{8,12},{12,8},{1,5},{5,1},{9,13},{13,9},{2,6},{6,2},{1... | collective-permute-start | bytes 3145736 | tf_op jit(solution)/shard_map/ppermute | solution.py:37
  136.2 68.8 %collective-permute-start.10 = (bf16[2048,256]{0,1:T(8,128)(2,1)S(1)}, bf16[2048,256]{0,1:T(8,128)(2,1)S(1)}, u32[]{:S(2)}, u32[]{:S(2)}) collective-permute-start(bf16[2048,256]{0,1:T(8,128)(2,1)S(1)} %get-tuple-element.49), channel_id=1, source_target_pairs={{0,8},{4,12},{8,0},{12,4},{1,9},{5,13},{9,1},{13,5},{2,10},{6,14},... | collective-permute-start | bytes 3145736 | tf_op jit(solution)/shard_map/ppermute | solution.py:37
  138.1 43.8 %copy-start.5 = (bf16[2048,1024]{0,1:T(8,128)(2,1)S(1)}, bf16[2048,1024]{0,1:T(8,128)(2,1)}, u32[]{:S(2)}) copy-start(bf16[2048,1024]{0,1:T(8,128)(2,1)} %convolution_bitcast_fusion.2) | copy-start | bytes 12582916
  147.0 80.1 %collective-permute-start.11 = (bf16[2048,256]{0,1:T(8,128)(2,1)}, bf16[2048,256]{0,1:T(8,128)(2,1)}, u32[]{:S(2)}, u32[]{:S(2)}) collective-permute-start(bf16[2048,256]{0,1:T(8,128)(2,1)} %get-tuple-element.50), channel_id=1, source_target_pairs={{0,12},{4,8},{8,4},{12,0},{1,13},{5,9},{9,5},{13,1},{2,14},{6,10},... | collective-permute-start | bytes 3145736 | tf_op jit(solution)/shard_map/ppermute | solution.py:37
  185.0 115.1 %collective-permute-start.12 = (bf16[2048,256]{0,1:T(8,128)(2,1)}, bf16[2048,256]{0,1:T(8,128)(2,1)}, u32[]{:S(2)}, u32[]{:S(2)}) collective-permute-start(bf16[2048,256]{0,1:T(8,128)(2,1)} %get-tuple-element.53), channel_id=1, source_target_pairs={{0,4},{4,0},{8,12},{12,8},{1,5},{5,1},{9,13},{13,9},{2,6},{6,2},{1... | collective-permute-start | bytes 3145736 | tf_op jit(solution)/shard_map/ppermute | solution.py:37
  185.4 117.0 %collective-permute-start.13 = (bf16[2048,256]{0,1:T(8,128)(2,1)S(1)}, bf16[2048,256]{0,1:T(8,128)(2,1)}, u32[]{:S(2)}, u32[]{:S(2)}) collective-permute-start(bf16[2048,256]{0,1:T(8,128)(2,1)S(1)} %get-tuple-element.54), channel_id=1, source_target_pairs={{0,8},{4,12},{8,0},{12,4},{1,9},{5,13},{9,1},{13,5},{2,10},{6,14},... | collective-permute-start | bytes 3145736 | tf_op jit(solution)/shard_map/ppermute | solution.py:37
  187.3 57.4 %collective-permute-start.6 = (bf16[2048,256]{0,1:T(8,128)(2,1)}, bf16[2048,256]{0,1:T(8,128)(2,1)S(1)}, u32[]{:S(2)}, u32[]{:S(2)}) collective-permute-start(bf16[2048,256]{0,1:T(8,128)(2,1)} %get-tuple-element.43), channel_id=1, source_target_pairs={{0,4},{4,0},{8,12},{12,8},{1,5},{5,1},{9,13},{13,9},{2,6},{6,2},{1... | collective-permute-start | bytes 3145736 | tf_op jit(solution)/shard_map/ppermute | solution.py:37
  205.0 67.4 %collective-permute-start.7 = (bf16[2048,256]{0,1:T(8,128)(2,1)}, bf16[2048,256]{0,1:T(8,128)(2,1)S(1)}, u32[]{:S(2)}, u32[]{:S(2)}) collective-permute-start(bf16[2048,256]{0,1:T(8,128)(2,1)} %get-tuple-element.44), channel_id=1, source_target_pairs={{0,8},{4,12},{8,0},{12,4},{1,9},{5,13},{9,1},{13,5},{2,10},{6,14},... | collective-permute-start | bytes 3145736 | tf_op jit(solution)/shard_map/ppermute | solution.py:37
  227.0 67.4 %collective-permute-start.8 = (bf16[2048,256]{0,1:T(8,128)(2,1)}, bf16[2048,256]{0,1:T(8,128)(2,1)S(1)}, u32[]{:S(2)}, u32[]{:S(2)}) collective-permute-start(bf16[2048,256]{0,1:T(8,128)(2,1)} %get-tuple-element.45), channel_id=1, source_target_pairs={{0,12},{4,8},{8,4},{12,0},{1,13},{5,9},{9,5},{13,1},{2,14},{6,10},... | collective-permute-start | bytes 3145736 | tf_op jit(solution)/shard_map/ppermute | solution.py:37
  243.3 51.1 %copy-start.4 = (bf16[2048,1024]{0,1:T(8,128)(2,1)S(1)}, bf16[2048,1024]{0,1:T(8,128)(2,1)}, u32[]{:S(2)}) copy-start(bf16[2048,1024]{0,1:T(8,128)(2,1)} %convolution_bitcast_fusion.1) | copy-start | bytes 12582916
  244.7 55.4 %copy-start.25 = (bf16[2048,256]{0,1:T(8,128)(2,1)S(1)}, bf16[2048,256]{0,1:T(8,128)(2,1)}, u32[]{:S(2)}) copy-start(bf16[2048,256]{0,1:T(8,128)(2,1)} %get-tuple-element.62) | copy-start | bytes 3145732
  244.7 57.7 %copy-start.24 = (bf16[2048,256]{0,1:T(8,128)(2,1)S(1)}, bf16[2048,256]{0,1:T(8,128)(2,1)}, u32[]{:S(2)}) copy-start(bf16[2048,256]{0,1:T(8,128)(2,1)} %get-tuple-element.63) | copy-start | bytes 3145732
  244.7 72.1 %collective-permute-start.14 = (bf16[2048,256]{0,1:T(8,128)(2,1)S(1)}, bf16[2048,256]{0,1:T(8,128)(2,1)S(1)}, u32[]{:S(2)}, u32[]{:S(2)}) collective-permute-start(bf16[2048,256]{0,1:T(8,128)(2,1)S(1)} %get-tuple-element.55), channel_id=1, source_target_pairs={{0,12},{4,8},{8,4},{12,0},{1,13},{5,9},{9,5},{13,1},{2,14},{6,10},... | collective-permute-start | bytes 3145736 | tf_op jit(solution)/shard_map/ppermute | solution.py:37
  297.5 122.0 %collective-permute-start.15 = (bf16[2048,256]{0,1:T(8,128)(2,1)}, bf16[2048,256]{0,1:T(8,128)(2,1)}, u32[]{:S(2)}, u32[]{:S(2)}) collective-permute-start(bf16[2048,256]{0,1:T(8,128)(2,1)} %get-tuple-element.57), channel_id=1, source_target_pairs={{0,4},{4,0},{8,12},{12,8},{1,5},{5,1},{9,13},{13,9},{2,6},{6,2},{1... | collective-permute-start | bytes 3145736 | tf_op jit(solution)/shard_map/ppermute | solution.py:37
  298.1 122.8 %collective-permute-start.16 = (bf16[2048,256]{0,1:T(8,128)(2,1)}, bf16[2048,256]{0,1:T(8,128)(2,1)}, u32[]{:S(2)}, u32[]{:S(2)}) collective-permute-start(bf16[2048,256]{0,1:T(8,128)(2,1)} %get-tuple-element.58), channel_id=1, source_target_pairs={{0,8},{4,12},{8,0},{12,4},{1,9},{5,13},{9,1},{13,5},{2,10},{6,14},... | collective-permute-start | bytes 3145736 | tf_op jit(solution)/shard_map/ppermute | solution.py:37
  300.0 40.8 %collective-permute-start.18 = (bf16[2048,256]{0,1:T(8,128)(2,1)S(1)}, bf16[2048,256]{0,1:T(8,128)(2,1)S(1)}, u32[]{:S(2)}, u32[]{:S(2)}) collective-permute-start(bf16[2048,256]{0,1:T(8,128)(2,1)S(1)} %copy-done.25), channel_id=1, source_target_pairs={{0,4},{4,0},{8,12},{12,8},{1,5},{5,1},{9,13},{13,9},{2,6},{6,2},{1... | collective-permute-start | bytes 3145736 | tf_op jit(solution)/shard_map/ppermute | solution.py:37
  302.4 59.9 %collective-permute-start.20 = (bf16[2048,256]{0,1:T(8,128)(2,1)S(1)}, bf16[2048,256]{0,1:T(8,128)(2,1)S(1)}, u32[]{:S(2)}, u32[]{:S(2)}) collective-permute-start(bf16[2048,256]{0,1:T(8,128)(2,1)S(1)} %copy-done.24), channel_id=1, source_target_pairs={{0,8},{4,12},{8,0},{12,4},{1,9},{5,13},{9,1},{13,5},{2,10},{6,14},... | collective-permute-start | bytes 3145736 | tf_op jit(solution)/shard_map/ppermute | solution.py:37
  316.8 67.4 %collective-permute-start.22 = (bf16[2048,256]{0,1:T(8,128)(2,1)S(1)}, bf16[2048,256]{0,1:T(8,128)(2,1)S(1)}, u32[]{:S(2)}, u32[]{:S(2)}) collective-permute-start(bf16[2048,256]{0,1:T(8,128)(2,1)S(1)} %copy-done.23), channel_id=1, source_target_pairs={{0,12},{4,8},{8,4},{12,0},{1,13},{5,9},{9,5},{13,1},{2,14},{6,10},... | collective-permute-start | bytes 3145736 | tf_op jit(solution)/shard_map/ppermute | solution.py:37
  334.4 50.8 %copy-start.35 = (f32[1024,1024]{1,0:T(8,128)S(1)}, f32[1024,1024]{1,0:T(8,128)}, u32[]{:S(2)}) copy-start(f32[1024,1024]{1,0:T(8,128)} %fusion.14) | copy-start | bytes 12582916
  340.8 53.2 %copy-start.18 = (bf16[2048,256]{0,1:T(8,128)(2,1)}, bf16[2048,256]{0,1:T(8,128)(2,1)S(1)}, u32[]{:S(2)}) copy-start(bf16[2048,256]{0,1:T(8,128)(2,1)S(1)} %collective-permute-done.18) | copy-start | bytes 3145732
  340.8 81.4 %collective-permute-start.17 = (bf16[2048,256]{0,1:T(8,128)(2,1)}, bf16[2048,256]{0,1:T(8,128)(2,1)}, u32[]{:S(2)}, u32[]{:S(2)}) collective-permute-start(bf16[2048,256]{0,1:T(8,128)(2,1)} %get-tuple-element.59), channel_id=1, source_target_pairs={{0,12},{4,8},{8,4},{12,0},{1,13},{5,9},{9,5},{13,1},{2,14},{6,10},... | collective-permute-start | bytes 3145736 | tf_op jit(solution)/shard_map/ppermute | solution.py:37
  410.4 124.4 %all-reduce.7.cloned.1.call-start = ((), (), s32[]{:S(2)}) async-start(), calls=%async_computation.1 | async-start | bytes 2097152
  416.9 48.6 %collective-permute-start.19 = (bf16[2048,256]{0,1:T(8,128)(2,1)}, bf16[2048,256]{0,1:T(8,128)(2,1)}, u32[]{:S(2)}, u32[]{:S(2)}) collective-permute-start(bf16[2048,256]{0,1:T(8,128)(2,1)} %get-tuple-element.85), channel_id=1, source_target_pairs={{0,4},{4,0},{8,12},{12,8},{1,5},{5,1},{9,13},{13,9},{2,6},{6,2},{1... | collective-permute-start | bytes 3145736 | tf_op jit(solution)/shard_map/ppermute | solution.py:37
  417.7 47.8 %collective-permute-start.21 = (bf16[2048,256]{0,1:T(8,128)(2,1)}, bf16[2048,256]{0,1:T(8,128)(2,1)}, u32[]{:S(2)}, u32[]{:S(2)}) collective-permute-start(bf16[2048,256]{0,1:T(8,128)(2,1)} %get-tuple-element.84), channel_id=1, source_target_pairs={{0,8},{4,12},{8,0},{12,4},{1,9},{5,13},{9,1},{13,5},{2,10},{6,14},... | collective-permute-start | bytes 3145736 | tf_op jit(solution)/shard_map/ppermute | solution.py:37
  419.6 45.9 %collective-permute-start.23 = (bf16[2048,256]{0,1:T(8,128)(2,1)}, bf16[2048,256]{0,1:T(8,128)(2,1)}, u32[]{:S(2)}, u32[]{:S(2)}) collective-permute-start(bf16[2048,256]{0,1:T(8,128)(2,1)} %get-tuple-element.83), channel_id=1, source_target_pairs={{0,12},{4,8},{8,4},{12,0},{1,13},{5,9},{9,5},{13,1},{2,14},{6,10},... | collective-permute-start | bytes 3145736 | tf_op jit(solution)/shard_map/ppermute | solution.py:37
  (34 other events, 299.8 us)
Sparse Core Ops, SparseCore 0:
  410.6 53.9 all-reduce.4
  481.8 53.0 all-reduce.6

commit v4 on v3

--- a/solution.py
+++ b/solution.py
@@ -55,60 +55,65 @@
     def rows(a, k):
         return a[k * step:(k + 1) * step]
 
-    def forward(k):
-        hidden = jnp.dot(rows(tokens, k), w1p, preferred_element_type=jnp.float32)
+    def forward(tok, cot, k):
+        hidden = jnp.dot(rows(tok, k), w1p, preferred_element_type=jnp.float32)
         hidden = hidden.astype(jnp.bfloat16)
-        backed = jnp.dot(rows(cotangent, k), w2p, preferred_element_type=jnp.float32)
+        backed = jnp.dot(rows(cot, k), w2p, preferred_element_type=jnp.float32)
         return [hidden[:, m * part:(m + 1) * part] for m in range(n_dev)], backed
 
     def add(acc, val):
         return val if acc is None else acc + val
 
-    pieces, backed = forward(0)
+    pieces, backed = forward(tokens, cotangent, 0)
     moved = exchange(pieces, n_dev)
+    pieces_next, backed_next = forward(tokens, cotangent, 1)
+    grad_tokens = jnp.zeros((tok_rows, feat), jnp.bfloat16)
     gf_acc = gs_acc = None
-    outs = []
-    returned_prev = None
-    for k in range(CHUNKS):
+    returned = None
+    grad_second = None
+    for j in range(1, CHUNKS + 1):
         masked = [
             jnp.where(moved[m] > 0, backed[:, m * part:(m + 1) * part], 0.0).astype(jnp.bfloat16)
             for m in range(n_dev)
         ]
-        active = jnp.maximum(jnp.concatenate(moved, axis=1), jnp.zeros((), jnp.bfloat16))
-        gs_k = lax.dot_general(
-            active, rows(cotangent, k), (((0,), (0,)), ((), ())), preferred_element_type=jnp.float32
-        )
-        if k + 1 < CHUNKS:
-            pieces, backed = forward(k + 1)
-            tied = (masked, pieces, backed, gs_acc, gf_acc, outs)
-            masked, pieces, backed, gs_acc, gf_acc, outs = lax.optimization_barrier(tied)
-            moved = exchange(pieces, n_dev)
-        gs_acc = add(gs_acc, gs_k)
+        tied = (masked, pieces_next, backed_next, moved, returned, tokens, cotangent,
+                gs_acc, gf_acc, grad_tokens)
+        (masked, pieces_next, backed_next, moved, returned, tokens, cotangent,
+         gs_acc, gf_acc, grad_tokens) = lax.optimization_barrier(tied)
+        moved_prev, returned_prev = moved, returned
+        if j < CHUNKS:
+            moved = exchange(pieces_next, n_dev)
+            backed = backed_next
+        returned = jnp.concatenate(exchange(masked, n_dev), axis=1)
+        if j + 1 < CHUNKS:
+            pieces_next, backed_next = forward(tokens, cotangent, j + 1)
+        active = jnp.maximum(jnp.concatenate(moved_prev, axis=1), jnp.zeros((), jnp.bfloat16))
+        gs_acc = add(gs_acc, lax.dot_general(
+            active, rows(cotangent, j - 1), (((0,), (0,)), ((), ())),
+            preferred_element_type=jnp.float32))
         if returned_prev is not None:
-            gt, gf = backward(returned_prev, tokens, k - 1, w1tp, step, n_dev, blk_local, sub)
-            outs = outs + [gt]
+            gt, gf = backward(returned_prev, rows(tokens, j - 2), w1tp, n_dev, blk_local, sub)
+            grad_tokens = lax.dynamic_update_slice(grad_tokens, gt, ((j - 2) * step, 0))
             gf_acc = add(gf_acc, gf)
-        returned_prev = jnp.concatenate(exchange(masked, n_dev), axis=1)
-    gs6 = gs_acc.reshape(n_dev, blk_local, blk_local, sub, blk_local, bs)
-    gsd = jnp.take(jnp.diagonal(gs6, axis1=1, axis2=4), order, axis=0)
-    second_term = gsd.transpose(2, 0, 1, 4, 3).reshape(bs, blk_local, bs) * grad_scale
-    grad_second = lax.psum_scatter(second_term, "dp", scatter_dimension=0, tiled=True)
-    returned_prev, grad_second = lax.optimization_barrier((returned_prev, grad_second))
-    gt, gf = backward(returned_prev, tokens, CHUNKS - 1, w1tp, step, n_dev, blk_local, sub)
-    outs = outs + [gt]
+        if j == CHUNKS:
+            gs6 = gs_acc.reshape(n_dev, blk_local, blk_local, sub, blk_local, bs)
+            gsd = jnp.take(jnp.diagonal(gs6, axis1=1, axis2=4), order, axis=0)
+            second_term = gsd.transpose(4, 2, 0, 1, 3).reshape(blk_local, bs, bs) * grad_scale
+            grad_second = lax.psum_scatter(second_term, "dp", scatter_dimension=1, tiled=True)
+            returned, grad_second, tokens = lax.optimization_barrier((returned, grad_second, tokens))
+    gt, gf = backward(returned, rows(tokens, CHUNKS - 1), w1tp, n_dev, blk_local, sub)
+    grad_tokens = lax.dynamic_update_slice(grad_tokens, gt, ((CHUNKS - 1) * step, 0))
     gf_acc = add(gf_acc, gf)
-
-    grad_tokens = jnp.concatenate(outs, axis=0)
-    first_term = jnp.take(gf_acc, order, axis=2).reshape(bs, blk_local, bs) * grad_scale
-    grad_first = lax.psum_scatter(first_term, "dp", scatter_dimension=0, tiled=True)
-    return (grad_tokens, grad_first.transpose(1, 0, 2), grad_second.transpose(1, 0, 2))
+    first_term = jnp.take(gf_acc, order, axis=2).reshape(blk_local, bs, bs) * grad_scale
+    grad_first = lax.psum_scatter(first_term, "dp", scatter_dimension=1, tiled=True)
+    return (grad_tokens, grad_first, grad_second)
 
 
-def backward(returned, tokens, k, w1tp, step, n_dev, blk_local, sub):
-    x = tokens[k * step:(k + 1) * step]
+def backward(returned, x, w1tp, n_dev, blk_local, sub):
+    step = x.shape[0]
     gt = jnp.dot(returned, w1tp, preferred_element_type=jnp.float32).astype(jnp.bfloat16)
     gf = jnp.einsum(
-        "tmcbq,tbi->ibmcq",
+        "tmcbq,tbi->bimcq",
         returned.reshape(step, n_dev, blk_local, blk_local, sub),
         x.reshape(step, blk_local, -1),
         preferred_element_type=jnp.float32,

time: 553 us -> 555 us (level)
  waiting for transfers between devices: 240 us -> 165 us
  local copies, waits for them, and re-layouts: 96.3 us -> 160 us
  other arithmetic: 37.5 us -> 54.7 us
    optimization_barrier x1 -> x7, local copies, waits for them, and re-layouts: 0.97 us -> 98.9 us  [the longest x5 76.7 us: shards(): lax.optimization_barrier(tied)]
    ppermute x24, waiting for transfers between devices: 169 us -> 106 us  [exchange(): lax.ppermute(pieces[m], 'tensor', [(i, i ^ m) for i in range(n_dev)])]
    unnamed x101 -> x78, local copies, waits for them, and re-layouts: 58.2 us -> 17.3 us
    unnamed x4, waiting for transfers between devices: 71.1 us -> 59 us
    add x1 -> x5, other arithmetic: 1.36 us -> 11.9 us  [add(): return val if acc is None else acc + val]
    slice x0 -> x7, local copies, waits for them, and re-layouts: none -> 9.24 us  [rows(): return a[k * step:(k + 1) * step]]
    broadcast_in_dim x2 -> x3, local copies, waits for them, and re-layouts: 0.68 us -> 6.28 us  [the longest x1 6.12 us: shards(): grad_tokens = jnp.zeros((tok_rows, feat), jnp.bfloat16)]
    concatenate x3 -> x4, other arithmetic: 15.9 us -> 20.1 us  [shards(): returned = jnp.concatenate(exchange(masked, n_dev), axis=1)]
  transfers between devices with their start and end apart: 26 -> 26, of which waited for: 11 -> 9; matrix products, arithmetic and copies ran while one was open for 41% -> 44% of each run, Pallas kernels for 0% -> 0%
where the time goes in v4:
time: 555 us; the launch traced here: 549 us
  waiting for transfers between devices  165 us (30%)
  local copies, waits for them, and re-layouts  160 us (29%)
  matrix products  135 us (24%)
  other arithmetic  54.7 us (10%)
  starting transfers between devices  17.5 us (3%)
  between operations  15.5 us (3%)
    ppermute x24, waiting for transfers between devices, exchange(): lax.ppermute(pieces[m], 'tensor', [(i, i ^ m) for i in range(n_dev)])  106 us
    optimization_barrier x5, local copies, waits for them, and re-layouts, shards(): lax.optimization_barrier(tied)  76.7 us
    unnamed x4, waiting for transfers between devices  59 us
    dot_general x4, matrix products, shards(): lax.dot_general(active, rows(cotangent, j - 1), (((0,), (0,)), ((), ())),...  36 us
    dot_general x4, matrix products, forward(): backed = jnp.dot(rows(cot, k), w2p, preferred_element_type=jnp.float32)  32.1 us
    dot_general x4, matrix products, forward(): hidden = jnp.dot(rows(tok, k), w1p, preferred_element_type=jnp.float32)  28.9 us
    dot_general x4, matrix products, backward(): jnp.dot(returned, w1tp, preferred_element_type=jnp.float32)  27.6 us
    optimization_barrier x2, local copies, waits for them, and re-layouts, shards(): lax.optimization_barrier((returned, grad_second, tokens))  22.2 us
  transfers between devices with their start and end apart: 26, of which 9 were waited for; matrix products, arithmetic and copies ran while one was open for 44% of the time, Pallas kernels for 0%

profile of v4, /device:TPU:0, one launch (start us, length us, event | category | flops | bytes accessed | tf_op | source)
XLA Modules:
  0.0 548.7 jit_solution(16549955289811571740)
XLA Ops:
  14.2 7.8 %convert_bitcast_fusion.1 = bf16[2048,1024]{0,1:T(8,128)(2,1)S(1)} fusion(bf16[1024,1024]{0,1:T(8,128)(2,1)S(1)} %bitcast.111, bf16[8192,1024]{1,0:T(8,128)(2,1)} %param.4), kind=kOutput, calls=%fused_computation.73 | convolution fusion | flops 4297064448 | bytes 10485760 | tf_op jit(solution)/shard_map/dot_general | solution.py:59
  28.8 8.4 %convert_bitcast_fusion = bf16[2048,1024]{0,1:T(8,128)(2,1)} fusion(bf16[1024,1024]{0,1:T(8,128)(2,1)S(1)} %bitcast.112, bf16[8192,1024]{1,0:T(8,128)(2,1)} %param.4), kind=kOutput, calls=%fused_computation.69 | convolution fusion | flops 4297064448 | bytes 10485760 | tf_op jit(solution)/shard_map/dot_general | solution.py:59
  42.0 7.1 %convolution_bitcast_fusion.1 = bf16[2048,1024]{0,1:T(8,128)(2,1)S(1)} fusion(bf16[1024,1024]{0,1:T(8,128)(2,1)S(1)} %bitcast.115, bf16[8192,1024]{1,0:T(8,128)(2,1)} %param.5), kind=kOutput, calls=%fused_computation.6 | convolution fusion | flops 4294967296 | bytes 10485760 | tf_op jit(solution)/shard_map/dot_general | solution.py:61
  51.7 7.0 %convolution_bitcast_fusion = bf16[2048,1024]{0,1:T(8,128)(2,1)S(1)} fusion(bf16[1024,1024]{0,1:T(8,128)(2,1)S(1)} %bitcast.116, bf16[8192,1024]{1,0:T(8,128)(2,1)} %param.5), kind=kOutput, calls=%fused_computation.5 | convolution fusion | flops 4294967296 | bytes 10485760 | tf_op jit(solution)/shard_map/dot_general | solution.py:61
  58.8 16.3 %collective-permute-done.2 = bf16[2048,256]{0,1:T(8,128)(2,1)} collective-permute-done((bf16[2048,256]{0,1:T(8,128)(2,1)}, bf16[2048,256]{0,1:T(8,128)(2,1)}, u32[]{:S(2)}, u32[]{:S(2)}) %collective-permute-start.2) | collective-permute-done | bytes 1048608 | tf_op jit(solution)/shard_map/ppermute | solution.py:37
  83.4 9.8 %fusion = f32[1024,1024]{1,0:T(8,128)} fusion(bf16[2048,256]{0,1:T(8,128)(2,1)} %collective-permute-done.2, bf16[2048,256]{0,1:T(8,128)(2,1)} %collective-permute-done.1, bf16[2048,256]{0,1:T(8,128)(2,1)} %collective-permute-done, bf16[2048,256]{0,1:T(8,128)(2,1)S(1)} %get-tuple-element.84, bf16[8192,1024]{1,0:T(8,128)(2,1)} %param.5), kind=kOutput, calls=%fused_computation.9 | convolution fusion | flops 4315938816 | bytes 12582912 | tf_op jit(solution)/shard_map/dot_general | solution.py:91
  93.2 8.5 %fusion.44 = bf16[2048,1024]{1,0:T(8,128)(2,1)} fusion(bf16[1024,1024]{0,1:T(8,128)(2,1)S(1)} %bitcast.117, bf16[8192,1024]{1,0:T(8,128)(2,1)} %param.5), kind=kOutput, calls=%fused_computation.64 | convolution fusion | flops 4294967296 | bytes 10485760 | tf_op jit(solution)/shard_map/dot_general | solution.py:61
  102.7 6.4 %fusion.58 = bf16[2048,1024]{0,1:T(8,128)(2,1)S(1)} fusion(bf16[1024,1024]{0,1:T(8,128)(2,1)} %bitcast.113, bf16[8192,1024]{1,0:T(8,128)(2,1)S(1)} %bitcast.92), kind=kOutput, calls=%fused_computation.76 | convolution fusion | flops 4297064448 | bytes 10485760 | tf_op jit(solution)/shard_map/dot_general | solution.py:59
  110.8 16.7 %collective-permute-done.8 = bf16[2048,256]{0,1:T(8,128)(2,1)} collective-permute-done((bf16[2048,256]{0,1:T(8,128)(2,1)}, bf16[2048,256]{0,1:T(8,128)(2,1)}, u32[]{:S(2)}, u32[]{:S(2)}) %collective-permute-start.8) | collective-permute-done | bytes 1048608 | tf_op jit(solution)/shard_map/ppermute | solution.py:37
  133.2 17.7 %collective-permute-done.4 = bf16[2048,256]{0,1:T(8,128)(2,1)} collective-permute-done((bf16[2048,256]{0,1:T(8,128)(2,1)}, bf16[2048,256]{0,1:T(8,128)(2,1)}, u32[]{:S(2)}, u32[]{:S(2)}) %collective-permute-start.4) | collective-permute-done | bytes 1048608 | tf_op jit(solution)/shard_map/ppermute | solution.py:37
  150.8 21.4 %collective-permute-done.5 = bf16[2048,256]{0,1:T(8,128)(2,1)} collective-permute-done((bf16[2048,256]{0,1:T(8,128)(2,1)}, bf16[2048,256]{0,1:T(8,128)(2,1)}, u32[]{:S(2)}, u32[]{:S(2)}) %collective-permute-start.5) | collective-permute-done | bytes 1048608 | tf_op jit(solution)/shard_map/ppermute | solution.py:37
  179.0 6.4 %fusion.61 = bf16[2048,1024]{0,1:T(8,128)(2,1)S(1)} fusion(bf16[1024,1024]{0,1:T(8,128)(2,1)} %bitcast.114, bf16[8192,1024]{1,0:T(8,128)(2,1)S(1)} %bitcast.92), kind=kOutput, calls=%fused_computation.77 | convolution fusion | flops 4297064448 | bytes 10485760 | tf_op jit(solution)/shard_map/dot_general | solution.py:59
  185.4 9.4 %fusion.39 = bf16[2048,1024]{1,0:T(8,128)(2,1)} fusion(bf16[1024,1024]{0,1:T(8,128)(2,1)} %bitcast.118, bf16[8192,1024]{1,0:T(8,128)(2,1)} %param.5), kind=kOutput, calls=%fused_computation.59 | convolution fusion | flops 4294967296 | bytes 10485760 | tf_op jit(solution)/shard_map/dot_general | solution.py:61
  196.8 9.6 %fusion.7 = f32[1024,1024]{1,0:T(8,128)} fusion(bf16[2048,256]{0,1:T(8,128)(2,1)} %collective-permute-done.5, bf16[2048,256]{0,1:T(8,128)(2,1)} %collective-permute-done.4, bf16[2048,256]{0,1:T(8,128)(2,1)} %collective-permute-done.3, bf16[2048,256]{0,1:T(8,128)(2,1)S(1)} %get-tuple-element.101, bf16[8192,1024]{1,0:T(8,128)(2,1)} %param.5), kind=kOutput, calls=%fused_computation.18 | convolution fusion | flops 4315938816 | bytes 12582912 | tf_op jit(solution)/shard_map/dot_general | solution.py:91
  212.6 6.7 %convert_dynamic-update-slice_fusion.3 = bf16[8192,1024]{1,0:T(8,128)(2,1)} fusion(bf16[8192,1024]{1,0:T(8,128)(2,1)} %broadcast_in_dim.144, bf16[2048,1024]{0,1:T(8,128)(2,1)S(1)} %pad_maximum_fusion, bf16[1024,1024]{1,0:T(8,128)(2,1)S(1)} %bitcast.107), kind=kOutput, calls=%fused_computation.57 | convolution fusion | flops 4297064448 | bytes 10485760 | tf_op jit(solution)/shard_map/dot_general | solution.py:114
  221.1 21.3 %copy.96 = bf16[8192,1024]{0,1:T(8,128)(2,1)} copy(bf16[8192,1024]{1,0:T(8,128)(2,1)} %param.4) | data formatting | bytes 33554432 | tf_op jit(solution)/shard_map/optimization_barrier | solution.py:82
  242.4 6.5 %copy.91 = bf16[2048,1024]{0,1:T(8,128)(2,1)} copy(bf16[2048,1024]{1,0:T(8,128)(2,1)} %fusion.44) | data formatting | bytes 8388608 | tf_op jit(solution)/shard_map/optimization_barrier | solution.py:82
  248.9 7.0 %add.49 = f32[1024,1024]{1,0:T(8,128)} add(f32[1024,1024]{1,0:T(8,128)} %fusion, f32[1024,1024]{1,0:T(8,128)} %fusion.7) | non-fusion elementwise | flops 1048576 | bytes 12582912 | tf_op jit(solution)/shard_map/add | solution.py:65
  262.0 7.6 %collective-permute-done.11 = bf16[2048,256]{0,1:T(8,128)(2,1)} collective-permute-done((bf16[2048,256]{0,1:T(8,128)(2,1)}, bf16[2048,256]{0,1:T(8,128)(2,1)}, u32[]{:S(2)}, u32[]{:S(2)}) %collective-permute-start.11) | collective-permute-done | bytes 1048608 | tf_op jit(solution)/shard_map/ppermute | solution.py:37
  277.6 9.6 %fusion.14 = f32[1024,1024]{1,0:T(8,128)} fusion(bf16[2048,256]{0,1:T(8,128)(2,1)} %collective-permute-done.11, bf16[2048,256]{0,1:T(8,128)(2,1)} %collective-permute-done.10, bf16[2048,256]{0,1:T(8,128)(2,1)} %collective-permute-done.9, bf16[2048,256]{0,1:T(8,128)(2,1)S(1)} %get-tuple-element.119, bf16[8192,1024]{1,0:T(8,128)(2,1)} %param.5), kind=kOutput, calls=%fused_computation.27 | convolution fusion | flops 4315938816 | bytes 12582912 | tf_op jit(solution)/shard_map/dot_general | solution.py:91
  287.2 21.3 %copy.105 = bf16[8192,1024]{0,1:T(8,128)(2,1)} copy(bf16[8192,1024]{1,0:T(8,128)(2,1)} %param.4) | data formatting | bytes 33554432 | tf_op jit(solution)/shard_map/optimization_barrier | solution.py:82
  313.3 6.7 %copy.101 = bf16[2048,1024]{0,1:T(8,128)(2,1)} copy(bf16[2048,1024]{1,0:T(8,128)(2,1)} %fusion.39) | data formatting | bytes 8388608 | tf_op jit(solution)/shard_map/optimization_barrier | solution.py:82
  331.0 6.2 %convert_dynamic-update-slice_fusion.2 = bf16[8192,1024]{1,0:T(8,128)(2,1)} fusion(bf16[8192,1024]{1,0:T(8,128)(2,1)} %convert_dynamic-update-slice_fusion.3, bf16[2048,1024]{0,1:T(8,128)(2,1)S(1)} %copy-done.7, bf16[1024,1024]{1,0:T(8,128)(2,1)S(1)} %bitcast.108), kind=kOutput, calls=%fused_computation.55 | convolution fusion | flops 4297064448 | bytes 10485760 | tf_op jit(solution)/shard_map/dot_general | solution.py:114
  346.1 21.6 %collective-permute-done.17 = bf16[2048,256]{0,1:T(8,128)(2,1)S(1)} collective-permute-done((bf16[2048,256]{0,1:T(8,128)(2,1)S(1)}, bf16[2048,256]{0,1:T(8,128)(2,1)S(1)}, u32[]{:S(2)}, u32[]{:S(2)}) %collective-permute-start.17) | collective-permute-done | bytes 1048608 | tf_op jit(solution)/shard_map/ppermute | solution.py:37
  372.4 7.0 %fusion.21 = f32[1024,1024]{1,0:T(8,128)S(1)} fusion(bf16[2048,256]{0,1:T(8,128)(2,1)S(1)} %collective-permute-done.17, bf16[2048,256]{0,1:T(8,128)(2,1)S(1)} %collective-permute-done.16, bf16[2048,256]{0,1:T(8,128)(2,1)} %collective-permute-done.15, bf16[2048,256]{0,1:T(8,128)(2,1)S(1)} %get-tuple-element.133, bf16[8192,1024]{1,0:T(8,128)(2,1)} %param.5), kind=kOutput, calls=%fused_computation.36 | convolution fusion | flops 4315938816 | bytes 12582912 | tf_op jit(solution)/shard_map/dot_general | solution.py:91
  402.0 20.9 %copy.110 = bf16[8192,1024]{0,1:T(8,128)(2,1)} copy(bf16[8192,1024]{1,0:T(8,128)(2,1)} %param.4) | data formatting | bytes 33554432 | tf_op jit(solution)/shard_map/optimization_barrier | solution.py:82
  428.8 23.1 %all-reduce.5.cloned.1.call-done = f32[4,256,256]{2,0,1:T(4,128)} async-done(((f32[4,256,256]{2,0,1:T(4,128)}), f32[4,256,256]{2,0,1:T(4,128)}) %all-reduce.5.cloned.1.call-update) | async-done | bytes 1048592
  452.9 6.9 %pad_maximum_fusion.3 = bf16[2048,1024]{0,1:T(8,128)(2,1)} fusion(bf16[2048,256]{0,1:T(8,128)(2,1)} %collective-permute-done.23, bf16[2048,256]{0,1:T(8,128)(2,1)} %collective-permute-done.22, bf16[2048,256]{0,1:T(8,128)(2,1)S(1)} %collective-permute-done.21, bf16[2048,256]{0,1:T(8,128)(2,1)S(1)} %copy-done.12), kind=kLoop, calls=%fused_computation.34 | loop fusion | flops 16777216 | bytes 8388608 | tf_op jit(solution)/shard_map/concatenate | solution.py:87
  459.8 21.3 %copy.113 = bf16[8192,1024]{0,1:T(8,128)(2,1)} copy(bf16[8192,1024]{1,0:T(8,128)(2,1)} %param.4) | data formatting | bytes 33554432 | tf_op jit(solution)/shard_map/optimization_barrier | solution.py:103
  488.6 8.5 %convert_dynamic-update-slice_fusion.1 = bf16[8192,1024]{1,0:T(8,128)(2,1)} fusion(bf16[8192,1024]{1,0:T(8,128)(2,1)} %convert_dynamic-update-slice_fusion.2, bf16[2048,1024]{0,1:T(8,128)(2,1)} %pad_maximum_fusion.2, bf16[1024,1024]{1,0:T(8,128)(2,1)S(1)} %bitcast.109), kind=kOutput, calls=%fused_computation.54 | convolution fusion | flops 4297064448 | bytes 10485760 | tf_op jit(solution)/shard_map/dot_general | solution.py:114
  497.8 6.2 %convert_dynamic-update-slice_fusion = bf16[8192,1024]{1,0:T(8,128)(2,1)} fusion(bf16[8192,1024]{1,0:T(8,128)(2,1)} %convert_dynamic-update-slice_fusion.1, bf16[2048,1024]{0,1:T(8,128)(2,1)S(1)} %copy-done.9, bf16[1024,1024]{1,0:T(8,128)(2,1)S(1)} %bitcast.110), kind=kOutput, calls=%fused_computation.52 | convolution fusion | flops 4297064448 | bytes 10485760 | tf_op jit(solution)/shard_map/dot_general | solution.py:114
  504.0 35.9 %all-reduce.7.cloned.1.call-done = f32[4,256,256]{2,0,1:T(4,128)} async-done(((f32[4,256,256]{2,0,1:T(4,128)}), f32[4,256,256]{2,0,1:T(4,128)}) %all-reduce.7.cloned.1.call-update) | async-done | bytes 1048592
  (180 shorter events, 136.6 us)
Async XLA Ops:
  7.2 444.7 %all-reduce.5.cloned.1.call-start = ((), (), s32[]{:S(2)}) async-start(), calls=%async_computation | async-start | bytes 2097152
  25.7 33.0 %collective-permute-start = (bf16[2048,256]{0,1:T(8,128)(2,1)}, bf16[2048,256]{0,1:T(8,128)(2,1)}, u32[]{:S(2)}, u32[]{:S(2)}) collective-permute-start(bf16[2048,256]{0,1:T(8,128)(2,1)} %get-tuple-element.183), channel_id=1, source_target_pairs={{0,4},{4,0},{8,12},{12,8},{1,5},{5,1},{9,13},{13,9},{2,6},{6,2},{1... | collective-permute-start | bytes 3145736 | tf_op jit(solution)/shard_map/ppermute | solution.py:37
  26.2 32.6 %collective-permute-start.1 = (bf16[2048,256]{0,1:T(8,128)(2,1)}, bf16[2048,256]{0,1:T(8,128)(2,1)}, u32[]{:S(2)}, u32[]{:S(2)}) collective-permute-start(bf16[2048,256]{0,1:T(8,128)(2,1)} %get-tuple-element.182), channel_id=1, source_target_pairs={{0,8},{4,12},{8,0},{12,4},{1,9},{5,13},{9,1},{13,5},{2,10},{6,14},... | collective-permute-start | bytes 3145736 | tf_op jit(solution)/shard_map/ppermute | solution.py:37
  28.7 46.4 %collective-permute-start.2 = (bf16[2048,256]{0,1:T(8,128)(2,1)}, bf16[2048,256]{0,1:T(8,128)(2,1)}, u32[]{:S(2)}, u32[]{:S(2)}) collective-permute-start(bf16[2048,256]{0,1:T(8,128)(2,1)} %get-tuple-element.181), channel_id=1, source_target_pairs={{0,12},{4,8},{8,4},{12,0},{1,13},{5,9},{9,5},{13,1},{2,14},{6,10},... | collective-permute-start | bytes 3145736 | tf_op jit(solution)/shard_map/ppermute | solution.py:37
  39.5 53.6 %copy-start.18 = (bf16[128,8,4,256]{3,1,2,0:T(8,128)(2,1)}, bf16[128,8,4,256]{3,1,2,0:T(8,128)(2,1)S(1)}, u32[]{:S(2)}) copy-start(bf16[128,8,4,256]{3,1,2,0:T(8,128)(2,1)S(1)} %copy.135) | copy-start | bytes 6291460
  79.4 22.3 %collective-permute-start.6 = (bf16[2048,256]{0,1:T(8,128)(2,1)S(1)}, bf16[2048,256]{0,1:T(8,128)(2,1)S(1)}, u32[]{:S(2)}, u32[]{:S(2)}) collective-permute-start(bf16[2048,256]{0,1:T(8,128)(2,1)S(1)} %get-tuple-element.81), channel_id=1, source_target_pairs={{0,4},{4,0},{8,12},{12,8},{1,5},{5,1},{9,13},{13,9},{2,6},{6,2},{1... | collective-permute-start | bytes 3145736 | tf_op jit(solution)/shard_map/ppermute | solution.py:37
  79.6 31.3 %collective-permute-start.7 = (bf16[2048,256]{0,1:T(8,128)(2,1)}, bf16[2048,256]{0,1:T(8,128)(2,1)}, u32[]{:S(2)}, u32[]{:S(2)}) collective-permute-start(bf16[2048,256]{0,1:T(8,128)(2,1)} %get-tuple-element.82), channel_id=1, source_target_pairs={{0,8},{4,12},{8,0},{12,4},{1,9},{5,13},{9,1},{13,5},{2,10},{6,14},... | collective-permute-start | bytes 3145736 | tf_op jit(solution)/shard_map/ppermute | solution.py:37
  81.2 46.3 %collective-permute-start.8 = (bf16[2048,256]{0,1:T(8,128)(2,1)}, bf16[2048,256]{0,1:T(8,128)(2,1)}, u32[]{:S(2)}, u32[]{:S(2)}) collective-permute-start(bf16[2048,256]{0,1:T(8,128)(2,1)} %get-tuple-element.83), channel_id=1, source_target_pairs={{0,12},{4,8},{8,4},{12,0},{1,13},{5,9},{9,5},{13,1},{2,14},{6,10},... | collective-permute-start | bytes 3145736 | tf_op jit(solution)/shard_map/ppermute | solution.py:37
  81.3 51.8 %collective-permute-start.3 = (bf16[2048,256]{0,1:T(8,128)(2,1)}, bf16[2048,256]{0,1:T(8,128)(2,1)}, u32[]{:S(2)}, u32[]{:S(2)}) collective-permute-start(bf16[2048,256]{0,1:T(8,128)(2,1)} %get-tuple-element.75), channel_id=1, source_target_pairs={{0,4},{4,0},{8,12},{12,8},{1,5},{5,1},{9,13},{13,9},{2,6},{6,2},{1... | collective-permute-start | bytes 3145736 | tf_op jit(solution)/shard_map/ppermute | solution.py:37
  81.8 69.1 %collective-permute-start.4 = (bf16[2048,256]{0,1:T(8,128)(2,1)}, bf16[2048,256]{0,1:T(8,128)(2,1)}, u32[]{:S(2)}, u32[]{:S(2)}) collective-permute-start(bf16[2048,256]{0,1:T(8,128)(2,1)} %get-tuple-element.76), channel_id=1, source_target_pairs={{0,8},{4,12},{8,0},{12,4},{1,9},{5,13},{9,1},{13,5},{2,10},{6,14},... | collective-permute-start | bytes 3145736 | tf_op jit(solution)/shard_map/ppermute | solution.py:37
  83.4 19.3 %slice-start.1 = ((s8[16777216]{0:T(1024)(128)(4,1)}), s8[4194304]{0:T(1024)(128)(4,1)S(1)}, s32[]{:S(2)}) async-start(s8[16777216]{0:T(1024)(128)(4,1)} %bitcast.91), calls=%async_computation.3 | async-start | bytes 8388608
  83.4 19.3 %slice-start.2 = ((s8[16777216]{0:T(1024)(128)(4,1)}), s8[4194304]{0:T(1024)(128)(4,1)S(1)}, s32[]{:S(2)}) async-start(s8[16777216]{0:T(1024)(128)(4,1)} %bitcast.91), calls=%async_computation.4 | async-start | bytes 8388608
  102.7 69.5 %collective-permute-start.5 = (bf16[2048,256]{0,1:T(8,128)(2,1)}, bf16[2048,256]{0,1:T(8,128)(2,1)}, u32[]{:S(2)}, u32[]{:S(2)}) collective-permute-start(bf16[2048,256]{0,1:T(8,128)(2,1)} %get-tuple-element.77), channel_id=1, source_target_pairs={{0,12},{4,8},{8,4},{12,0},{1,13},{5,9},{9,5},{13,1},{2,14},{6,10},... | collective-permute-start | bytes 3145736 | tf_op jit(solution)/shard_map/ppermute | solution.py:37
  133.2 79.4 %copy-start.5 = (bf16[2048,1024]{0,1:T(8,128)(2,1)}, bf16[2048,1024]{0,1:T(8,128)(2,1)S(1)}, u32[]{:S(2)}) copy-start(bf16[2048,1024]{0,1:T(8,128)(2,1)S(1)} %pad_maximum_fusion) | copy-start | bytes 12582916
  177.1 42.1 %collective-permute-start.12 = (bf16[2048,256]{0,1:T(8,128)(2,1)}, bf16[2048,256]{0,1:T(8,128)(2,1)}, u32[]{:S(2)}, u32[]{:S(2)}) collective-permute-start(bf16[2048,256]{0,1:T(8,128)(2,1)} %get-tuple-element.97), channel_id=1, source_target_pairs={{0,4},{4,0},{8,12},{12,8},{1,5},{5,1},{9,13},{13,9},{2,6},{6,2},{1... | collective-permute-start | bytes 3145736 | tf_op jit(solution)/shard_map/ppermute | solution.py:37
  177.5 80.7 %collective-permute-start.13 = (bf16[2048,256]{0,1:T(8,128)(2,1)}, bf16[2048,256]{0,1:T(8,128)(2,1)}, u32[]{:S(2)}, u32[]{:S(2)}) collective-permute-start(bf16[2048,256]{0,1:T(8,128)(2,1)} %get-tuple-element.98), channel_id=1, source_target_pairs={{0,8},{4,12},{8,0},{12,4},{1,9},{5,13},{9,1},{13,5},{2,10},{6,14},... | collective-permute-start | bytes 3145736 | tf_op jit(solution)/shard_map/ppermute | solution.py:37
  179.0 79.1 %collective-permute-start.14 = (bf16[2048,256]{0,1:T(8,128)(2,1)}, bf16[2048,256]{0,1:T(8,128)(2,1)}, u32[]{:S(2)}, u32[]{:S(2)}) collective-permute-start(bf16[2048,256]{0,1:T(8,128)(2,1)} %get-tuple-element.99), channel_id=1, source_target_pairs={{0,12},{4,8},{8,4},{12,0},{1,13},{5,9},{9,5},{13,1},{2,14},{6,10},... | collective-permute-start | bytes 3145736 | tf_op jit(solution)/shard_map/ppermute | solution.py:37
  194.9 67.2 %collective-permute-start.10 = (bf16[2048,256]{0,1:T(8,128)(2,1)}, bf16[2048,256]{0,1:T(8,128)(2,1)}, u32[]{:S(2)}, u32[]{:S(2)}) collective-permute-start(bf16[2048,256]{0,1:T(8,128)(2,1)} %get-tuple-element.92), channel_id=1, source_target_pairs={{0,8},{4,12},{8,0},{12,4},{1,9},{5,13},{9,1},{13,5},{2,10},{6,14},... | collective-permute-start | bytes 3145736 | tf_op jit(solution)/shard_map/ppermute | solution.py:37
  196.3 73.4 %collective-permute-start.11 = (bf16[2048,256]{0,1:T(8,128)(2,1)}, bf16[2048,256]{0,1:T(8,128)(2,1)}, u32[]{:S(2)}, u32[]{:S(2)}) collective-permute-start(bf16[2048,256]{0,1:T(8,128)(2,1)} %get-tuple-element.93), channel_id=1, source_target_pairs={{0,12},{4,8},{8,4},{12,0},{1,13},{5,9},{9,5},{13,1},{2,14},{6,10},... | collective-permute-start | bytes 3145736 | tf_op jit(solution)/shard_map/ppermute | solution.py:37
  219.3 50.4 %collective-permute-start.9 = (bf16[2048,256]{0,1:T(8,128)(2,1)}, bf16[2048,256]{0,1:T(8,128)(2,1)}, u32[]{:S(2)}, u32[]{:S(2)}) collective-permute-start(bf16[2048,256]{0,1:T(8,128)(2,1)} %get-tuple-element.91), channel_id=1, source_target_pairs={{0,4},{4,0},{8,12},{12,8},{1,5},{5,1},{9,13},{13,9},{2,6},{6,2},{1... | collective-permute-start | bytes 3145736 | tf_op jit(solution)/shard_map/ppermute | solution.py:37
  274.8 54.3 %collective-permute-start.18 = (bf16[2048,256]{0,1:T(8,128)(2,1)}, bf16[2048,256]{0,1:T(8,128)(2,1)}, u32[]{:S(2)}, u32[]{:S(2)}) collective-permute-start(bf16[2048,256]{0,1:T(8,128)(2,1)} %get-tuple-element.113), channel_id=1, source_target_pairs={{0,4},{4,0},{8,12},{12,8},{1,5},{5,1},{9,13},{13,9},{2,6},{6,2},{1... | collective-permute-start | bytes 3145736 | tf_op jit(solution)/shard_map/ppermute | solution.py:37
  275.5 61.7 %collective-permute-start.19 = (bf16[2048,256]{0,1:T(8,128)(2,1)}, bf16[2048,256]{0,1:T(8,128)(2,1)}, u32[]{:S(2)}, u32[]{:S(2)}) collective-permute-start(bf16[2048,256]{0,1:T(8,128)(2,1)} %get-tuple-element.114), channel_id=1, source_target_pairs={{0,8},{4,12},{8,0},{12,4},{1,9},{5,13},{9,1},{13,5},{2,10},{6,14},... | collective-permute-start | bytes 3145736 | tf_op jit(solution)/shard_map/ppermute | solution.py:37
  276.9 60.2 %collective-permute-start.20 = (bf16[2048,256]{0,1:T(8,128)(2,1)}, bf16[2048,256]{0,1:T(8,128)(2,1)}, u32[]{:S(2)}, u32[]{:S(2)}) collective-permute-start(bf16[2048,256]{0,1:T(8,128)(2,1)} %get-tuple-element.115), channel_id=1, source_target_pairs={{0,12},{4,8},{8,4},{12,0},{1,13},{5,9},{9,5},{13,1},{2,14},{6,10},... | collective-permute-start | bytes 3145736 | tf_op jit(solution)/shard_map/ppermute | solution.py:37
  277.0 64.0 %collective-permute-start.15 = (bf16[2048,256]{0,1:T(8,128)(2,1)}, bf16[2048,256]{0,1:T(8,128)(2,1)}, u32[]{:S(2)}, u32[]{:S(2)}) collective-permute-start(bf16[2048,256]{0,1:T(8,128)(2,1)} %get-tuple-element.109), channel_id=1, source_target_pairs={{0,4},{4,0},{8,12},{12,8},{1,5},{5,1},{9,13},{13,9},{2,6},{6,2},{1... | collective-permute-start | bytes 3145736 | tf_op jit(solution)/shard_map/ppermute | solution.py:37
  320.1 26.1 %collective-permute-start.16 = (bf16[2048,256]{0,1:T(8,128)(2,1)S(1)}, bf16[2048,256]{0,1:T(8,128)(2,1)S(1)}, u32[]{:S(2)}, u32[]{:S(2)}) collective-permute-start(bf16[2048,256]{0,1:T(8,128)(2,1)S(1)} %copy-done.22), channel_id=1, source_target_pairs={{0,8},{4,12},{8,0},{12,4},{1,9},{5,13},{9,1},{13,5},{2,10},{6,14},... | collective-permute-start | bytes 3145736 | tf_op jit(solution)/shard_map/ppermute | solution.py:37
  329.2 38.5 %collective-permute-start.17 = (bf16[2048,256]{0,1:T(8,128)(2,1)S(1)}, bf16[2048,256]{0,1:T(8,128)(2,1)S(1)}, u32[]{:S(2)}, u32[]{:S(2)}) collective-permute-start(bf16[2048,256]{0,1:T(8,128)(2,1)S(1)} %copy-done.21), channel_id=1, source_target_pairs={{0,12},{4,8},{8,4},{12,0},{1,13},{5,9},{9,5},{13,1},{2,14},{6,10},... | collective-permute-start | bytes 3145736 | tf_op jit(solution)/shard_map/ppermute | solution.py:37
  337.2 30.5 %copy-start.1 = (bf16[2048,1024]{0,1:T(8,128)(2,1)S(1)}, bf16[2048,1024]{0,1:T(8,128)(2,1)}, u32[]{:S(2)}) copy-start(bf16[2048,1024]{0,1:T(8,128)(2,1)} %copy.101) | copy-start | bytes 12582916
  398.6 141.3 %all-reduce.7.cloned.1.call-start = ((), (), s32[]{:S(2)}) async-start(), calls=%async_computation.1 | async-start | bytes 2097152
  398.7 54.1 %collective-permute-start.21 = (bf16[2048,256]{0,1:T(8,128)(2,1)}, bf16[2048,256]{0,1:T(8,128)(2,1)S(1)}, u32[]{:S(2)}, u32[]{:S(2)}) collective-permute-start(bf16[2048,256]{0,1:T(8,128)(2,1)} %get-tuple-element.129), channel_id=1, source_target_pairs={{0,4},{4,0},{8,12},{12,8},{1,5},{5,1},{9,13},{13,9},{2,6},{6,2},{1... | collective-permute-start | bytes 3145736 | tf_op jit(solution)/shard_map/ppermute | solution.py:37
  399.0 53.8 %collective-permute-start.22 = (bf16[2048,256]{0,1:T(8,128)(2,1)}, bf16[2048,256]{0,1:T(8,128)(2,1)}, u32[]{:S(2)}, u32[]{:S(2)}) collective-permute-start(bf16[2048,256]{0,1:T(8,128)(2,1)} %get-tuple-element.130), channel_id=1, source_target_pairs={{0,8},{4,12},{8,0},{12,4},{1,9},{5,13},{9,1},{13,5},{2,10},{6,14},... | collective-permute-start | bytes 3145736 | tf_op jit(solution)/shard_map/ppermute | solution.py:37
  400.5 52.3 %collective-permute-start.23 = (bf16[2048,256]{0,1:T(8,128)(2,1)}, bf16[2048,256]{0,1:T(8,128)(2,1)}, u32[]{:S(2)}, u32[]{:S(2)}) collective-permute-start(bf16[2048,256]{0,1:T(8,128)(2,1)} %get-tuple-element.131), channel_id=1, source_target_pairs={{0,12},{4,8},{8,4},{12,0},{1,13},{5,9},{9,5},{13,1},{2,14},{6,10},... | collective-permute-start | bytes 3145736 | tf_op jit(solution)/shard_map/ppermute | solution.py:37
  426.5 26.4 %copy-start.12 = (bf16[2048,256]{0,1:T(8,128)(2,1)S(1)}, bf16[2048,256]{0,1:T(8,128)(2,1)}, u32[]{:S(2)}) copy-start(bf16[2048,256]{0,1:T(8,128)(2,1)} %get-tuple-element.128) | copy-start | bytes 3145732
  (32 other events, 177.7 us)
Sparse Core Ops, SparseCore 0:
  398.8 53.0 all-reduce.4
  488.7 51.1 all-reduce.6

commit v5 on v2

--- a/solution.py
+++ b/solution.py
@@ -52,9 +52,11 @@
     w1p, w2p, w1tp = expanded_weights(w_first, w_second, n_dev, order)
     step = tok_rows // CHUNKS
 
+    eye = jnp.eye(blk_local, dtype=jnp.bool_)
     gf_acc = None
     gs_acc = None
     outs = []
+    pending = []
     for k in range(CHUNKS):
         x = tokens[k * step:(k + 1) * step]
         cot = cotangent[k * step:(k + 1) * step]
@@ -69,24 +71,32 @@
         gs = lax.dot_general(
             active, cot, (((0,), (0,)), ((), ())), preferred_element_type=jnp.float32
         )
+        gs_acc = gs if gs_acc is None else gs_acc + gs
+        if len(pending) == 2:
+            masked, done = lax.optimization_barrier((masked, pending.pop(0)))
+            outs.append(done[0])
+            gf_acc = done[1] if gf_acc is None else gf_acc + done[1]
         returned = jnp.concatenate(exchange(masked, n_dev), axis=1)
         gt = jnp.dot(returned, w1tp, preferred_element_type=jnp.float32).astype(jnp.bfloat16)
-        outs.append(gt)
         gf = lax.dot_general(
             x, returned, (((0,), (0,)), ((), ())), preferred_element_type=jnp.float32
         )
+        pending.append((gt, gf))
+    for gt, gf in pending:
+        outs.append(gt)
         gf_acc = gf if gf_acc is None else gf_acc + gf
-        gs_acc = gs if gs_acc is None else gs_acc + gs
 
     grad_tokens = jnp.concatenate(outs, axis=0)
     gs6 = gs_acc.reshape(n_dev, blk_local, blk_local, sub, blk_local, bs)
-    gsd = jnp.take(jnp.diagonal(gs6, axis1=1, axis2=4), order, axis=0)
-    second_term = gsd.transpose(2, 0, 1, 4, 3).reshape(bs, blk_local, bs) * grad_scale
+    gsd = jnp.sum(jnp.where(eye[None, :, None, None, :, None], gs6, 0.0), axis=4)
+    gsd = jnp.take(gsd, order, axis=0)
+    second_term = gsd.transpose(3, 0, 2, 1, 4).reshape(bs, blk_local, bs) * grad_scale
     grad_second = lax.psum_scatter(second_term, "dp", scatter_dimension=0, tiled=True)
     gf_acc, grad_second = lax.optimization_barrier((gf_acc, grad_second))
     gf6 = gf_acc.reshape(blk_local, bs, n_dev, blk_local, blk_local, sub)
-    gfd = jnp.take(jnp.diagonal(gf6, axis1=0, axis2=4), order, axis=1)
-    first_term = gfd.transpose(0, 4, 1, 2, 3).reshape(bs, blk_local, bs) * grad_scale
+    gfd = jnp.sum(jnp.where(eye[:, None, None, None, :, None], gf6, 0.0), axis=4)
+    gfd = jnp.take(gfd, order, axis=2)
+    first_term = gfd.transpose(1, 0, 2, 3, 4).reshape(bs, blk_local, bs) * grad_scale
     grad_first = lax.psum_scatter(first_term, "dp", scatter_dimension=0, tiled=True)
     return (grad_tokens, grad_first.transpose(1, 0, 2), grad_second.transpose(1, 0, 2))
 

time: 517 us -> 481 us (0.930)
  waiting for transfers between devices: 239 us -> 192 us
  other arithmetic: 28.1 us -> 41.9 us
    unnamed x4, waiting for transfers between devices: 65 us -> 38.8 us
    ppermute x24, waiting for transfers between devices: 174 us -> 153 us  [exchange(): lax.ppermute(pieces[m], 'tensor', [(i, i ^ m) for i in range(n_dev)])]
    reduce_sum x0 -> x2, other arithmetic: none -> 8.96 us  [the longest x1 5.27 us: shards(): jnp.sum(jnp.where(eye[None, :, None, None, :, None], gs6, 0.0), axis=4)]
    dot_general x4, matrix products: 23.3 us -> 30.5 us  [shards(): jnp.dot(returned, w1tp, preferred_element_type=jnp.float32)]
    unnamed x93 -> x75, local copies, waits for them, and re-layouts: 7.98 us -> 14.4 us
    gather x4 -> x2, local copies, waits for them, and re-layouts: 7.08 us -> 1.23 us  [the longest x1 0.62 us: shards(): gsd = jnp.take(gsd, order, axis=0)]
    concatenate x1, other arithmetic: 8.57 us -> 13.8 us  [shards(): grad_tokens = jnp.concatenate(outs, axis=0)]
    reshape x2 -> x1, local copies, waits for them, and re-layouts: 10.7 us -> 5.61 us  [shards(): gs6 = gs_acc.reshape(n_dev, blk_local, blk_local, sub, blk_local, bs)]
  transfers between devices with their start and end apart: 26 -> 26, of which waited for: 13 -> 13; matrix products, arithmetic and copies ran while one was open for 31% -> 43% of each run, Pallas kernels for 0% -> 0%
where the time goes in v5:
time: 481 us; the launch traced here: 476 us
  waiting for transfers between devices  192 us (40%)
  matrix products  159 us (33%)
  local copies, waits for them, and re-layouts  46.9 us (10%)
  other arithmetic  41.9 us (9%)
  starting transfers between devices  20.7 us (4%)
  between operations  15.8 us (3%)
    ppermute x24, waiting for transfers between devices, exchange(): lax.ppermute(pieces[m], 'tensor', [(i, i ^ m) for i in range(n_dev)])  153 us
    unnamed x4, waiting for transfers between devices  38.8 us
    dot_general x4, matrix products, shards(): lax.dot_general(active, cot, (((0,), (0,)), ((), ())), preferred_element_...  38.6 us
    dot_general x4, matrix products, shards(): lax.dot_general(x, returned, (((0,), (0,)), ((), ())), preferred_element_...  33.5 us
    dot_general x4, matrix products, shards(): jnp.dot(x, w1p, preferred_element_type=jnp.float32).astype(jnp.bfloat16)  31.2 us
    dot_general x4, matrix products, shards(): jnp.dot(returned, w1tp, preferred_element_type=jnp.float32)  30.5 us
    dot_general x4, matrix products, shards(): backed = jnp.dot(cot, w2p, preferred_element_type=jnp.float32)  25.8 us
    ppermute x24, starting transfers between devices, exchange(): lax.ppermute(pieces[m], 'tensor', [(i, i ^ m) for i in range(n_dev)])  20.4 us
  transfers between devices with their start and end apart: 26, of which 13 were waited for; matrix products, arithmetic and copies ran while one was open for 43% of the time, Pallas kernels for 0%

profile of v5, /device:TPU:0, one launch (start us, length us, event | category | flops | bytes accessed | tf_op | source)
XLA Modules:
  0.0 476.4 jit_solution(731653643766897131)
XLA Ops:
  13.7 7.2 %convert_bitcast_fusion.2 = bf16[2048,1024]{0,1:T(8,128)(2,1)S(1)} fusion(bf16[1024,1024]{0,1:T(8,128)(2,1)S(1)} %bitcast.86, bf16[8192,1024]{1,0:T(8,128)(2,1)} %param.4), kind=kOutput, calls=%fused_computation.50 | convolution fusion | flops 4297064448 | bytes 10485760 | tf_op jit(solution)/shard_map/dot_general | solution.py:63
  26.2 7.2 %convert_bitcast_fusion.3 = bf16[2048,1024]{0,1:T(8,128)(2,1)S(1)} fusion(bf16[1024,1024]{0,1:T(8,128)(2,1)S(1)} %bitcast.87, bf16[8192,1024]{1,0:T(8,128)(2,1)} %param.4), kind=kOutput, calls=%fused_computation.51 | convolution fusion | flops 4297064448 | bytes 10485760 | tf_op jit(solution)/shard_map/dot_general | solution.py:63
  38.1 6.1 %convolution_bitcast_fusion.2 = bf16[2048,1024]{0,1:T(8,128)(2,1)} fusion(bf16[1024,1024]{0,1:T(8,128)(2,1)S(1)} %bitcast.90, bf16[8192,1024]{1,0:T(8,128)(2,1)S(1)} %bitcast.96), kind=kOutput, calls=%fused_computation.7 | convolution fusion | flops 4294967296 | bytes 10485760 | tf_op jit(solution)/shard_map/dot_general | solution.py:64
  44.3 6.2 %convolution_bitcast_fusion.3 = bf16[2048,1024]{0,1:T(8,128)(2,1)} fusion(bf16[1024,1024]{0,1:T(8,128)(2,1)S(1)} %bitcast.91, bf16[8192,1024]{1,0:T(8,128)(2,1)S(1)} %bitcast.96), kind=kOutput, calls=%fused_computation.8 | convolution fusion | flops 4294967296 | bytes 10485760 | tf_op jit(solution)/shard_map/dot_general | solution.py:64
  50.5 8.4 %convert_bitcast_fusion = bf16[2048,1024]{0,1:T(8,128)(2,1)} fusion(bf16[1024,1024]{0,1:T(8,128)(2,1)S(1)} %bitcast.88, bf16[8192,1024]{1,0:T(8,128)(2,1)} %param.4), kind=kOutput, calls=%fused_computation.48 | convolution fusion | flops 4297064448 | bytes 10485760 | tf_op jit(solution)/shard_map/dot_general | solution.py:63
  58.9 6.3 %convolution_bitcast_fusion = bf16[2048,1024]{0,1:T(8,128)(2,1)} fusion(bf16[1024,1024]{0,1:T(8,128)(2,1)S(1)} %bitcast.92, bf16[8192,1024]{1,0:T(8,128)(2,1)S(1)} %bitcast.96), kind=kOutput, calls=%fused_computation.5 | convolution fusion | flops 4294967296 | bytes 10485760 | tf_op jit(solution)/shard_map/dot_general | solution.py:64
  65.2 8.4 %convert_bitcast_fusion.1 = bf16[2048,1024]{0,1:T(8,128)(2,1)} fusion(bf16[1024,1024]{0,1:T(8,128)(2,1)S(1)} %bitcast.89, bf16[8192,1024]{1,0:T(8,128)(2,1)} %param.4), kind=kOutput, calls=%fused_computation.49 | convolution fusion | flops 4297064448 | bytes 10485760 | tf_op jit(solution)/shard_map/dot_general | solution.py:63
  83.5 7.1 %convolution_bitcast_fusion.1 = bf16[2048,1024]{0,1:T(8,128)(2,1)S(1)} fusion(bf16[1024,1024]{0,1:T(8,128)(2,1)S(1)} %bitcast.93, bf16[8192,1024]{1,0:T(8,128)(2,1)} %param.5), kind=kOutput, calls=%fused_computation.6 | convolution fusion | flops 4294967296 | bytes 10485760 | tf_op jit(solution)/shard_map/dot_general | solution.py:64
  97.8 7.8 %fusion = f32[1024,1024]{1,0:T(8,128)S(1)} fusion(bf16[2048,256]{0,1:T(8,128)(2,1)} %collective-permute-done.7, bf16[2048,256]{0,1:T(8,128)(2,1)} %collective-permute-done.5, bf16[2048,256]{0,1:T(8,128)(2,1)} %collective-permute-done.3, bf16[2048,256]{0,1:T(8,128)(2,1)S(1)} %get-tuple-element.50, bf16[8192,1024]{1,0:T(8,128)(2,1)} %param.5), kind=kOutput, calls=%fused_computation.12 | convolution fusion | flops 4315938816 | bytes 12582912 | tf_op jit(solution)/shard_map/dot_general | solution.py:71
  107.5 9.4 %collective-permute-done.2 = bf16[2048,256]{0,1:T(8,128)(2,1)S(1)} collective-permute-done((bf16[2048,256]{0,1:T(8,128)(2,1)S(1)}, bf16[2048,256]{0,1:T(8,128)(2,1)S(1)}, u32[]{:S(2)}, u32[]{:S(2)}) %collective-permute-start.2) | collective-permute-done | bytes 1048608 | tf_op jit(solution)/shard_map/ppermute | solution.py:37
  122.4 9.5 %fusion.14 = f32[1024,1024]{1,0:T(8,128)} fusion(bf16[2048,256]{0,1:T(8,128)(2,1)S(1)} %collective-permute-done.2, bf16[2048,256]{0,1:T(8,128)(2,1)} %collective-permute-done.1, bf16[2048,256]{0,1:T(8,128)(2,1)} %collective-permute-done, bf16[2048,256]{0,1:T(8,128)(2,1)S(1)} %get-tuple-element.55, bf16[8192,1024]{1,0:T(8,128)(2,1)} %param.5), kind=kOutput, calls=%fused_computation.28 | convolution fusion | flops 4315938816 | bytes 12582912 | tf_op jit(solution)/shard_map/dot_general | solution.py:71
  131.9 7.8 %collective-permute-done.14 = bf16[2048,256]{0,1:T(8,128)(2,1)S(1)} collective-permute-done((bf16[2048,256]{0,1:T(8,128)(2,1)S(1)}, bf16[2048,256]{0,1:T(8,128)(2,1)S(1)}, u32[]{:S(2)}, u32[]{:S(2)}) %collective-permute-start.14) | collective-permute-done | bytes 1048608 | tf_op jit(solution)/shard_map/ppermute | solution.py:37
  139.7 22.1 %collective-permute-done.16 = bf16[2048,256]{0,1:T(8,128)(2,1)S(1)} collective-permute-done((bf16[2048,256]{0,1:T(8,128)(2,1)S(1)}, bf16[2048,256]{0,1:T(8,128)(2,1)S(1)}, u32[]{:S(2)}, u32[]{:S(2)}) %collective-permute-start.16) | collective-permute-done | bytes 1048608 | tf_op jit(solution)/shard_map/ppermute | solution.py:37
  167.1 8.7 %fusion.7 = f32[1024,1024]{1,0:T(8,128)} fusion(bf16[2048,256]{0,1:T(8,128)(2,1)S(1)} %collective-permute-done.16, bf16[2048,256]{0,1:T(8,128)(2,1)S(1)} %collective-permute-done.14, bf16[2048,256]{0,1:T(8,128)(2,1)S(1)} %collective-permute-done.12, bf16[2048,256]{0,1:T(8,128)(2,1)S(1)} %get-tuple-element.45, bf16[8192,1024]{1,0:T(8,128)(2,1)} %param.5), kind=kOutput, calls=%fused_computation.20 | convolution fusion | flops 4315938816 | bytes 12582912 | tf_op jit(solution)/shard_map/dot_general | solution.py:71
  175.7 8.9 %collective-permute-done.10 = bf16[2048,256]{0,1:T(8,128)(2,1)S(1)} collective-permute-done((bf16[2048,256]{0,1:T(8,128)(2,1)S(1)}, bf16[2048,256]{0,1:T(8,128)(2,1)S(1)}, u32[]{:S(2)}, u32[]{:S(2)}) %collective-permute-start.10) | collective-permute-done | bytes 1048608 | tf_op jit(solution)/shard_map/ppermute | solution.py:37
  185.5 21.2 %collective-permute-done.11 = bf16[2048,256]{0,1:T(8,128)(2,1)S(1)} collective-permute-done((bf16[2048,256]{0,1:T(8,128)(2,1)S(1)}, bf16[2048,256]{0,1:T(8,128)(2,1)S(1)}, u32[]{:S(2)}, u32[]{:S(2)}) %collective-permute-start.11) | collective-permute-done | bytes 1048608 | tf_op jit(solution)/shard_map/ppermute | solution.py:37
  210.6 12.6 %add_add_fusion = f32[1024,1024]{1,0:T(8,128)} fusion(f32[1024,1024]{1,0:T(8,128)} %fusion.14, f32[1024,1024]{1,0:T(8,128)S(1)} %fusion, f32[1024,1024]{1,0:T(8,128)} %fusion.7, bf16[8192,1024]{1,0:T(8,128)(2,1)} %param.5, bf16[2048,256]{0,1:T(8,128)(2,1)S(1)} %collective-permute-done.11, bf16[2048,256]{0,1:T(8,128)(2,1)S(1)} %collective-permute-done.10, ...), kind=kOutput, calls=%fused_computation.47 | convolution fusion | flops 4319084544 | bytes 25165824 | tf_op jit(solution)/shard_map/dot_general | solution.py:71
  239.2 12.6 %collective-permute-done.8 = bf16[2048,256]{0,1:T(8,128)(2,1)} collective-permute-done((bf16[2048,256]{0,1:T(8,128)(2,1)}, bf16[2048,256]{0,1:T(8,128)(2,1)}, u32[]{:S(2)}, u32[]{:S(2)}) %collective-permute-start.8) | collective-permute-done | bytes 1048608 | tf_op jit(solution)/shard_map/ppermute | solution.py:37
  251.8 9.1 %convolution_convert_fusion.3 = bf16[2048,1024]{1,0:T(8,128)(2,1)} fusion(bf16[1024,1024]{1,0:T(8,128)(2,1)} %bitcast.82, bf16[2048,256]{0,1:T(8,128)(2,1)} %collective-permute-done.8, bf16[2048,256]{0,1:T(8,128)(2,1)} %collective-permute-done.6, bf16[2048,256]{0,1:T(8,128)(2,1)} %collective-permute-done.4, bf16[2048,256]{0,1:T(8,128)(2,1)S(1)} %copy-done.16), kind=kOutput, calls=%fused_computation.55 | convolution fusion | flops 4313841664 | bytes 10485760 | tf_op jit(solution)/shard_map/dot_general | solution.py:80
  260.9 9.8 %fusion.48 = f32[1024,1024]{0,1:T(8,128)} fusion(bf16[8192,1024]{1,0:T(8,128)(2,1)} %param.4, bf16[2048,256]{0,1:T(8,128)(2,1)} %collective-permute-done.8, bf16[2048,256]{0,1:T(8,128)(2,1)} %collective-permute-done.6, bf16[2048,256]{0,1:T(8,128)(2,1)} %collective-permute-done.4, bf16[2048,256]{0,1:T(8,128)(2,1)S(1)} %copy-done.16), kind=kOutput, calls=%fused_computation.76 | convolution fusion | flops 4311744512 | bytes 12582912 | tf_op jit(solution)/shard_map/dot_general | solution.py:81
  274.5 22.1 %collective-permute-done.17 = bf16[2048,256]{0,1:T(8,128)(2,1)S(1)} collective-permute-done((bf16[2048,256]{0,1:T(8,128)(2,1)}, bf16[2048,256]{0,1:T(8,128)(2,1)S(1)}, u32[]{:S(2)}, u32[]{:S(2)}) %collective-permute-start.17) | collective-permute-done | bytes 1048608 | tf_op jit(solution)/shard_map/ppermute | solution.py:37
  296.6 8.8 %fusion.51 = f32[1024,1024]{0,1:T(8,128)} fusion(bf16[8192,1024]{1,0:T(8,128)(2,1)} %param.4, bf16[2048,256]{0,1:T(8,128)(2,1)S(1)} %collective-permute-done.17, bf16[2048,256]{0,1:T(8,128)(2,1)S(1)} %collective-permute-done.15, bf16[2048,256]{0,1:T(8,128)(2,1)S(1)} %collective-permute-done.13, bf16[2048,256]{0,1:T(8,128)(2,1)S(1)} %copy-done.17), kind=kOutput, calls=%fused_computation.77 | convolution fusion | flops 4311744512 | bytes 12582912 | tf_op jit(solution)/shard_map/dot_general | solution.py:81
  305.4 6.5 %convolution_convert_fusion.2 = bf16[2048,1024]{1,0:T(8,128)(2,1)} fusion(bf16[1024,1024]{1,0:T(8,128)(2,1)S(1)} %bitcast.83, bf16[2048,256]{0,1:T(8,128)(2,1)S(1)} %collective-permute-done.17, bf16[2048,256]{0,1:T(8,128)(2,1)S(1)} %collective-permute-done.15, bf16[2048,256]{0,1:T(8,128)(2,1)S(1)} %collective-permute-done.13, ...), kind=kOutput, calls=%fused_computation.54 | convolution fusion | flops 4313841664 | bytes 10485760 | tf_op jit(solution)/shard_map/dot_general | solution.py:80
  320.5 21.2 %collective-permute-done.20 = bf16[2048,256]{0,1:T(8,128)(2,1)} collective-permute-done((bf16[2048,256]{0,1:T(8,128)(2,1)}, bf16[2048,256]{0,1:T(8,128)(2,1)}, u32[]{:S(2)}, u32[]{:S(2)}) %collective-permute-start.20) | collective-permute-done | bytes 1048608 | tf_op jit(solution)/shard_map/ppermute | solution.py:37
  345.3 8.6 %convolution_convert_fusion.1 = bf16[2048,1024]{1,0:T(8,128)(2,1)} fusion(bf16[2048,1024]{0,1:T(8,128)(2,1)} %constant_dynamic-update-slice_fusion, bf16[1024,1024]{1,0:T(8,128)(2,1)S(1)} %bitcast.84), kind=kOutput, calls=%fused_computation.53 | convolution fusion | flops 4297064448 | bytes 10485760 | tf_op jit(solution)/shard_map/dot_general | solution.py:80
  353.9 10.6 %collective-permute-done.22 = bf16[2048,256]{0,1:T(8,128)(2,1)} collective-permute-done((bf16[2048,256]{0,1:T(8,128)(2,1)}, bf16[2048,256]{0,1:T(8,128)(2,1)}, u32[]{:S(2)}, u32[]{:S(2)}) %collective-permute-start.22) | collective-permute-done | bytes 1048608 | tf_op jit(solution)/shard_map/ppermute | solution.py:37
  365.9 6.0 %fusion.45 = f32[1024,1024]{1,0:T(8,128)} fusion(bf16[2048,1024]{0,1:T(8,128)(2,1)S(1)} %copy-done.19, bf16[8192,1024]{1,0:T(8,128)(2,1)S(1)} %bitcast.98), kind=kOutput, calls=%fused_computation.73 | convolution fusion | flops 4294967296 | bytes 12582912 | tf_op jit(solution)/shard_map/dot_general | solution.py:81
  371.9 14.6 %collective-permute-done.23 = bf16[2048,256]{0,1:T(8,128)(2,1)S(1)} collective-permute-done((bf16[2048,256]{0,1:T(8,128)(2,1)}, bf16[2048,256]{0,1:T(8,128)(2,1)S(1)}, u32[]{:S(2)}, u32[]{:S(2)}) %collective-permute-start.23) | collective-permute-done | bytes 1048608 | tf_op jit(solution)/shard_map/ppermute | solution.py:37
  386.6 6.3 %convolution_convert_fusion = bf16[2048,1024]{1,0:T(8,128)(2,1)} fusion(bf16[2048,1024]{0,1:T(8,128)(2,1)S(1)} %constant_dynamic-update-slice_fusion.4, bf16[1024,1024]{1,0:T(8,128)(2,1)S(1)} %bitcast.85), kind=kOutput, calls=%fused_computation.52 | convolution fusion | flops 4297064448 | bytes 10485760 | tf_op jit(solution)/shard_map/dot_general | solution.py:80
  392.9 8.9 %bitcast_add_fusion = f32[1024,1024]{0,1:T(8,128)} fusion(f32[1024,1024]{1,0:T(8,128)} %fusion.45, f32[1024,1024]{0,1:T(8,128)} %fusion.48, f32[1024,1024]{0,1:T(8,128)} %fusion.51, bf16[2048,1024]{0,1:T(8,128)(2,1)S(1)} %constant_dynamic-update-slice_fusion.4, bf16[8192,1024]{1,0:T(8,128)(2,1)S(1)} %bitcast.98), kind=kOutput, calls=%fused_computation.43 | convolution fusion | flops 4298113024 | bytes 25165824 | tf_op jit(solution)/shard_map/dot_general | solution.py:81
  414.8 13.8 %pad_maximum_fusion = bf16[8192,1024]{1,0:T(8,128)(2,1)} fusion(bf16[2048,1024]{1,0:T(8,128)(2,1)} %convolution_convert_fusion, bf16[2048,1024]{1,0:T(8,128)(2,1)} %convolution_convert_fusion.1, bf16[2048,1024]{1,0:T(8,128)(2,1)} %convolution_convert_fusion.2, bf16[2048,1024]{1,0:T(8,128)(2,1)} %convolution_convert_fusion.3), kind=kLoop, calls=%fused_computation.4 | loop fusion | flops 67108864 | bytes 33554432 | tf_op jit(solution)/shard_map/concatenate | solution.py:89
  428.6 38.8 %all-reduce.7.cloned.1.call-done = f32[256,4,256]{2,1,0:T(4,128)} async-done(((f32[256,4,256]{2,1,0:T(4,128)}), f32[256,4,256]{2,1,0:T(4,128)}) %all-reduce.7.cloned.1.call-update) | async-done | bytes 1048592
  (159 shorter events, 98.1 us)
Async XLA Ops:
  7.2 307.9 %all-reduce.5.cloned.1.call-start = ((), (), s32[]{:S(2)}) async-start(), calls=%async_computation | async-start | bytes 2097152
  7.3 66.3 %copy-start.20 = (pred[4,4]{0,1:T(4,128)(4,1)}, pred[4,4]{0,1:T(4,128)(4,1)S(1)}, u32[]{:S(2)}) copy-start(pred[4,4]{0,1:T(4,128)(4,1)S(1)} %iota_compare_fusion) | copy-start | bytes 52
  22.7 68.0 %collective-permute-start.3 = (bf16[2048,256]{0,1:T(8,128)(2,1)}, bf16[2048,256]{0,1:T(8,128)(2,1)}, u32[]{:S(2)}, u32[]{:S(2)}) collective-permute-start(bf16[2048,256]{0,1:T(8,128)(2,1)} %get-tuple-element.60), channel_id=1, source_target_pairs={{0,4},{4,0},{8,12},{12,8},{1,5},{5,1},{9,13},{13,9},{2,6},{6,2},{1... | collective-permute-start | bytes 3145736 | tf_op jit(solution)/shard_map/ppermute | solution.py:37
  23.1 68.8 %collective-permute-start.5 = (bf16[2048,256]{0,1:T(8,128)(2,1)}, bf16[2048,256]{0,1:T(8,128)(2,1)}, u32[]{:S(2)}, u32[]{:S(2)}) collective-permute-start(bf16[2048,256]{0,1:T(8,128)(2,1)} %get-tuple-element.62), channel_id=1, source_target_pairs={{0,8},{4,12},{8,0},{12,4},{1,9},{5,13},{9,1},{13,5},{2,10},{6,14},... | collective-permute-start | bytes 3145736 | tf_op jit(solution)/shard_map/ppermute | solution.py:37
  25.6 66.6 %collective-permute-start.7 = (bf16[2048,256]{0,1:T(8,128)(2,1)}, bf16[2048,256]{0,1:T(8,128)(2,1)}, u32[]{:S(2)}, u32[]{:S(2)}) collective-permute-start(bf16[2048,256]{0,1:T(8,128)(2,1)} %get-tuple-element.61), channel_id=1, source_target_pairs={{0,12},{4,8},{8,4},{12,0},{1,13},{5,9},{9,5},{13,1},{2,14},{6,10},... | collective-permute-start | bytes 3145736 | tf_op jit(solution)/shard_map/ppermute | solution.py:37
  35.1 70.5 %collective-permute-start = (bf16[2048,256]{0,1:T(8,128)(2,1)}, bf16[2048,256]{0,1:T(8,128)(2,1)}, u32[]{:S(2)}, u32[]{:S(2)}) collective-permute-start(bf16[2048,256]{0,1:T(8,128)(2,1)} %get-tuple-element.65), channel_id=1, source_target_pairs={{0,4},{4,0},{8,12},{12,8},{1,5},{5,1},{9,13},{13,9},{2,6},{6,2},{1... | collective-permute-start | bytes 3145736 | tf_op jit(solution)/shard_map/ppermute | solution.py:37
  35.8 70.6 %collective-permute-start.1 = (bf16[2048,256]{0,1:T(8,128)(2,1)}, bf16[2048,256]{0,1:T(8,128)(2,1)}, u32[]{:S(2)}, u32[]{:S(2)}) collective-permute-start(bf16[2048,256]{0,1:T(8,128)(2,1)} %get-tuple-element.64), channel_id=1, source_target_pairs={{0,8},{4,12},{8,0},{12,4},{1,9},{5,13},{9,1},{13,5},{2,10},{6,14},... | collective-permute-start | bytes 3145736 | tf_op jit(solution)/shard_map/ppermute | solution.py:37
  90.7 26.2 %collective-permute-start.2 = (bf16[2048,256]{0,1:T(8,128)(2,1)S(1)}, bf16[2048,256]{0,1:T(8,128)(2,1)S(1)}, u32[]{:S(2)}, u32[]{:S(2)}) collective-permute-start(bf16[2048,256]{0,1:T(8,128)(2,1)S(1)} %copy-done.15), channel_id=1, source_target_pairs={{0,12},{4,8},{8,4},{12,0},{1,13},{5,9},{9,5},{13,1},{2,14},{6,10},... | collective-permute-start | bytes 3145736 | tf_op jit(solution)/shard_map/ppermute | solution.py:37
  92.0 39.9 %collective-permute-start.12 = (bf16[2048,256]{0,1:T(8,128)(2,1)S(1)}, bf16[2048,256]{0,1:T(8,128)(2,1)S(1)}, u32[]{:S(2)}, u32[]{:S(2)}) collective-permute-start(bf16[2048,256]{0,1:T(8,128)(2,1)S(1)} %copy-done.14), channel_id=1, source_target_pairs={{0,4},{4,0},{8,12},{12,8},{1,5},{5,1},{9,13},{13,9},{2,6},{6,2},{1... | collective-permute-start | bytes 3145736 | tf_op jit(solution)/shard_map/ppermute | solution.py:37
  92.2 47.5 %collective-permute-start.14 = (bf16[2048,256]{0,1:T(8,128)(2,1)S(1)}, bf16[2048,256]{0,1:T(8,128)(2,1)S(1)}, u32[]{:S(2)}, u32[]{:S(2)}) collective-permute-start(bf16[2048,256]{0,1:T(8,128)(2,1)S(1)} %copy-done.13), channel_id=1, source_target_pairs={{0,8},{4,12},{8,0},{12,4},{1,9},{5,13},{9,1},{13,5},{2,10},{6,14},... | collective-permute-start | bytes 3145736 | tf_op jit(solution)/shard_map/ppermute | solution.py:37
  97.8 20.8 %copy-start.1 = (bf16[2048,1024]{0,1:T(8,128)(2,1)S(1)}, bf16[2048,1024]{0,1:T(8,128)(2,1)}, u32[]{:S(2)}) copy-start(bf16[2048,1024]{0,1:T(8,128)(2,1)} %convolution_bitcast_fusion.3) | copy-start | bytes 12582916
  105.6 56.2 %collective-permute-start.16 = (bf16[2048,256]{0,1:T(8,128)(2,1)S(1)}, bf16[2048,256]{0,1:T(8,128)(2,1)S(1)}, u32[]{:S(2)}, u32[]{:S(2)}) collective-permute-start(bf16[2048,256]{0,1:T(8,128)(2,1)S(1)} %copy-done.12), channel_id=1, source_target_pairs={{0,12},{4,8},{8,4},{12,0},{1,13},{5,9},{9,5},{13,1},{2,14},{6,10},... | collective-permute-start | bytes 3145736 | tf_op jit(solution)/shard_map/ppermute | solution.py:37
  106.3 78.3 %collective-permute-start.10 = (bf16[2048,256]{0,1:T(8,128)(2,1)S(1)}, bf16[2048,256]{0,1:T(8,128)(2,1)S(1)}, u32[]{:S(2)}, u32[]{:S(2)}) collective-permute-start(bf16[2048,256]{0,1:T(8,128)(2,1)S(1)} %copy-done.11), channel_id=1, source_target_pairs={{0,8},{4,12},{8,0},{12,4},{1,9},{5,13},{9,1},{13,5},{2,10},{6,14},... | collective-permute-start | bytes 3145736 | tf_op jit(solution)/shard_map/ppermute | solution.py:37
  116.9 89.9 %collective-permute-start.11 = (bf16[2048,256]{0,1:T(8,128)(2,1)S(1)}, bf16[2048,256]{0,1:T(8,128)(2,1)S(1)}, u32[]{:S(2)}, u32[]{:S(2)}) collective-permute-start(bf16[2048,256]{0,1:T(8,128)(2,1)S(1)} %copy-done.10), channel_id=1, source_target_pairs={{0,12},{4,8},{8,4},{12,0},{1,13},{5,9},{9,5},{13,1},{2,14},{6,10},... | collective-permute-start | bytes 3145736 | tf_op jit(solution)/shard_map/ppermute | solution.py:37
  122.4 40.9 %copy-start = (bf16[2048,1024]{0,1:T(8,128)(2,1)S(1)}, bf16[2048,1024]{0,1:T(8,128)(2,1)}, u32[]{:S(2)}) copy-start(bf16[2048,1024]{0,1:T(8,128)(2,1)} %convolution_bitcast_fusion) | copy-start | bytes 12582916
  131.9 74.9 %collective-permute-start.9 = (bf16[2048,256]{0,1:T(8,128)(2,1)S(1)}, bf16[2048,256]{0,1:T(8,128)(2,1)S(1)}, u32[]{:S(2)}, u32[]{:S(2)}) collective-permute-start(bf16[2048,256]{0,1:T(8,128)(2,1)S(1)} %copy-done.9), channel_id=1, source_target_pairs={{0,4},{4,0},{8,12},{12,8},{1,5},{5,1},{9,13},{13,9},{2,6},{6,2},{1... | collective-permute-start | bytes 3145736 | tf_op jit(solution)/shard_map/ppermute | solution.py:37
  139.7 99.4 %collective-permute-start.4 = (bf16[2048,256]{0,1:T(8,128)(2,1)}, bf16[2048,256]{0,1:T(8,128)(2,1)}, u32[]{:S(2)}, u32[]{:S(2)}) collective-permute-start(bf16[2048,256]{0,1:T(8,128)(2,1)} %get-tuple-element.54), channel_id=1, source_target_pairs={{0,4},{4,0},{8,12},{12,8},{1,5},{5,1},{9,13},{13,9},{2,6},{6,2},{1... | collective-permute-start | bytes 3145736 | tf_op jit(solution)/shard_map/ppermute | solution.py:37
  161.8 77.3 %collective-permute-start.6 = (bf16[2048,256]{0,1:T(8,128)(2,1)}, bf16[2048,256]{0,1:T(8,128)(2,1)}, u32[]{:S(2)}, u32[]{:S(2)}) collective-permute-start(bf16[2048,256]{0,1:T(8,128)(2,1)} %get-tuple-element.53), channel_id=1, source_target_pairs={{0,8},{4,12},{8,0},{12,4},{1,9},{5,13},{9,1},{13,5},{2,10},{6,14},... | collective-permute-start | bytes 3145736 | tf_op jit(solution)/shard_map/ppermute | solution.py:37
  184.6 67.1 %collective-permute-start.8 = (bf16[2048,256]{0,1:T(8,128)(2,1)}, bf16[2048,256]{0,1:T(8,128)(2,1)}, u32[]{:S(2)}, u32[]{:S(2)}) collective-permute-start(bf16[2048,256]{0,1:T(8,128)(2,1)} %get-tuple-element.52), channel_id=1, source_target_pairs={{0,12},{4,8},{8,4},{12,0},{1,13},{5,9},{9,5},{13,1},{2,14},{6,10},... | collective-permute-start | bytes 3145736 | tf_op jit(solution)/shard_map/ppermute | solution.py:37
  236.7 230.7 %all-reduce.7.cloned.1.call-start = ((), (), s32[]{:S(2)}) async-start(), calls=%async_computation.1 | async-start | bytes 2097152
  236.9 36.2 %collective-permute-start.13 = (bf16[2048,256]{0,1:T(8,128)(2,1)}, bf16[2048,256]{0,1:T(8,128)(2,1)S(1)}, u32[]{:S(2)}, u32[]{:S(2)}) collective-permute-start(bf16[2048,256]{0,1:T(8,128)(2,1)} %get-tuple-element.49), channel_id=1, source_target_pairs={{0,4},{4,0},{8,12},{12,8},{1,5},{5,1},{9,13},{13,9},{2,6},{6,2},{1... | collective-permute-start | bytes 3145736 | tf_op jit(solution)/shard_map/ppermute | solution.py:37
  237.2 37.3 %collective-permute-start.15 = (bf16[2048,256]{0,1:T(8,128)(2,1)}, bf16[2048,256]{0,1:T(8,128)(2,1)S(1)}, u32[]{:S(2)}, u32[]{:S(2)}) collective-permute-start(bf16[2048,256]{0,1:T(8,128)(2,1)} %get-tuple-element.48), channel_id=1, source_target_pairs={{0,8},{4,12},{8,0},{12,4},{1,9},{5,13},{9,1},{13,5},{2,10},{6,14},... | collective-permute-start | bytes 3145736 | tf_op jit(solution)/shard_map/ppermute | solution.py:37
  239.1 57.5 %collective-permute-start.17 = (bf16[2048,256]{0,1:T(8,128)(2,1)}, bf16[2048,256]{0,1:T(8,128)(2,1)S(1)}, u32[]{:S(2)}, u32[]{:S(2)}) collective-permute-start(bf16[2048,256]{0,1:T(8,128)(2,1)} %get-tuple-element.47), channel_id=1, source_target_pairs={{0,12},{4,8},{8,4},{12,0},{1,13},{5,9},{9,5},{13,1},{2,14},{6,10},... | collective-permute-start | bytes 3145736 | tf_op jit(solution)/shard_map/ppermute | solution.py:37
  260.9 35.7 %copy-start.17 = (bf16[2048,256]{0,1:T(8,128)(2,1)S(1)}, bf16[2048,256]{0,1:T(8,128)(2,1)}, u32[]{:S(2)}) copy-start(bf16[2048,256]{0,1:T(8,128)(2,1)} %get-tuple-element.46) | copy-start | bytes 3145732
  270.7 45.4 %collective-permute-start.18 = (bf16[2048,256]{0,1:T(8,128)(2,1)}, bf16[2048,256]{0,1:T(8,128)(2,1)}, u32[]{:S(2)}, u32[]{:S(2)}) collective-permute-start(bf16[2048,256]{0,1:T(8,128)(2,1)} %get-tuple-element.20), channel_id=1, source_target_pairs={{0,4},{4,0},{8,12},{12,8},{1,5},{5,1},{9,13},{13,9},{2,6},{6,2},{1... | collective-permute-start | bytes 3145736 | tf_op jit(solution)/shard_map/ppermute | solution.py:37
  271.2 48.3 %collective-permute-start.19 = (bf16[2048,256]{0,1:T(8,128)(2,1)}, bf16[2048,256]{0,1:T(8,128)(2,1)S(1)}, u32[]{:S(2)}, u32[]{:S(2)}) collective-permute-start(bf16[2048,256]{0,1:T(8,128)(2,1)} %get-tuple-element.21), channel_id=1, source_target_pairs={{0,8},{4,12},{8,0},{12,4},{1,9},{5,13},{9,1},{13,5},{2,10},{6,14},... | collective-permute-start | bytes 3145736 | tf_op jit(solution)/shard_map/ppermute | solution.py:37
  273.1 68.6 %collective-permute-start.20 = (bf16[2048,256]{0,1:T(8,128)(2,1)}, bf16[2048,256]{0,1:T(8,128)(2,1)}, u32[]{:S(2)}, u32[]{:S(2)}) collective-permute-start(bf16[2048,256]{0,1:T(8,128)(2,1)} %get-tuple-element.22), channel_id=1, source_target_pairs={{0,12},{4,8},{8,4},{12,0},{1,13},{5,9},{9,5},{13,1},{2,14},{6,10},... | collective-permute-start | bytes 3145736 | tf_op jit(solution)/shard_map/ppermute | solution.py:37
  311.9 32.1 %collective-permute-start.21 = (bf16[2048,256]{0,1:T(8,128)(2,1)}, bf16[2048,256]{0,1:T(8,128)(2,1)}, u32[]{:S(2)}, u32[]{:S(2)}) collective-permute-start(bf16[2048,256]{0,1:T(8,128)(2,1)} %get-tuple-element.24), channel_id=1, source_target_pairs={{0,4},{4,0},{8,12},{12,8},{1,5},{5,1},{9,13},{13,9},{2,6},{6,2},{1... | collective-permute-start | bytes 3145736 | tf_op jit(solution)/shard_map/ppermute | solution.py:37
  312.1 52.5 %collective-permute-start.22 = (bf16[2048,256]{0,1:T(8,128)(2,1)}, bf16[2048,256]{0,1:T(8,128)(2,1)}, u32[]{:S(2)}, u32[]{:S(2)}) collective-permute-start(bf16[2048,256]{0,1:T(8,128)(2,1)} %get-tuple-element.25), channel_id=1, source_target_pairs={{0,8},{4,12},{8,0},{12,4},{1,9},{5,13},{9,1},{13,5},{2,10},{6,14},... | collective-permute-start | bytes 3145736 | tf_op jit(solution)/shard_map/ppermute | solution.py:37
  316.1 29.2 %copy-start.8 = (bf16[128,8,4,256]{3,1,2,0:T(8,128)(2,1)S(1)}, bf16[128,8,4,256]{3,1,2,0:T(8,128)(2,1)}, u32[]{:S(2)}) copy-start(bf16[128,8,4,256]{3,1,2,0:T(8,128)(2,1)} %copy.44) | copy-start | bytes 6291460
  316.2 70.4 %collective-permute-start.23 = (bf16[2048,256]{0,1:T(8,128)(2,1)}, bf16[2048,256]{0,1:T(8,128)(2,1)S(1)}, u32[]{:S(2)}, u32[]{:S(2)}) collective-permute-start(bf16[2048,256]{0,1:T(8,128)(2,1)} %get-tuple-element.26), channel_id=1, source_target_pairs={{0,12},{4,8},{8,4},{12,0},{1,13},{5,9},{9,5},{13,1},{2,14},{6,10},... | collective-permute-start | bytes 3145736 | tf_op jit(solution)/shard_map/ppermute | solution.py:37
  319.5 46.3 %slice-start.4 = ((s8[16777216]{0:T(1024)(128)(4,1)}), s8[4194304]{0:T(1024)(128)(4,1)S(1)}, s32[]{:S(2)}) async-start(s8[16777216]{0:T(1024)(128)(4,1)} %bitcast.97), calls=%async_computation.6 | async-start | bytes 8388608
  (25 other events, 257.7 us)
Sparse Core Ops, SparseCore 0:
  236.8 53.3 all-reduce.4
  414.2 53.1 all-reduce.6

commit v6 on v5

--- a/solution.py
+++ b/solution.py
@@ -55,7 +55,7 @@
     eye = jnp.eye(blk_local, dtype=jnp.bool_)
     gf_acc = None
     gs_acc = None
-    outs = []
+    grad_tokens = jnp.zeros((tok_rows, feat), jnp.bfloat16)
     pending = []
     for k in range(CHUNKS):
         x = tokens[k * step:(k + 1) * step]
@@ -74,19 +74,18 @@
         gs_acc = gs if gs_acc is None else gs_acc + gs
         if len(pending) == 2:
             masked, done = lax.optimization_barrier((masked, pending.pop(0)))
-            outs.append(done[0])
+            grad_tokens = lax.dynamic_update_slice(grad_tokens, done[0], (done[2], 0))
             gf_acc = done[1] if gf_acc is None else gf_acc + done[1]
         returned = jnp.concatenate(exchange(masked, n_dev), axis=1)
         gt = jnp.dot(returned, w1tp, preferred_element_type=jnp.float32).astype(jnp.bfloat16)
         gf = lax.dot_general(
             x, returned, (((0,), (0,)), ((), ())), preferred_element_type=jnp.float32
         )
-        pending.append((gt, gf))
-    for gt, gf in pending:
-        outs.append(gt)
+        pending.append((gt, gf, k * step))
+    for gt, gf, at in pending:
+        grad_tokens = lax.dynamic_update_slice(grad_tokens, gt, (at, 0))
         gf_acc = gf if gf_acc is None else gf_acc + gf
 
-    grad_tokens = jnp.concatenate(outs, axis=0)
     gs6 = gs_acc.reshape(n_dev, blk_local, blk_local, sub, blk_local, bs)
     gsd = jnp.sum(jnp.where(eye[None, :, None, None, :, None], gs6, 0.0), axis=4)
     gsd = jnp.take(gsd, order, axis=0)

time: 481 us -> 480 us (level)
  local copies, waits for them, and re-layouts: 46.9 us -> 61.1 us
  other arithmetic: 41.9 us -> 28.2 us
    concatenate x1 -> x0, other arithmetic: 13.8 us -> none  [shards(): grad_tokens = jnp.concatenate(outs, axis=0)]
    dynamic_update_slice x0 -> x2, local copies, waits for them, and re-layouts: none -> 7.18 us  [shards(): grad_tokens = lax.dynamic_update_slice(grad_tokens, done[0], (done[2], 0))]
    broadcast_in_dim x0 -> x1, local copies, waits for them, and re-layouts: none -> 6.56 us  [shards(): grad_tokens = jnp.zeros((tok_rows, feat), jnp.bfloat16)]
    unnamed x75 -> x87, local copies, waits for them, and re-layouts: 14.4 us -> 17.1 us
  transfers between devices with their start and end apart: 26 -> 26, of which waited for: 13 -> 11; matrix products, arithmetic and copies ran while one was open for 43% -> 44% of each run, Pallas kernels for 0% -> 0%
where the time goes in v6:
time: 480 us; the launch traced here: 476 us
  waiting for transfers between devices  189 us (39%)
  matrix products  163 us (34%)
  local copies, waits for them, and re-layouts  61.1 us (13%)
  other arithmetic  28.2 us (6%)
  starting transfers between devices  18.5 us (4%)
  between operations  15.5 us (3%)
    ppermute x24, waiting for transfers between devices, exchange(): lax.ppermute(pieces[m], 'tensor', [(i, i ^ m) for i in range(n_dev)])  152 us
    unnamed x4, waiting for transfers between devices  37.8 us
    dot_general x4, matrix products, shards(): lax.dot_general(x, returned, (((0,), (0,)), ((), ())), preferred_element_...  35.3 us
    dot_general x4, matrix products, shards(): lax.dot_general(active, cot, (((0,), (0,)), ((), ())), preferred_element_...  34.3 us
    dot_general x4, matrix products, shards(): jnp.dot(returned, w1tp, preferred_element_type=jnp.float32)  31.9 us
    dot_general x4, matrix products, shards(): jnp.dot(x, w1p, preferred_element_type=jnp.float32).astype(jnp.bfloat16)  30.9 us
    dot_general x4, matrix products, shards(): backed = jnp.dot(cot, w2p, preferred_element_type=jnp.float32)  30.5 us
    ppermute x24, starting transfers between devices, exchange(): lax.ppermute(pieces[m], 'tensor', [(i, i ^ m) for i in range(n_dev)])  18.2 us
  transfers between devices with their start and end apart: 26, of which 11 were waited for; matrix products, arithmetic and copies ran while one was open for 44% of the time, Pallas kernels for 0%

profile of v6, /device:TPU:0, one launch (start us, length us, event | category | flops | bytes accessed | tf_op | source)
XLA Modules:
  0.0 475.6 jit_solution(8363402595101807698)
XLA Ops:
  14.7 7.8 %convert_bitcast_fusion = bf16[2048,1024]{0,1:T(8,128)(2,1)S(1)} fusion(bf16[1024,1024]{0,1:T(8,128)(2,1)S(1)} %bitcast.86, bf16[8192,1024]{1,0:T(8,128)(2,1)} %param.4), kind=kOutput, calls=%fused_computation.49 | convolution fusion | flops 4297064448 | bytes 10485760 | tf_op jit(solution)/shard_map/dot_general | solution.py:63
  28.3 7.0 %convert_bitcast_fusion.1 = bf16[2048,1024]{0,1:T(8,128)(2,1)S(1)} fusion(bf16[1024,1024]{0,1:T(8,128)(2,1)S(1)} %bitcast.87, bf16[8192,1024]{1,0:T(8,128)(2,1)} %param.4), kind=kOutput, calls=%fused_computation.50 | convolution fusion | flops 4297064448 | bytes 10485760 | tf_op jit(solution)/shard_map/dot_general | solution.py:63
  40.4 7.5 %convert_bitcast_fusion.2 = bf16[2048,1024]{0,1:T(8,128)(2,1)S(1)} fusion(bf16[1024,1024]{0,1:T(8,128)(2,1)} %bitcast.88, bf16[8192,1024]{1,0:T(8,128)(2,1)} %param.4), kind=kOutput, calls=%fused_computation.51 | convolution fusion | flops 4297064448 | bytes 10485760 | tf_op jit(solution)/shard_map/dot_general | solution.py:63
  47.9 8.6 %convert_bitcast_fusion.3 = bf16[2048,1024]{0,1:T(8,128)(2,1)S(1)} fusion(bf16[1024,1024]{0,1:T(8,128)(2,1)S(1)} %bitcast.89, bf16[8192,1024]{1,0:T(8,128)(2,1)} %param.4), kind=kOutput, calls=%fused_computation.52 | convolution fusion | flops 4297064448 | bytes 10485760 | tf_op jit(solution)/shard_map/dot_general | solution.py:63
  57.1 11.1 %convolution_bitcast_fusion = bf16[2048,1024]{0,1:T(8,128)(2,1)} fusion(bf16[1024,1024]{0,1:T(8,128)(2,1)S(1)} %bitcast.90, bf16[8192,1024]{1,0:T(8,128)(2,1)} %param.5), kind=kOutput, calls=%fused_computation.4 | convolution fusion | flops 4294967296 | bytes 10485760 | tf_op jit(solution)/shard_map/dot_general | solution.py:64
  68.2 6.2 %convolution_bitcast_fusion.1 = bf16[2048,1024]{0,1:T(8,128)(2,1)} fusion(bf16[1024,1024]{0,1:T(8,128)(2,1)S(1)} %bitcast.91, bf16[8192,1024]{1,0:T(8,128)(2,1)S(1)} %bitcast.96), kind=kOutput, calls=%fused_computation.5 | convolution fusion | flops 4294967296 | bytes 10485760 | tf_op jit(solution)/shard_map/dot_general | solution.py:64
  74.4 6.2 %convolution_bitcast_fusion.2 = bf16[2048,1024]{0,1:T(8,128)(2,1)} fusion(bf16[1024,1024]{0,1:T(8,128)(2,1)S(1)} %bitcast.92, bf16[8192,1024]{1,0:T(8,128)(2,1)S(1)} %bitcast.96), kind=kOutput, calls=%fused_computation.6 | convolution fusion | flops 4294967296 | bytes 10485760 | tf_op jit(solution)/shard_map/dot_general | solution.py:64
  88.2 7.1 %convolution_bitcast_fusion.3 = bf16[2048,1024]{0,1:T(8,128)(2,1)S(1)} fusion(bf16[1024,1024]{0,1:T(8,128)(2,1)S(1)} %bitcast.93, bf16[8192,1024]{1,0:T(8,128)(2,1)} %param.5), kind=kOutput, calls=%fused_computation.7 | convolution fusion | flops 4294967296 | bytes 10485760 | tf_op jit(solution)/shard_map/dot_general | solution.py:64
  102.4 7.8 %fusion.7 = f32[1024,1024]{1,0:T(8,128)S(1)} fusion(bf16[2048,256]{0,1:T(8,128)(2,1)} %collective-permute-done.16, bf16[2048,256]{0,1:T(8,128)(2,1)} %collective-permute-done.14, bf16[2048,256]{0,1:T(8,128)(2,1)} %collective-permute-done.12, bf16[2048,256]{0,1:T(8,128)(2,1)S(1)} %get-tuple-element.49, bf16[8192,1024]{1,0:T(8,128)(2,1)} %param.5), kind=kOutput, calls=%fused_computation.19 | convolution fusion | flops 4315938816 | bytes 12582912 | tf_op jit(solution)/shard_map/dot_general | solution.py:71
  111.1 29.9 %collective-permute-done.7 = bf16[2048,256]{0,1:T(8,128)(2,1)S(1)} collective-permute-done((bf16[2048,256]{0,1:T(8,128)(2,1)S(1)}, bf16[2048,256]{0,1:T(8,128)(2,1)S(1)}, u32[]{:S(2)}, u32[]{:S(2)}) %collective-permute-start.7) | collective-permute-done | bytes 1048608 | tf_op jit(solution)/shard_map/ppermute | solution.py:37
  142.2 21.7 %collective-permute-done.5 = bf16[2048,256]{0,1:T(8,128)(2,1)S(1)} collective-permute-done((bf16[2048,256]{0,1:T(8,128)(2,1)S(1)}, bf16[2048,256]{0,1:T(8,128)(2,1)S(1)}, u32[]{:S(2)}, u32[]{:S(2)}) %collective-permute-start.5) | collective-permute-done | bytes 1048608 | tf_op jit(solution)/shard_map/ppermute | solution.py:37
  167.5 6.8 %fusion = f32[1024,1024]{1,0:T(8,128)S(1)} fusion(bf16[2048,256]{0,1:T(8,128)(2,1)S(1)} %collective-permute-done.7, bf16[2048,256]{0,1:T(8,128)(2,1)S(1)} %collective-permute-done.5, bf16[2048,256]{0,1:T(8,128)(2,1)S(1)} %collective-permute-done.3, bf16[2048,256]{0,1:T(8,128)(2,1)S(1)} %get-tuple-element.54, bf16[8192,1024]{1,0:T(8,128)(2,1)} %param.5), kind=kOutput, calls=%fused_computation.11 | convolution fusion | flops 4315938816 | bytes 12582912 | tf_op jit(solution)/shard_map/dot_general | solution.py:71
  174.3 11.6 %collective-permute-done.2 = bf16[2048,256]{0,1:T(8,128)(2,1)S(1)} collective-permute-done((bf16[2048,256]{0,1:T(8,128)(2,1)S(1)}, bf16[2048,256]{0,1:T(8,128)(2,1)S(1)}, u32[]{:S(2)}, u32[]{:S(2)}) %collective-permute-start.2) | collective-permute-done | bytes 1048608 | tf_op jit(solution)/shard_map/ppermute | solution.py:37
  186.1 22.5 %collective-permute-done.1 = bf16[2048,256]{0,1:T(8,128)(2,1)S(1)} collective-permute-done((bf16[2048,256]{0,1:T(8,128)(2,1)S(1)}, bf16[2048,256]{0,1:T(8,128)(2,1)S(1)}, u32[]{:S(2)}, u32[]{:S(2)}) %collective-permute-start.1) | collective-permute-done | bytes 1048608 | tf_op jit(solution)/shard_map/ppermute | solution.py:37
  213.7 8.8 %fusion.14 = f32[1024,1024]{1,0:T(8,128)} fusion(bf16[2048,256]{0,1:T(8,128)(2,1)S(1)} %collective-permute-done.2, bf16[2048,256]{0,1:T(8,128)(2,1)S(1)} %collective-permute-done.1, bf16[2048,256]{0,1:T(8,128)(2,1)S(1)} %collective-permute-done, bf16[2048,256]{0,1:T(8,128)(2,1)S(1)} %get-tuple-element.59, bf16[8192,1024]{1,0:T(8,128)(2,1)} %param.5), kind=kOutput, calls=%fused_computation.27 | convolution fusion | flops 4315938816 | bytes 12582912 | tf_op jit(solution)/shard_map/dot_general | solution.py:71
  228.9 10.9 %add_add_fusion = f32[1024,1024]{1,0:T(8,128)} fusion(f32[1024,1024]{1,0:T(8,128)} %fusion.14, f32[1024,1024]{1,0:T(8,128)S(1)} %fusion, f32[1024,1024]{1,0:T(8,128)S(1)} %fusion.7, bf16[8192,1024]{1,0:T(8,128)(2,1)} %param.5, bf16[2048,256]{0,1:T(8,128)(2,1)} %collective-permute-done.11, bf16[2048,256]{0,1:T(8,128)(2,1)} %collective-permute-done.10, ...), kind=kOutput, calls=%fused_computation.46 | convolution fusion | flops 4319084544 | bytes 25165824 | tf_op jit(solution)/shard_map/dot_general | solution.py:71
  239.8 5.6 %reshape.95 = f32[4,4,4,16,4,256]{5,4,3,2,1,0:T(4,128)} reshape(f32[1024,1024]{1,0:T(8,128)} %add_add_fusion) | data formatting | bytes 8388608 | tf_op jit(solution)/shard_map/reshape | solution.py:89
  245.4 5.3 %select_reduce_fusion.1 = f32[4,4,4,16,256]{4,3,2,1,0:T(8,128)S(1)} fusion(f32[4,4,4,16,4,256]{5,4,3,2,1,0:T(4,128)} %reshape.95, pred[4,4]{1,0:T(4,128)(4,1)S(1)} %copy.33), kind=kLoop, calls=%fused_computation.45 | loop fusion | flops 1835008 | bytes 5242896 | tf_op jit(solution)/shard_map/reduce_sum | solution.py:90
  257.0 9.2 %convolution_convert_fusion = bf16[2048,1024]{1,0:T(8,128)(2,1)} fusion(bf16[1024,1024]{1,0:T(8,128)(2,1)} %bitcast.82, bf16[2048,256]{0,1:T(8,128)(2,1)} %collective-permute-done.17, bf16[2048,256]{0,1:T(8,128)(2,1)} %collective-permute-done.15, bf16[2048,256]{0,1:T(8,128)(2,1)} %collective-permute-done.13, bf16[2048,256]{0,1:T(8,128)(2,1)S(1)} %copy-done.21), kind=kOutput, calls=%fused_computation.53 | convolution fusion | flops 4313841664 | bytes 10485760 | tf_op jit(solution)/shard_map/dot_general | solution.py:80
  266.2 9.7 %fusion.51 = f32[1024,1024]{0,1:T(8,128)} fusion(bf16[8192,1024]{1,0:T(8,128)(2,1)} %param.4, bf16[2048,256]{0,1:T(8,128)(2,1)} %collective-permute-done.17, bf16[2048,256]{0,1:T(8,128)(2,1)} %collective-permute-done.15, bf16[2048,256]{0,1:T(8,128)(2,1)} %collective-permute-done.13, bf16[2048,256]{0,1:T(8,128)(2,1)S(1)} %copy-done.21), kind=kOutput, calls=%fused_computation.76 | convolution fusion | flops 4311744512 | bytes 12582912 | tf_op jit(solution)/shard_map/dot_general | solution.py:81
  279.1 22.8 %collective-permute-done.6 = bf16[2048,256]{0,1:T(8,128)(2,1)} collective-permute-done((bf16[2048,256]{0,1:T(8,128)(2,1)}, bf16[2048,256]{0,1:T(8,128)(2,1)}, u32[]{:S(2)}, u32[]{:S(2)}) %collective-permute-start.6) | collective-permute-done | bytes 1048608 | tf_op jit(solution)/shard_map/ppermute | solution.py:37
  302.0 9.5 %fusion.48 = f32[1024,1024]{0,1:T(8,128)} fusion(bf16[8192,1024]{1,0:T(8,128)(2,1)} %param.4, bf16[2048,256]{0,1:T(8,128)(2,1)} %collective-permute-done.8, bf16[2048,256]{0,1:T(8,128)(2,1)} %collective-permute-done.6, bf16[2048,256]{0,1:T(8,128)(2,1)S(1)} %collective-permute-done.4, bf16[2048,256]{0,1:T(8,128)(2,1)S(1)} %copy-done.22), kind=kOutput, calls=%fused_computation.75 | convolution fusion | flops 4311744512 | bytes 12582912 | tf_op jit(solution)/shard_map/dot_general | solution.py:81
  311.4 8.1 %convolution_convert_fusion.1 = bf16[2048,1024]{1,0:T(8,128)(2,1)} fusion(bf16[1024,1024]{1,0:T(8,128)(2,1)S(1)} %bitcast.83, bf16[2048,256]{0,1:T(8,128)(2,1)} %collective-permute-done.8, bf16[2048,256]{0,1:T(8,128)(2,1)} %collective-permute-done.6, bf16[2048,256]{0,1:T(8,128)(2,1)S(1)} %collective-permute-done.4, bf16[2048,256]{0,1:T(8,128)(2,1)S(1)} %copy-done.22), kind=kOutput, calls=%fused_computation.54 | convolution fusion | flops 4313841664 | bytes 10485760 | tf_op jit(solution)/shard_map/dot_general | solution.py:80
  321.4 6.6 %broadcast_in_dim.150 = bf16[8192,1024]{1,0:T(8,128)(2,1)} broadcast(bf16[]{:T(256)} %constant.38.clone.1), dimensions={} | broadcast | bytes 16777218 | tf_op jit(solution)/shard_map/broadcast_in_dim | solution.py:58
  348.2 20.8 %collective-permute-done.20 = bf16[2048,256]{0,1:T(8,128)(2,1)} collective-permute-done((bf16[2048,256]{0,1:T(8,128)(2,1)}, bf16[2048,256]{0,1:T(8,128)(2,1)}, u32[]{:S(2)}, u32[]{:S(2)}) %collective-permute-start.20) | collective-permute-done | bytes 1048608 | tf_op jit(solution)/shard_map/ppermute | solution.py:37
  370.4 7.8 %fusion.45 = f32[1024,1024]{1,0:T(8,128)S(1)} fusion(bf16[2048,1024]{0,1:T(8,128)(2,1)S(1)} %constant_dynamic-update-slice_fusion, bf16[8192,1024]{1,0:T(8,128)(2,1)} %param.4), kind=kOutput, calls=%fused_computation.72 | convolution fusion | flops 4294967296 | bytes 12582912 | tf_op jit(solution)/shard_map/dot_general | solution.py:81
  378.2 13.2 %collective-permute-done.23 = bf16[2048,256]{0,1:T(8,128)(2,1)S(1)} collective-permute-done((bf16[2048,256]{0,1:T(8,128)(2,1)}, bf16[2048,256]{0,1:T(8,128)(2,1)S(1)}, u32[]{:S(2)}, u32[]{:S(2)}) %collective-permute-start.23) | collective-permute-done | bytes 1048608 | tf_op jit(solution)/shard_map/ppermute | solution.py:37
  393.4 8.3 %bitcast_add_fusion = f32[1024,1024]{0,1:T(8,128)} fusion(f32[1024,1024]{1,0:T(8,128)S(1)} %fusion.45, f32[1024,1024]{0,1:T(8,128)S(1)} %copy-done.32, f32[1024,1024]{0,1:T(8,128)S(1)} %copy-done.31, bf16[2048,1024]{0,1:T(8,128)(2,1)S(1)} %constant_dynamic-update-slice_fusion.4, bf16[8192,1024]{1,0:T(8,128)(2,1)} %param.4), kind=kOutput, calls=%fused_computation.42 | convolution fusion | flops 4298113024 | bytes 25165824 | tf_op jit(solution)/shard_map/dot_general | solution.py:81
  401.7 5.7 %reshape.96 = f32[4,256,4,4,4,16]{1,0,5,4,3,2:T(4,128)} reshape(f32[1024,1024]{0,1:T(8,128)} %bitcast_add_fusion) | data formatting | bytes 8388608 | tf_op jit(solution)/shard_map/reshape | solution.py:95
  413.7 8.5 %convert_dynamic-update-slice_fusion.1 = bf16[8192,1024]{1,0:T(8,128)(2,1)} fusion(bf16[8192,1024]{1,0:T(8,128)(2,1)} %constant_dynamic-update-slice_fusion.8, bf16[2048,1024]{0,1:T(8,128)(2,1)} %copy-done.24, bf16[1024,1024]{1,0:T(8,128)(2,1)S(1)} %bitcast.84), kind=kOutput, calls=%fused_computation.48 | convolution fusion | flops 4297064448 | bytes 10485760 | tf_op jit(solution)/shard_map/dot_general | solution.py:80
  422.9 6.2 %convert_dynamic-update-slice_fusion = bf16[8192,1024]{1,0:T(8,128)(2,1)} fusion(bf16[8192,1024]{1,0:T(8,128)(2,1)} %convert_dynamic-update-slice_fusion.1, bf16[2048,1024]{0,1:T(8,128)(2,1)S(1)} %copy-done.27, bf16[1024,1024]{1,0:T(8,128)(2,1)S(1)} %bitcast.85), kind=kOutput, calls=%fused_computation.47 | convolution fusion | flops 4297064448 | bytes 10485760 | tf_op jit(solution)/shard_map/dot_general | solution.py:80
  429.1 37.8 %all-reduce.7.cloned.1.call-done = f32[256,4,256]{2,1,0:T(4,128)} async-done(((f32[256,4,256]{2,1,0:T(4,128)}), f32[256,4,256]{2,1,0:T(4,128)}) %all-reduce.7.cloned.1.call-update) | async-done | bytes 1048592
  (172 shorter events, 93.8 us)
Async XLA Ops:
  7.2 330.0 %all-reduce.5.cloned.1.call-start = ((), (), s32[]{:S(2)}) async-start(), calls=%async_computation | async-start | bytes 2097152
  7.3 33.0 %copy-start.28 = (pred[4,4]{0,1:T(4,128)(4,1)}, pred[4,4]{0,1:T(4,128)(4,1)S(1)}, u32[]{:S(2)}) copy-start(pred[4,4]{0,1:T(4,128)(4,1)S(1)} %iota_compare_fusion) | copy-start | bytes 52
  24.3 71.0 %collective-permute-start.12 = (bf16[2048,256]{0,1:T(8,128)(2,1)}, bf16[2048,256]{0,1:T(8,128)(2,1)}, u32[]{:S(2)}, u32[]{:S(2)}) collective-permute-start(bf16[2048,256]{0,1:T(8,128)(2,1)} %get-tuple-element.64), channel_id=1, source_target_pairs={{0,4},{4,0},{8,12},{12,8},{1,5},{5,1},{9,13},{13,9},{2,6},{6,2},{1... | collective-permute-start | bytes 3145736 | tf_op jit(solution)/shard_map/ppermute | solution.py:37
  24.8 71.3 %collective-permute-start.16 = (bf16[2048,256]{0,1:T(8,128)(2,1)}, bf16[2048,256]{0,1:T(8,128)(2,1)}, u32[]{:S(2)}, u32[]{:S(2)}) collective-permute-start(bf16[2048,256]{0,1:T(8,128)(2,1)} %get-tuple-element.65), channel_id=1, source_target_pairs={{0,12},{4,8},{8,4},{12,0},{1,13},{5,9},{9,5},{13,1},{2,14},{6,10},... | collective-permute-start | bytes 3145736 | tf_op jit(solution)/shard_map/ppermute | solution.py:37
  27.4 69.5 %collective-permute-start.14 = (bf16[2048,256]{0,1:T(8,128)(2,1)}, bf16[2048,256]{0,1:T(8,128)(2,1)}, u32[]{:S(2)}, u32[]{:S(2)}) collective-permute-start(bf16[2048,256]{0,1:T(8,128)(2,1)} %get-tuple-element.66), channel_id=1, source_target_pairs={{0,8},{4,12},{8,0},{12,4},{1,9},{5,13},{9,1},{13,5},{2,10},{6,14},... | collective-permute-start | bytes 3145736 | tf_op jit(solution)/shard_map/ppermute | solution.py:37
  39.1 183.5 %collective-permute-start.11 = (bf16[2048,256]{0,1:T(8,128)(2,1)}, bf16[2048,256]{0,1:T(8,128)(2,1)}, u32[]{:S(2)}, u32[]{:S(2)}) collective-permute-start(bf16[2048,256]{0,1:T(8,128)(2,1)} %get-tuple-element.67), channel_id=1, source_target_pairs={{0,12},{4,8},{8,4},{12,0},{1,13},{5,9},{9,5},{13,1},{2,14},{6,10},... | collective-permute-start | bytes 3145736 | tf_op jit(solution)/shard_map/ppermute | solution.py:37
  39.5 183.3 %collective-permute-start.10 = (bf16[2048,256]{0,1:T(8,128)(2,1)}, bf16[2048,256]{0,1:T(8,128)(2,1)}, u32[]{:S(2)}, u32[]{:S(2)}) collective-permute-start(bf16[2048,256]{0,1:T(8,128)(2,1)} %get-tuple-element.68), channel_id=1, source_target_pairs={{0,8},{4,12},{8,0},{12,4},{1,9},{5,13},{9,1},{13,5},{2,10},{6,14},... | collective-permute-start | bytes 3145736 | tf_op jit(solution)/shard_map/ppermute | solution.py:37
  47.9 34.6 %copy-start.6 = (bf16[2048,1024]{0,1:T(8,128)(2,1)}, bf16[2048,1024]{0,1:T(8,128)(2,1)S(1)}, u32[]{:S(2)}) copy-start(bf16[2048,1024]{0,1:T(8,128)(2,1)S(1)} %convert_bitcast_fusion.2) | copy-start | bytes 12582916
  56.5 24.4 %copy-start.5 = (bf16[2048,1024]{0,1:T(8,128)(2,1)}, bf16[2048,1024]{0,1:T(8,128)(2,1)S(1)}, u32[]{:S(2)}) copy-start(bf16[2048,1024]{0,1:T(8,128)(2,1)S(1)} %convert_bitcast_fusion.3) | copy-start | bytes 12582916
  95.3 14.9 %collective-permute-start.3 = (bf16[2048,256]{0,1:T(8,128)(2,1)S(1)}, bf16[2048,256]{0,1:T(8,128)(2,1)S(1)}, u32[]{:S(2)}, u32[]{:S(2)}) collective-permute-start(bf16[2048,256]{0,1:T(8,128)(2,1)S(1)} %copy-done.20), channel_id=1, source_target_pairs={{0,4},{4,0},{8,12},{12,8},{1,5},{5,1},{9,13},{13,9},{2,6},{6,2},{1... | collective-permute-start | bytes 3145736 | tf_op jit(solution)/shard_map/ppermute | solution.py:37
  96.1 44.9 %collective-permute-start.7 = (bf16[2048,256]{0,1:T(8,128)(2,1)S(1)}, bf16[2048,256]{0,1:T(8,128)(2,1)S(1)}, u32[]{:S(2)}, u32[]{:S(2)}) collective-permute-start(bf16[2048,256]{0,1:T(8,128)(2,1)S(1)} %copy-done.19), channel_id=1, source_target_pairs={{0,12},{4,8},{8,4},{12,0},{1,13},{5,9},{9,5},{13,1},{2,14},{6,10},... | collective-permute-start | bytes 3145736 | tf_op jit(solution)/shard_map/ppermute | solution.py:37
  96.8 67.0 %collective-permute-start.5 = (bf16[2048,256]{0,1:T(8,128)(2,1)S(1)}, bf16[2048,256]{0,1:T(8,128)(2,1)S(1)}, u32[]{:S(2)}, u32[]{:S(2)}) collective-permute-start(bf16[2048,256]{0,1:T(8,128)(2,1)S(1)} %copy-done.18), channel_id=1, source_target_pairs={{0,8},{4,12},{8,0},{12,4},{1,9},{5,13},{9,1},{13,5},{2,10},{6,14},... | collective-permute-start | bytes 3145736 | tf_op jit(solution)/shard_map/ppermute | solution.py:37
  102.4 38.6 %copy-start.16 = (bf16[2048,256]{0,1:T(8,128)(2,1)S(1)}, bf16[2048,256]{0,1:T(8,128)(2,1)}, u32[]{:S(2)}) copy-start(bf16[2048,256]{0,1:T(8,128)(2,1)} %get-tuple-element.74) | copy-start | bytes 3145732
  102.4 61.4 %copy-start.1 = (bf16[2048,1024]{0,1:T(8,128)(2,1)S(1)}, bf16[2048,1024]{0,1:T(8,128)(2,1)}, u32[]{:S(2)}) copy-start(bf16[2048,1024]{0,1:T(8,128)(2,1)} %convolution_bitcast_fusion.2) | copy-start | bytes 12582916
  110.2 75.7 %collective-permute-start.2 = (bf16[2048,256]{0,1:T(8,128)(2,1)S(1)}, bf16[2048,256]{0,1:T(8,128)(2,1)S(1)}, u32[]{:S(2)}, u32[]{:S(2)}) collective-permute-start(bf16[2048,256]{0,1:T(8,128)(2,1)S(1)} %copy-done.17), channel_id=1, source_target_pairs={{0,12},{4,8},{8,4},{12,0},{1,13},{5,9},{9,5},{13,1},{2,14},{6,10},... | collective-permute-start | bytes 3145736 | tf_op jit(solution)/shard_map/ppermute | solution.py:37
  141.0 67.6 %collective-permute-start.1 = (bf16[2048,256]{0,1:T(8,128)(2,1)S(1)}, bf16[2048,256]{0,1:T(8,128)(2,1)S(1)}, u32[]{:S(2)}, u32[]{:S(2)}) collective-permute-start(bf16[2048,256]{0,1:T(8,128)(2,1)S(1)} %copy-done.16), channel_id=1, source_target_pairs={{0,8},{4,12},{8,0},{12,4},{1,9},{5,13},{9,1},{13,5},{2,10},{6,14},... | collective-permute-start | bytes 3145736 | tf_op jit(solution)/shard_map/ppermute | solution.py:37
  163.8 45.5 %collective-permute-start = (bf16[2048,256]{0,1:T(8,128)(2,1)S(1)}, bf16[2048,256]{0,1:T(8,128)(2,1)S(1)}, u32[]{:S(2)}, u32[]{:S(2)}) collective-permute-start(bf16[2048,256]{0,1:T(8,128)(2,1)S(1)} %get-tuple-element.75), channel_id=1, source_target_pairs={{0,4},{4,0},{8,12},{12,8},{1,5},{5,1},{9,13},{13,9},{2,6},{6,2},{1... | collective-permute-start | bytes 3145736 | tf_op jit(solution)/shard_map/ppermute | solution.py:37
  185.9 38.2 %collective-permute-start.9 = (bf16[2048,256]{0,1:T(8,128)(2,1)S(1)}, bf16[2048,256]{0,1:T(8,128)(2,1)S(1)}, u32[]{:S(2)}, u32[]{:S(2)}) collective-permute-start(bf16[2048,256]{0,1:T(8,128)(2,1)S(1)} %copy-done.15), channel_id=1, source_target_pairs={{0,4},{4,0},{8,12},{12,8},{1,5},{5,1},{9,13},{13,9},{2,6},{6,2},{1... | collective-permute-start | bytes 3145736 | tf_op jit(solution)/shard_map/ppermute | solution.py:37
  208.6 44.9 %collective-permute-start.17 = (bf16[2048,256]{0,1:T(8,128)(2,1)}, bf16[2048,256]{0,1:T(8,128)(2,1)}, u32[]{:S(2)}, u32[]{:S(2)}) collective-permute-start(bf16[2048,256]{0,1:T(8,128)(2,1)} %get-tuple-element.51), channel_id=1, source_target_pairs={{0,12},{4,8},{8,4},{12,0},{1,13},{5,9},{9,5},{13,1},{2,14},{6,10},... | collective-permute-start | bytes 3145736 | tf_op jit(solution)/shard_map/ppermute | solution.py:37
  209.3 47.7 %collective-permute-start.15 = (bf16[2048,256]{0,1:T(8,128)(2,1)}, bf16[2048,256]{0,1:T(8,128)(2,1)}, u32[]{:S(2)}, u32[]{:S(2)}) collective-permute-start(bf16[2048,256]{0,1:T(8,128)(2,1)} %get-tuple-element.52), channel_id=1, source_target_pairs={{0,8},{4,12},{8,0},{12,4},{1,9},{5,13},{9,1},{13,5},{2,10},{6,14},... | collective-permute-start | bytes 3145736 | tf_op jit(solution)/shard_map/ppermute | solution.py:37
  222.6 34.4 %collective-permute-start.13 = (bf16[2048,256]{0,1:T(8,128)(2,1)}, bf16[2048,256]{0,1:T(8,128)(2,1)}, u32[]{:S(2)}, u32[]{:S(2)}) collective-permute-start(bf16[2048,256]{0,1:T(8,128)(2,1)} %get-tuple-element.53), channel_id=1, source_target_pairs={{0,4},{4,0},{8,12},{12,8},{1,5},{5,1},{9,13},{13,9},{2,6},{6,2},{1... | collective-permute-start | bytes 3145736 | tf_op jit(solution)/shard_map/ppermute | solution.py:37
  222.8 56.3 %collective-permute-start.8 = (bf16[2048,256]{0,1:T(8,128)(2,1)}, bf16[2048,256]{0,1:T(8,128)(2,1)}, u32[]{:S(2)}, u32[]{:S(2)}) collective-permute-start(bf16[2048,256]{0,1:T(8,128)(2,1)} %get-tuple-element.56), channel_id=1, source_target_pairs={{0,12},{4,8},{8,4},{12,0},{1,13},{5,9},{9,5},{13,1},{2,14},{6,10},... | collective-permute-start | bytes 3145736 | tf_op jit(solution)/shard_map/ppermute | solution.py:37
  224.1 77.8 %collective-permute-start.6 = (bf16[2048,256]{0,1:T(8,128)(2,1)}, bf16[2048,256]{0,1:T(8,128)(2,1)}, u32[]{:S(2)}, u32[]{:S(2)}) collective-permute-start(bf16[2048,256]{0,1:T(8,128)(2,1)} %get-tuple-element.57), channel_id=1, source_target_pairs={{0,8},{4,12},{8,0},{12,4},{1,9},{5,13},{9,1},{13,5},{2,10},{6,14},... | collective-permute-start | bytes 3145736 | tf_op jit(solution)/shard_map/ppermute | solution.py:37
  253.3 213.6 %all-reduce.7.cloned.1.call-start = ((), (), s32[]{:S(2)}) async-start(), calls=%async_computation.1 | async-start | bytes 2097152
  253.5 48.4 %collective-permute-start.4 = (bf16[2048,256]{0,1:T(8,128)(2,1)}, bf16[2048,256]{0,1:T(8,128)(2,1)S(1)}, u32[]{:S(2)}, u32[]{:S(2)}) collective-permute-start(bf16[2048,256]{0,1:T(8,128)(2,1)} %get-tuple-element.58), channel_id=1, source_target_pairs={{0,4},{4,0},{8,12},{12,8},{1,5},{5,1},{9,13},{13,9},{2,6},{6,2},{1... | collective-permute-start | bytes 3145736 | tf_op jit(solution)/shard_map/ppermute | solution.py:37
  266.2 35.8 %copy-start.22 = (bf16[2048,256]{0,1:T(8,128)(2,1)S(1)}, bf16[2048,256]{0,1:T(8,128)(2,1)}, u32[]{:S(2)}) copy-start(bf16[2048,256]{0,1:T(8,128)(2,1)} %get-tuple-element.55) | copy-start | bytes 3145732
  275.9 62.4 %collective-permute-start.21 = (bf16[2048,256]{0,1:T(8,128)(2,1)}, bf16[2048,256]{0,1:T(8,128)(2,1)S(1)}, u32[]{:S(2)}, u32[]{:S(2)}) collective-permute-start(bf16[2048,256]{0,1:T(8,128)(2,1)} %get-tuple-element.28), channel_id=1, source_target_pairs={{0,4},{4,0},{8,12},{12,8},{1,5},{5,1},{9,13},{13,9},{2,6},{6,2},{1... | collective-permute-start | bytes 3145736 | tf_op jit(solution)/shard_map/ppermute | solution.py:37
  275.9 64.9 %collective-permute-start.22 = (bf16[2048,256]{0,1:T(8,128)(2,1)}, bf16[2048,256]{0,1:T(8,128)(2,1)S(1)}, u32[]{:S(2)}, u32[]{:S(2)}) collective-permute-start(bf16[2048,256]{0,1:T(8,128)(2,1)} %get-tuple-element.29), channel_id=1, source_target_pairs={{0,8},{4,12},{8,0},{12,4},{1,9},{5,13},{9,1},{13,5},{2,10},{6,14},... | collective-permute-start | bytes 3145736 | tf_op jit(solution)/shard_map/ppermute | solution.py:37
  319.5 22.4 %collective-permute-start.18 = (bf16[2048,256]{0,1:T(8,128)(2,1)}, bf16[2048,256]{0,1:T(8,128)(2,1)}, u32[]{:S(2)}, u32[]{:S(2)}) collective-permute-start(bf16[2048,256]{0,1:T(8,128)(2,1)} %get-tuple-element.24), channel_id=1, source_target_pairs={{0,4},{4,0},{8,12},{12,8},{1,5},{5,1},{9,13},{13,9},{2,6},{6,2},{1... | collective-permute-start | bytes 3145736 | tf_op jit(solution)/shard_map/ppermute | solution.py:37
  319.5 27.4 %collective-permute-start.19 = (bf16[2048,256]{0,1:T(8,128)(2,1)}, bf16[2048,256]{0,1:T(8,128)(2,1)}, u32[]{:S(2)}, u32[]{:S(2)}) collective-permute-start(bf16[2048,256]{0,1:T(8,128)(2,1)} %get-tuple-element.25), channel_id=1, source_target_pairs={{0,8},{4,12},{8,0},{12,4},{1,9},{5,13},{9,1},{13,5},{2,10},{6,14},... | collective-permute-start | bytes 3145736 | tf_op jit(solution)/shard_map/ppermute | solution.py:37
  321.0 48.0 %collective-permute-start.20 = (bf16[2048,256]{0,1:T(8,128)(2,1)}, bf16[2048,256]{0,1:T(8,128)(2,1)}, u32[]{:S(2)}, u32[]{:S(2)}) collective-permute-start(bf16[2048,256]{0,1:T(8,128)(2,1)} %get-tuple-element.26), channel_id=1, source_target_pairs={{0,12},{4,8},{8,4},{12,0},{1,13},{5,9},{9,5},{13,1},{2,14},{6,10},... | collective-permute-start | bytes 3145736 | tf_op jit(solution)/shard_map/ppermute | solution.py:37
  338.3 53.0 %collective-permute-start.23 = (bf16[2048,256]{0,1:T(8,128)(2,1)}, bf16[2048,256]{0,1:T(8,128)(2,1)S(1)}, u32[]{:S(2)}, u32[]{:S(2)}) collective-permute-start(bf16[2048,256]{0,1:T(8,128)(2,1)} %get-tuple-element.30), channel_id=1, source_target_pairs={{0,12},{4,8},{8,4},{12,0},{1,13},{5,9},{9,5},{13,1},{2,14},{6,10},... | collective-permute-start | bytes 3145736 | tf_op jit(solution)/shard_map/ppermute | solution.py:37
  (31 other events, 292.3 us)
Sparse Core Ops, SparseCore 0:
  253.4 52.9 all-reduce.4
  413.8 53.0 all-reduce.6

commit v7 on v6

--- a/solution.py
+++ b/solution.py
@@ -36,6 +36,17 @@
     for m in range(1, n_dev):
         outs.append(lax.ppermute(pieces[m], "tensor", [(i, i ^ m) for i in range(n_dev)]))
     return outs
+
+
+def dp_reduce_scatter(x):
+    n = lax.axis_size("dp")
+    didx = lax.axis_index("dp")
+    blocks = x.reshape((n, x.shape[0] // n) + x.shape[1:])
+    acc = lax.dynamic_index_in_dim(blocks, didx, axis=0, keepdims=False)
+    for m in range(1, n):
+        send = lax.dynamic_index_in_dim(blocks, jnp.bitwise_xor(didx, m), axis=0, keepdims=False)
+        acc = acc + lax.ppermute(send, "dp", [(i, i ^ m) for i in range(n)])
+    return acc
 
 
 def shards(tokens, cotangent, w_first, w_second):
@@ -96,7 +107,7 @@
     gfd = jnp.sum(jnp.where(eye[:, None, None, None, :, None], gf6, 0.0), axis=4)
     gfd = jnp.take(gfd, order, axis=2)
     first_term = gfd.transpose(1, 0, 2, 3, 4).reshape(bs, blk_local, bs) * grad_scale
-    grad_first = lax.psum_scatter(first_term, "dp", scatter_dimension=0, tiled=True)
+    grad_first = dp_reduce_scatter(first_term)
     return (grad_tokens, grad_first.transpose(1, 0, 2), grad_second.transpose(1, 0, 2))
 
 

time: 480 us -> 457 us (0.952)
  waiting for transfers between devices: 189 us -> 153 us
  local copies, waits for them, and re-layouts: 61.1 us -> 66.1 us
    unnamed x4 -> x2, waiting for transfers between devices: 37.8 us -> 0.02 us
    dynamic_slice x0 -> x5, local copies, waits for them, and re-layouts: none -> 6.65 us  [the longest x2 3.67 us: dp_reduce_scatter(): acc = lax.dynamic_index_in_dim(blocks, didx, axis=0, keepdims=False)]
    unnamed x87 -> x84, local copies, waits for them, and re-layouts: 17.1 us -> 16.2 us
  transfers between devices with their start and end apart: 26 -> 28, of which waited for: 11 -> 11; matrix products, arithmetic and copies ran while one was open for 44% -> 47% of each run, Pallas kernels for 0% -> 0%
where the time goes in v7:
time: 457 us; the launch traced here: 451 us
  matrix products  165 us (36%)
  waiting for transfers between devices  153 us (33%)
  local copies, waits for them, and re-layouts  66.1 us (14%)
  other arithmetic  28.5 us (6%)
  starting transfers between devices  22.8 us (5%)
  between operations  15.6 us (3%)
    ppermute x24, waiting for transfers between devices, exchange(): lax.ppermute(pieces[m], 'tensor', [(i, i ^ m) for i in range(n_dev)])  151 us
    dot_general x4, matrix products, shards(): lax.dot_general(x, returned, (((0,), (0,)), ((), ())), preferred_element_...  35.7 us
    dot_general x4, matrix products, shards(): lax.dot_general(active, cot, (((0,), (0,)), ((), ())), preferred_element_...  34.3 us
    dot_general x4, matrix products, shards(): jnp.dot(returned, w1tp, preferred_element_type=jnp.float32)  33 us
    dot_general x4, matrix products, shards(): backed = jnp.dot(cot, w2p, preferred_element_type=jnp.float32)  31 us
    dot_general x4, matrix products, shards(): jnp.dot(x, w1p, preferred_element_type=jnp.float32).astype(jnp.bfloat16)  30.9 us
    ppermute x24, starting transfers between devices, exchange(): lax.ppermute(pieces[m], 'tensor', [(i, i ^ m) for i in range(n_dev)])  18.2 us
    unnamed x84, local copies, waits for them, and re-layouts  16.2 us
  transfers between devices with their start and end apart: 28, of which 11 were waited for; matrix products, arithmetic and copies ran while one was open for 47% of the time, Pallas kernels for 0%

profile of v7, /device:TPU:0, one launch (start us, length us, event | category | flops | bytes accessed | tf_op | source)
XLA Modules:
  0.0 450.9 jit_solution(5764175663654072917)
XLA Ops:
  14.7 7.8 %convert_bitcast_fusion = bf16[2048,1024]{0,1:T(8,128)(2,1)S(1)} fusion(bf16[1024,1024]{0,1:T(8,128)(2,1)S(1)} %bitcast.103, bf16[8192,1024]{1,0:T(8,128)(2,1)} %param.4), kind=kOutput, calls=%fused_computation.49 | convolution fusion | flops 4297064448 | bytes 10485760 | tf_op jit(solution)/shard_map/dot_general | solution.py:74
  28.3 7.0 %convert_bitcast_fusion.1 = bf16[2048,1024]{0,1:T(8,128)(2,1)S(1)} fusion(bf16[1024,1024]{0,1:T(8,128)(2,1)S(1)} %bitcast.104, bf16[8192,1024]{1,0:T(8,128)(2,1)} %param.4), kind=kOutput, calls=%fused_computation.50 | convolution fusion | flops 4297064448 | bytes 10485760 | tf_op jit(solution)/shard_map/dot_general | solution.py:74
  40.4 7.5 %convert_bitcast_fusion.2 = bf16[2048,1024]{0,1:T(8,128)(2,1)S(1)} fusion(bf16[1024,1024]{0,1:T(8,128)(2,1)} %bitcast.105, bf16[8192,1024]{1,0:T(8,128)(2,1)} %param.4), kind=kOutput, calls=%fused_computation.51 | convolution fusion | flops 4297064448 | bytes 10485760 | tf_op jit(solution)/shard_map/dot_general | solution.py:74
  47.9 8.6 %convert_bitcast_fusion.3 = bf16[2048,1024]{0,1:T(8,128)(2,1)S(1)} fusion(bf16[1024,1024]{0,1:T(8,128)(2,1)S(1)} %bitcast.106, bf16[8192,1024]{1,0:T(8,128)(2,1)} %param.4), kind=kOutput, calls=%fused_computation.52 | convolution fusion | flops 4297064448 | bytes 10485760 | tf_op jit(solution)/shard_map/dot_general | solution.py:74
  57.1 11.2 %convolution_bitcast_fusion = bf16[2048,1024]{0,1:T(8,128)(2,1)} fusion(bf16[1024,1024]{0,1:T(8,128)(2,1)S(1)} %bitcast.99, bf16[8192,1024]{1,0:T(8,128)(2,1)} %param.5), kind=kOutput, calls=%fused_computation.4 | convolution fusion | flops 4294967296 | bytes 10485760 | tf_op jit(solution)/shard_map/dot_general | solution.py:75
  68.3 6.2 %convolution_bitcast_fusion.1 = bf16[2048,1024]{0,1:T(8,128)(2,1)} fusion(bf16[1024,1024]{0,1:T(8,128)(2,1)S(1)} %bitcast.100, bf16[8192,1024]{1,0:T(8,128)(2,1)S(1)} %bitcast.112), kind=kOutput, calls=%fused_computation.5 | convolution fusion | flops 4294967296 | bytes 10485760 | tf_op jit(solution)/shard_map/dot_general | solution.py:75
  74.5 6.1 %convolution_bitcast_fusion.2 = bf16[2048,1024]{0,1:T(8,128)(2,1)} fusion(bf16[1024,1024]{0,1:T(8,128)(2,1)S(1)} %bitcast.101, bf16[8192,1024]{1,0:T(8,128)(2,1)S(1)} %bitcast.112), kind=kOutput, calls=%fused_computation.6 | convolution fusion | flops 4294967296 | bytes 10485760 | tf_op jit(solution)/shard_map/dot_general | solution.py:75
  88.3 7.5 %convolution_bitcast_fusion.3 = bf16[2048,1024]{0,1:T(8,128)(2,1)S(1)} fusion(bf16[1024,1024]{0,1:T(8,128)(2,1)} %bitcast.102, bf16[8192,1024]{1,0:T(8,128)(2,1)} %param.5), kind=kOutput, calls=%fused_computation.7 | convolution fusion | flops 4294967296 | bytes 10485760 | tf_op jit(solution)/shard_map/dot_general | solution.py:75
  102.7 7.8 %fusion.7 = f32[1024,1024]{1,0:T(8,128)S(1)} fusion(bf16[2048,256]{0,1:T(8,128)(2,1)} %collective-permute-done.16, bf16[2048,256]{0,1:T(8,128)(2,1)} %collective-permute-done.14, bf16[2048,256]{0,1:T(8,128)(2,1)} %collective-permute-done.12, bf16[2048,256]{0,1:T(8,128)(2,1)S(1)} %get-tuple-element.46, bf16[8192,1024]{1,0:T(8,128)(2,1)} %param.5), kind=kOutput, calls=%fused_computation.19 | convolution fusion | flops 4315938816 | bytes 12582912 | tf_op jit(solution)/shard_map/dot_general | solution.py:82
  111.4 29.6 %collective-permute-done.7 = bf16[2048,256]{0,1:T(8,128)(2,1)S(1)} collective-permute-done((bf16[2048,256]{0,1:T(8,128)(2,1)S(1)}, bf16[2048,256]{0,1:T(8,128)(2,1)S(1)}, u32[]{:S(2)}, u32[]{:S(2)}) %collective-permute-start.7) | collective-permute-done | bytes 1048608 | tf_op jit(solution)/shard_map/ppermute | solution.py:37
  142.2 21.7 %collective-permute-done.5 = bf16[2048,256]{0,1:T(8,128)(2,1)S(1)} collective-permute-done((bf16[2048,256]{0,1:T(8,128)(2,1)S(1)}, bf16[2048,256]{0,1:T(8,128)(2,1)S(1)}, u32[]{:S(2)}, u32[]{:S(2)}) %collective-permute-start.5) | collective-permute-done | bytes 1048608 | tf_op jit(solution)/shard_map/ppermute | solution.py:37
  167.6 6.8 %fusion = f32[1024,1024]{1,0:T(8,128)S(1)} fusion(bf16[2048,256]{0,1:T(8,128)(2,1)S(1)} %collective-permute-done.7, bf16[2048,256]{0,1:T(8,128)(2,1)S(1)} %collective-permute-done.5, bf16[2048,256]{0,1:T(8,128)(2,1)S(1)} %collective-permute-done.3, bf16[2048,256]{0,1:T(8,128)(2,1)S(1)} %get-tuple-element.51, bf16[8192,1024]{1,0:T(8,128)(2,1)} %param.5), kind=kOutput, calls=%fused_computation.11 | convolution fusion | flops 4315938816 | bytes 12582912 | tf_op jit(solution)/shard_map/dot_general | solution.py:82
  174.3 11.6 %collective-permute-done.2 = bf16[2048,256]{0,1:T(8,128)(2,1)S(1)} collective-permute-done((bf16[2048,256]{0,1:T(8,128)(2,1)S(1)}, bf16[2048,256]{0,1:T(8,128)(2,1)S(1)}, u32[]{:S(2)}, u32[]{:S(2)}) %collective-permute-start.2) | collective-permute-done | bytes 1048608 | tf_op jit(solution)/shard_map/ppermute | solution.py:37
  186.1 22.5 %collective-permute-done.1 = bf16[2048,256]{0,1:T(8,128)(2,1)S(1)} collective-permute-done((bf16[2048,256]{0,1:T(8,128)(2,1)S(1)}, bf16[2048,256]{0,1:T(8,128)(2,1)S(1)}, u32[]{:S(2)}, u32[]{:S(2)}) %collective-permute-start.1) | collective-permute-done | bytes 1048608 | tf_op jit(solution)/shard_map/ppermute | solution.py:37
  213.7 8.8 %fusion.14 = f32[1024,1024]{1,0:T(8,128)} fusion(bf16[2048,256]{0,1:T(8,128)(2,1)S(1)} %collective-permute-done.2, bf16[2048,256]{0,1:T(8,128)(2,1)S(1)} %collective-permute-done.1, bf16[2048,256]{0,1:T(8,128)(2,1)S(1)} %collective-permute-done, bf16[2048,256]{0,1:T(8,128)(2,1)S(1)} %get-tuple-element.56, bf16[8192,1024]{1,0:T(8,128)(2,1)} %param.5), kind=kOutput, calls=%fused_computation.27 | convolution fusion | flops 4315938816 | bytes 12582912 | tf_op jit(solution)/shard_map/dot_general | solution.py:82
  228.7 10.9 %add_add_fusion = f32[1024,1024]{1,0:T(8,128)} fusion(f32[1024,1024]{1,0:T(8,128)} %fusion.14, f32[1024,1024]{1,0:T(8,128)S(1)} %fusion, f32[1024,1024]{1,0:T(8,128)S(1)} %fusion.7, bf16[8192,1024]{1,0:T(8,128)(2,1)} %param.5, bf16[2048,256]{0,1:T(8,128)(2,1)} %collective-permute-done.11, bf16[2048,256]{0,1:T(8,128)(2,1)} %collective-permute-done.10, ...), kind=kOutput, calls=%fused_computation.46 | convolution fusion | flops 4319084544 | bytes 25165824 | tf_op jit(solution)/shard_map/dot_general | solution.py:82
  239.6 6.0 %reshape.97 = f32[4,4,4,16,4,256]{5,4,3,2,1,0:T(4,128)} reshape(f32[1024,1024]{1,0:T(8,128)} %add_add_fusion) | data formatting | bytes 8388608 | tf_op jit(solution)/shard_map/reshape | solution.py:100
  245.6 5.3 %select_reduce_fusion.1 = f32[4,4,4,16,256]{4,3,2,1,0:T(8,128)S(1)} fusion(f32[4,4,4,16,4,256]{5,4,3,2,1,0:T(4,128)} %reshape.97, pred[4,4]{1,0:T(4,128)(4,1)S(1)} %copy.35), kind=kLoop, calls=%fused_computation.45 | loop fusion | flops 1835008 | bytes 5242896 | tf_op jit(solution)/shard_map/reduce_sum | solution.py:101
  257.0 9.2 %convolution_convert_fusion = bf16[2048,1024]{1,0:T(8,128)(2,1)} fusion(bf16[1024,1024]{1,0:T(8,128)(2,1)} %bitcast.95, bf16[2048,256]{0,1:T(8,128)(2,1)} %collective-permute-done.17, bf16[2048,256]{0,1:T(8,128)(2,1)} %collective-permute-done.15, bf16[2048,256]{0,1:T(8,128)(2,1)} %collective-permute-done.13, bf16[2048,256]{0,1:T(8,128)(2,1)S(1)} %copy-done.20), kind=kOutput, calls=%fused_computation.53 | convolution fusion | flops 4313841664 | bytes 10485760 | tf_op jit(solution)/shard_map/dot_general | solution.py:91
  266.2 9.7 %fusion.51 = f32[1024,1024]{0,1:T(8,128)} fusion(bf16[8192,1024]{1,0:T(8,128)(2,1)} %param.4, bf16[2048,256]{0,1:T(8,128)(2,1)} %collective-permute-done.17, bf16[2048,256]{0,1:T(8,128)(2,1)} %collective-permute-done.15, bf16[2048,256]{0,1:T(8,128)(2,1)} %collective-permute-done.13, bf16[2048,256]{0,1:T(8,128)(2,1)S(1)} %copy-done.20), kind=kOutput, calls=%fused_computation.76 | convolution fusion | flops 4311744512 | bytes 12582912 | tf_op jit(solution)/shard_map/dot_general | solution.py:92
  279.1 22.8 %collective-permute-done.6 = bf16[2048,256]{0,1:T(8,128)(2,1)} collective-permute-done((bf16[2048,256]{0,1:T(8,128)(2,1)}, bf16[2048,256]{0,1:T(8,128)(2,1)}, u32[]{:S(2)}, u32[]{:S(2)}) %collective-permute-start.6) | collective-permute-done | bytes 1048608 | tf_op jit(solution)/shard_map/ppermute | solution.py:37
  302.0 9.7 %fusion.48 = f32[1024,1024]{0,1:T(8,128)} fusion(bf16[8192,1024]{1,0:T(8,128)(2,1)} %param.4, bf16[2048,256]{0,1:T(8,128)(2,1)} %collective-permute-done.8, bf16[2048,256]{0,1:T(8,128)(2,1)} %collective-permute-done.6, bf16[2048,256]{0,1:T(8,128)(2,1)S(1)} %collective-permute-done.4, bf16[2048,256]{0,1:T(8,128)(2,1)S(1)} %copy-done.21), kind=kOutput, calls=%fused_computation.75 | convolution fusion | flops 4311744512 | bytes 12582912 | tf_op jit(solution)/shard_map/dot_general | solution.py:92
  311.6 8.1 %convolution_convert_fusion.1 = bf16[2048,1024]{1,0:T(8,128)(2,1)} fusion(bf16[1024,1024]{1,0:T(8,128)(2,1)S(1)} %bitcast.97, bf16[2048,256]{0,1:T(8,128)(2,1)} %collective-permute-done.8, bf16[2048,256]{0,1:T(8,128)(2,1)} %collective-permute-done.6, bf16[2048,256]{0,1:T(8,128)(2,1)S(1)} %collective-permute-done.4, bf16[2048,256]{0,1:T(8,128)(2,1)S(1)} %copy-done.21), kind=kOutput, calls=%fused_computation.54 | convolution fusion | flops 4313841664 | bytes 10485760 | tf_op jit(solution)/shard_map/dot_general | solution.py:91
  321.5 6.6 %broadcast_in_dim.150 = bf16[8192,1024]{1,0:T(8,128)(2,1)} broadcast(bf16[]{:T(256)} %constant.53.clone.1), dimensions={} | broadcast | bytes 16777218 | tf_op jit(solution)/shard_map/broadcast_in_dim | solution.py:69
  330.6 4.7 %constant_dynamic-update-slice_fusion.8 = bf16[8192,1024]{1,0:T(8,128)(2,1)} fusion(bf16[8192,1024]{1,0:T(8,128)(2,1)} %constant_dynamic-update-slice_fusion.9, bf16[2048,1024]{1,0:T(8,128)(2,1)} %convolution_convert_fusion, s32[]{:T(128)S(6)} %select_n.183), kind=kLoop, calls=%fused_computation.141 | loop fusion | bytes 8388612 | tf_op jit(solution)/shard_map/dynamic_update_slice | solution.py:88
  348.2 20.8 %collective-permute-done.20 = bf16[2048,256]{0,1:T(8,128)(2,1)} collective-permute-done((bf16[2048,256]{0,1:T(8,128)(2,1)}, bf16[2048,256]{0,1:T(8,128)(2,1)}, u32[]{:S(2)}, u32[]{:S(2)}) %collective-permute-start.20) | collective-permute-done | bytes 1048608 | tf_op jit(solution)/shard_map/ppermute | solution.py:37
  370.4 7.8 %fusion.45 = f32[1024,1024]{1,0:T(8,128)S(1)} fusion(bf16[2048,1024]{0,1:T(8,128)(2,1)S(1)} %constant_dynamic-update-slice_fusion, bf16[8192,1024]{1,0:T(8,128)(2,1)} %param.4), kind=kOutput, calls=%fused_computation.72 | convolution fusion | flops 4294967296 | bytes 12582912 | tf_op jit(solution)/shard_map/dot_general | solution.py:92
  378.2 13.2 %collective-permute-done.23 = bf16[2048,256]{0,1:T(8,128)(2,1)S(1)} collective-permute-done((bf16[2048,256]{0,1:T(8,128)(2,1)}, bf16[2048,256]{0,1:T(8,128)(2,1)S(1)}, u32[]{:S(2)}, u32[]{:S(2)}) %collective-permute-start.23) | collective-permute-done | bytes 1048608 | tf_op jit(solution)/shard_map/ppermute | solution.py:37
  393.4 8.5 %bitcast_add_fusion = f32[1024,1024]{0,1:T(8,128)} fusion(f32[1024,1024]{1,0:T(8,128)S(1)} %fusion.45, f32[1024,1024]{0,1:T(8,128)S(1)} %copy-done.31, f32[1024,1024]{0,1:T(8,128)S(1)} %copy-done.30, bf16[2048,1024]{0,1:T(8,128)(2,1)S(1)} %constant_dynamic-update-slice_fusion.4, bf16[8192,1024]{1,0:T(8,128)(2,1)} %param.4), kind=kOutput, calls=%fused_computation.42 | convolution fusion | flops 4298113024 | bytes 25165824 | tf_op jit(solution)/shard_map/dot_general | solution.py:92
  401.9 5.7 %reshape.98 = f32[4,256,4,4,4,16]{1,0,5,4,3,2:T(4,128)} reshape(f32[1024,1024]{0,1:T(8,128)} %bitcast_add_fusion) | data formatting | bytes 8388608 | tf_op jit(solution)/shard_map/reshape | solution.py:106
  424.3 9.6 %convert_dynamic-update-slice_fusion.1 = bf16[8192,1024]{1,0:T(8,128)(2,1)} fusion(bf16[8192,1024]{1,0:T(8,128)(2,1)} %constant_dynamic-update-slice_fusion.8, bf16[2048,1024]{0,1:T(8,128)(2,1)} %copy-done.23, bf16[1024,1024]{1,0:T(8,128)(2,1)} %bitcast.96), kind=kOutput, calls=%fused_computation.48 | convolution fusion | flops 4297064448 | bytes 10485760 | tf_op jit(solution)/shard_map/dot_general | solution.py:91
  433.9 6.2 %convert_dynamic-update-slice_fusion = bf16[8192,1024]{1,0:T(8,128)(2,1)} fusion(bf16[8192,1024]{1,0:T(8,128)(2,1)} %convert_dynamic-update-slice_fusion.1, bf16[2048,1024]{0,1:T(8,128)(2,1)S(1)} %copy-done.26, bf16[1024,1024]{1,0:T(8,128)(2,1)S(1)} %bitcast.98), kind=kOutput, calls=%fused_computation.47 | convolution fusion | flops 4297064448 | bytes 10485760 | tf_op jit(solution)/shard_map/dot_general | solution.py:91
  (177 shorter events, 99.9 us)
Async XLA Ops:
  7.2 330.3 %all-reduce.3.cloned.1.call-start = ((), (), s32[]{:S(2)}) async-start(), calls=%async_computation | async-start | bytes 2097152
  24.3 71.5 %collective-permute-start.12 = (bf16[2048,256]{0,1:T(8,128)(2,1)}, bf16[2048,256]{0,1:T(8,128)(2,1)}, u32[]{:S(2)}, u32[]{:S(2)}) collective-permute-start(bf16[2048,256]{0,1:T(8,128)(2,1)} %get-tuple-element.61), channel_id=1, source_target_pairs={{0,4},{4,0},{8,12},{12,8},{1,5},{5,1},{9,13},{13,9},{2,6},{6,2},{1... | collective-permute-start | bytes 3145736 | tf_op jit(solution)/shard_map/ppermute | solution.py:37
  24.8 71.8 %collective-permute-start.16 = (bf16[2048,256]{0,1:T(8,128)(2,1)}, bf16[2048,256]{0,1:T(8,128)(2,1)}, u32[]{:S(2)}, u32[]{:S(2)}) collective-permute-start(bf16[2048,256]{0,1:T(8,128)(2,1)} %get-tuple-element.62), channel_id=1, source_target_pairs={{0,12},{4,8},{8,4},{12,0},{1,13},{5,9},{9,5},{13,1},{2,14},{6,10},... | collective-permute-start | bytes 3145736 | tf_op jit(solution)/shard_map/ppermute | solution.py:37
  27.4 70.0 %collective-permute-start.14 = (bf16[2048,256]{0,1:T(8,128)(2,1)}, bf16[2048,256]{0,1:T(8,128)(2,1)}, u32[]{:S(2)}, u32[]{:S(2)}) collective-permute-start(bf16[2048,256]{0,1:T(8,128)(2,1)} %get-tuple-element.63), channel_id=1, source_target_pairs={{0,8},{4,12},{8,0},{12,4},{1,9},{5,13},{9,1},{13,5},{2,10},{6,14},... | collective-permute-start | bytes 3145736 | tf_op jit(solution)/shard_map/ppermute | solution.py:37
  39.1 183.5 %collective-permute-start.11 = (bf16[2048,256]{0,1:T(8,128)(2,1)}, bf16[2048,256]{0,1:T(8,128)(2,1)}, u32[]{:S(2)}, u32[]{:S(2)}) collective-permute-start(bf16[2048,256]{0,1:T(8,128)(2,1)} %get-tuple-element.64), channel_id=1, source_target_pairs={{0,12},{4,8},{8,4},{12,0},{1,13},{5,9},{9,5},{13,1},{2,14},{6,10},... | collective-permute-start | bytes 3145736 | tf_op jit(solution)/shard_map/ppermute | solution.py:37
  39.5 183.3 %collective-permute-start.10 = (bf16[2048,256]{0,1:T(8,128)(2,1)}, bf16[2048,256]{0,1:T(8,128)(2,1)}, u32[]{:S(2)}, u32[]{:S(2)}) collective-permute-start(bf16[2048,256]{0,1:T(8,128)(2,1)} %get-tuple-element.65), channel_id=1, source_target_pairs={{0,8},{4,12},{8,0},{12,4},{1,9},{5,13},{9,1},{13,5},{2,10},{6,14},... | collective-permute-start | bytes 3145736 | tf_op jit(solution)/shard_map/ppermute | solution.py:37
  47.9 34.8 %copy-start.6 = (bf16[2048,1024]{0,1:T(8,128)(2,1)}, bf16[2048,1024]{0,1:T(8,128)(2,1)S(1)}, u32[]{:S(2)}) copy-start(bf16[2048,1024]{0,1:T(8,128)(2,1)S(1)} %convert_bitcast_fusion.2) | copy-start | bytes 12582916
  95.9 14.6 %collective-permute-start.3 = (bf16[2048,256]{0,1:T(8,128)(2,1)S(1)}, bf16[2048,256]{0,1:T(8,128)(2,1)S(1)}, u32[]{:S(2)}, u32[]{:S(2)}) collective-permute-start(bf16[2048,256]{0,1:T(8,128)(2,1)S(1)} %copy-done.19), channel_id=1, source_target_pairs={{0,4},{4,0},{8,12},{12,8},{1,5},{5,1},{9,13},{13,9},{2,6},{6,2},{1... | collective-permute-start | bytes 3145736 | tf_op jit(solution)/shard_map/ppermute | solution.py:37
  96.6 44.4 %collective-permute-start.7 = (bf16[2048,256]{0,1:T(8,128)(2,1)S(1)}, bf16[2048,256]{0,1:T(8,128)(2,1)S(1)}, u32[]{:S(2)}, u32[]{:S(2)}) collective-permute-start(bf16[2048,256]{0,1:T(8,128)(2,1)S(1)} %copy-done.18), channel_id=1, source_target_pairs={{0,12},{4,8},{8,4},{12,0},{1,13},{5,9},{9,5},{13,1},{2,14},{6,10},... | collective-permute-start | bytes 3145736 | tf_op jit(solution)/shard_map/ppermute | solution.py:37
  97.4 66.4 %collective-permute-start.5 = (bf16[2048,256]{0,1:T(8,128)(2,1)S(1)}, bf16[2048,256]{0,1:T(8,128)(2,1)S(1)}, u32[]{:S(2)}, u32[]{:S(2)}) collective-permute-start(bf16[2048,256]{0,1:T(8,128)(2,1)S(1)} %copy-done.17), channel_id=1, source_target_pairs={{0,8},{4,12},{8,0},{12,4},{1,9},{5,13},{9,1},{13,5},{2,10},{6,14},... | collective-permute-start | bytes 3145736 | tf_op jit(solution)/shard_map/ppermute | solution.py:37
  102.7 38.3 %copy-start.15 = (bf16[2048,256]{0,1:T(8,128)(2,1)S(1)}, bf16[2048,256]{0,1:T(8,128)(2,1)}, u32[]{:S(2)}) copy-start(bf16[2048,256]{0,1:T(8,128)(2,1)} %get-tuple-element.71) | copy-start | bytes 3145732
  102.7 61.1 %copy-start.1 = (bf16[2048,1024]{0,1:T(8,128)(2,1)S(1)}, bf16[2048,1024]{0,1:T(8,128)(2,1)}, u32[]{:S(2)}) copy-start(bf16[2048,1024]{0,1:T(8,128)(2,1)} %convolution_bitcast_fusion.2) | copy-start | bytes 12582916
  110.5 75.4 %collective-permute-start.2 = (bf16[2048,256]{0,1:T(8,128)(2,1)S(1)}, bf16[2048,256]{0,1:T(8,128)(2,1)S(1)}, u32[]{:S(2)}, u32[]{:S(2)}) collective-permute-start(bf16[2048,256]{0,1:T(8,128)(2,1)S(1)} %copy-done.16), channel_id=1, source_target_pairs={{0,12},{4,8},{8,4},{12,0},{1,13},{5,9},{9,5},{13,1},{2,14},{6,10},... | collective-permute-start | bytes 3145736 | tf_op jit(solution)/shard_map/ppermute | solution.py:37
  141.0 67.6 %collective-permute-start.1 = (bf16[2048,256]{0,1:T(8,128)(2,1)S(1)}, bf16[2048,256]{0,1:T(8,128)(2,1)S(1)}, u32[]{:S(2)}, u32[]{:S(2)}) collective-permute-start(bf16[2048,256]{0,1:T(8,128)(2,1)S(1)} %copy-done.15), channel_id=1, source_target_pairs={{0,8},{4,12},{8,0},{12,4},{1,9},{5,13},{9,1},{13,5},{2,10},{6,14},... | collective-permute-start | bytes 3145736 | tf_op jit(solution)/shard_map/ppermute | solution.py:37
  163.8 45.5 %collective-permute-start = (bf16[2048,256]{0,1:T(8,128)(2,1)S(1)}, bf16[2048,256]{0,1:T(8,128)(2,1)S(1)}, u32[]{:S(2)}, u32[]{:S(2)}) collective-permute-start(bf16[2048,256]{0,1:T(8,128)(2,1)S(1)} %get-tuple-element.72), channel_id=1, source_target_pairs={{0,4},{4,0},{8,12},{12,8},{1,5},{5,1},{9,13},{13,9},{2,6},{6,2},{1... | collective-permute-start | bytes 3145736 | tf_op jit(solution)/shard_map/ppermute | solution.py:37
  185.9 38.2 %collective-permute-start.9 = (bf16[2048,256]{0,1:T(8,128)(2,1)S(1)}, bf16[2048,256]{0,1:T(8,128)(2,1)S(1)}, u32[]{:S(2)}, u32[]{:S(2)}) collective-permute-start(bf16[2048,256]{0,1:T(8,128)(2,1)S(1)} %copy-done.14), channel_id=1, source_target_pairs={{0,4},{4,0},{8,12},{12,8},{1,5},{5,1},{9,13},{13,9},{2,6},{6,2},{1... | collective-permute-start | bytes 3145736 | tf_op jit(solution)/shard_map/ppermute | solution.py:37
  208.6 44.8 %collective-permute-start.17 = (bf16[2048,256]{0,1:T(8,128)(2,1)}, bf16[2048,256]{0,1:T(8,128)(2,1)}, u32[]{:S(2)}, u32[]{:S(2)}) collective-permute-start(bf16[2048,256]{0,1:T(8,128)(2,1)} %get-tuple-element.48), channel_id=1, source_target_pairs={{0,12},{4,8},{8,4},{12,0},{1,13},{5,9},{9,5},{13,1},{2,14},{6,10},... | collective-permute-start | bytes 3145736 | tf_op jit(solution)/shard_map/ppermute | solution.py:37
  209.3 47.7 %collective-permute-start.15 = (bf16[2048,256]{0,1:T(8,128)(2,1)}, bf16[2048,256]{0,1:T(8,128)(2,1)}, u32[]{:S(2)}, u32[]{:S(2)}) collective-permute-start(bf16[2048,256]{0,1:T(8,128)(2,1)} %get-tuple-element.49), channel_id=1, source_target_pairs={{0,8},{4,12},{8,0},{12,4},{1,9},{5,13},{9,1},{13,5},{2,10},{6,14},... | collective-permute-start | bytes 3145736 | tf_op jit(solution)/shard_map/ppermute | solution.py:37
  222.6 34.4 %collective-permute-start.13 = (bf16[2048,256]{0,1:T(8,128)(2,1)}, bf16[2048,256]{0,1:T(8,128)(2,1)}, u32[]{:S(2)}, u32[]{:S(2)}) collective-permute-start(bf16[2048,256]{0,1:T(8,128)(2,1)} %get-tuple-element.50), channel_id=1, source_target_pairs={{0,4},{4,0},{8,12},{12,8},{1,5},{5,1},{9,13},{13,9},{2,6},{6,2},{1... | collective-permute-start | bytes 3145736 | tf_op jit(solution)/shard_map/ppermute | solution.py:37
  222.8 56.3 %collective-permute-start.8 = (bf16[2048,256]{0,1:T(8,128)(2,1)}, bf16[2048,256]{0,1:T(8,128)(2,1)}, u32[]{:S(2)}, u32[]{:S(2)}) collective-permute-start(bf16[2048,256]{0,1:T(8,128)(2,1)} %get-tuple-element.53), channel_id=1, source_target_pairs={{0,12},{4,8},{8,4},{12,0},{1,13},{5,9},{9,5},{13,1},{2,14},{6,10},... | collective-permute-start | bytes 3145736 | tf_op jit(solution)/shard_map/ppermute | solution.py:37
  224.1 77.9 %collective-permute-start.6 = (bf16[2048,256]{0,1:T(8,128)(2,1)}, bf16[2048,256]{0,1:T(8,128)(2,1)}, u32[]{:S(2)}, u32[]{:S(2)}) collective-permute-start(bf16[2048,256]{0,1:T(8,128)(2,1)} %get-tuple-element.54), channel_id=1, source_target_pairs={{0,8},{4,12},{8,0},{12,4},{1,9},{5,13},{9,1},{13,5},{2,10},{6,14},... | collective-permute-start | bytes 3145736 | tf_op jit(solution)/shard_map/ppermute | solution.py:37
  253.4 48.5 %collective-permute-start.4 = (bf16[2048,256]{0,1:T(8,128)(2,1)}, bf16[2048,256]{0,1:T(8,128)(2,1)S(1)}, u32[]{:S(2)}, u32[]{:S(2)}) collective-permute-start(bf16[2048,256]{0,1:T(8,128)(2,1)} %get-tuple-element.55), channel_id=1, source_target_pairs={{0,4},{4,0},{8,12},{12,8},{1,5},{5,1},{9,13},{13,9},{2,6},{6,2},{1... | collective-permute-start | bytes 3145736 | tf_op jit(solution)/shard_map/ppermute | solution.py:37
  266.2 35.8 %copy-start.21 = (bf16[2048,256]{0,1:T(8,128)(2,1)S(1)}, bf16[2048,256]{0,1:T(8,128)(2,1)}, u32[]{:S(2)}) copy-start(bf16[2048,256]{0,1:T(8,128)(2,1)} %get-tuple-element.52) | copy-start | bytes 3145732
  276.0 62.6 %collective-permute-start.21 = (bf16[2048,256]{0,1:T(8,128)(2,1)}, bf16[2048,256]{0,1:T(8,128)(2,1)S(1)}, u32[]{:S(2)}, u32[]{:S(2)}) collective-permute-start(bf16[2048,256]{0,1:T(8,128)(2,1)} %get-tuple-element.28), channel_id=1, source_target_pairs={{0,4},{4,0},{8,12},{12,8},{1,5},{5,1},{9,13},{13,9},{2,6},{6,2},{1... | collective-permute-start | bytes 3145736 | tf_op jit(solution)/shard_map/ppermute | solution.py:37
  276.0 65.1 %collective-permute-start.22 = (bf16[2048,256]{0,1:T(8,128)(2,1)}, bf16[2048,256]{0,1:T(8,128)(2,1)S(1)}, u32[]{:S(2)}, u32[]{:S(2)}) collective-permute-start(bf16[2048,256]{0,1:T(8,128)(2,1)} %get-tuple-element.29), channel_id=1, source_target_pairs={{0,8},{4,12},{8,0},{12,4},{1,9},{5,13},{9,1},{13,5},{2,10},{6,14},... | collective-permute-start | bytes 3145736 | tf_op jit(solution)/shard_map/ppermute | solution.py:37
  319.7 22.4 %collective-permute-start.18 = (bf16[2048,256]{0,1:T(8,128)(2,1)}, bf16[2048,256]{0,1:T(8,128)(2,1)}, u32[]{:S(2)}, u32[]{:S(2)}) collective-permute-start(bf16[2048,256]{0,1:T(8,128)(2,1)} %get-tuple-element.24), channel_id=1, source_target_pairs={{0,4},{4,0},{8,12},{12,8},{1,5},{5,1},{9,13},{13,9},{2,6},{6,2},{1... | collective-permute-start | bytes 3145736 | tf_op jit(solution)/shard_map/ppermute | solution.py:37
  319.7 27.2 %collective-permute-start.19 = (bf16[2048,256]{0,1:T(8,128)(2,1)}, bf16[2048,256]{0,1:T(8,128)(2,1)}, u32[]{:S(2)}, u32[]{:S(2)}) collective-permute-start(bf16[2048,256]{0,1:T(8,128)(2,1)} %get-tuple-element.25), channel_id=1, source_target_pairs={{0,8},{4,12},{8,0},{12,4},{1,9},{5,13},{9,1},{13,5},{2,10},{6,14},... | collective-permute-start | bytes 3145736 | tf_op jit(solution)/shard_map/ppermute | solution.py:37
  321.2 47.8 %collective-permute-start.20 = (bf16[2048,256]{0,1:T(8,128)(2,1)}, bf16[2048,256]{0,1:T(8,128)(2,1)}, u32[]{:S(2)}, u32[]{:S(2)}) collective-permute-start(bf16[2048,256]{0,1:T(8,128)(2,1)} %get-tuple-element.26), channel_id=1, source_target_pairs={{0,12},{4,8},{8,4},{12,0},{1,13},{5,9},{9,5},{13,1},{2,14},{6,10},... | collective-permute-start | bytes 3145736 | tf_op jit(solution)/shard_map/ppermute | solution.py:37
  338.6 52.8 %collective-permute-start.23 = (bf16[2048,256]{0,1:T(8,128)(2,1)}, bf16[2048,256]{0,1:T(8,128)(2,1)S(1)}, u32[]{:S(2)}, u32[]{:S(2)}) collective-permute-start(bf16[2048,256]{0,1:T(8,128)(2,1)} %get-tuple-element.30), channel_id=1, source_target_pairs={{0,12},{4,8},{8,4},{12,0},{1,13},{5,9},{9,5},{13,1},{2,14},{6,10},... | collective-permute-start | bytes 3145736 | tf_op jit(solution)/shard_map/ppermute | solution.py:37
  419.7 21.4 %collective-permute-start.24 = (f32[64,4,256]{2,0,1:T(8,128)S(1)}, f32[64,4,256]{2,0,1:T(8,128)S(1)}, u32[]{:S(2)}, u32[]{:S(2)}) collective-permute-start(f32[64,4,256]{2,0,1:T(8,128)S(1)} %bitcast.110), channel_id=1, source_target_pairs={{0,1},{1,0},{2,3},{3,2},{4,5},{5,4},{6,7},{7,6},{8,9},{9,8},{10,11... | collective-permute-start | bytes 786440 | tf_op jit(solution)/shard_map/ppermute | solution.py:48
  421.7 21.3 %collective-permute-start.25 = (f32[64,4,256]{2,0,1:T(8,128)S(1)}, f32[64,4,256]{2,0,1:T(8,128)S(1)}, u32[]{:S(2)}, u32[]{:S(2)}) collective-permute-start(f32[64,4,256]{2,0,1:T(8,128)S(1)} %bitcast.109), channel_id=1, source_target_pairs={{0,2},{1,3},{2,0},{3,1},{4,6},{5,7},{6,4},{7,5},{8,10},{9,11},{10,... | collective-permute-start | bytes 786440 | tf_op jit(solution)/shard_map/ppermute | solution.py:48
  424.3 18.7 %collective-permute-start.26 = (f32[64,4,256]{2,0,1:T(8,128)S(1)}, f32[64,4,256]{2,0,1:T(8,128)S(1)}, u32[]{:S(2)}, u32[]{:S(2)}) collective-permute-start(f32[64,4,256]{2,0,1:T(8,128)S(1)} %bitcast.108), channel_id=1, source_target_pairs={{0,3},{1,2},{2,1},{3,0},{4,7},{5,6},{6,5},{7,4},{8,11},{9,10},{10,... | collective-permute-start | bytes 786440 | tf_op jit(solution)/shard_map/ppermute | solution.py:48
  (32 other events, 356.3 us)
Sparse Core Ops, SparseCore 0:
  253.5 52.9 all-reduce.2

commit v8 on v7

--- a/solution.py
+++ b/solution.py
@@ -6,7 +6,7 @@
 from jax.sharding import PartitionSpec as P
 
 NB = 16
-CHUNKS = 4
+SIZES = (2, 2, 2, 1, 1)
 
 
 def expanded_weights(w_first, w_second, n_dev, order):
@@ -61,16 +61,18 @@
     idx = lax.axis_index("tensor")
     order = jnp.bitwise_xor(idx, jnp.arange(n_dev, dtype=idx.dtype))
     w1p, w2p, w1tp = expanded_weights(w_first, w_second, n_dev, order)
-    step = tok_rows // CHUNKS
+    unit = tok_rows // sum(SIZES)
+    offsets = [unit * sum(SIZES[:k]) for k in range(len(SIZES) + 1)]
 
     eye = jnp.eye(blk_local, dtype=jnp.bool_)
     gf_acc = None
     gs_acc = None
     grad_tokens = jnp.zeros((tok_rows, feat), jnp.bfloat16)
     pending = []
-    for k in range(CHUNKS):
-        x = tokens[k * step:(k + 1) * step]
-        cot = cotangent[k * step:(k + 1) * step]
+    last = len(SIZES) - 1
+    for k in range(len(SIZES)):
+        x = tokens[offsets[k]:offsets[k + 1]]
+        cot = cotangent[offsets[k]:offsets[k + 1]]
         hidden = jnp.dot(x, w1p, preferred_element_type=jnp.float32).astype(jnp.bfloat16)
         backed = jnp.dot(cot, w2p, preferred_element_type=jnp.float32)
         moved = exchange([hidden[:, m * part:(m + 1) * part] for m in range(n_dev)], n_dev)
@@ -89,13 +91,25 @@
             gf_acc = done[1] if gf_acc is None else gf_acc + done[1]
         returned = jnp.concatenate(exchange(masked, n_dev), axis=1)
         gt = jnp.dot(returned, w1tp, preferred_element_type=jnp.float32).astype(jnp.bfloat16)
-        gf = lax.dot_general(
-            x, returned, (((0,), (0,)), ((), ())), preferred_element_type=jnp.float32
-        )
-        pending.append((gt, gf, k * step))
+        if k < last:
+            gf = lax.dot_general(
+                x, returned, (((0,), (0,)), ((), ())), preferred_element_type=jnp.float32
+            )
+        else:
+            gf = jnp.einsum(
+                "tmcbq,tbi->bimcq",
+                returned.reshape(-1, n_dev, blk_local, blk_local, sub),
+                x.reshape(-1, blk_local, bs),
+                preferred_element_type=jnp.float32,
+            )
+        pending.append((gt, gf, offsets[k]))
+    gf_last = None
     for gt, gf, at in pending:
         grad_tokens = lax.dynamic_update_slice(grad_tokens, gt, (at, 0))
-        gf_acc = gf if gf_acc is None else gf_acc + gf
+        if at == offsets[last]:
+            gf_last = gf
+        else:
+            gf_acc = gf if gf_acc is None else gf_acc + gf
 
     gs6 = gs_acc.reshape(n_dev, blk_local, blk_local, sub, blk_local, bs)
     gsd = jnp.sum(jnp.where(eye[None, :, None, None, :, None], gs6, 0.0), axis=4)
@@ -105,7 +119,7 @@
     gf_acc, grad_second = lax.optimization_barrier((gf_acc, grad_second))
     gf6 = gf_acc.reshape(blk_local, bs, n_dev, blk_local, blk_local, sub)
     gfd = jnp.sum(jnp.where(eye[:, None, None, None, :, None], gf6, 0.0), axis=4)
-    gfd = jnp.take(gfd, order, axis=2)
+    gfd = jnp.take(gfd + gf_last, order, axis=2)
     first_term = gfd.transpose(1, 0, 2, 3, 4).reshape(bs, blk_local, bs) * grad_scale
     grad_first = dp_reduce_scatter(first_term)
     return (grad_tokens, grad_first.transpose(1, 0, 2), grad_second.transpose(1, 0, 2))

time: 457 us -> 517 us (1.13)
  waiting for transfers between devices: 153 us -> 202 us
    ppermute x24 -> x30, waiting for transfers between devices: 151 us -> 190 us  [exchange(): lax.ppermute(pieces[m], 'tensor', [(i, i ^ m) for i in range(n_dev)])]
    ppermute x3, waiting for transfers between devices: 1.85 us -> 11.9 us  [dp_reduce_scatter(): acc = acc + lax.ppermute(send, 'dp', [(i, i ^ m) for i in range(n)])]
    dot_general x4 -> x5, matrix products: 31 us -> 40.3 us  [shards(): backed = jnp.dot(cot, w2p, preferred_element_type=jnp.float32)]
    dot_general x4 -> x5, matrix products: 30.9 us -> 23.7 us  [shards(): jnp.dot(x, w1p, preferred_element_type=jnp.float32).astype(jnp.bfloat16)]
    slice x4 -> x5, other arithmetic: 15.5 us -> 19.1 us  [shards(): hidden[:, m * part:(m + 1) * part]]
    unnamed x84 -> x128, local copies, waits for them, and re-layouts: 16.2 us -> 19.7 us
    ppermute x24 -> x30, starting transfers between devices: 18.2 us -> 20.7 us  [exchange(): lax.ppermute(pieces[m], 'tensor', [(i, i ^ m) for i in range(n_dev)])]
    dot_general x4 -> x5, matrix products: 34.3 us -> 32.1 us  [shards(): lax.dot_general(active, cot, (((0,), (0,)), ((), ())), preferred_element_...]
  transfers between devices with their start and end apart: 28 -> 34, of which waited for: 11 -> 16; matrix products, arithmetic and copies ran while one was open for 47% -> 44% of each run, Pallas kernels for 0% -> 0%
where the time goes in v8:
time: 517 us; the launch traced here: 508 us
  waiting for transfers between devices  202 us (39%)
  matrix products  161 us (31%)
  local copies, waits for them, and re-layouts  71.1 us (14%)
  other arithmetic  32.2 us (6%)
  starting transfers between devices  25.5 us (5%)
  between operations  15.8 us (3%)
    ppermute x30, waiting for transfers between devices, exchange(): lax.ppermute(pieces[m], 'tensor', [(i, i ^ m) for i in range(n_dev)])  190 us
    dot_general x5, matrix products, shards(): backed = jnp.dot(cot, w2p, preferred_element_type=jnp.float32)  40.3 us
    dot_general x5, matrix products, shards(): lax.dot_general(active, cot, (((0,), (0,)), ((), ())), preferred_element_...  32.1 us
    dot_general x5, matrix products, shards(): jnp.dot(returned, w1tp, preferred_element_type=jnp.float32)  31.5 us
    dot_general x4, matrix products, shards(): lax.dot_general(x, returned, (((0,), (0,)), ((), ())), preferred_element_...  30.6 us
    dot_general x5, matrix products, shards(): jnp.dot(x, w1p, preferred_element_type=jnp.float32).astype(jnp.bfloat16)  23.7 us
    ppermute x30, starting transfers between devices, exchange(): lax.ppermute(pieces[m], 'tensor', [(i, i ^ m) for i in range(n_dev)])  20.7 us
    unnamed x128, local copies, waits for them, and re-layouts  19.7 us
  transfers between devices with their start and end apart: 34, of which 16 were waited for; matrix products, arithmetic and copies ran while one was open for 44% of the time, Pallas kernels for 0%

profile of v8, /device:TPU:0, one launch (start us, length us, event | category | flops | bytes accessed | tf_op | source)
XLA Modules:
  0.0 507.7 jit_solution(10756607972870057295)
XLA Ops:
  28.7 6.7 %convert_bitcast_fusion = bf16[2048,1024]{0,1:T(8,128)(2,1)} fusion(bf16[1024,1024]{0,1:T(8,128)(2,1)S(1)} %bitcast.127, bf16[8192,1024]{1,0:T(8,128)(2,1)S(1)} %bitcast.111), kind=kOutput, calls=%fused_computation.37 | convolution fusion | flops 4297064448 | bytes 10485760 | tf_op jit(solution)/shard_map/dot_general | solution.py:76
  40.7 10.0 %convolution_bitcast_fusion = bf16[2048,1024]{0,1:T(8,128)(2,1)} fusion(bf16[1024,1024]{0,1:T(8,128)(2,1)S(1)} %bitcast.130, bf16[8192,1024]{1,0:T(8,128)(2,1)} %param.5), kind=kOutput, calls=%fused_computation.4 | convolution fusion | flops 4294967296 | bytes 10485760 | tf_op jit(solution)/shard_map/dot_general | solution.py:77
  50.7 8.4 %convolution_bitcast_fusion.1 = bf16[2048,1024]{0,1:T(8,128)(2,1)} fusion(bf16[1024,1024]{0,1:T(8,128)(2,1)S(1)} %bitcast.131, bf16[8192,1024]{1,0:T(8,128)(2,1)} %param.5), kind=kOutput, calls=%fused_computation.5 | convolution fusion | flops 4294967296 | bytes 10485760 | tf_op jit(solution)/shard_map/dot_general | solution.py:77
  69.5 10.9 %convolution_bitcast_fusion.2 = bf16[2048,1024]{0,1:T(8,128)(2,1)} fusion(bf16[1024,1024]{0,1:T(8,128)(2,1)} %bitcast.133, bf16[8192,1024]{1,0:T(8,128)(2,1)} %param.5), kind=kOutput, calls=%fused_computation.6 | convolution fusion | flops 4294967296 | bytes 10485760 | tf_op jit(solution)/shard_map/dot_general | solution.py:77
  80.4 5.5 %convolution_bitcast_fusion.3 = bf16[1024,1024]{0,1:T(8,128)(2,1)} fusion(bf16[1024,1024]{0,1:T(8,128)(2,1)S(1)} %bitcast.134, bf16[8192,1024]{1,0:T(8,128)(2,1)} %param.5), kind=kOutput, calls=%fused_computation.61 | convolution fusion | flops 2147483648 | bytes 6291456 | tf_op jit(solution)/shard_map/dot_general | solution.py:77
  115.6 13.3 %collective-permute-done.14 = bf16[2048,256]{0,1:T(8,128)(2,1)S(1)} collective-permute-done((bf16[2048,256]{0,1:T(8,128)(2,1)}, bf16[2048,256]{0,1:T(8,128)(2,1)S(1)}, u32[]{:S(2)}, u32[]{:S(2)}) %collective-permute-start.14) | collective-permute-done | bytes 1048608 | tf_op jit(solution)/shard_map/ppermute | solution.py:37
  128.9 21.9 %collective-permute-done.16 = bf16[2048,256]{0,1:T(8,128)(2,1)S(1)} collective-permute-done((bf16[2048,256]{0,1:T(8,128)(2,1)}, bf16[2048,256]{0,1:T(8,128)(2,1)S(1)}, u32[]{:S(2)}, u32[]{:S(2)}) %collective-permute-start.16) | collective-permute-done | bytes 1048608 | tf_op jit(solution)/shard_map/ppermute | solution.py:37
  155.0 7.1 %fusion.7 = f32[1024,1024]{1,0:T(8,128)S(1)} fusion(bf16[2048,256]{0,1:T(8,128)(2,1)S(1)} %collective-permute-done.16, bf16[2048,256]{0,1:T(8,128)(2,1)S(1)} %collective-permute-done.14, bf16[2048,256]{0,1:T(8,128)(2,1)S(1)} %collective-permute-done.12, bf16[2048,256]{0,1:T(8,128)(2,1)} %get-tuple-element.55, bf16[8192,1024]{1,0:T(8,128)(2,1)} %param.5), kind=kOutput, calls=%fused_computation.18 | convolution fusion | flops 4315938816 | bytes 12582912 | tf_op jit(solution)/shard_map/dot_general | solution.py:84
  163.6 10.2 %collective-permute-done.5 = bf16[2048,256]{0,1:T(8,128)(2,1)S(1)} collective-permute-done((bf16[2048,256]{0,1:T(8,128)(2,1)S(1)}, bf16[2048,256]{0,1:T(8,128)(2,1)S(1)}, u32[]{:S(2)}, u32[]{:S(2)}) %collective-permute-start.5) | collective-permute-done | bytes 1048608 | tf_op jit(solution)/shard_map/ppermute | solution.py:37
  173.8 21.9 %collective-permute-done.7 = bf16[2048,256]{0,1:T(8,128)(2,1)S(1)} collective-permute-done((bf16[2048,256]{0,1:T(8,128)(2,1)S(1)}, bf16[2048,256]{0,1:T(8,128)(2,1)S(1)}, u32[]{:S(2)}, u32[]{:S(2)}) %collective-permute-start.7) | collective-permute-done | bytes 1048608 | tf_op jit(solution)/shard_map/ppermute | solution.py:37
  200.2 7.2 %fusion = f32[1024,1024]{1,0:T(8,128)S(1)} fusion(bf16[2048,256]{0,1:T(8,128)(2,1)S(1)} %collective-permute-done.7, bf16[2048,256]{0,1:T(8,128)(2,1)} %copy-done.35, bf16[2048,256]{0,1:T(8,128)(2,1)S(1)} %collective-permute-done.3, bf16[2048,256]{0,1:T(8,128)(2,1)S(1)} %get-tuple-element.60, bf16[8192,1024]{1,0:T(8,128)(2,1)} %param.5), kind=kOutput, calls=%fused_computation.10 | convolution fusion | flops 4315938816 | bytes 12582912 | tf_op jit(solution)/shard_map/dot_general | solution.py:84
  208.8 10.0 %collective-permute-done.1 = bf16[2048,256]{0,1:T(8,128)(2,1)S(1)} collective-permute-done((bf16[2048,256]{0,1:T(8,128)(2,1)S(1)}, bf16[2048,256]{0,1:T(8,128)(2,1)S(1)}, u32[]{:S(2)}, u32[]{:S(2)}) %collective-permute-start.1) | collective-permute-done | bytes 1048608 | tf_op jit(solution)/shard_map/ppermute | solution.py:37
  218.8 21.9 %collective-permute-done.2 = bf16[2048,256]{0,1:T(8,128)(2,1)S(1)} collective-permute-done((bf16[2048,256]{0,1:T(8,128)(2,1)S(1)}, bf16[2048,256]{0,1:T(8,128)(2,1)S(1)}, u32[]{:S(2)}, u32[]{:S(2)}) %collective-permute-start.2) | collective-permute-done | bytes 1048608 | tf_op jit(solution)/shard_map/ppermute | solution.py:37
  244.2 6.8 %fusion.14 = f32[1024,1024]{1,0:T(8,128)S(1)} fusion(bf16[2048,256]{0,1:T(8,128)(2,1)S(1)} %collective-permute-done.2, bf16[2048,256]{0,1:T(8,128)(2,1)S(1)} %collective-permute-done.1, bf16[2048,256]{0,1:T(8,128)(2,1)S(1)} %collective-permute-done, bf16[2048,256]{0,1:T(8,128)(2,1)S(1)} %get-tuple-element.65, bf16[8192,1024]{1,0:T(8,128)(2,1)} %param.5), kind=kOutput, calls=%fused_computation.26 | convolution fusion | flops 4315938816 | bytes 12582912 | tf_op jit(solution)/shard_map/dot_general | solution.py:84
  251.0 6.5 %add_add_fusion = f32[1024,1024]{1,0:T(8,128)} fusion(f32[1024,1024]{1,0:T(8,128)S(1)} %fusion.57, f32[1024,1024]{1,0:T(8,128)S(1)} %fusion.14, f32[1024,1024]{1,0:T(8,128)S(1)} %fusion, f32[1024,1024]{1,0:T(8,128)S(1)} %fusion.7, bf16[8192,1024]{1,0:T(8,128)(2,1)} %param.5, bf16[1024,256]{0,1:T(8,128)(2,1)S(1)} %copy-done.25, ...), kind=kOutput, calls=%fused_computation.36 | convolution fusion | flops 2162163712 | bytes 25165824 | tf_op jit(solution)/shard_map/dot_general | solution.py:84
  257.4 5.8 %reshape.103 = f32[4,4,4,16,4,256]{5,4,3,2,1,0:T(4,128)} reshape(f32[1024,1024]{1,0:T(8,128)} %add_add_fusion) | data formatting | bytes 8388608 | tf_op jit(solution)/shard_map/reshape | solution.py:114
  273.0 12.7 %collective-permute-done.17 = bf16[2048,256]{0,1:T(8,128)(2,1)} collective-permute-done((bf16[2048,256]{0,1:T(8,128)(2,1)}, bf16[2048,256]{0,1:T(8,128)(2,1)}, u32[]{:S(2)}, u32[]{:S(2)}) %collective-permute-start.17) | collective-permute-done | bytes 1048608 | tf_op jit(solution)/shard_map/ppermute | solution.py:37
  285.7 9.4 %convolution_convert_fusion.1 = bf16[2048,1024]{1,0:T(8,128)(2,1)} fusion(bf16[1024,1024]{1,0:T(8,128)(2,1)} %bitcast.120, bf16[2048,256]{0,1:T(8,128)(2,1)} %collective-permute-done.17, bf16[2048,256]{0,1:T(8,128)(2,1)} %collective-permute-done.15, bf16[2048,256]{0,1:T(8,128)(2,1)} %collective-permute-done.13, bf16[2048,256]{0,1:T(8,128)(2,1)S(1)} %copy-done.33), kind=kOutput, calls=%fused_computation.41 | convolution fusion | flops 4313841664 | bytes 10485760 | tf_op jit(solution)/shard_map/dot_general | solution.py:93
  295.1 9.8 %fusion.42 = f32[1024,1024]{0,1:T(8,128)} fusion(bf16[8192,1024]{1,0:T(8,128)(2,1)} %param.4, bf16[2048,256]{0,1:T(8,128)(2,1)} %collective-permute-done.17, bf16[2048,256]{0,1:T(8,128)(2,1)} %collective-permute-done.15, bf16[2048,256]{0,1:T(8,128)(2,1)} %collective-permute-done.13, bf16[2048,256]{0,1:T(8,128)(2,1)S(1)} %copy-done.33), kind=kOutput, calls=%fused_computation.60 | convolution fusion | flops 4311744512 | bytes 12582912 | tf_op jit(solution)/shard_map/dot_general | solution.py:95
  308.6 21.9 %collective-permute-done.8 = bf16[2048,256]{0,1:T(8,128)(2,1)S(1)} collective-permute-done((bf16[2048,256]{0,1:T(8,128)(2,1)}, bf16[2048,256]{0,1:T(8,128)(2,1)S(1)}, u32[]{:S(2)}, u32[]{:S(2)}) %collective-permute-start.8) | collective-permute-done | bytes 1048608 | tf_op jit(solution)/shard_map/ppermute | solution.py:37
  330.6 6.7 %fusion.39 = f32[1024,1024]{0,1:T(8,128)} fusion(bf16[8192,1024]{1,0:T(8,128)(2,1)S(1)} %bitcast.113, bf16[2048,256]{0,1:T(8,128)(2,1)S(1)} %collective-permute-done.8, bf16[2048,256]{0,1:T(8,128)(2,1)S(1)} %collective-permute-done.6, bf16[2048,256]{0,1:T(8,128)(2,1)S(1)} %collective-permute-done.4, bf16[2048,256]{0,1:T(8,128)(2,1)S(1)} %copy-done.34), kind=kOutput, calls=%fused_computation.59 | convolution fusion | flops 4311744512 | bytes 12582912 | tf_op jit(solution)/shard_map/dot_general | solution.py:95
  337.4 6.2 %convolution_convert_fusion.2 = bf16[2048,1024]{1,0:T(8,128)(2,1)} fusion(bf16[1024,1024]{1,0:T(8,128)(2,1)S(1)} %bitcast.122, bf16[2048,256]{0,1:T(8,128)(2,1)S(1)} %collective-permute-done.8, bf16[2048,256]{0,1:T(8,128)(2,1)S(1)} %collective-permute-done.6, bf16[2048,256]{0,1:T(8,128)(2,1)S(1)} %collective-permute-done.4, bf16[2048,256]{0,1:T(8,128)(2,1)S(1)} %copy-done.34), kind=kOutput, calls=%fused_computation.42 | convolution fusion | flops 4313841664 | bytes 10485760 | tf_op jit(solution)/shard_map/dot_general | solution.py:93
  346.2 6.6 %broadcast_in_dim.159 = bf16[8192,1024]{1,0:T(8,128)(2,1)} broadcast(bf16[]{:T(256)} %constant.47.clone.1), dimensions={} | broadcast | bytes 16777218 | tf_op jit(solution)/shard_map/broadcast_in_dim | solution.py:70
  371.6 20.9 %collective-permute-done.22 = bf16[2048,256]{0,1:T(8,128)(2,1)} collective-permute-done((bf16[2048,256]{0,1:T(8,128)(2,1)}, bf16[2048,256]{0,1:T(8,128)(2,1)}, u32[]{:S(2)}, u32[]{:S(2)}) %collective-permute-start.22) | collective-permute-done | bytes 1048608 | tf_op jit(solution)/shard_map/ppermute | solution.py:37
  393.8 20.1 %collective-permute-done.23 = bf16[2048,256]{0,1:T(8,128)(2,1)S(1)} collective-permute-done((bf16[2048,256]{0,1:T(8,128)(2,1)}, bf16[2048,256]{0,1:T(8,128)(2,1)S(1)}, u32[]{:S(2)}, u32[]{:S(2)}) %collective-permute-start.23) | collective-permute-done | bytes 1048608 | tf_op jit(solution)/shard_map/ppermute | solution.py:37
  414.0 6.3 %convolution_convert_fusion = bf16[2048,1024]{1,0:T(8,128)(2,1)} fusion(bf16[2048,1024]{0,1:T(8,128)(2,1)S(1)} %constant_dynamic-update-slice_fusion, bf16[1024,1024]{1,0:T(8,128)(2,1)S(1)} %bitcast.123), kind=kOutput, calls=%fused_computation.40 | convolution fusion | flops 4297064448 | bytes 10485760 | tf_op jit(solution)/shard_map/dot_general | solution.py:93
  420.3 6.4 %fusion.36 = f32[1024,1024]{0,1:T(8,128)} fusion(bf16[2048,1024]{0,1:T(8,128)(2,1)S(1)} %constant_dynamic-update-slice_fusion, bf16[8192,1024]{1,0:T(8,128)(2,1)S(1)} %bitcast.115), kind=kOutput, calls=%fused_computation.58 | convolution fusion | flops 4294967296 | bytes 12582912 | tf_op jit(solution)/shard_map/dot_general | solution.py:95
  433.7 7.6 %bitcast_add_fusion = f32[1024,1024]{0,1:T(8,128)} fusion(f32[1024,1024]{0,1:T(8,128)} %fusion.36, f32[1024,1024]{0,1:T(8,128)S(1)} %copy-done.2, f32[1024,1024]{0,1:T(8,128)S(1)} %copy-done.1, bf16[1024,1024]{0,1:T(8,128)(2,1)S(1)} %constant_dynamic-update-slice_fusion.4, bf16[8192,1024]{1,0:T(8,128)(2,1)} %param.4), kind=kOutput, calls=%fused_computation.33 | convolution fusion | flops 2150629376 | bytes 20971520 | tf_op jit(solution)/shard_map/dot_general | solution.py:95
  445.1 5.6 %reshape.104 = f32[4,256,4,4,4,16]{1,0,5,4,3,2:T(4,128)} reshape(f32[1024,1024]{0,1:T(8,128)} %bitcast_add_fusion) | data formatting | bytes 8388608 | tf_op jit(solution)/shard_map/reshape | solution.py:120
  456.7 8.2 %collective-permute-done.29 = bf16[1024,256]{0,1:T(8,128)(2,1)S(1)} collective-permute-done((bf16[1024,256]{0,1:T(8,128)(2,1)}, bf16[1024,256]{0,1:T(8,128)(2,1)S(1)}, u32[]{:S(2)}, u32[]{:S(2)}) %collective-permute-start.29) | collective-permute-done | bytes 524320 | tf_op jit(solution)/shard_map/ppermute | solution.py:37
  481.7 5.9 %convert_dynamic-update-slice_fusion = bf16[8192,1024]{1,0:T(8,128)(2,1)} fusion(bf16[8192,1024]{1,0:T(8,128)(2,1)} %convert_dynamic-update-slice_fusion.1, bf16[1024,1024]{0,1:T(8,128)(2,1)} %copy-done.11, bf16[1024,1024]{1,0:T(8,128)(2,1)} %bitcast.121), kind=kOutput, calls=%fused_computation.108 | convolution fusion | flops 2148532224 | bytes 6291456 | tf_op jit(solution)/shard_map/dot_general | solution.py:93
  488.0 11.8 %collective-permute-done.31 = f32[64,4,256]{2,0,1:T(8,128)S(1)} collective-permute-done((f32[64,4,256]{2,0,1:T(8,128)S(1)}, f32[64,4,256]{2,0,1:T(8,128)S(1)}, u32[]{:S(2)}, u32[]{:S(2)}) %collective-permute-start.31) | collective-permute-done | bytes 262176 | tf_op jit(solution)/shard_map/ppermute | solution.py:48
  (243 shorter events, 151.5 us)
Async XLA Ops:
  7.2 354.0 %all-reduce.3.cloned.1.call-start = ((), (), s32[]{:S(2)}) async-start(), calls=%async_computation | async-start | bytes 2097152
  19.9 71.7 %collective-permute-start.10 = (bf16[1024,256]{0,1:T(8,128)(2,1)}, bf16[1024,256]{0,1:T(8,128)(2,1)}, u32[]{:S(2)}, u32[]{:S(2)}) collective-permute-start(bf16[1024,256]{0,1:T(8,128)(2,1)} %get-tuple-element.97), channel_id=1, source_target_pairs={{0,8},{4,12},{8,0},{12,4},{1,9},{5,13},{9,1},{13,5},{2,10},{6,14},... | collective-permute-start | bytes 1572872 | tf_op jit(solution)/shard_map/ppermute | solution.py:37
  22.9 75.7 %collective-permute-start.11 = (bf16[1024,256]{0,1:T(8,128)(2,1)}, bf16[1024,256]{0,1:T(8,128)(2,1)}, u32[]{:S(2)}, u32[]{:S(2)}) collective-permute-start(bf16[1024,256]{0,1:T(8,128)(2,1)} %get-tuple-element.96), channel_id=1, source_target_pairs={{0,12},{4,8},{8,4},{12,0},{1,13},{5,9},{9,5},{13,1},{2,14},{6,10},... | collective-permute-start | bytes 1572872 | tf_op jit(solution)/shard_map/ppermute | solution.py:37
  22.9 76.2 %collective-permute-start.9 = (bf16[1024,256]{0,1:T(8,128)(2,1)}, bf16[1024,256]{0,1:T(8,128)(2,1)}, u32[]{:S(2)}, u32[]{:S(2)}) collective-permute-start(bf16[1024,256]{0,1:T(8,128)(2,1)} %get-tuple-element.98), channel_id=1, source_target_pairs={{0,4},{4,0},{8,12},{12,8},{1,5},{5,1},{9,13},{13,9},{2,6},{6,2},{1... | collective-permute-start | bytes 1572872 | tf_op jit(solution)/shard_map/ppermute | solution.py:37
  26.7 74.1 %collective-permute-start.18 = (bf16[1024,256]{0,1:T(8,128)(2,1)}, bf16[1024,256]{0,1:T(8,128)(2,1)S(1)}, u32[]{:S(2)}, u32[]{:S(2)}) collective-permute-start(bf16[1024,256]{0,1:T(8,128)(2,1)} %get-tuple-element.95), channel_id=1, source_target_pairs={{0,4},{4,0},{8,12},{12,8},{1,5},{5,1},{9,13},{13,9},{2,6},{6,2},{1... | collective-permute-start | bytes 1572872 | tf_op jit(solution)/shard_map/ppermute | solution.py:37
  27.0 78.1 %collective-permute-start.19 = (bf16[1024,256]{0,1:T(8,128)(2,1)}, bf16[1024,256]{0,1:T(8,128)(2,1)}, u32[]{:S(2)}, u32[]{:S(2)}) collective-permute-start(bf16[1024,256]{0,1:T(8,128)(2,1)} %get-tuple-element.94), channel_id=1, source_target_pairs={{0,8},{4,12},{8,0},{12,4},{1,9},{5,13},{9,1},{13,5},{2,10},{6,14},... | collective-permute-start | bytes 1572872 | tf_op jit(solution)/shard_map/ppermute | solution.py:37
  91.6 14.2 %collective-permute-start.20 = (bf16[1024,256]{0,1:T(8,128)(2,1)}, bf16[1024,256]{0,1:T(8,128)(2,1)S(1)}, u32[]{:S(2)}, u32[]{:S(2)}) collective-permute-start(bf16[1024,256]{0,1:T(8,128)(2,1)} %get-tuple-element.93), channel_id=1, source_target_pairs={{0,12},{4,8},{8,4},{12,0},{1,13},{5,9},{9,5},{13,1},{2,14},{6,10},... | collective-permute-start | bytes 1572872 | tf_op jit(solution)/shard_map/ppermute | solution.py:37
  98.6 16.6 %collective-permute-start.12 = (bf16[2048,256]{0,1:T(8,128)(2,1)}, bf16[2048,256]{0,1:T(8,128)(2,1)S(1)}, u32[]{:S(2)}, u32[]{:S(2)}) collective-permute-start(bf16[2048,256]{0,1:T(8,128)(2,1)} %get-tuple-element.70), channel_id=1, source_target_pairs={{0,4},{4,0},{8,12},{12,8},{1,5},{5,1},{9,13},{13,9},{2,6},{6,2},{1... | collective-permute-start | bytes 3145736 | tf_op jit(solution)/shard_map/ppermute | solution.py:37
  99.0 29.8 %collective-permute-start.14 = (bf16[2048,256]{0,1:T(8,128)(2,1)}, bf16[2048,256]{0,1:T(8,128)(2,1)S(1)}, u32[]{:S(2)}, u32[]{:S(2)}) collective-permute-start(bf16[2048,256]{0,1:T(8,128)(2,1)} %get-tuple-element.72), channel_id=1, source_target_pairs={{0,8},{4,12},{8,0},{12,4},{1,9},{5,13},{9,1},{13,5},{2,10},{6,14},... | collective-permute-start | bytes 3145736 | tf_op jit(solution)/shard_map/ppermute | solution.py:37
  100.7 50.1 %collective-permute-start.16 = (bf16[2048,256]{0,1:T(8,128)(2,1)}, bf16[2048,256]{0,1:T(8,128)(2,1)S(1)}, u32[]{:S(2)}, u32[]{:S(2)}) collective-permute-start(bf16[2048,256]{0,1:T(8,128)(2,1)} %get-tuple-element.71), channel_id=1, source_target_pairs={{0,12},{4,8},{8,4},{12,0},{1,13},{5,9},{9,5},{13,1},{2,14},{6,10},... | collective-permute-start | bytes 3145736 | tf_op jit(solution)/shard_map/ppermute | solution.py:37
  105.2 57.0 %collective-permute-start.3 = (bf16[2048,256]{0,1:T(8,128)(2,1)S(1)}, bf16[2048,256]{0,1:T(8,128)(2,1)S(1)}, u32[]{:S(2)}, u32[]{:S(2)}) collective-permute-start(bf16[2048,256]{0,1:T(8,128)(2,1)S(1)} %copy-done.32), channel_id=1, source_target_pairs={{0,4},{4,0},{8,12},{12,8},{1,5},{5,1},{9,13},{13,9},{2,6},{6,2},{1... | collective-permute-start | bytes 3145736 | tf_op jit(solution)/shard_map/ppermute | solution.py:37
  105.9 68.0 %collective-permute-start.5 = (bf16[2048,256]{0,1:T(8,128)(2,1)S(1)}, bf16[2048,256]{0,1:T(8,128)(2,1)S(1)}, u32[]{:S(2)}, u32[]{:S(2)}) collective-permute-start(bf16[2048,256]{0,1:T(8,128)(2,1)S(1)} %copy-done.31), channel_id=1, source_target_pairs={{0,8},{4,12},{8,0},{12,4},{1,9},{5,13},{9,1},{13,5},{2,10},{6,14},... | collective-permute-start | bytes 3145736 | tf_op jit(solution)/shard_map/ppermute | solution.py:37
  115.2 80.6 %collective-permute-start.7 = (bf16[2048,256]{0,1:T(8,128)(2,1)S(1)}, bf16[2048,256]{0,1:T(8,128)(2,1)S(1)}, u32[]{:S(2)}, u32[]{:S(2)}) collective-permute-start(bf16[2048,256]{0,1:T(8,128)(2,1)S(1)} %copy-done.30), channel_id=1, source_target_pairs={{0,12},{4,8},{8,4},{12,0},{1,13},{5,9},{9,5},{13,1},{2,14},{6,10},... | collective-permute-start | bytes 3145736 | tf_op jit(solution)/shard_map/ppermute | solution.py:37
  128.9 78.5 %collective-permute-start = (bf16[2048,256]{0,1:T(8,128)(2,1)S(1)}, bf16[2048,256]{0,1:T(8,128)(2,1)S(1)}, u32[]{:S(2)}, u32[]{:S(2)}) collective-permute-start(bf16[2048,256]{0,1:T(8,128)(2,1)S(1)} %copy-done.29), channel_id=1, source_target_pairs={{0,4},{4,0},{8,12},{12,8},{1,5},{5,1},{9,13},{13,9},{2,6},{6,2},{1... | collective-permute-start | bytes 3145736 | tf_op jit(solution)/shard_map/ppermute | solution.py:37
  150.8 68.0 %collective-permute-start.1 = (bf16[2048,256]{0,1:T(8,128)(2,1)S(1)}, bf16[2048,256]{0,1:T(8,128)(2,1)S(1)}, u32[]{:S(2)}, u32[]{:S(2)}) collective-permute-start(bf16[2048,256]{0,1:T(8,128)(2,1)S(1)} %copy-done.28), channel_id=1, source_target_pairs={{0,8},{4,12},{8,0},{12,4},{1,9},{5,13},{9,1},{13,5},{2,10},{6,14},... | collective-permute-start | bytes 3145736 | tf_op jit(solution)/shard_map/ppermute | solution.py:37
  162.1 78.5 %collective-permute-start.2 = (bf16[2048,256]{0,1:T(8,128)(2,1)S(1)}, bf16[2048,256]{0,1:T(8,128)(2,1)S(1)}, u32[]{:S(2)}, u32[]{:S(2)}) collective-permute-start(bf16[2048,256]{0,1:T(8,128)(2,1)S(1)} %copy-done.27), channel_id=1, source_target_pairs={{0,12},{4,8},{8,4},{12,0},{1,13},{5,9},{9,5},{13,1},{2,14},{6,10},... | collective-permute-start | bytes 3145736 | tf_op jit(solution)/shard_map/ppermute | solution.py:37
  173.8 98.1 %collective-permute-start.13 = (bf16[2048,256]{0,1:T(8,128)(2,1)}, bf16[2048,256]{0,1:T(8,128)(2,1)}, u32[]{:S(2)}, u32[]{:S(2)}) collective-permute-start(bf16[2048,256]{0,1:T(8,128)(2,1)} %get-tuple-element.59), channel_id=1, source_target_pairs={{0,4},{4,0},{8,12},{12,8},{1,5},{5,1},{9,13},{13,9},{2,6},{6,2},{1... | collective-permute-start | bytes 3145736 | tf_op jit(solution)/shard_map/ppermute | solution.py:37
  195.7 77.3 %collective-permute-start.15 = (bf16[2048,256]{0,1:T(8,128)(2,1)}, bf16[2048,256]{0,1:T(8,128)(2,1)}, u32[]{:S(2)}, u32[]{:S(2)}) collective-permute-start(bf16[2048,256]{0,1:T(8,128)(2,1)} %get-tuple-element.58), channel_id=1, source_target_pairs={{0,8},{4,12},{8,0},{12,4},{1,9},{5,13},{9,1},{13,5},{2,10},{6,14},... | collective-permute-start | bytes 3145736 | tf_op jit(solution)/shard_map/ppermute | solution.py:37
  207.3 78.4 %collective-permute-start.17 = (bf16[2048,256]{0,1:T(8,128)(2,1)}, bf16[2048,256]{0,1:T(8,128)(2,1)}, u32[]{:S(2)}, u32[]{:S(2)}) collective-permute-start(bf16[2048,256]{0,1:T(8,128)(2,1)} %get-tuple-element.57), channel_id=1, source_target_pairs={{0,12},{4,8},{8,4},{12,0},{1,13},{5,9},{9,5},{13,1},{2,14},{6,10},... | collective-permute-start | bytes 3145736 | tf_op jit(solution)/shard_map/ppermute | solution.py:37
  271.1 33.9 %collective-permute-start.4 = (bf16[2048,256]{0,1:T(8,128)(2,1)}, bf16[2048,256]{0,1:T(8,128)(2,1)S(1)}, u32[]{:S(2)}, u32[]{:S(2)}) collective-permute-start(bf16[2048,256]{0,1:T(8,128)(2,1)} %get-tuple-element.64), channel_id=1, source_target_pairs={{0,4},{4,0},{8,12},{12,8},{1,5},{5,1},{9,13},{13,9},{2,6},{6,2},{1... | collective-permute-start | bytes 3145736 | tf_op jit(solution)/shard_map/ppermute | solution.py:37
  271.5 37.1 %collective-permute-start.6 = (bf16[2048,256]{0,1:T(8,128)(2,1)}, bf16[2048,256]{0,1:T(8,128)(2,1)S(1)}, u32[]{:S(2)}, u32[]{:S(2)}) collective-permute-start(bf16[2048,256]{0,1:T(8,128)(2,1)} %get-tuple-element.63), channel_id=1, source_target_pairs={{0,8},{4,12},{8,0},{12,4},{1,9},{5,13},{9,1},{13,5},{2,10},{6,14},... | collective-permute-start | bytes 3145736 | tf_op jit(solution)/shard_map/ppermute | solution.py:37
  271.9 58.6 %collective-permute-start.8 = (bf16[2048,256]{0,1:T(8,128)(2,1)}, bf16[2048,256]{0,1:T(8,128)(2,1)S(1)}, u32[]{:S(2)}, u32[]{:S(2)}) collective-permute-start(bf16[2048,256]{0,1:T(8,128)(2,1)} %get-tuple-element.62), channel_id=1, source_target_pairs={{0,12},{4,8},{8,4},{12,0},{1,13},{5,9},{9,5},{13,1},{2,14},{6,10},... | collective-permute-start | bytes 3145736 | tf_op jit(solution)/shard_map/ppermute | solution.py:37
  343.6 16.5 %collective-permute-start.24 = (bf16[1024,256]{0,1:T(8,128)(2,1)S(1)}, bf16[1024,256]{0,1:T(8,128)(2,1)S(1)}, u32[]{:S(2)}, u32[]{:S(2)}) collective-permute-start(bf16[1024,256]{0,1:T(8,128)(2,1)S(1)} %copy-done.38), channel_id=1, source_target_pairs={{0,4},{4,0},{8,12},{12,8},{1,5},{5,1},{9,13},{13,9},{2,6},{6,2},{1... | collective-permute-start | bytes 1572872 | tf_op jit(solution)/shard_map/ppermute | solution.py:37
  343.7 21.0 %collective-permute-start.25 = (bf16[1024,256]{0,1:T(8,128)(2,1)}, bf16[1024,256]{0,1:T(8,128)(2,1)}, u32[]{:S(2)}, u32[]{:S(2)}) collective-permute-start(bf16[1024,256]{0,1:T(8,128)(2,1)} %get-tuple-element.38), channel_id=1, source_target_pairs={{0,8},{4,12},{8,0},{12,4},{1,9},{5,13},{9,1},{13,5},{2,10},{6,14},... | collective-permute-start | bytes 1572872 | tf_op jit(solution)/shard_map/ppermute | solution.py:37
  344.1 25.0 %collective-permute-start.26 = (bf16[1024,256]{0,1:T(8,128)(2,1)}, bf16[1024,256]{0,1:T(8,128)(2,1)}, u32[]{:S(2)}, u32[]{:S(2)}) collective-permute-start(bf16[1024,256]{0,1:T(8,128)(2,1)} %get-tuple-element.39), channel_id=1, source_target_pairs={{0,12},{4,8},{8,4},{12,0},{1,13},{5,9},{9,5},{13,1},{2,14},{6,10},... | collective-permute-start | bytes 1572872 | tf_op jit(solution)/shard_map/ppermute | solution.py:37
  345.5 24.6 %collective-permute-start.21 = (bf16[2048,256]{0,1:T(8,128)(2,1)}, bf16[2048,256]{0,1:T(8,128)(2,1)}, u32[]{:S(2)}, u32[]{:S(2)}) collective-permute-start(bf16[2048,256]{0,1:T(8,128)(2,1)} %get-tuple-element.31), channel_id=1, source_target_pairs={{0,4},{4,0},{8,12},{12,8},{1,5},{5,1},{9,13},{13,9},{2,6},{6,2},{1... | collective-permute-start | bytes 3145736 | tf_op jit(solution)/shard_map/ppermute | solution.py:37
  345.9 46.6 %collective-permute-start.22 = (bf16[2048,256]{0,1:T(8,128)(2,1)}, bf16[2048,256]{0,1:T(8,128)(2,1)}, u32[]{:S(2)}, u32[]{:S(2)}) collective-permute-start(bf16[2048,256]{0,1:T(8,128)(2,1)} %get-tuple-element.32), channel_id=1, source_target_pairs={{0,8},{4,12},{8,0},{12,4},{1,9},{5,13},{9,1},{13,5},{2,10},{6,14},... | collective-permute-start | bytes 3145736 | tf_op jit(solution)/shard_map/ppermute | solution.py:37
  360.1 53.8 %collective-permute-start.23 = (bf16[2048,256]{0,1:T(8,128)(2,1)}, bf16[2048,256]{0,1:T(8,128)(2,1)S(1)}, u32[]{:S(2)}, u32[]{:S(2)}) collective-permute-start(bf16[2048,256]{0,1:T(8,128)(2,1)} %get-tuple-element.33), channel_id=1, source_target_pairs={{0,12},{4,8},{8,4},{12,0},{1,13},{5,9},{9,5},{13,1},{2,14},{6,10},... | collective-permute-start | bytes 3145736 | tf_op jit(solution)/shard_map/ppermute | solution.py:37
  426.7 29.8 %collective-permute-start.27 = (bf16[1024,256]{0,1:T(8,128)(2,1)}, bf16[1024,256]{0,1:T(8,128)(2,1)S(1)}, u32[]{:S(2)}, u32[]{:S(2)}) collective-permute-start(bf16[1024,256]{0,1:T(8,128)(2,1)} %get-tuple-element.41), channel_id=1, source_target_pairs={{0,4},{4,0},{8,12},{12,8},{1,5},{5,1},{9,13},{13,9},{2,6},{6,2},{1... | collective-permute-start | bytes 1572872 | tf_op jit(solution)/shard_map/ppermute | solution.py:37
  427.1 29.5 %collective-permute-start.28 = (bf16[1024,256]{0,1:T(8,128)(2,1)}, bf16[1024,256]{0,1:T(8,128)(2,1)S(1)}, u32[]{:S(2)}, u32[]{:S(2)}) collective-permute-start(bf16[1024,256]{0,1:T(8,128)(2,1)} %get-tuple-element.42), channel_id=1, source_target_pairs={{0,8},{4,12},{8,0},{12,4},{1,9},{5,13},{9,1},{13,5},{2,10},{6,14},... | collective-permute-start | bytes 1572872 | tf_op jit(solution)/shard_map/ppermute | solution.py:37
  478.5 21.4 %collective-permute-start.31 = (f32[64,4,256]{2,0,1:T(8,128)S(1)}, f32[64,4,256]{2,0,1:T(8,128)S(1)}, u32[]{:S(2)}, u32[]{:S(2)}) collective-permute-start(f32[64,4,256]{2,0,1:T(8,128)S(1)} %bitcast.137), channel_id=1, source_target_pairs={{0,2},{1,3},{2,0},{3,1},{4,6},{5,7},{6,4},{7,5},{8,10},{9,11},{10,... | collective-permute-start | bytes 786440 | tf_op jit(solution)/shard_map/ppermute | solution.py:48
  481.6 18.3 %collective-permute-start.32 = (f32[64,4,256]{2,0,1:T(8,128)S(1)}, f32[64,4,256]{2,0,1:T(8,128)S(1)}, u32[]{:S(2)}, u32[]{:S(2)}) collective-permute-start(f32[64,4,256]{2,0,1:T(8,128)S(1)} %bitcast.138), channel_id=1, source_target_pairs={{0,3},{1,2},{2,1},{3,0},{4,7},{5,6},{6,5},{7,4},{8,11},{9,10},{10,... | collective-permute-start | bytes 786440 | tf_op jit(solution)/shard_map/ppermute | solution.py:48
  (58 other events, 988.7 us)
Sparse Core Ops, SparseCore 0:
  271.2 52.1 all-reduce.2

commit v9 on v7

--- a/solution.py
+++ b/solution.py
@@ -87,15 +87,33 @@
             masked, done = lax.optimization_barrier((masked, pending.pop(0)))
             grad_tokens = lax.dynamic_update_slice(grad_tokens, done[0], (done[2], 0))
             gf_acc = done[1] if gf_acc is None else gf_acc + done[1]
-        returned = jnp.concatenate(exchange(masked, n_dev), axis=1)
-        gt = jnp.dot(returned, w1tp, preferred_element_type=jnp.float32).astype(jnp.bfloat16)
-        gf = lax.dot_general(
-            x, returned, (((0,), (0,)), ((), ())), preferred_element_type=jnp.float32
-        )
+        if k + 1 < CHUNKS:
+            returned = jnp.concatenate(exchange(masked, n_dev), axis=1)
+            gt = jnp.dot(returned, w1tp, preferred_element_type=jnp.float32).astype(jnp.bfloat16)
+            gf = lax.dot_general(
+                x, returned, (((0,), (0,)), ((), ())), preferred_element_type=jnp.float32
+            )
+        else:
+            gt = None
+            gf = []
+            for m, piece in enumerate(exchange(masked, n_dev)):
+                term = jnp.dot(piece, w1tp[m * part:(m + 1) * part],
+                               preferred_element_type=jnp.float32)
+                gt = term if gt is None else gt + term
+                g = lax.dot_general(
+                    x, piece, (((0,), (0,)), ((), ())), preferred_element_type=jnp.float32
+                ).reshape(blk_local, bs, blk_local, blk_local, sub)
+                gf.append(jnp.sum(jnp.where(eye[:, None, None, :, None], g, 0.0), axis=3))
+            gt = gt.astype(jnp.bfloat16)
+            gf = jnp.stack(gf, axis=2)
         pending.append((gt, gf, k * step))
+    gf_last = None
     for gt, gf, at in pending:
         grad_tokens = lax.dynamic_update_slice(grad_tokens, gt, (at, 0))
-        gf_acc = gf if gf_acc is None else gf_acc + gf
+        if at == (CHUNKS - 1) * step:
+            gf_last = gf
+        else:
+            gf_acc = gf if gf_acc is None else gf_acc + gf
 
     gs6 = gs_acc.reshape(n_dev, blk_local, blk_local, sub, blk_local, bs)
     gsd = jnp.sum(jnp.where(eye[None, :, None, None, :, None], gs6, 0.0), axis=4)
@@ -105,7 +123,7 @@
     gf_acc, grad_second = lax.optimization_barrier((gf_acc, grad_second))
     gf6 = gf_acc.reshape(blk_local, bs, n_dev, blk_local, blk_local, sub)
     gfd = jnp.sum(jnp.where(eye[:, None, None, None, :, None], gf6, 0.0), axis=4)
-    gfd = jnp.take(gfd, order, axis=2)
+    gfd = jnp.take(gfd + gf_last, order, axis=2)
     first_term = gfd.transpose(1, 0, 2, 3, 4).reshape(bs, blk_local, bs) * grad_scale
     grad_first = dp_reduce_scatter(first_term)
     return (grad_tokens, grad_first.transpose(1, 0, 2), grad_second.transpose(1, 0, 2))

time: 457 us -> 486 us (1.063)
  matrix products: 165 us -> 203 us
  waiting for transfers between devices: 153 us -> 138 us
    dot_general x0 -> x8, matrix products: none -> 43.6 us  [the longest x4 27.8 us: shards(): jnp.dot(piece, w1tp[m * part:(m + 1) * part], preferred_element_type=jnp....]
    ppermute x24, waiting for transfers between devices: 151 us -> 138 us  [exchange(): lax.ppermute(pieces[m], 'tensor', [(i, i ^ m) for i in range(n_dev)])]
    dot_general x4 -> x3, matrix products: 33 us -> 25.2 us  [shards(): jnp.dot(returned, w1tp, preferred_element_type=jnp.float32)]
    dot_general x4 -> x3, matrix products: 35.7 us -> 28.9 us  [shards(): lax.dot_general(x, returned, (((0,), (0,)), ((), ())), preferred_element_...]
    dot_general x4, matrix products: 34.3 us -> 40.5 us  [shards(): lax.dot_general(active, cot, (((0,), (0,)), ((), ())), preferred_element_...]
    reshape x0 -> x4, local copies, waits for them, and re-layouts: none -> 5.22 us  [shards(): g = lax.dot_general(x, piece, (((0,), (0,)), ((), ())), preferred_element...]
    unnamed x84 -> x89, local copies, waits for them, and re-layouts: 16.2 us -> 14.3 us
  transfers between devices with their start and end apart: 28 -> 28, of which waited for: 11 -> 11; matrix products, arithmetic and copies ran while one was open for 47% -> 56% of each run, Pallas kernels for 0% -> 0%
where the time goes in v9:
time: 486 us; the launch traced here: 481 us
  matrix products  203 us (42%)
  waiting for transfers between devices  138 us (28%)
  local copies, waits for them, and re-layouts  70.4 us (14%)
  other arithmetic  31.9 us (7%)
  starting transfers between devices  22.1 us (5%)
  between operations  15.8 us (3%)
    ppermute x24, waiting for transfers between devices, exchange(): lax.ppermute(pieces[m], 'tensor', [(i, i ^ m) for i in range(n_dev)])  138 us
    dot_general x4, matrix products, shards(): lax.dot_general(active, cot, (((0,), (0,)), ((), ())), preferred_element_...  40.5 us
    dot_general x4, matrix products, shards(): backed = jnp.dot(cot, w2p, preferred_element_type=jnp.float32)  33.6 us
    dot_general x4, matrix products, shards(): jnp.dot(x, w1p, preferred_element_type=jnp.float32).astype(jnp.bfloat16)  31.2 us
    dot_general x3, matrix products, shards(): lax.dot_general(x, returned, (((0,), (0,)), ((), ())), preferred_element_...  28.9 us
    dot_general x4, matrix products, shards(): jnp.dot(piece, w1tp[m * part:(m + 1) * part], preferred_element_type=jnp....  27.8 us
    dot_general x3, matrix products, shards(): jnp.dot(returned, w1tp, preferred_element_type=jnp.float32)  25.2 us
    ppermute x24, starting transfers between devices, exchange(): lax.ppermute(pieces[m], 'tensor', [(i, i ^ m) for i in range(n_dev)])  17.5 us
  transfers between devices with their start and end apart: 28, of which 11 were waited for; matrix products, arithmetic and copies ran while one was open for 56% of the time, Pallas kernels for 0%

profile of v9, /device:TPU:0, one launch (start us, length us, event | category | flops | bytes accessed | tf_op | source)
XLA Modules:
  0.0 481.4 jit_solution(696524269319732608)
XLA Ops:
  13.7 7.3 %convert_bitcast_fusion = bf16[2048,1024]{0,1:T(8,128)(2,1)S(1)} fusion(bf16[1024,1024]{0,1:T(8,128)(2,1)S(1)} %bitcast.149, bf16[8192,1024]{1,0:T(8,128)(2,1)} %param.4), kind=kOutput, calls=%fused_computation.49 | convolution fusion | flops 4297064448 | bytes 10485760 | tf_op jit(solution)/shard_map/dot_general | solution.py:74
  26.2 7.0 %convert_bitcast_fusion.2 = bf16[2048,1024]{0,1:T(8,128)(2,1)S(1)} fusion(bf16[1024,1024]{0,1:T(8,128)(2,1)S(1)} %bitcast.150, bf16[8192,1024]{1,0:T(8,128)(2,1)} %param.4), kind=kOutput, calls=%fused_computation.51 | convolution fusion | flops 4297064448 | bytes 10485760 | tf_op jit(solution)/shard_map/dot_general | solution.py:74
  37.2 9.2 %convolution_bitcast_fusion = bf16[2048,1024]{0,1:T(8,128)(2,1)} fusion(bf16[1024,1024]{0,1:T(8,128)(2,1)S(1)} %bitcast.145, bf16[8192,1024]{1,0:T(8,128)(2,1)} %param.5), kind=kOutput, calls=%fused_computation.5 | convolution fusion | flops 4294967296 | bytes 10485760 | tf_op jit(solution)/shard_map/dot_general | solution.py:75
  46.4 8.4 %convolution_bitcast_fusion.2 = bf16[2048,1024]{0,1:T(8,128)(2,1)} fusion(bf16[1024,1024]{0,1:T(8,128)(2,1)S(1)} %bitcast.146, bf16[8192,1024]{1,0:T(8,128)(2,1)} %param.5), kind=kOutput, calls=%fused_computation.7 | convolution fusion | flops 4294967296 | bytes 10485760 | tf_op jit(solution)/shard_map/dot_general | solution.py:75
  54.8 8.4 %convert_bitcast_fusion.3 = bf16[2048,1024]{0,1:T(8,128)(2,1)} fusion(bf16[1024,1024]{0,1:T(8,128)(2,1)S(1)} %bitcast.151, bf16[8192,1024]{1,0:T(8,128)(2,1)} %param.4), kind=kOutput, calls=%fused_computation.52 | convolution fusion | flops 4297064448 | bytes 10485760 | tf_op jit(solution)/shard_map/dot_general | solution.py:74
  63.3 8.9 %convolution_bitcast_fusion.3 = bf16[2048,1024]{0,1:T(8,128)(2,1)} fusion(bf16[1024,1024]{0,1:T(8,128)(2,1)S(1)} %bitcast.147, bf16[8192,1024]{1,0:T(8,128)(2,1)} %param.5), kind=kOutput, calls=%fused_computation.8 | convolution fusion | flops 4294967296 | bytes 10485760 | tf_op jit(solution)/shard_map/dot_general | solution.py:75
  72.2 8.4 %convert_bitcast_fusion.1 = bf16[2048,1024]{0,1:T(8,128)(2,1)} fusion(bf16[1024,1024]{0,1:T(8,128)(2,1)S(1)} %bitcast.152, bf16[8192,1024]{1,0:T(8,128)(2,1)} %param.4), kind=kOutput, calls=%fused_computation.50 | convolution fusion | flops 4297064448 | bytes 10485760 | tf_op jit(solution)/shard_map/dot_general | solution.py:74
  96.5 7.1 %convolution_bitcast_fusion.1 = bf16[2048,1024]{0,1:T(8,128)(2,1)S(1)} fusion(bf16[1024,1024]{0,1:T(8,128)(2,1)S(1)} %bitcast.148, bf16[8192,1024]{1,0:T(8,128)(2,1)} %param.5), kind=kOutput, calls=%fused_computation.6 | convolution fusion | flops 4294967296 | bytes 10485760 | tf_op jit(solution)/shard_map/dot_general | solution.py:75
  110.2 9.7 %fusion.8 = f32[1024,1024]{1,0:T(8,128)} fusion(bf16[2048,256]{0,1:T(8,128)(2,1)} %collective-permute-done.16, bf16[2048,256]{0,1:T(8,128)(2,1)} %collective-permute-done.14, bf16[2048,256]{0,1:T(8,128)(2,1)} %collective-permute-done.12, bf16[2048,256]{0,1:T(8,128)(2,1)S(1)} %get-tuple-element.50, bf16[8192,1024]{1,0:T(8,128)(2,1)} %param.5), kind=kOutput, calls=%fused_computation.21 | convolution fusion | flops 4315938816 | bytes 12582912 | tf_op jit(solution)/shard_map/dot_general | solution.py:82
  121.4 7.6 %collective-permute-done.7 = bf16[2048,256]{0,1:T(8,128)(2,1)S(1)} collective-permute-done((bf16[2048,256]{0,1:T(8,128)(2,1)S(1)}, bf16[2048,256]{0,1:T(8,128)(2,1)S(1)}, u32[]{:S(2)}, u32[]{:S(2)}) %collective-permute-start.7) | collective-permute-done | bytes 1048608 | tf_op jit(solution)/shard_map/ppermute | solution.py:37
  133.7 9.5 %fusion.1 = f32[1024,1024]{1,0:T(8,128)} fusion(bf16[2048,256]{0,1:T(8,128)(2,1)S(1)} %collective-permute-done.7, bf16[2048,256]{0,1:T(8,128)(2,1)} %collective-permute-done.5, bf16[2048,256]{0,1:T(8,128)(2,1)} %collective-permute-done.3, bf16[2048,256]{0,1:T(8,128)(2,1)S(1)} %get-tuple-element.55, bf16[8192,1024]{1,0:T(8,128)(2,1)} %param.5), kind=kOutput, calls=%fused_computation.13 | convolution fusion | flops 4315938816 | bytes 12582912 | tf_op jit(solution)/shard_map/dot_general | solution.py:82
  143.8 7.9 %collective-permute-done.1 = bf16[2048,256]{0,1:T(8,128)(2,1)S(1)} collective-permute-done((bf16[2048,256]{0,1:T(8,128)(2,1)S(1)}, bf16[2048,256]{0,1:T(8,128)(2,1)S(1)}, u32[]{:S(2)}, u32[]{:S(2)}) %collective-permute-start.1) | collective-permute-done | bytes 1048608 | tf_op jit(solution)/shard_map/ppermute | solution.py:37
  151.7 22.2 %collective-permute-done.2 = bf16[2048,256]{0,1:T(8,128)(2,1)S(1)} collective-permute-done((bf16[2048,256]{0,1:T(8,128)(2,1)S(1)}, bf16[2048,256]{0,1:T(8,128)(2,1)S(1)}, u32[]{:S(2)}, u32[]{:S(2)}) %collective-permute-start.2) | collective-permute-done | bytes 1048608 | tf_op jit(solution)/shard_map/ppermute | solution.py:37
  178.8 8.7 %fusion.15 = f32[1024,1024]{1,0:T(8,128)} fusion(bf16[2048,256]{0,1:T(8,128)(2,1)S(1)} %collective-permute-done.2, bf16[2048,256]{0,1:T(8,128)(2,1)S(1)} %collective-permute-done.1, bf16[2048,256]{0,1:T(8,128)(2,1)S(1)} %collective-permute-done, bf16[2048,256]{0,1:T(8,128)(2,1)S(1)} %get-tuple-element.60, bf16[8192,1024]{1,0:T(8,128)(2,1)} %param.5), kind=kOutput, calls=%fused_computation.29 | convolution fusion | flops 4315938816 | bytes 12582912 | tf_op jit(solution)/shard_map/dot_general | solution.py:82
  187.5 9.1 %collective-permute-done.10 = bf16[2048,256]{0,1:T(8,128)(2,1)S(1)} collective-permute-done((bf16[2048,256]{0,1:T(8,128)(2,1)S(1)}, bf16[2048,256]{0,1:T(8,128)(2,1)S(1)}, u32[]{:S(2)}, u32[]{:S(2)}) %collective-permute-start.10) | collective-permute-done | bytes 1048608 | tf_op jit(solution)/shard_map/ppermute | solution.py:37
  197.2 21.7 %collective-permute-done.11 = bf16[2048,256]{0,1:T(8,128)(2,1)S(1)} collective-permute-done((bf16[2048,256]{0,1:T(8,128)(2,1)S(1)}, bf16[2048,256]{0,1:T(8,128)(2,1)S(1)}, u32[]{:S(2)}, u32[]{:S(2)}) %collective-permute-start.11) | collective-permute-done | bytes 1048608 | tf_op jit(solution)/shard_map/ppermute | solution.py:37
  222.4 12.6 %add_add_fusion = f32[1024,1024]{1,0:T(8,128)} fusion(f32[1024,1024]{1,0:T(8,128)} %fusion.15, f32[1024,1024]{1,0:T(8,128)} %fusion.1, f32[1024,1024]{1,0:T(8,128)S(1)} %copy-done.35, bf16[8192,1024]{1,0:T(8,128)(2,1)} %param.5, bf16[2048,256]{0,1:T(8,128)(2,1)S(1)} %collective-permute-done.11, bf16[2048,256]{0,1:T(8,128)(2,1)S(1)} %collective-permute-done.10, ...), kind=kOutput, calls=%fused_computation.47 | convolution fusion | flops 4319084544 | bytes 25165824 | tf_op jit(solution)/shard_map/dot_general | solution.py:82
  235.0 6.0 %reshape.120 = f32[4,4,4,16,4,256]{5,4,3,2,1,0:T(4,128)} reshape(f32[1024,1024]{1,0:T(8,128)} %add_add_fusion) | data formatting | bytes 8388608 | tf_op jit(solution)/shard_map/reshape | solution.py:118
  250.9 13.1 %collective-permute-done.8 = bf16[2048,256]{0,1:T(8,128)(2,1)} collective-permute-done((bf16[2048,256]{0,1:T(8,128)(2,1)}, bf16[2048,256]{0,1:T(8,128)(2,1)}, u32[]{:S(2)}, u32[]{:S(2)}) %collective-permute-start.8) | collective-permute-done | bytes 1048608 | tf_op jit(solution)/shard_map/ppermute | solution.py:37
  263.9 9.6 %convolution_convert_fusion.1 = bf16[2048,1024]{1,0:T(8,128)(2,1)} fusion(bf16[1024,1024]{1,0:T(8,128)(2,1)} %bitcast.142, bf16[2048,256]{0,1:T(8,128)(2,1)} %collective-permute-done.8, bf16[2048,256]{0,1:T(8,128)(2,1)} %collective-permute-done.6, bf16[2048,256]{0,1:T(8,128)(2,1)} %collective-permute-done.4, bf16[2048,256]{0,1:T(8,128)(2,1)} %get-tuple-element.56), kind=kOutput, calls=%fused_computation.54 | convolution fusion | flops 4313841664 | bytes 10485760 | tf_op jit(solution)/shard_map/dot_general | solution.py:92
  273.5 9.8 %fusion.55 = f32[1024,1024]{0,1:T(8,128)} fusion(bf16[8192,1024]{1,0:T(8,128)(2,1)} %param.4, bf16[2048,256]{0,1:T(8,128)(2,1)} %collective-permute-done.8, bf16[2048,256]{0,1:T(8,128)(2,1)} %collective-permute-done.6, bf16[2048,256]{0,1:T(8,128)(2,1)} %collective-permute-done.4, bf16[2048,256]{0,1:T(8,128)(2,1)S(1)} %copy-done.26), kind=kOutput, calls=%fused_computation.81 | convolution fusion | flops 4311744512 | bytes 12582912 | tf_op jit(solution)/shard_map/dot_general | solution.py:93
  286.6 22.2 %collective-permute-done.17 = bf16[2048,256]{0,1:T(8,128)(2,1)S(1)} collective-permute-done((bf16[2048,256]{0,1:T(8,128)(2,1)S(1)}, bf16[2048,256]{0,1:T(8,128)(2,1)S(1)}, u32[]{:S(2)}, u32[]{:S(2)}) %collective-permute-start.17) | collective-permute-done | bytes 1048608 | tf_op jit(solution)/shard_map/ppermute | solution.py:37
  308.8 8.9 %fusion.58 = f32[1024,1024]{0,1:T(8,128)} fusion(bf16[8192,1024]{1,0:T(8,128)(2,1)} %param.4, bf16[2048,256]{0,1:T(8,128)(2,1)S(1)} %collective-permute-done.17, bf16[2048,256]{0,1:T(8,128)(2,1)S(1)} %collective-permute-done.15, bf16[2048,256]{0,1:T(8,128)(2,1)S(1)} %collective-permute-done.13, bf16[2048,256]{0,1:T(8,128)(2,1)S(1)} %copy-done.24), kind=kOutput, calls=%fused_computation.82 | convolution fusion | flops 4311744512 | bytes 12582912 | tf_op jit(solution)/shard_map/dot_general | solution.py:93
  317.7 6.2 %convolution_convert_fusion = bf16[2048,1024]{1,0:T(8,128)(2,1)} fusion(bf16[1024,1024]{1,0:T(8,128)(2,1)S(1)} %bitcast.144, bf16[2048,256]{0,1:T(8,128)(2,1)S(1)} %collective-permute-done.17, bf16[2048,256]{0,1:T(8,128)(2,1)S(1)} %collective-permute-done.15, bf16[2048,256]{0,1:T(8,128)(2,1)S(1)} %collective-permute-done.13, ...), kind=kOutput, calls=%fused_computation.53 | convolution fusion | flops 4313841664 | bytes 10485760 | tf_op jit(solution)/shard_map/dot_general | solution.py:92
  331.1 6.6 %broadcast_in_dim.184 = bf16[8192,1024]{1,0:T(8,128)(2,1)} broadcast(bf16[]{:T(256)} %constant.53.clone.1), dimensions={} | broadcast | bytes 16777218 | tf_op jit(solution)/shard_map/broadcast_in_dim | solution.py:69
  355.2 16.6 %collective-permute-done.20 = bf16[2048,256]{0,1:T(8,128)(2,1)} collective-permute-done((bf16[2048,256]{0,1:T(8,128)(2,1)}, bf16[2048,256]{0,1:T(8,128)(2,1)}, u32[]{:S(2)}, u32[]{:S(2)}) %collective-permute-start.20) | collective-permute-done | bytes 1048608 | tf_op jit(solution)/shard_map/ppermute | solution.py:37
  373.2 10.1 %bitcast_add_fusion = f32[1024,1024]{0,1:T(8,128)} fusion(f32[1024,1024]{0,1:T(8,128)S(1)} %copy-done.33, f32[1024,1024]{0,1:T(8,128)S(1)} %copy-done.34, bf16[2048,1024]{0,1:T(8,128)(2,1)S(1)} %constant_dynamic-update-slice_fusion, bf16[8192,1024]{1,0:T(8,128)(2,1)} %param.4), kind=kOutput, calls=%fused_computation.44 | convolution fusion | flops 4297064448 | bytes 20971520 | tf_op jit(solution)/shard_map/dot_general | solution.py:93
  404.2 12.6 %collective-permute-done.23 = bf16[2048,256]{0,1:T(8,128)(2,1)} collective-permute-done((bf16[2048,256]{0,1:T(8,128)(2,1)}, bf16[2048,256]{0,1:T(8,128)(2,1)}, u32[]{:S(2)}, u32[]{:S(2)}) %collective-permute-start.23) | collective-permute-done | bytes 1048608 | tf_op jit(solution)/shard_map/ppermute | solution.py:37
  440.7 9.4 %convert_dynamic-update-slice_fusion = bf16[8192,1024]{1,0:T(8,128)(2,1)} fusion(bf16[8192,1024]{1,0:T(8,128)(2,1)} %constant_dynamic-update-slice_fusion.4, bf16[2048,1024]{0,1:T(8,128)(2,1)} %copy-done.29, bf16[1024,1024]{1,0:T(8,128)(2,1)} %bitcast.143), kind=kOutput, calls=%fused_computation.48 | convolution fusion | flops 4297064448 | bytes 10485760 | tf_op jit(solution)/shard_map/dot_general | solution.py:92
  450.2 6.0 %fusion.125 = f32[2048,1024]{1,0:T(8,128)} fusion(bf16[2048,256]{0,1:T(8,128)(2,1)} %collective-permute-done.21, bf16[256,1024]{1,0:T(8,128)(2,1)S(1)} %bitcast.140), kind=kOutput, calls=%fused_computation.184 | convolution fusion | flops 1073741824 | bytes 9961472 | tf_op jit(solution)/shard_map/dot_general | solution.py:100
  456.2 6.0 %fusion.126 = f32[2048,1024]{1,0:T(8,128)} fusion(bf16[2048,256]{0,1:T(8,128)(2,1)} %collective-permute-done.22, bf16[256,1024]{1,0:T(8,128)(2,1)S(1)} %bitcast.139), kind=kOutput, calls=%fused_computation.185 | convolution fusion | flops 1073741824 | bytes 9961472 | tf_op jit(solution)/shard_map/dot_general | solution.py:100
  462.2 10.1 %fusion = bf16[8192,1024]{1,0:T(8,128)(2,1)} fusion(bf16[8192,1024]{1,0:T(8,128)(2,1)} %convert_dynamic-update-slice_fusion, f32[2048,1024]{1,0:T(8,128)} %fusion.126, f32[2048,1024]{1,0:T(8,128)S(1)} %bitcast.133, f32[2048,1024]{1,0:T(8,128)} %fusion.125, bf16[2048,256]{0,1:T(8,128)(2,1)} %collective-permute-done.23, bf16[256,1024]{1,0:T(8,128)(2,1)S(1)} %bitcast.138), kind=kOutput, calls=%fused_computation.9 | convolution fusion | flops 1082130432 | bytes 30932992 | tf_op jit(solution)/shard_map/dot_general | solution.py:100
  (195 shorter events, 138.6 us)
Async XLA Ops:
  7.2 337.9 %all-reduce.3.cloned.1.call-start = ((), (), s32[]{:S(2)}) async-start(), calls=%async_computation | async-start | bytes 2097152
  7.3 73.3 %copy-start.30 = (pred[4,4]{0,1:T(4,128)(4,1)}, pred[4,4]{0,1:T(4,128)(4,1)S(1)}, u32[]{:S(2)}) copy-start(pred[4,4]{0,1:T(4,128)(4,1)S(1)} %iota_compare_fusion) | copy-start | bytes 52
  22.7 80.9 %collective-permute-start.12 = (bf16[2048,256]{0,1:T(8,128)(2,1)}, bf16[2048,256]{0,1:T(8,128)(2,1)}, u32[]{:S(2)}, u32[]{:S(2)}) collective-permute-start(bf16[2048,256]{0,1:T(8,128)(2,1)} %get-tuple-element.65), channel_id=1, source_target_pairs={{0,4},{4,0},{8,12},{12,8},{1,5},{5,1},{9,13},{13,9},{2,6},{6,2},{1... | collective-permute-start | bytes 3145736 | tf_op jit(solution)/shard_map/ppermute | solution.py:37
  23.2 80.9 %collective-permute-start.14 = (bf16[2048,256]{0,1:T(8,128)(2,1)}, bf16[2048,256]{0,1:T(8,128)(2,1)}, u32[]{:S(2)}, u32[]{:S(2)}) collective-permute-start(bf16[2048,256]{0,1:T(8,128)(2,1)} %get-tuple-element.67), channel_id=1, source_target_pairs={{0,8},{4,12},{8,0},{12,4},{1,9},{5,13},{9,1},{13,5},{2,10},{6,14},... | collective-permute-start | bytes 3145736 | tf_op jit(solution)/shard_map/ppermute | solution.py:37
  25.7 79.2 %collective-permute-start.16 = (bf16[2048,256]{0,1:T(8,128)(2,1)}, bf16[2048,256]{0,1:T(8,128)(2,1)}, u32[]{:S(2)}, u32[]{:S(2)}) collective-permute-start(bf16[2048,256]{0,1:T(8,128)(2,1)} %get-tuple-element.66), channel_id=1, source_target_pairs={{0,12},{4,8},{8,4},{12,0},{1,13},{5,9},{9,5},{13,1},{2,14},{6,10},... | collective-permute-start | bytes 3145736 | tf_op jit(solution)/shard_map/ppermute | solution.py:37
  35.1 84.8 %collective-permute-start.3 = (bf16[2048,256]{0,1:T(8,128)(2,1)}, bf16[2048,256]{0,1:T(8,128)(2,1)}, u32[]{:S(2)}, u32[]{:S(2)}) collective-permute-start(bf16[2048,256]{0,1:T(8,128)(2,1)} %get-tuple-element.71), channel_id=1, source_target_pairs={{0,4},{4,0},{8,12},{12,8},{1,5},{5,1},{9,13},{13,9},{2,6},{6,2},{1... | collective-permute-start | bytes 3145736 | tf_op jit(solution)/shard_map/ppermute | solution.py:37
  35.8 84.7 %collective-permute-start.5 = (bf16[2048,256]{0,1:T(8,128)(2,1)}, bf16[2048,256]{0,1:T(8,128)(2,1)}, u32[]{:S(2)}, u32[]{:S(2)}) collective-permute-start(bf16[2048,256]{0,1:T(8,128)(2,1)} %get-tuple-element.73), channel_id=1, source_target_pairs={{0,8},{4,12},{8,0},{12,4},{1,9},{5,13},{9,1},{13,5},{2,10},{6,14},... | collective-permute-start | bytes 3145736 | tf_op jit(solution)/shard_map/ppermute | solution.py:37
  103.6 25.4 %collective-permute-start.7 = (bf16[2048,256]{0,1:T(8,128)(2,1)S(1)}, bf16[2048,256]{0,1:T(8,128)(2,1)S(1)}, u32[]{:S(2)}, u32[]{:S(2)}) collective-permute-start(bf16[2048,256]{0,1:T(8,128)(2,1)S(1)} %copy-done.23), channel_id=1, source_target_pairs={{0,12},{4,8},{8,4},{12,0},{1,13},{5,9},{9,5},{13,1},{2,14},{6,10},... | collective-permute-start | bytes 3145736 | tf_op jit(solution)/shard_map/ppermute | solution.py:37
  104.1 39.1 %collective-permute-start = (bf16[2048,256]{0,1:T(8,128)(2,1)S(1)}, bf16[2048,256]{0,1:T(8,128)(2,1)S(1)}, u32[]{:S(2)}, u32[]{:S(2)}) collective-permute-start(bf16[2048,256]{0,1:T(8,128)(2,1)S(1)} %copy-done.22), channel_id=1, source_target_pairs={{0,4},{4,0},{8,12},{12,8},{1,5},{5,1},{9,13},{13,9},{2,6},{6,2},{1... | collective-permute-start | bytes 3145736 | tf_op jit(solution)/shard_map/ppermute | solution.py:37
  104.9 46.8 %collective-permute-start.1 = (bf16[2048,256]{0,1:T(8,128)(2,1)S(1)}, bf16[2048,256]{0,1:T(8,128)(2,1)S(1)}, u32[]{:S(2)}, u32[]{:S(2)}) collective-permute-start(bf16[2048,256]{0,1:T(8,128)(2,1)S(1)} %copy-done.21), channel_id=1, source_target_pairs={{0,8},{4,12},{8,0},{12,4},{1,9},{5,13},{9,1},{13,5},{2,10},{6,14},... | collective-permute-start | bytes 3145736 | tf_op jit(solution)/shard_map/ppermute | solution.py:37
  120.0 54.0 %collective-permute-start.2 = (bf16[2048,256]{0,1:T(8,128)(2,1)S(1)}, bf16[2048,256]{0,1:T(8,128)(2,1)S(1)}, u32[]{:S(2)}, u32[]{:S(2)}) collective-permute-start(bf16[2048,256]{0,1:T(8,128)(2,1)S(1)} %copy-done.20), channel_id=1, source_target_pairs={{0,12},{4,8},{8,4},{12,0},{1,13},{5,9},{9,5},{13,1},{2,14},{6,10},... | collective-permute-start | bytes 3145736 | tf_op jit(solution)/shard_map/ppermute | solution.py:37
  120.5 76.2 %collective-permute-start.10 = (bf16[2048,256]{0,1:T(8,128)(2,1)S(1)}, bf16[2048,256]{0,1:T(8,128)(2,1)S(1)}, u32[]{:S(2)}, u32[]{:S(2)}) collective-permute-start(bf16[2048,256]{0,1:T(8,128)(2,1)S(1)} %copy-done.19), channel_id=1, source_target_pairs={{0,8},{4,12},{8,0},{12,4},{1,9},{5,13},{9,1},{13,5},{2,10},{6,14},... | collective-permute-start | bytes 3145736 | tf_op jit(solution)/shard_map/ppermute | solution.py:37
  129.0 89.9 %collective-permute-start.11 = (bf16[2048,256]{0,1:T(8,128)(2,1)S(1)}, bf16[2048,256]{0,1:T(8,128)(2,1)S(1)}, u32[]{:S(2)}, u32[]{:S(2)}) collective-permute-start(bf16[2048,256]{0,1:T(8,128)(2,1)S(1)} %copy-done.18), channel_id=1, source_target_pairs={{0,12},{4,8},{8,4},{12,0},{1,13},{5,9},{9,5},{13,1},{2,14},{6,10},... | collective-permute-start | bytes 3145736 | tf_op jit(solution)/shard_map/ppermute | solution.py:37
  133.7 41.4 %copy-start = (bf16[2048,1024]{0,1:T(8,128)(2,1)S(1)}, bf16[2048,1024]{0,1:T(8,128)(2,1)}, u32[]{:S(2)}) copy-start(bf16[2048,1024]{0,1:T(8,128)(2,1)} %convolution_bitcast_fusion.3) | copy-start | bytes 12582916
  143.2 75.7 %collective-permute-start.9 = (bf16[2048,256]{0,1:T(8,128)(2,1)S(1)}, bf16[2048,256]{0,1:T(8,128)(2,1)S(1)}, u32[]{:S(2)}, u32[]{:S(2)}) collective-permute-start(bf16[2048,256]{0,1:T(8,128)(2,1)S(1)} %copy-done.17), channel_id=1, source_target_pairs={{0,4},{4,0},{8,12},{12,8},{1,5},{5,1},{9,13},{13,9},{2,6},{6,2},{1... | collective-permute-start | bytes 3145736 | tf_op jit(solution)/shard_map/ppermute | solution.py:37
  151.7 98.6 %collective-permute-start.4 = (bf16[2048,256]{0,1:T(8,128)(2,1)}, bf16[2048,256]{0,1:T(8,128)(2,1)}, u32[]{:S(2)}, u32[]{:S(2)}) collective-permute-start(bf16[2048,256]{0,1:T(8,128)(2,1)} %get-tuple-element.59), channel_id=1, source_target_pairs={{0,4},{4,0},{8,12},{12,8},{1,5},{5,1},{9,13},{13,9},{2,6},{6,2},{1... | collective-permute-start | bytes 3145736 | tf_op jit(solution)/shard_map/ppermute | solution.py:37
  173.9 76.9 %collective-permute-start.6 = (bf16[2048,256]{0,1:T(8,128)(2,1)}, bf16[2048,256]{0,1:T(8,128)(2,1)}, u32[]{:S(2)}, u32[]{:S(2)}) collective-permute-start(bf16[2048,256]{0,1:T(8,128)(2,1)} %get-tuple-element.58), channel_id=1, source_target_pairs={{0,8},{4,12},{8,0},{12,4},{1,9},{5,13},{9,1},{13,5},{2,10},{6,14},... | collective-permute-start | bytes 3145736 | tf_op jit(solution)/shard_map/ppermute | solution.py:37
  196.7 67.3 %collective-permute-start.8 = (bf16[2048,256]{0,1:T(8,128)(2,1)}, bf16[2048,256]{0,1:T(8,128)(2,1)}, u32[]{:S(2)}, u32[]{:S(2)}) collective-permute-start(bf16[2048,256]{0,1:T(8,128)(2,1)} %get-tuple-element.57), channel_id=1, source_target_pairs={{0,12},{4,8},{8,4},{12,0},{1,13},{5,9},{9,5},{13,1},{2,14},{6,10},... | collective-permute-start | bytes 3145736 | tf_op jit(solution)/shard_map/ppermute | solution.py:37
  248.9 34.4 %collective-permute-start.13 = (bf16[2048,256]{0,1:T(8,128)(2,1)}, bf16[2048,256]{0,1:T(8,128)(2,1)S(1)}, u32[]{:S(2)}, u32[]{:S(2)}) collective-permute-start(bf16[2048,256]{0,1:T(8,128)(2,1)} %get-tuple-element.54), channel_id=1, source_target_pairs={{0,4},{4,0},{8,12},{12,8},{1,5},{5,1},{9,13},{13,9},{2,6},{6,2},{1... | collective-permute-start | bytes 3145736 | tf_op jit(solution)/shard_map/ppermute | solution.py:37
  249.1 37.5 %collective-permute-start.15 = (bf16[2048,256]{0,1:T(8,128)(2,1)}, bf16[2048,256]{0,1:T(8,128)(2,1)S(1)}, u32[]{:S(2)}, u32[]{:S(2)}) collective-permute-start(bf16[2048,256]{0,1:T(8,128)(2,1)} %get-tuple-element.53), channel_id=1, source_target_pairs={{0,8},{4,12},{8,0},{12,4},{1,9},{5,13},{9,1},{13,5},{2,10},{6,14},... | collective-permute-start | bytes 3145736 | tf_op jit(solution)/shard_map/ppermute | solution.py:37
  250.3 58.5 %collective-permute-start.17 = (bf16[2048,256]{0,1:T(8,128)(2,1)S(1)}, bf16[2048,256]{0,1:T(8,128)(2,1)S(1)}, u32[]{:S(2)}, u32[]{:S(2)}) collective-permute-start(bf16[2048,256]{0,1:T(8,128)(2,1)S(1)} %copy-done.25), channel_id=1, source_target_pairs={{0,12},{4,8},{8,4},{12,0},{1,13},{5,9},{9,5},{13,1},{2,14},{6,10},... | collective-permute-start | bytes 3145736 | tf_op jit(solution)/shard_map/ppermute | solution.py:37
  273.5 35.3 %copy-start.24 = (bf16[2048,256]{0,1:T(8,128)(2,1)S(1)}, bf16[2048,256]{0,1:T(8,128)(2,1)}, u32[]{:S(2)}) copy-start(bf16[2048,256]{0,1:T(8,128)(2,1)} %get-tuple-element.51) | copy-start | bytes 3145732
  323.9 27.9 %collective-permute-start.18 = (bf16[2048,256]{0,1:T(8,128)(2,1)}, bf16[2048,256]{0,1:T(8,128)(2,1)}, u32[]{:S(2)}, u32[]{:S(2)}) collective-permute-start(bf16[2048,256]{0,1:T(8,128)(2,1)} %get-tuple-element.24), channel_id=1, source_target_pairs={{0,4},{4,0},{8,12},{12,8},{1,5},{5,1},{9,13},{13,9},{2,6},{6,2},{1... | collective-permute-start | bytes 3145736 | tf_op jit(solution)/shard_map/ppermute | solution.py:37
  324.0 29.9 %collective-permute-start.19 = (bf16[2048,256]{0,1:T(8,128)(2,1)}, bf16[2048,256]{0,1:T(8,128)(2,1)}, u32[]{:S(2)}, u32[]{:S(2)}) collective-permute-start(bf16[2048,256]{0,1:T(8,128)(2,1)} %get-tuple-element.25), channel_id=1, source_target_pairs={{0,8},{4,12},{8,0},{12,4},{1,9},{5,13},{9,1},{13,5},{2,10},{6,14},... | collective-permute-start | bytes 3145736 | tf_op jit(solution)/shard_map/ppermute | solution.py:37
  325.0 46.8 %collective-permute-start.20 = (bf16[2048,256]{0,1:T(8,128)(2,1)}, bf16[2048,256]{0,1:T(8,128)(2,1)}, u32[]{:S(2)}, u32[]{:S(2)}) collective-permute-start(bf16[2048,256]{0,1:T(8,128)(2,1)} %get-tuple-element.26), channel_id=1, source_target_pairs={{0,12},{4,8},{8,4},{12,0},{1,13},{5,9},{9,5},{13,1},{2,14},{6,10},... | collective-permute-start | bytes 3145736 | tf_op jit(solution)/shard_map/ppermute | solution.py:37
  325.8 57.5 %collective-permute-start.21 = (bf16[2048,256]{0,1:T(8,128)(2,1)}, bf16[2048,256]{0,1:T(8,128)(2,1)}, u32[]{:S(2)}, u32[]{:S(2)}) collective-permute-start(bf16[2048,256]{0,1:T(8,128)(2,1)} %get-tuple-element.28), channel_id=1, source_target_pairs={{0,4},{4,0},{8,12},{12,8},{1,5},{5,1},{9,13},{13,9},{2,6},{6,2},{1... | collective-permute-start | bytes 3145736 | tf_op jit(solution)/shard_map/ppermute | solution.py:37
  326.1 69.1 %collective-permute-start.22 = (bf16[2048,256]{0,1:T(8,128)(2,1)}, bf16[2048,256]{0,1:T(8,128)(2,1)}, u32[]{:S(2)}, u32[]{:S(2)}) collective-permute-start(bf16[2048,256]{0,1:T(8,128)(2,1)} %get-tuple-element.29), channel_id=1, source_target_pairs={{0,8},{4,12},{8,0},{12,4},{1,9},{5,13},{9,1},{13,5},{2,10},{6,14},... | collective-permute-start | bytes 3145736 | tf_op jit(solution)/shard_map/ppermute | solution.py:37
  346.0 27.1 %copy-start.34 = (f32[1024,1024]{0,1:T(8,128)S(1)}, f32[1024,1024]{0,1:T(8,128)}, u32[]{:S(2)}) copy-start(f32[1024,1024]{0,1:T(8,128)} %fusion.58) | copy-start | bytes 12582916
  351.8 64.9 %collective-permute-start.23 = (bf16[2048,256]{0,1:T(8,128)(2,1)}, bf16[2048,256]{0,1:T(8,128)(2,1)}, u32[]{:S(2)}, u32[]{:S(2)}) collective-permute-start(bf16[2048,256]{0,1:T(8,128)(2,1)} %get-tuple-element.30), channel_id=1, source_target_pairs={{0,12},{4,8},{8,4},{12,0},{1,13},{5,9},{9,5},{13,1},{2,14},{6,10},... | collective-permute-start | bytes 3145736 | tf_op jit(solution)/shard_map/ppermute | solution.py:37
  434.4 39.0 %collective-permute-start.24 = (f32[64,4,256]{2,0,1:T(8,128)S(1)}, f32[64,4,256]{2,0,1:T(8,128)S(1)}, u32[]{:S(2)}, u32[]{:S(2)}) collective-permute-start(f32[64,4,256]{2,0,1:T(8,128)S(1)} %bitcast.158), channel_id=1, source_target_pairs={{0,1},{1,0},{2,3},{3,2},{4,5},{5,4},{6,7},{7,6},{8,9},{9,8},{10,11... | collective-permute-start | bytes 786440 | tf_op jit(solution)/shard_map/ppermute | solution.py:48
  437.5 35.8 %collective-permute-start.25 = (f32[64,4,256]{2,0,1:T(8,128)S(1)}, f32[64,4,256]{2,0,1:T(8,128)S(1)}, u32[]{:S(2)}, u32[]{:S(2)}) collective-permute-start(f32[64,4,256]{2,0,1:T(8,128)S(1)} %bitcast.159), channel_id=1, source_target_pairs={{0,2},{1,3},{2,0},{3,1},{4,6},{5,7},{6,4},{7,5},{8,10},{9,11},{10,... | collective-permute-start | bytes 786440 | tf_op jit(solution)/shard_map/ppermute | solution.py:48
  440.4 32.9 %collective-permute-start.26 = (f32[64,4,256]{2,0,1:T(8,128)S(1)}, f32[64,4,256]{2,0,1:T(8,128)S(1)}, u32[]{:S(2)}, u32[]{:S(2)}) collective-permute-start(f32[64,4,256]{2,0,1:T(8,128)S(1)} %bitcast.160), channel_id=1, source_target_pairs={{0,3},{1,2},{2,1},{3,0},{4,7},{5,6},{6,5},{7,4},{8,11},{9,10},{10,... | collective-permute-start | bytes 786440 | tf_op jit(solution)/shard_map/ppermute | solution.py:48
  (34 other events, 300.2 us)
Sparse Core Ops, SparseCore 0:
  249.0 52.7 all-reduce.2

commit v10 on v7

--- a/solution.py
+++ b/solution.py
@@ -101,7 +101,7 @@
     gsd = jnp.sum(jnp.where(eye[None, :, None, None, :, None], gs6, 0.0), axis=4)
     gsd = jnp.take(gsd, order, axis=0)
     second_term = gsd.transpose(3, 0, 2, 1, 4).reshape(bs, blk_local, bs) * grad_scale
-    grad_second = lax.psum_scatter(second_term, "dp", scatter_dimension=0, tiled=True)
+    grad_second = dp_reduce_scatter(second_term)
     gf_acc, grad_second = lax.optimization_barrier((gf_acc, grad_second))
     gf6 = gf_acc.reshape(blk_local, bs, n_dev, blk_local, blk_local, sub)
     gfd = jnp.sum(jnp.where(eye[:, None, None, None, :, None], gf6, 0.0), axis=4)

time: 457 us -> 486 us (1.063)
  waiting for transfers between devices: 153 us -> 201 us
  local copies, waits for them, and re-layouts: 66.1 us -> 48.4 us
  between operations: 15.6 us -> 1.42 us
  matrix products: 165 us -> 170 us
    ppermute x24, waiting for transfers between devices: 151 us -> 185 us  [exchange(): lax.ppermute(pieces[m], 'tensor', [(i, i ^ m) for i in range(n_dev)])]
    ppermute x3 -> x6, waiting for transfers between devices: 1.85 us -> 15.9 us  [dp_reduce_scatter(): acc = acc + lax.ppermute(send, 'dp', [(i, i ^ m) for i in range(n)])]
    ppermute x3 -> x6, starting transfers between devices: 4.52 us -> 11.3 us  [dp_reduce_scatter(): acc = acc + lax.ppermute(send, 'dp', [(i, i ^ m) for i in range(n)])]
    dynamic_update_slice x2, local copies, waits for them, and re-layouts: 7.18 us -> 1.15 us  [shards(): grad_tokens = lax.dynamic_update_slice(grad_tokens, done[0], (done[2], 0))]
    unnamed x84 -> x70, local copies, waits for them, and re-layouts: 16.2 us -> 12.5 us
  transfers between devices with their start and end apart: 28 -> 30, of which waited for: 11 -> 13; matrix products, arithmetic and copies ran while one was open for 47% -> 37% of each run, Pallas kernels for 0% -> 0%
where the time goes in v10:
time: 486 us; the launch traced here: 479 us
  waiting for transfers between devices  201 us (41%)
  matrix products  170 us (35%)
  local copies, waits for them, and re-layouts  48.4 us (10%)
  other arithmetic  30.4 us (6%)
  starting transfers between devices  27.6 us (6%)
    ppermute x24, waiting for transfers between devices, exchange(): lax.ppermute(pieces[m], 'tensor', [(i, i ^ m) for i in range(n_dev)])  185 us
    dot_general x4, matrix products, shards(): lax.dot_general(x, returned, (((0,), (0,)), ((), ())), preferred_element_...  39.4 us
    dot_general x4, matrix products, shards(): lax.dot_general(active, cot, (((0,), (0,)), ((), ())), preferred_element_...  34.2 us
    dot_general x4, matrix products, shards(): backed = jnp.dot(cot, w2p, preferred_element_type=jnp.float32)  33.3 us
    dot_general x4, matrix products, shards(): jnp.dot(returned, w1tp, preferred_element_type=jnp.float32)  33 us
    dot_general x4, matrix products, shards(): jnp.dot(x, w1p, preferred_element_type=jnp.float32).astype(jnp.bfloat16)  29.9 us
    ppermute x24, starting transfers between devices, exchange(): lax.ppermute(pieces[m], 'tensor', [(i, i ^ m) for i in range(n_dev)])  16.3 us
    ppermute x6, waiting for transfers between devices, dp_reduce_scatter(): acc = acc + lax.ppermute(send, 'dp', [(i, i ^ m) for i in range(n)])  15.9 us
  transfers between devices with their start and end apart: 30, of which 13 were waited for; matrix products, arithmetic and copies ran while one was open for 37% of the time, Pallas kernels for 0%

profile of v10, /device:TPU:0, one launch (start us, length us, event | category | flops | bytes accessed | tf_op | source)
XLA Modules:
  0.0 478.7 jit_solution(9714915830157482814)
XLA Ops:
  8.9 7.2 %convert_bitcast_fusion = bf16[2048,1024]{0,1:T(8,128)(2,1)S(1)} fusion(bf16[1024,1024]{0,1:T(8,128)(2,1)S(1)} %bitcast.117, bf16[8192,1024]{1,0:T(8,128)(2,1)} %param.4), kind=kOutput, calls=%fused_computation.49 | convolution fusion | flops 4297064448 | bytes 10485760 | tf_op jit(solution)/shard_map/dot_general | solution.py:74
  22.0 7.0 %convert_bitcast_fusion.1 = bf16[2048,1024]{0,1:T(8,128)(2,1)S(1)} fusion(bf16[1024,1024]{0,1:T(8,128)(2,1)S(1)} %bitcast.118, bf16[8192,1024]{1,0:T(8,128)(2,1)} %param.4), kind=kOutput, calls=%fused_computation.50 | convolution fusion | flops 4297064448 | bytes 10485760 | tf_op jit(solution)/shard_map/dot_general | solution.py:74
  32.2 7.0 %convert_bitcast_fusion.2 = bf16[2048,1024]{0,1:T(8,128)(2,1)S(1)} fusion(bf16[1024,1024]{0,1:T(8,128)(2,1)S(1)} %bitcast.119, bf16[8192,1024]{1,0:T(8,128)(2,1)} %param.4), kind=kOutput, calls=%fused_computation.51 | convolution fusion | flops 4297064448 | bytes 10485760 | tf_op jit(solution)/shard_map/dot_general | solution.py:74
  39.3 8.6 %convert_bitcast_fusion.3 = bf16[2048,1024]{0,1:T(8,128)(2,1)S(1)} fusion(bf16[1024,1024]{0,1:T(8,128)(2,1)S(1)} %bitcast.120, bf16[8192,1024]{1,0:T(8,128)(2,1)} %param.4), kind=kOutput, calls=%fused_computation.52 | convolution fusion | flops 4297064448 | bytes 10485760 | tf_op jit(solution)/shard_map/dot_general | solution.py:74
  48.3 9.3 %convolution_bitcast_fusion = bf16[2048,1024]{0,1:T(8,128)(2,1)} fusion(bf16[1024,1024]{0,1:T(8,128)(2,1)S(1)} %bitcast.113, bf16[8192,1024]{1,0:T(8,128)(2,1)} %param.5), kind=kOutput, calls=%fused_computation.4 | convolution fusion | flops 4294967296 | bytes 10485760 | tf_op jit(solution)/shard_map/dot_general | solution.py:75
  57.7 8.5 %convolution_bitcast_fusion.1 = bf16[2048,1024]{0,1:T(8,128)(2,1)} fusion(bf16[1024,1024]{0,1:T(8,128)(2,1)S(1)} %bitcast.114, bf16[8192,1024]{1,0:T(8,128)(2,1)} %param.5), kind=kOutput, calls=%fused_computation.5 | convolution fusion | flops 4294967296 | bytes 10485760 | tf_op jit(solution)/shard_map/dot_general | solution.py:75
  66.2 8.3 %convolution_bitcast_fusion.2 = bf16[2048,1024]{0,1:T(8,128)(2,1)} fusion(bf16[1024,1024]{0,1:T(8,128)(2,1)S(1)} %bitcast.115, bf16[8192,1024]{1,0:T(8,128)(2,1)} %param.5), kind=kOutput, calls=%fused_computation.6 | convolution fusion | flops 4294967296 | bytes 10485760 | tf_op jit(solution)/shard_map/dot_general | solution.py:75
  77.9 7.1 %convolution_bitcast_fusion.3 = bf16[2048,1024]{0,1:T(8,128)(2,1)S(1)} fusion(bf16[1024,1024]{0,1:T(8,128)(2,1)S(1)} %bitcast.116, bf16[8192,1024]{1,0:T(8,128)(2,1)} %param.5), kind=kOutput, calls=%fused_computation.7 | convolution fusion | flops 4294967296 | bytes 10485760 | tf_op jit(solution)/shard_map/dot_general | solution.py:75
  91.8 7.8 %fusion.7 = f32[1024,1024]{1,0:T(8,128)S(1)} fusion(bf16[2048,256]{0,1:T(8,128)(2,1)} %collective-permute-done.16, bf16[2048,256]{0,1:T(8,128)(2,1)} %collective-permute-done.14, bf16[2048,256]{0,1:T(8,128)(2,1)} %collective-permute-done.12, bf16[2048,256]{0,1:T(8,128)(2,1)S(1)} %get-tuple-element.40, bf16[8192,1024]{1,0:T(8,128)(2,1)} %param.5), kind=kOutput, calls=%fused_computation.19 | convolution fusion | flops 4315938816 | bytes 12582912 | tf_op jit(solution)/shard_map/dot_general | solution.py:82
  100.4 34.2 %collective-permute-done.7 = bf16[2048,256]{0,1:T(8,128)(2,1)S(1)} collective-permute-done((bf16[2048,256]{0,1:T(8,128)(2,1)S(1)}, bf16[2048,256]{0,1:T(8,128)(2,1)S(1)}, u32[]{:S(2)}, u32[]{:S(2)}) %collective-permute-start.7) | collective-permute-done | bytes 1048608 | tf_op jit(solution)/shard_map/ppermute | solution.py:37
  135.8 21.7 %collective-permute-done.5 = bf16[2048,256]{0,1:T(8,128)(2,1)S(1)} collective-permute-done((bf16[2048,256]{0,1:T(8,128)(2,1)S(1)}, bf16[2048,256]{0,1:T(8,128)(2,1)S(1)}, u32[]{:S(2)}, u32[]{:S(2)}) %collective-permute-start.5) | collective-permute-done | bytes 1048608 | tf_op jit(solution)/shard_map/ppermute | solution.py:37
  161.6 6.7 %fusion = f32[1024,1024]{1,0:T(8,128)S(1)} fusion(bf16[2048,256]{0,1:T(8,128)(2,1)S(1)} %collective-permute-done.7, bf16[2048,256]{0,1:T(8,128)(2,1)S(1)} %collective-permute-done.5, bf16[2048,256]{0,1:T(8,128)(2,1)S(1)} %collective-permute-done.3, bf16[2048,256]{0,1:T(8,128)(2,1)S(1)} %get-tuple-element.45, bf16[8192,1024]{1,0:T(8,128)(2,1)} %param.5), kind=kOutput, calls=%fused_computation.11 | convolution fusion | flops 4315938816 | bytes 12582912 | tf_op jit(solution)/shard_map/dot_general | solution.py:82
  168.3 11.3 %collective-permute-done.2 = bf16[2048,256]{0,1:T(8,128)(2,1)S(1)} collective-permute-done((bf16[2048,256]{0,1:T(8,128)(2,1)S(1)}, bf16[2048,256]{0,1:T(8,128)(2,1)S(1)}, u32[]{:S(2)}, u32[]{:S(2)}) %collective-permute-start.2) | collective-permute-done | bytes 1048608 | tf_op jit(solution)/shard_map/ppermute | solution.py:37
  179.8 22.5 %collective-permute-done.1 = bf16[2048,256]{0,1:T(8,128)(2,1)S(1)} collective-permute-done((bf16[2048,256]{0,1:T(8,128)(2,1)S(1)}, bf16[2048,256]{0,1:T(8,128)(2,1)S(1)}, u32[]{:S(2)}, u32[]{:S(2)}) %collective-permute-start.1) | collective-permute-done | bytes 1048608 | tf_op jit(solution)/shard_map/ppermute | solution.py:37
  207.5 8.8 %fusion.14 = f32[1024,1024]{1,0:T(8,128)} fusion(bf16[2048,256]{0,1:T(8,128)(2,1)S(1)} %collective-permute-done.2, bf16[2048,256]{0,1:T(8,128)(2,1)S(1)} %collective-permute-done.1, bf16[2048,256]{0,1:T(8,128)(2,1)S(1)} %collective-permute-done, bf16[2048,256]{0,1:T(8,128)(2,1)S(1)} %get-tuple-element.50, bf16[8192,1024]{1,0:T(8,128)(2,1)} %param.5), kind=kOutput, calls=%fused_computation.27 | convolution fusion | flops 4315938816 | bytes 12582912 | tf_op jit(solution)/shard_map/dot_general | solution.py:82
  220.5 10.9 %add_add_fusion = f32[1024,1024]{1,0:T(8,128)} fusion(f32[1024,1024]{1,0:T(8,128)} %fusion.14, f32[1024,1024]{1,0:T(8,128)S(1)} %fusion, f32[1024,1024]{1,0:T(8,128)S(1)} %fusion.7, bf16[8192,1024]{1,0:T(8,128)(2,1)} %param.5, bf16[2048,256]{0,1:T(8,128)(2,1)} %collective-permute-done.11, bf16[2048,256]{0,1:T(8,128)(2,1)} %collective-permute-done.10, ...), kind=kOutput, calls=%fused_computation.46 | convolution fusion | flops 4319084544 | bytes 25165824 | tf_op jit(solution)/shard_map/dot_general | solution.py:82
  231.4 5.8 %reshape.99 = f32[4,4,4,16,4,256]{5,4,3,2,1,0:T(4,128)} reshape(f32[1024,1024]{1,0:T(8,128)} %add_add_fusion) | data formatting | bytes 8388608 | tf_op jit(solution)/shard_map/reshape | solution.py:100
  249.3 8.5 %collective-permute-done.24 = f32[64,4,256]{2,0,1:T(8,128)S(1)} collective-permute-done((f32[64,4,256]{2,0,1:T(8,128)S(1)}, f32[64,4,256]{2,0,1:T(8,128)S(1)}, u32[]{:S(2)}, u32[]{:S(2)}) %collective-permute-start.24) | collective-permute-done | bytes 262176 | tf_op jit(solution)/shard_map/ppermute | solution.py:48
  261.5 6.1 %collective-permute-done.25 = f32[64,4,256]{2,0,1:T(8,128)S(1)} collective-permute-done((f32[64,4,256]{2,0,1:T(8,128)S(1)}, f32[64,4,256]{2,0,1:T(8,128)S(1)}, u32[]{:S(2)}, u32[]{:S(2)}) %collective-permute-start.25) | collective-permute-done | bytes 262176 | tf_op jit(solution)/shard_map/ppermute | solution.py:48
  270.3 8.5 %convolution_convert_fusion = bf16[2048,1024]{1,0:T(8,128)(2,1)} fusion(bf16[1024,1024]{1,0:T(8,128)(2,1)S(1)} %bitcast.109, bf16[2048,256]{0,1:T(8,128)(2,1)} %collective-permute-done.17, bf16[2048,256]{0,1:T(8,128)(2,1)} %collective-permute-done.15, bf16[2048,256]{0,1:T(8,128)(2,1)} %collective-permute-done.13, bf16[2048,256]{0,1:T(8,128)(2,1)S(1)} %copy-done.21), kind=kOutput, calls=%fused_computation.53 | convolution fusion | flops 4313841664 | bytes 10485760 | tf_op jit(solution)/shard_map/dot_general | solution.py:91
  278.8 9.8 %fusion.51 = f32[1024,1024]{0,1:T(8,128)} fusion(bf16[8192,1024]{1,0:T(8,128)(2,1)} %param.4, bf16[2048,256]{0,1:T(8,128)(2,1)} %collective-permute-done.17, bf16[2048,256]{0,1:T(8,128)(2,1)} %collective-permute-done.15, bf16[2048,256]{0,1:T(8,128)(2,1)} %collective-permute-done.13, bf16[2048,256]{0,1:T(8,128)(2,1)S(1)} %copy-done.21), kind=kOutput, calls=%fused_computation.76 | convolution fusion | flops 4311744512 | bytes 12582912 | tf_op jit(solution)/shard_map/dot_general | solution.py:92
  293.4 22.3 %collective-permute-done.6 = bf16[2048,256]{0,1:T(8,128)(2,1)} collective-permute-done((bf16[2048,256]{0,1:T(8,128)(2,1)}, bf16[2048,256]{0,1:T(8,128)(2,1)}, u32[]{:S(2)}, u32[]{:S(2)}) %collective-permute-start.6) | collective-permute-done | bytes 1048608 | tf_op jit(solution)/shard_map/ppermute | solution.py:37
  315.6 10.0 %fusion.48 = f32[1024,1024]{0,1:T(8,128)} fusion(bf16[8192,1024]{1,0:T(8,128)(2,1)} %param.4, bf16[2048,256]{0,1:T(8,128)(2,1)} %collective-permute-done.8, bf16[2048,256]{0,1:T(8,128)(2,1)} %collective-permute-done.6, bf16[2048,256]{0,1:T(8,128)(2,1)} %collective-permute-done.4, bf16[2048,256]{0,1:T(8,128)(2,1)} %get-tuple-element.46), kind=kOutput, calls=%fused_computation.75 | convolution fusion | flops 4311744512 | bytes 12582912 | tf_op jit(solution)/shard_map/dot_general | solution.py:92
  325.7 8.4 %convolution_convert_fusion.1 = bf16[2048,1024]{1,0:T(8,128)(2,1)} fusion(bf16[1024,1024]{1,0:T(8,128)(2,1)S(1)} %bitcast.110, bf16[2048,256]{0,1:T(8,128)(2,1)} %collective-permute-done.8, bf16[2048,256]{0,1:T(8,128)(2,1)} %collective-permute-done.6, bf16[2048,256]{0,1:T(8,128)(2,1)} %collective-permute-done.4, bf16[2048,256]{0,1:T(8,128)(2,1)S(1)} %copy-done.22), kind=kOutput, calls=%fused_computation.54 | convolution fusion | flops 4313841664 | bytes 10485760 | tf_op jit(solution)/shard_map/dot_general | solution.py:91
  346.4 14.2 %collective-permute-done.22 = bf16[2048,256]{0,1:T(8,128)(2,1)} collective-permute-done((bf16[2048,256]{0,1:T(8,128)(2,1)}, bf16[2048,256]{0,1:T(8,128)(2,1)}, u32[]{:S(2)}, u32[]{:S(2)}) %collective-permute-start.22) | collective-permute-done | bytes 1048608 | tf_op jit(solution)/shard_map/ppermute | solution.py:37
  361.9 21.0 %collective-permute-done.19 = bf16[2048,256]{0,1:T(8,128)(2,1)S(1)} collective-permute-done((bf16[2048,256]{0,1:T(8,128)(2,1)}, bf16[2048,256]{0,1:T(8,128)(2,1)S(1)}, u32[]{:S(2)}, u32[]{:S(2)}) %collective-permute-start.19) | collective-permute-done | bytes 1048608 | tf_op jit(solution)/shard_map/ppermute | solution.py:37
  383.0 21.4 %collective-permute-done.20 = bf16[2048,256]{0,1:T(8,128)(2,1)S(1)} collective-permute-done((bf16[2048,256]{0,1:T(8,128)(2,1)S(1)}, bf16[2048,256]{0,1:T(8,128)(2,1)S(1)}, u32[]{:S(2)}, u32[]{:S(2)}) %collective-permute-start.20) | collective-permute-done | bytes 1048608 | tf_op jit(solution)/shard_map/ppermute | solution.py:37
  404.5 10.4 %fusion.45 = f32[1024,1024]{1,0:T(8,128)} fusion(bf16[2048,1024]{0,1:T(8,128)(2,1)S(1)} %constant_dynamic-update-slice_fusion, bf16[8192,1024]{1,0:T(8,128)(2,1)} %param.4), kind=kOutput, calls=%fused_computation.72 | convolution fusion | flops 4294967296 | bytes 12582912 | tf_op jit(solution)/shard_map/dot_general | solution.py:92
  414.9 12.0 %collective-permute-done.23 = bf16[2048,256]{0,1:T(8,128)(2,1)S(1)} collective-permute-done((bf16[2048,256]{0,1:T(8,128)(2,1)S(1)}, bf16[2048,256]{0,1:T(8,128)(2,1)S(1)}, u32[]{:S(2)}, u32[]{:S(2)}) %collective-permute-start.23) | collective-permute-done | bytes 1048608 | tf_op jit(solution)/shard_map/ppermute | solution.py:37
  428.9 9.1 %bitcast_add_fusion = f32[1024,1024]{0,1:T(8,128)} fusion(f32[1024,1024]{1,0:T(8,128)} %fusion.45, f32[1024,1024]{0,1:T(8,128)S(1)} %copy-done.29, f32[1024,1024]{0,1:T(8,128)S(1)} %copy-done.28, bf16[2048,1024]{0,1:T(8,128)(2,1)S(1)} %constant_dynamic-update-slice_fusion.4, bf16[8192,1024]{1,0:T(8,128)(2,1)} %param.4), kind=kOutput, calls=%fused_computation.42 | convolution fusion | flops 4298113024 | bytes 25165824 | tf_op jit(solution)/shard_map/dot_general | solution.py:92
  460.2 9.8 %convert_dynamic-update-slice_fusion.1 = bf16[8192,1024]{1,0:T(8,128)(2,1)} fusion(bf16[8192,1024]{1,0:T(8,128)(2,1)} %copy-done, bf16[2048,1024]{0,1:T(8,128)(2,1)} %copy-done.23, bf16[1024,1024]{1,0:T(8,128)(2,1)} %bitcast.111), kind=kOutput, calls=%fused_computation.48 | convolution fusion | flops 4297064448 | bytes 10485760 | tf_op jit(solution)/shard_map/dot_general | solution.py:91
  470.0 6.2 %convert_dynamic-update-slice_fusion = bf16[8192,1024]{1,0:T(8,128)(2,1)} fusion(bf16[8192,1024]{1,0:T(8,128)(2,1)} %convert_dynamic-update-slice_fusion.1, bf16[2048,1024]{0,1:T(8,128)(2,1)S(1)} %copy-done.25, bf16[1024,1024]{1,0:T(8,128)(2,1)S(1)} %bitcast.112), kind=kOutput, calls=%fused_computation.47 | convolution fusion | flops 4297064448 | bytes 10485760 | tf_op jit(solution)/shard_map/dot_general | solution.py:91
  (169 shorter events, 106.7 us)
Async XLA Ops:
  0.7 77.1 %copy-start.26 = (pred[4,4]{0,1:T(4,128)(4,1)}, pred[4,4]{0,1:T(4,128)(4,1)S(1)}, u32[]{:S(2)}) copy-start(pred[4,4]{0,1:T(4,128)(4,1)S(1)} %iota_compare_fusion) | copy-start | bytes 52
  17.9 67.1 %collective-permute-start.12 = (bf16[2048,256]{0,1:T(8,128)(2,1)}, bf16[2048,256]{0,1:T(8,128)(2,1)}, u32[]{:S(2)}, u32[]{:S(2)}) collective-permute-start(bf16[2048,256]{0,1:T(8,128)(2,1)} %get-tuple-element.55), channel_id=1, source_target_pairs={{0,4},{4,0},{8,12},{12,8},{1,5},{5,1},{9,13},{13,9},{2,6},{6,2},{1... | collective-permute-start | bytes 3145736 | tf_op jit(solution)/shard_map/ppermute | solution.py:37
  18.4 67.4 %collective-permute-start.16 = (bf16[2048,256]{0,1:T(8,128)(2,1)}, bf16[2048,256]{0,1:T(8,128)(2,1)}, u32[]{:S(2)}, u32[]{:S(2)}) collective-permute-start(bf16[2048,256]{0,1:T(8,128)(2,1)} %get-tuple-element.56), channel_id=1, source_target_pairs={{0,12},{4,8},{8,4},{12,0},{1,13},{5,9},{9,5},{13,1},{2,14},{6,10},... | collective-permute-start | bytes 3145736 | tf_op jit(solution)/shard_map/ppermute | solution.py:37
  21.0 65.5 %collective-permute-start.14 = (bf16[2048,256]{0,1:T(8,128)(2,1)}, bf16[2048,256]{0,1:T(8,128)(2,1)}, u32[]{:S(2)}, u32[]{:S(2)}) collective-permute-start(bf16[2048,256]{0,1:T(8,128)(2,1)} %get-tuple-element.57), channel_id=1, source_target_pairs={{0,8},{4,12},{8,0},{12,4},{1,9},{5,13},{9,1},{13,5},{2,10},{6,14},... | collective-permute-start | bytes 3145736 | tf_op jit(solution)/shard_map/ppermute | solution.py:37
  31.0 185.3 %collective-permute-start.11 = (bf16[2048,256]{0,1:T(8,128)(2,1)}, bf16[2048,256]{0,1:T(8,128)(2,1)}, u32[]{:S(2)}, u32[]{:S(2)}) collective-permute-start(bf16[2048,256]{0,1:T(8,128)(2,1)} %get-tuple-element.58), channel_id=1, source_target_pairs={{0,12},{4,8},{8,4},{12,0},{1,13},{5,9},{9,5},{13,1},{2,14},{6,10},... | collective-permute-start | bytes 3145736 | tf_op jit(solution)/shard_map/ppermute | solution.py:37
  31.3 185.2 %collective-permute-start.10 = (bf16[2048,256]{0,1:T(8,128)(2,1)}, bf16[2048,256]{0,1:T(8,128)(2,1)}, u32[]{:S(2)}, u32[]{:S(2)}) collective-permute-start(bf16[2048,256]{0,1:T(8,128)(2,1)} %get-tuple-element.59), channel_id=1, source_target_pairs={{0,8},{4,12},{8,0},{12,4},{1,9},{5,13},{9,1},{13,5},{2,10},{6,14},... | collective-permute-start | bytes 3145736 | tf_op jit(solution)/shard_map/ppermute | solution.py:37
  85.1 14.5 %collective-permute-start.3 = (bf16[2048,256]{0,1:T(8,128)(2,1)S(1)}, bf16[2048,256]{0,1:T(8,128)(2,1)S(1)}, u32[]{:S(2)}, u32[]{:S(2)}) collective-permute-start(bf16[2048,256]{0,1:T(8,128)(2,1)S(1)} %copy-done.18), channel_id=1, source_target_pairs={{0,4},{4,0},{8,12},{12,8},{1,5},{5,1},{9,13},{13,9},{2,6},{6,2},{1... | collective-permute-start | bytes 3145736 | tf_op jit(solution)/shard_map/ppermute | solution.py:37
  85.8 48.8 %collective-permute-start.7 = (bf16[2048,256]{0,1:T(8,128)(2,1)S(1)}, bf16[2048,256]{0,1:T(8,128)(2,1)S(1)}, u32[]{:S(2)}, u32[]{:S(2)}) collective-permute-start(bf16[2048,256]{0,1:T(8,128)(2,1)S(1)} %copy-done.17), channel_id=1, source_target_pairs={{0,12},{4,8},{8,4},{12,0},{1,13},{5,9},{9,5},{13,1},{2,14},{6,10},... | collective-permute-start | bytes 3145736 | tf_op jit(solution)/shard_map/ppermute | solution.py:37
  86.5 70.9 %collective-permute-start.5 = (bf16[2048,256]{0,1:T(8,128)(2,1)S(1)}, bf16[2048,256]{0,1:T(8,128)(2,1)S(1)}, u32[]{:S(2)}, u32[]{:S(2)}) collective-permute-start(bf16[2048,256]{0,1:T(8,128)(2,1)S(1)} %copy-done.16), channel_id=1, source_target_pairs={{0,8},{4,12},{8,0},{12,4},{1,9},{5,13},{9,1},{13,5},{2,10},{6,14},... | collective-permute-start | bytes 3145736 | tf_op jit(solution)/shard_map/ppermute | solution.py:37
  99.6 80.0 %collective-permute-start.2 = (bf16[2048,256]{0,1:T(8,128)(2,1)S(1)}, bf16[2048,256]{0,1:T(8,128)(2,1)S(1)}, u32[]{:S(2)}, u32[]{:S(2)}) collective-permute-start(bf16[2048,256]{0,1:T(8,128)(2,1)S(1)} %copy-done.15), channel_id=1, source_target_pairs={{0,12},{4,8},{8,4},{12,0},{1,13},{5,9},{9,5},{13,1},{2,14},{6,10},... | collective-permute-start | bytes 3145736 | tf_op jit(solution)/shard_map/ppermute | solution.py:37
  134.6 67.6 %collective-permute-start.1 = (bf16[2048,256]{0,1:T(8,128)(2,1)S(1)}, bf16[2048,256]{0,1:T(8,128)(2,1)S(1)}, u32[]{:S(2)}, u32[]{:S(2)}) collective-permute-start(bf16[2048,256]{0,1:T(8,128)(2,1)S(1)} %copy-done.14), channel_id=1, source_target_pairs={{0,8},{4,12},{8,0},{12,4},{1,9},{5,13},{9,1},{13,5},{2,10},{6,14},... | collective-permute-start | bytes 3145736 | tf_op jit(solution)/shard_map/ppermute | solution.py:37
  157.5 45.5 %collective-permute-start = (bf16[2048,256]{0,1:T(8,128)(2,1)S(1)}, bf16[2048,256]{0,1:T(8,128)(2,1)S(1)}, u32[]{:S(2)}, u32[]{:S(2)}) collective-permute-start(bf16[2048,256]{0,1:T(8,128)(2,1)S(1)} %get-tuple-element.66), channel_id=1, source_target_pairs={{0,4},{4,0},{8,12},{12,8},{1,5},{5,1},{9,13},{13,9},{2,6},{6,2},{1... | collective-permute-start | bytes 3145736 | tf_op jit(solution)/shard_map/ppermute | solution.py:37
  179.6 37.0 %collective-permute-start.9 = (bf16[2048,256]{0,1:T(8,128)(2,1)}, bf16[2048,256]{0,1:T(8,128)(2,1)S(1)}, u32[]{:S(2)}, u32[]{:S(2)}) collective-permute-start(bf16[2048,256]{0,1:T(8,128)(2,1)} %get-tuple-element.60), channel_id=1, source_target_pairs={{0,4},{4,0},{8,12},{12,8},{1,5},{5,1},{9,13},{13,9},{2,6},{6,2},{1... | collective-permute-start | bytes 3145736 | tf_op jit(solution)/shard_map/ppermute | solution.py:37
  202.2 67.5 %collective-permute-start.17 = (bf16[2048,256]{0,1:T(8,128)(2,1)}, bf16[2048,256]{0,1:T(8,128)(2,1)}, u32[]{:S(2)}, u32[]{:S(2)}) collective-permute-start(bf16[2048,256]{0,1:T(8,128)(2,1)} %get-tuple-element.42), channel_id=1, source_target_pairs={{0,12},{4,8},{8,4},{12,0},{1,13},{5,9},{9,5},{13,1},{2,14},{6,10},... | collective-permute-start | bytes 3145736 | tf_op jit(solution)/shard_map/ppermute | solution.py:37
  202.9 67.3 %collective-permute-start.15 = (bf16[2048,256]{0,1:T(8,128)(2,1)}, bf16[2048,256]{0,1:T(8,128)(2,1)}, u32[]{:S(2)}, u32[]{:S(2)}) collective-permute-start(bf16[2048,256]{0,1:T(8,128)(2,1)} %get-tuple-element.43), channel_id=1, source_target_pairs={{0,8},{4,12},{8,0},{12,4},{1,9},{5,13},{9,1},{13,5},{2,10},{6,14},... | collective-permute-start | bytes 3145736 | tf_op jit(solution)/shard_map/ppermute | solution.py:37
  216.3 53.9 %collective-permute-start.13 = (bf16[2048,256]{0,1:T(8,128)(2,1)}, bf16[2048,256]{0,1:T(8,128)(2,1)}, u32[]{:S(2)}, u32[]{:S(2)}) collective-permute-start(bf16[2048,256]{0,1:T(8,128)(2,1)} %get-tuple-element.44), channel_id=1, source_target_pairs={{0,4},{4,0},{8,12},{12,8},{1,5},{5,1},{9,13},{13,9},{2,6},{6,2},{1... | collective-permute-start | bytes 3145736 | tf_op jit(solution)/shard_map/ppermute | solution.py:37
  244.3 13.5 %collective-permute-start.24 = (f32[64,4,256]{2,0,1:T(8,128)S(1)}, f32[64,4,256]{2,0,1:T(8,128)S(1)}, u32[]{:S(2)}, u32[]{:S(2)}) collective-permute-start(f32[64,4,256]{2,0,1:T(8,128)S(1)} %bitcast.127), channel_id=1, source_target_pairs={{0,1},{1,0},{2,3},{3,2},{4,5},{5,4},{6,7},{7,6},{8,9},{9,8},{10,11... | collective-permute-start | bytes 786440 | tf_op jit(solution)/shard_map/ppermute | solution.py:48
  246.6 21.0 %collective-permute-start.25 = (f32[64,4,256]{2,0,1:T(8,128)S(1)}, f32[64,4,256]{2,0,1:T(8,128)S(1)}, u32[]{:S(2)}, u32[]{:S(2)}) collective-permute-start(f32[64,4,256]{2,0,1:T(8,128)S(1)} %bitcast.126), channel_id=1, source_target_pairs={{0,2},{1,3},{2,0},{3,1},{4,6},{5,7},{6,4},{7,5},{8,10},{9,11},{10,... | collective-permute-start | bytes 786440 | tf_op jit(solution)/shard_map/ppermute | solution.py:48
  257.8 9.8 %collective-permute-start.26 = (f32[64,4,256]{2,0,1:T(8,128)S(1)}, f32[64,4,256]{2,0,1:T(8,128)S(1)}, u32[]{:S(2)}, u32[]{:S(2)}) collective-permute-start(f32[64,4,256]{2,0,1:T(8,128)S(1)} %bitcast.125), channel_id=1, source_target_pairs={{0,3},{1,2},{2,1},{3,0},{4,7},{5,6},{6,5},{7,4},{8,11},{9,10},{10,... | collective-permute-start | bytes 786440 | tf_op jit(solution)/shard_map/ppermute | solution.py:48
  267.6 25.8 %collective-permute-start.8 = (bf16[2048,256]{0,1:T(8,128)(2,1)}, bf16[2048,256]{0,1:T(8,128)(2,1)}, u32[]{:S(2)}, u32[]{:S(2)}) collective-permute-start(bf16[2048,256]{0,1:T(8,128)(2,1)} %get-tuple-element.47), channel_id=1, source_target_pairs={{0,12},{4,8},{8,4},{12,0},{1,13},{5,9},{9,5},{13,1},{2,14},{6,10},... | collective-permute-start | bytes 3145736 | tf_op jit(solution)/shard_map/ppermute | solution.py:37
  267.6 48.0 %collective-permute-start.6 = (bf16[2048,256]{0,1:T(8,128)(2,1)}, bf16[2048,256]{0,1:T(8,128)(2,1)}, u32[]{:S(2)}, u32[]{:S(2)}) collective-permute-start(bf16[2048,256]{0,1:T(8,128)(2,1)} %get-tuple-element.48), channel_id=1, source_target_pairs={{0,8},{4,12},{8,0},{12,4},{1,9},{5,13},{9,1},{13,5},{2,10},{6,14},... | collective-permute-start | bytes 3145736 | tf_op jit(solution)/shard_map/ppermute | solution.py:37
  269.8 45.9 %collective-permute-start.4 = (bf16[2048,256]{0,1:T(8,128)(2,1)}, bf16[2048,256]{0,1:T(8,128)(2,1)}, u32[]{:S(2)}, u32[]{:S(2)}) collective-permute-start(bf16[2048,256]{0,1:T(8,128)(2,1)} %get-tuple-element.49), channel_id=1, source_target_pairs={{0,4},{4,0},{8,12},{12,8},{1,5},{5,1},{9,13},{13,9},{2,6},{6,2},{1... | collective-permute-start | bytes 3145736 | tf_op jit(solution)/shard_map/ppermute | solution.py:37
  334.1 8.5 %collective-permute-start.21 = (bf16[2048,256]{0,1:T(8,128)(2,1)}, bf16[2048,256]{0,1:T(8,128)(2,1)}, u32[]{:S(2)}, u32[]{:S(2)}) collective-permute-start(bf16[2048,256]{0,1:T(8,128)(2,1)} %get-tuple-element.28), channel_id=1, source_target_pairs={{0,4},{4,0},{8,12},{12,8},{1,5},{5,1},{9,13},{13,9},{2,6},{6,2},{1... | collective-permute-start | bytes 3145736 | tf_op jit(solution)/shard_map/ppermute | solution.py:37
  334.3 26.3 %collective-permute-start.22 = (bf16[2048,256]{0,1:T(8,128)(2,1)}, bf16[2048,256]{0,1:T(8,128)(2,1)}, u32[]{:S(2)}, u32[]{:S(2)}) collective-permute-start(bf16[2048,256]{0,1:T(8,128)(2,1)} %get-tuple-element.29), channel_id=1, source_target_pairs={{0,8},{4,12},{8,0},{12,4},{1,9},{5,13},{9,1},{13,5},{2,10},{6,14},... | collective-permute-start | bytes 3145736 | tf_op jit(solution)/shard_map/ppermute | solution.py:37
  334.7 27.1 %collective-permute-start.18 = (bf16[2048,256]{0,1:T(8,128)(2,1)}, bf16[2048,256]{0,1:T(8,128)(2,1)S(1)}, u32[]{:S(2)}, u32[]{:S(2)}) collective-permute-start(bf16[2048,256]{0,1:T(8,128)(2,1)} %get-tuple-element.24), channel_id=1, source_target_pairs={{0,4},{4,0},{8,12},{12,8},{1,5},{5,1},{9,13},{13,9},{2,6},{6,2},{1... | collective-permute-start | bytes 3145736 | tf_op jit(solution)/shard_map/ppermute | solution.py:37
  334.7 48.2 %collective-permute-start.19 = (bf16[2048,256]{0,1:T(8,128)(2,1)}, bf16[2048,256]{0,1:T(8,128)(2,1)S(1)}, u32[]{:S(2)}, u32[]{:S(2)}) collective-permute-start(bf16[2048,256]{0,1:T(8,128)(2,1)} %get-tuple-element.25), channel_id=1, source_target_pairs={{0,8},{4,12},{8,0},{12,4},{1,9},{5,13},{9,1},{13,5},{2,10},{6,14},... | collective-permute-start | bytes 3145736 | tf_op jit(solution)/shard_map/ppermute | solution.py:37
  342.0 72.9 %copy-start = (bf16[8192,1024]{1,0:T(8,128)(2,1)}, bf16[8192,1024]{1,0:T(8,128)(2,1)S(1)}, u32[]{:S(2)}) copy-start(bf16[8192,1024]{1,0:T(8,128)(2,1)S(1)} %constant_dynamic-update-slice_fusion.8) | copy-start | bytes 50331652
  342.4 62.1 %collective-permute-start.20 = (bf16[2048,256]{0,1:T(8,128)(2,1)S(1)}, bf16[2048,256]{0,1:T(8,128)(2,1)S(1)}, u32[]{:S(2)}, u32[]{:S(2)}) collective-permute-start(bf16[2048,256]{0,1:T(8,128)(2,1)S(1)} %copy-done.19), channel_id=1, source_target_pairs={{0,12},{4,8},{8,4},{12,0},{1,13},{5,9},{9,5},{13,1},{2,14},{6,10},... | collective-permute-start | bytes 3145736 | tf_op jit(solution)/shard_map/ppermute | solution.py:37
  344.1 82.8 %collective-permute-start.23 = (bf16[2048,256]{0,1:T(8,128)(2,1)S(1)}, bf16[2048,256]{0,1:T(8,128)(2,1)S(1)}, u32[]{:S(2)}, u32[]{:S(2)}) collective-permute-start(bf16[2048,256]{0,1:T(8,128)(2,1)S(1)} %copy-done.20), channel_id=1, source_target_pairs={{0,12},{4,8},{8,4},{12,0},{1,13},{5,9},{9,5},{13,1},{2,14},{6,10},... | collective-permute-start | bytes 3145736 | tf_op jit(solution)/shard_map/ppermute | solution.py:37
  455.7 20.8 %collective-permute-start.27 = (f32[64,4,256]{2,0,1:T(8,128)S(1)}, f32[64,4,256]{2,0,1:T(8,128)S(1)}, u32[]{:S(2)}, u32[]{:S(2)}) collective-permute-start(f32[64,4,256]{2,0,1:T(8,128)S(1)} %bitcast.124), channel_id=1, source_target_pairs={{0,1},{1,0},{2,3},{3,2},{4,5},{5,4},{6,7},{7,6},{8,9},{9,8},{10,11... | collective-permute-start | bytes 786440 | tf_op jit(solution)/shard_map/ppermute | solution.py:48
  456.0 21.8 %collective-permute-start.28 = (f32[64,4,256]{2,0,1:T(8,128)S(1)}, f32[64,4,256]{2,0,1:T(8,128)S(1)}, u32[]{:S(2)}, u32[]{:S(2)}) collective-permute-start(f32[64,4,256]{2,0,1:T(8,128)S(1)} %bitcast.123), channel_id=1, source_target_pairs={{0,2},{1,3},{2,0},{3,1},{4,6},{5,7},{6,4},{7,5},{8,10},{9,11},{10,... | collective-permute-start | bytes 786440 | tf_op jit(solution)/shard_map/ppermute | solution.py:48
  459.4 18.4 %collective-permute-start.29 = (f32[64,4,256]{2,0,1:T(8,128)S(1)}, f32[64,4,256]{2,0,1:T(8,128)S(1)}, u32[]{:S(2)}, u32[]{:S(2)}) collective-permute-start(f32[64,4,256]{2,0,1:T(8,128)S(1)} %bitcast.122), channel_id=1, source_target_pairs={{0,3},{1,2},{2,1},{3,0},{4,7},{5,6},{6,5},{7,4},{8,11},{9,10},{10,... | collective-permute-start | bytes 786440 | tf_op jit(solution)/shard_map/ppermute | solution.py:48
  (28 other events, 435.3 us)

commit v11 on v10

--- a/solution.py
+++ b/solution.py
@@ -49,6 +49,15 @@
     return acc
 
 
+def second_gradient(gs_acc, order, n_dev, blk_local, sub, bs, grad_scale):
+    eye = jnp.eye(blk_local, dtype=jnp.bool_)
+    gs6 = gs_acc.reshape(n_dev, blk_local, blk_local, sub, blk_local, bs)
+    gsd = jnp.sum(jnp.where(eye[None, :, None, None, :, None], gs6, 0.0), axis=4)
+    gsd = jnp.take(gsd, order, axis=0)
+    second_term = gsd.transpose(3, 0, 2, 1, 4).reshape(bs, blk_local, bs) * grad_scale
+    return dp_reduce_scatter(second_term)
+
+
 def shards(tokens, cotangent, w_first, w_second):
     tok_rows = tokens.shape[0]
     blk_local, bs, _ = w_first.shape
@@ -88,6 +97,9 @@
             grad_tokens = lax.dynamic_update_slice(grad_tokens, done[0], (done[2], 0))
             gf_acc = done[1] if gf_acc is None else gf_acc + done[1]
         returned = jnp.concatenate(exchange(masked, n_dev), axis=1)
+        if k + 1 == CHUNKS:
+            grad_second = second_gradient(gs_acc, order, n_dev, blk_local, sub, bs, grad_scale)
+            returned, grad_second = lax.optimization_barrier((returned, grad_second))
         gt = jnp.dot(returned, w1tp, preferred_element_type=jnp.float32).astype(jnp.bfloat16)
         gf = lax.dot_general(
             x, returned, (((0,), (0,)), ((), ())), preferred_element_type=jnp.float32
@@ -97,12 +109,6 @@
         grad_tokens = lax.dynamic_update_slice(grad_tokens, gt, (at, 0))
         gf_acc = gf if gf_acc is None else gf_acc + gf
 
-    gs6 = gs_acc.reshape(n_dev, blk_local, blk_local, sub, blk_local, bs)
-    gsd = jnp.sum(jnp.where(eye[None, :, None, None, :, None], gs6, 0.0), axis=4)
-    gsd = jnp.take(gsd, order, axis=0)
-    second_term = gsd.transpose(3, 0, 2, 1, 4).reshape(bs, blk_local, bs) * grad_scale
-    grad_second = dp_reduce_scatter(second_term)
-    gf_acc, grad_second = lax.optimization_barrier((gf_acc, grad_second))
     gf6 = gf_acc.reshape(blk_local, bs, n_dev, blk_local, blk_local, sub)
     gfd = jnp.sum(jnp.where(eye[:, None, None, None, :, None], gf6, 0.0), axis=4)
     gfd = jnp.take(gfd, order, axis=2)

time: 486 us -> 470 us (0.967)
  waiting for transfers between devices: 201 us -> 187 us
  matrix products: 170 us -> 162 us
    ppermute x24, waiting for transfers between devices: 185 us -> 171 us  [exchange(): lax.ppermute(pieces[m], 'tensor', [(i, i ^ m) for i in range(n_dev)])]
    dot_general x4, matrix products: 39.4 us -> 31.4 us  [shards(): lax.dot_general(x, returned, (((0,), (0,)), ((), ())), preferred_element_...]
    unnamed x70 -> x75, local copies, waits for them, and re-layouts: 12.5 us -> 4.99 us
    dynamic_update_slice x2, local copies, waits for them, and re-layouts: 1.15 us -> 7.24 us  [shards(): grad_tokens = lax.dynamic_update_slice(grad_tokens, done[0], (done[2], 0))]
  transfers between devices with their start and end apart: 30 -> 30, of which waited for: 13 -> 12; matrix products, arithmetic and copies ran while one was open for 37% -> 42% of each run, Pallas kernels for 0% -> 0%
where the time goes in v11:
time: 470 us; the launch traced here: 463 us
  waiting for transfers between devices  187 us (40%)
  matrix products  162 us (34%)
  local copies, waits for them, and re-layouts  51.5 us (11%)
  other arithmetic  32.9 us (7%)
  starting transfers between devices  28.2 us (6%)
    ppermute x24, waiting for transfers between devices, exchange(): lax.ppermute(pieces[m], 'tensor', [(i, i ^ m) for i in range(n_dev)])  171 us
    dot_general x4, matrix products, shards(): lax.dot_general(active, cot, (((0,), (0,)), ((), ())), preferred_element_...  34.2 us
    dot_general x4, matrix products, shards(): backed = jnp.dot(cot, w2p, preferred_element_type=jnp.float32)  33.3 us
    dot_general x4, matrix products, shards(): jnp.dot(returned, w1tp, preferred_element_type=jnp.float32)  32.8 us
    dot_general x4, matrix products, shards(): lax.dot_general(x, returned, (((0,), (0,)), ((), ())), preferred_element_...  31.4 us
    dot_general x4, matrix products, shards(): jnp.dot(x, w1p, preferred_element_type=jnp.float32).astype(jnp.bfloat16)  29.9 us
    ppermute x24, starting transfers between devices, exchange(): lax.ppermute(pieces[m], 'tensor', [(i, i ^ m) for i in range(n_dev)])  16.8 us
    slice x4, other arithmetic, shards(): hidden[:, m * part:(m + 1) * part]  15.8 us
  transfers between devices with their start and end apart: 30, of which 12 were waited for; matrix products, arithmetic and copies ran while one was open for 42% of the time, Pallas kernels for 0%

profile of v11, /device:TPU:0, one launch (start us, length us, event | category | flops | bytes accessed | tf_op | source)
XLA Modules:
  0.0 462.7 jit_solution(12673520385938558002)
XLA Ops:
  8.9 7.2 %convert_bitcast_fusion = bf16[2048,1024]{0,1:T(8,128)(2,1)S(1)} fusion(bf16[1024,1024]{0,1:T(8,128)(2,1)S(1)} %bitcast.117, bf16[8192,1024]{1,0:T(8,128)(2,1)} %param.4), kind=kOutput, calls=%fused_computation.50 | convolution fusion | flops 4297064448 | bytes 10485760 | tf_op jit(solution)/shard_map/dot_general | solution.py:83
  22.0 7.0 %convert_bitcast_fusion.1 = bf16[2048,1024]{0,1:T(8,128)(2,1)S(1)} fusion(bf16[1024,1024]{0,1:T(8,128)(2,1)S(1)} %bitcast.118, bf16[8192,1024]{1,0:T(8,128)(2,1)} %param.4), kind=kOutput, calls=%fused_computation.51 | convolution fusion | flops 4297064448 | bytes 10485760 | tf_op jit(solution)/shard_map/dot_general | solution.py:83
  32.1 7.0 %convert_bitcast_fusion.2 = bf16[2048,1024]{0,1:T(8,128)(2,1)S(1)} fusion(bf16[1024,1024]{0,1:T(8,128)(2,1)S(1)} %bitcast.119, bf16[8192,1024]{1,0:T(8,128)(2,1)} %param.4), kind=kOutput, calls=%fused_computation.52 | convolution fusion | flops 4297064448 | bytes 10485760 | tf_op jit(solution)/shard_map/dot_general | solution.py:83
  39.2 8.6 %convert_bitcast_fusion.3 = bf16[2048,1024]{0,1:T(8,128)(2,1)S(1)} fusion(bf16[1024,1024]{0,1:T(8,128)(2,1)S(1)} %bitcast.120, bf16[8192,1024]{1,0:T(8,128)(2,1)} %param.4), kind=kOutput, calls=%fused_computation.53 | convolution fusion | flops 4297064448 | bytes 10485760 | tf_op jit(solution)/shard_map/dot_general | solution.py:83
  48.3 9.3 %convolution_bitcast_fusion = bf16[2048,1024]{0,1:T(8,128)(2,1)} fusion(bf16[1024,1024]{0,1:T(8,128)(2,1)S(1)} %bitcast.113, bf16[8192,1024]{1,0:T(8,128)(2,1)} %param.5), kind=kOutput, calls=%fused_computation.4 | convolution fusion | flops 4294967296 | bytes 10485760 | tf_op jit(solution)/shard_map/dot_general | solution.py:84
  57.6 8.6 %convolution_bitcast_fusion.1 = bf16[2048,1024]{0,1:T(8,128)(2,1)} fusion(bf16[1024,1024]{0,1:T(8,128)(2,1)S(1)} %bitcast.114, bf16[8192,1024]{1,0:T(8,128)(2,1)} %param.5), kind=kOutput, calls=%fused_computation.5 | convolution fusion | flops 4294967296 | bytes 10485760 | tf_op jit(solution)/shard_map/dot_general | solution.py:84
  66.2 8.3 %convolution_bitcast_fusion.2 = bf16[2048,1024]{0,1:T(8,128)(2,1)} fusion(bf16[1024,1024]{0,1:T(8,128)(2,1)S(1)} %bitcast.115, bf16[8192,1024]{1,0:T(8,128)(2,1)} %param.5), kind=kOutput, calls=%fused_computation.6 | convolution fusion | flops 4294967296 | bytes 10485760 | tf_op jit(solution)/shard_map/dot_general | solution.py:84
  77.8 7.1 %convolution_bitcast_fusion.3 = bf16[2048,1024]{0,1:T(8,128)(2,1)S(1)} fusion(bf16[1024,1024]{0,1:T(8,128)(2,1)S(1)} %bitcast.116, bf16[8192,1024]{1,0:T(8,128)(2,1)} %param.5), kind=kOutput, calls=%fused_computation.7 | convolution fusion | flops 4294967296 | bytes 10485760 | tf_op jit(solution)/shard_map/dot_general | solution.py:84
  91.7 7.8 %fusion.7 = f32[1024,1024]{1,0:T(8,128)S(1)} fusion(bf16[2048,256]{0,1:T(8,128)(2,1)} %collective-permute-done.16, bf16[2048,256]{0,1:T(8,128)(2,1)} %collective-permute-done.14, bf16[2048,256]{0,1:T(8,128)(2,1)} %collective-permute-done.12, bf16[2048,256]{0,1:T(8,128)(2,1)S(1)} %get-tuple-element.40, bf16[8192,1024]{1,0:T(8,128)(2,1)} %param.5), kind=kOutput, calls=%fused_computation.20 | convolution fusion | flops 4315938816 | bytes 12582912 | tf_op jit(solution)/shard_map/dot_general | solution.py:91
  100.4 34.2 %collective-permute-done.7 = bf16[2048,256]{0,1:T(8,128)(2,1)S(1)} collective-permute-done((bf16[2048,256]{0,1:T(8,128)(2,1)S(1)}, bf16[2048,256]{0,1:T(8,128)(2,1)S(1)}, u32[]{:S(2)}, u32[]{:S(2)}) %collective-permute-start.7) | collective-permute-done | bytes 1048608 | tf_op jit(solution)/shard_map/ppermute | solution.py:37
  135.8 21.7 %collective-permute-done.5 = bf16[2048,256]{0,1:T(8,128)(2,1)S(1)} collective-permute-done((bf16[2048,256]{0,1:T(8,128)(2,1)S(1)}, bf16[2048,256]{0,1:T(8,128)(2,1)S(1)}, u32[]{:S(2)}, u32[]{:S(2)}) %collective-permute-start.5) | collective-permute-done | bytes 1048608 | tf_op jit(solution)/shard_map/ppermute | solution.py:37
  161.5 6.7 %fusion = f32[1024,1024]{1,0:T(8,128)S(1)} fusion(bf16[2048,256]{0,1:T(8,128)(2,1)S(1)} %collective-permute-done.7, bf16[2048,256]{0,1:T(8,128)(2,1)S(1)} %collective-permute-done.5, bf16[2048,256]{0,1:T(8,128)(2,1)S(1)} %collective-permute-done.3, bf16[2048,256]{0,1:T(8,128)(2,1)S(1)} %get-tuple-element.45, bf16[8192,1024]{1,0:T(8,128)(2,1)} %param.5), kind=kOutput, calls=%fused_computation.12 | convolution fusion | flops 4315938816 | bytes 12582912 | tf_op jit(solution)/shard_map/dot_general | solution.py:91
  168.2 11.3 %collective-permute-done.2 = bf16[2048,256]{0,1:T(8,128)(2,1)S(1)} collective-permute-done((bf16[2048,256]{0,1:T(8,128)(2,1)S(1)}, bf16[2048,256]{0,1:T(8,128)(2,1)S(1)}, u32[]{:S(2)}, u32[]{:S(2)}) %collective-permute-start.2) | collective-permute-done | bytes 1048608 | tf_op jit(solution)/shard_map/ppermute | solution.py:37
  179.8 22.5 %collective-permute-done.1 = bf16[2048,256]{0,1:T(8,128)(2,1)S(1)} collective-permute-done((bf16[2048,256]{0,1:T(8,128)(2,1)S(1)}, bf16[2048,256]{0,1:T(8,128)(2,1)S(1)}, u32[]{:S(2)}, u32[]{:S(2)}) %collective-permute-start.1) | collective-permute-done | bytes 1048608 | tf_op jit(solution)/shard_map/ppermute | solution.py:37
  207.4 8.8 %fusion.14 = f32[1024,1024]{1,0:T(8,128)} fusion(bf16[2048,256]{0,1:T(8,128)(2,1)S(1)} %collective-permute-done.2, bf16[2048,256]{0,1:T(8,128)(2,1)S(1)} %collective-permute-done.1, bf16[2048,256]{0,1:T(8,128)(2,1)S(1)} %collective-permute-done, bf16[2048,256]{0,1:T(8,128)(2,1)S(1)} %get-tuple-element.50, bf16[8192,1024]{1,0:T(8,128)(2,1)} %param.5), kind=kOutput, calls=%fused_computation.28 | convolution fusion | flops 4315938816 | bytes 12582912 | tf_op jit(solution)/shard_map/dot_general | solution.py:91
  220.5 10.9 %add_add_fusion = f32[1024,1024]{1,0:T(8,128)} fusion(f32[1024,1024]{1,0:T(8,128)} %fusion.14, f32[1024,1024]{1,0:T(8,128)S(1)} %fusion, f32[1024,1024]{1,0:T(8,128)S(1)} %fusion.7, bf16[8192,1024]{1,0:T(8,128)(2,1)} %param.5, bf16[2048,256]{0,1:T(8,128)(2,1)} %collective-permute-done.11, bf16[2048,256]{0,1:T(8,128)(2,1)} %collective-permute-done.10, ...), kind=kOutput, calls=%fused_computation.48 | convolution fusion | flops 4319084544 | bytes 25165824 | tf_op jit(solution)/shard_map/dot_general | solution.py:91
  231.4 5.7 %reshape.99 = f32[4,4,4,16,4,256]{5,4,3,2,1,0:T(4,128)} reshape(f32[1024,1024]{1,0:T(8,128)} %add_add_fusion) | data formatting | bytes 8388608 | tf_op jit(solution)/shard_map/reshape | solution.py:54
  249.2 8.4 %collective-permute-done.24 = f32[64,4,256]{2,0,1:T(8,128)S(1)} collective-permute-done((f32[64,4,256]{2,0,1:T(8,128)S(1)}, f32[64,4,256]{2,0,1:T(8,128)S(1)}, u32[]{:S(2)}, u32[]{:S(2)}) %collective-permute-start.24) | collective-permute-done | bytes 262176 | tf_op jit(solution)/shard_map/ppermute | solution.py:48
  261.4 6.2 %collective-permute-done.25 = f32[64,4,256]{2,0,1:T(8,128)S(1)} collective-permute-done((f32[64,4,256]{2,0,1:T(8,128)S(1)}, f32[64,4,256]{2,0,1:T(8,128)S(1)}, u32[]{:S(2)}, u32[]{:S(2)}) %collective-permute-start.25) | collective-permute-done | bytes 262176 | tf_op jit(solution)/shard_map/ppermute | solution.py:48
  270.3 8.7 %convolution_convert_fusion = bf16[2048,1024]{1,0:T(8,128)(2,1)} fusion(bf16[1024,1024]{1,0:T(8,128)(2,1)S(1)} %bitcast.109, bf16[2048,256]{0,1:T(8,128)(2,1)} %collective-permute-done.17, bf16[2048,256]{0,1:T(8,128)(2,1)} %collective-permute-done.15, bf16[2048,256]{0,1:T(8,128)(2,1)} %collective-permute-done.13, bf16[2048,256]{0,1:T(8,128)(2,1)S(1)} %copy-done.20), kind=kOutput, calls=%fused_computation.54 | convolution fusion | flops 4313841664 | bytes 10485760 | tf_op jit(solution)/shard_map/dot_general | solution.py:103
  279.0 8.6 %fusion.51 = f32[1024,1024]{0,1:T(8,128)} fusion(bf16[8192,1024]{1,0:T(8,128)(2,1)S(1)} %bitcast.129, bf16[2048,256]{0,1:T(8,128)(2,1)} %collective-permute-done.17, bf16[2048,256]{0,1:T(8,128)(2,1)} %collective-permute-done.15, bf16[2048,256]{0,1:T(8,128)(2,1)} %collective-permute-done.13, bf16[2048,256]{0,1:T(8,128)(2,1)S(1)} %copy-done.20), kind=kOutput, calls=%fused_computation.77 | convolution fusion | flops 4311744512 | bytes 12582912 | tf_op jit(solution)/shard_map/dot_general | solution.py:104
  293.1 22.3 %collective-permute-done.6 = bf16[2048,256]{0,1:T(8,128)(2,1)} collective-permute-done((bf16[2048,256]{0,1:T(8,128)(2,1)S(1)}, bf16[2048,256]{0,1:T(8,128)(2,1)}, u32[]{:S(2)}, u32[]{:S(2)}) %collective-permute-start.6) | collective-permute-done | bytes 1048608 | tf_op jit(solution)/shard_map/ppermute | solution.py:37
  315.4 8.1 %fusion.48 = f32[1024,1024]{0,1:T(8,128)} fusion(bf16[8192,1024]{1,0:T(8,128)(2,1)S(1)} %bitcast.129, bf16[2048,256]{0,1:T(8,128)(2,1)S(1)} %collective-permute-done.8, bf16[2048,256]{0,1:T(8,128)(2,1)} %collective-permute-done.6, bf16[2048,256]{0,1:T(8,128)(2,1)} %collective-permute-done.4, bf16[2048,256]{0,1:T(8,128)(2,1)S(1)} %copy-done.21), kind=kOutput, calls=%fused_computation.76 | convolution fusion | flops 4311744512 | bytes 12582912 | tf_op jit(solution)/shard_map/dot_general | solution.py:104
  323.5 8.0 %convolution_convert_fusion.1 = bf16[2048,1024]{1,0:T(8,128)(2,1)} fusion(bf16[1024,1024]{1,0:T(8,128)(2,1)S(1)} %bitcast.110, bf16[2048,256]{0,1:T(8,128)(2,1)S(1)} %collective-permute-done.8, bf16[2048,256]{0,1:T(8,128)(2,1)} %collective-permute-done.6, bf16[2048,256]{0,1:T(8,128)(2,1)} %collective-permute-done.4, bf16[2048,256]{0,1:T(8,128)(2,1)S(1)} %copy-done.21), kind=kOutput, calls=%fused_computation.55 | convolution fusion | flops 4313841664 | bytes 10485760 | tf_op jit(solution)/shard_map/dot_general | solution.py:103
  333.2 6.6 %broadcast_in_dim.150 = bf16[8192,1024]{1,0:T(8,128)(2,1)} broadcast(bf16[]{:T(256)} %constant.85.clone.1), dimensions={} | broadcast | bytes 16777218 | tf_op jit(solution)/shard_map/broadcast_in_dim | solution.py:78
  347.4 13.2 %collective-permute-done.23 = bf16[2048,256]{0,1:T(8,128)(2,1)} collective-permute-done((bf16[2048,256]{0,1:T(8,128)(2,1)}, bf16[2048,256]{0,1:T(8,128)(2,1)}, u32[]{:S(2)}, u32[]{:S(2)}) %collective-permute-start.23) | collective-permute-done | bytes 1048608 | tf_op jit(solution)/shard_map/ppermute | solution.py:37
  363.2 19.5 %collective-permute-done.19 = bf16[2048,256]{0,1:T(8,128)(2,1)S(1)} collective-permute-done((bf16[2048,256]{0,1:T(8,128)(2,1)}, bf16[2048,256]{0,1:T(8,128)(2,1)S(1)}, u32[]{:S(2)}, u32[]{:S(2)}) %collective-permute-start.19) | collective-permute-done | bytes 1048608 | tf_op jit(solution)/shard_map/ppermute | solution.py:37
  382.8 22.5 %collective-permute-done.20 = bf16[2048,256]{0,1:T(8,128)(2,1)S(1)} collective-permute-done((bf16[2048,256]{0,1:T(8,128)(2,1)S(1)}, bf16[2048,256]{0,1:T(8,128)(2,1)S(1)}, u32[]{:S(2)}, u32[]{:S(2)}) %collective-permute-start.20) | collective-permute-done | bytes 1048608 | tf_op jit(solution)/shard_map/ppermute | solution.py:37
  407.3 6.4 %fusion.45 = f32[1024,1024]{1,0:T(8,128)S(1)} fusion(bf16[2048,1024]{0,1:T(8,128)(2,1)S(1)} %constant_dynamic-update-slice_fusion, bf16[8192,1024]{1,0:T(8,128)(2,1)} %param.4), kind=kOutput, calls=%fused_computation.73 | convolution fusion | flops 4294967296 | bytes 12582912 | tf_op jit(solution)/shard_map/dot_general | solution.py:104
  413.8 8.3 %bitcast_add_fusion = f32[1024,1024]{0,1:T(8,128)} fusion(f32[1024,1024]{1,0:T(8,128)S(1)} %fusion.45, f32[1024,1024]{0,1:T(8,128)S(1)} %copy-done.29, f32[1024,1024]{0,1:T(8,128)S(1)} %copy-done.28, bf16[2048,1024]{0,1:T(8,128)(2,1)S(1)} %pad_maximum_fusion.2, bf16[8192,1024]{1,0:T(8,128)(2,1)} %param.4), kind=kOutput, calls=%fused_computation.43 | convolution fusion | flops 4298113024 | bytes 25165824 | tf_op jit(solution)/shard_map/dot_general | solution.py:104
  444.3 9.9 %convert_dynamic-update-slice_fusion.1 = bf16[8192,1024]{1,0:T(8,128)(2,1)} fusion(bf16[8192,1024]{1,0:T(8,128)(2,1)} %constant_dynamic-update-slice_fusion.4, bf16[2048,1024]{0,1:T(8,128)(2,1)} %copy-done.25, bf16[1024,1024]{1,0:T(8,128)(2,1)} %bitcast.111), kind=kOutput, calls=%fused_computation.49 | convolution fusion | flops 4297064448 | bytes 10485760 | tf_op jit(solution)/shard_map/dot_general | solution.py:103
  454.2 6.2 %convert_dynamic-update-slice_fusion = bf16[8192,1024]{1,0:T(8,128)(2,1)} fusion(bf16[8192,1024]{1,0:T(8,128)(2,1)} %convert_dynamic-update-slice_fusion.1, bf16[2048,1024]{0,1:T(8,128)(2,1)S(1)} %copy-done.4, bf16[1024,1024]{1,0:T(8,128)(2,1)S(1)} %bitcast.112), kind=kOutput, calls=%fused_computation.46 | convolution fusion | flops 4297064448 | bytes 10485760 | tf_op jit(solution)/shard_map/dot_general | solution.py:103
  (175 shorter events, 105.3 us)
Async XLA Ops:
  0.7 77.0 %copy-start.26 = (pred[4,4]{0,1:T(4,128)(4,1)}, pred[4,4]{0,1:T(4,128)(4,1)S(1)}, u32[]{:S(2)}) copy-start(pred[4,4]{0,1:T(4,128)(4,1)S(1)} %iota_compare_fusion) | copy-start | bytes 52
  18.0 67.0 %collective-permute-start.12 = (bf16[2048,256]{0,1:T(8,128)(2,1)}, bf16[2048,256]{0,1:T(8,128)(2,1)}, u32[]{:S(2)}, u32[]{:S(2)}) collective-permute-start(bf16[2048,256]{0,1:T(8,128)(2,1)} %get-tuple-element.55), channel_id=1, source_target_pairs={{0,4},{4,0},{8,12},{12,8},{1,5},{5,1},{9,13},{13,9},{2,6},{6,2},{1... | collective-permute-start | bytes 3145736 | tf_op jit(solution)/shard_map/ppermute | solution.py:37
  18.4 67.3 %collective-permute-start.16 = (bf16[2048,256]{0,1:T(8,128)(2,1)}, bf16[2048,256]{0,1:T(8,128)(2,1)}, u32[]{:S(2)}, u32[]{:S(2)}) collective-permute-start(bf16[2048,256]{0,1:T(8,128)(2,1)} %get-tuple-element.56), channel_id=1, source_target_pairs={{0,12},{4,8},{8,4},{12,0},{1,13},{5,9},{9,5},{13,1},{2,14},{6,10},... | collective-permute-start | bytes 3145736 | tf_op jit(solution)/shard_map/ppermute | solution.py:37
  21.0 65.5 %collective-permute-start.14 = (bf16[2048,256]{0,1:T(8,128)(2,1)}, bf16[2048,256]{0,1:T(8,128)(2,1)}, u32[]{:S(2)}, u32[]{:S(2)}) collective-permute-start(bf16[2048,256]{0,1:T(8,128)(2,1)} %get-tuple-element.57), channel_id=1, source_target_pairs={{0,8},{4,12},{8,0},{12,4},{1,9},{5,13},{9,1},{13,5},{2,10},{6,14},... | collective-permute-start | bytes 3145736 | tf_op jit(solution)/shard_map/ppermute | solution.py:37
  30.9 185.3 %collective-permute-start.11 = (bf16[2048,256]{0,1:T(8,128)(2,1)}, bf16[2048,256]{0,1:T(8,128)(2,1)}, u32[]{:S(2)}, u32[]{:S(2)}) collective-permute-start(bf16[2048,256]{0,1:T(8,128)(2,1)} %get-tuple-element.58), channel_id=1, source_target_pairs={{0,12},{4,8},{8,4},{12,0},{1,13},{5,9},{9,5},{13,1},{2,14},{6,10},... | collective-permute-start | bytes 3145736 | tf_op jit(solution)/shard_map/ppermute | solution.py:37
  31.3 185.1 %collective-permute-start.10 = (bf16[2048,256]{0,1:T(8,128)(2,1)}, bf16[2048,256]{0,1:T(8,128)(2,1)}, u32[]{:S(2)}, u32[]{:S(2)}) collective-permute-start(bf16[2048,256]{0,1:T(8,128)(2,1)} %get-tuple-element.59), channel_id=1, source_target_pairs={{0,8},{4,12},{8,0},{12,4},{1,9},{5,13},{9,1},{13,5},{2,10},{6,14},... | collective-permute-start | bytes 3145736 | tf_op jit(solution)/shard_map/ppermute | solution.py:37
  85.0 14.5 %collective-permute-start.3 = (bf16[2048,256]{0,1:T(8,128)(2,1)S(1)}, bf16[2048,256]{0,1:T(8,128)(2,1)S(1)}, u32[]{:S(2)}, u32[]{:S(2)}) collective-permute-start(bf16[2048,256]{0,1:T(8,128)(2,1)S(1)} %copy-done.18), channel_id=1, source_target_pairs={{0,4},{4,0},{8,12},{12,8},{1,5},{5,1},{9,13},{13,9},{2,6},{6,2},{1... | collective-permute-start | bytes 3145736 | tf_op jit(solution)/shard_map/ppermute | solution.py:37
  85.7 48.9 %collective-permute-start.7 = (bf16[2048,256]{0,1:T(8,128)(2,1)S(1)}, bf16[2048,256]{0,1:T(8,128)(2,1)S(1)}, u32[]{:S(2)}, u32[]{:S(2)}) collective-permute-start(bf16[2048,256]{0,1:T(8,128)(2,1)S(1)} %copy-done.17), channel_id=1, source_target_pairs={{0,12},{4,8},{8,4},{12,0},{1,13},{5,9},{9,5},{13,1},{2,14},{6,10},... | collective-permute-start | bytes 3145736 | tf_op jit(solution)/shard_map/ppermute | solution.py:37
  86.5 71.0 %collective-permute-start.5 = (bf16[2048,256]{0,1:T(8,128)(2,1)S(1)}, bf16[2048,256]{0,1:T(8,128)(2,1)S(1)}, u32[]{:S(2)}, u32[]{:S(2)}) collective-permute-start(bf16[2048,256]{0,1:T(8,128)(2,1)S(1)} %copy-done.16), channel_id=1, source_target_pairs={{0,8},{4,12},{8,0},{12,4},{1,9},{5,13},{9,1},{13,5},{2,10},{6,14},... | collective-permute-start | bytes 3145736 | tf_op jit(solution)/shard_map/ppermute | solution.py:37
  91.7 65.8 %copy-start.1 = (bf16[2048,1024]{0,1:T(8,128)(2,1)S(1)}, bf16[2048,1024]{0,1:T(8,128)(2,1)}, u32[]{:S(2)}) copy-start(bf16[2048,1024]{0,1:T(8,128)(2,1)} %convolution_bitcast_fusion.2) | copy-start | bytes 12582916
  99.5 80.0 %collective-permute-start.2 = (bf16[2048,256]{0,1:T(8,128)(2,1)S(1)}, bf16[2048,256]{0,1:T(8,128)(2,1)S(1)}, u32[]{:S(2)}, u32[]{:S(2)}) collective-permute-start(bf16[2048,256]{0,1:T(8,128)(2,1)S(1)} %copy-done.15), channel_id=1, source_target_pairs={{0,12},{4,8},{8,4},{12,0},{1,13},{5,9},{9,5},{13,1},{2,14},{6,10},... | collective-permute-start | bytes 3145736 | tf_op jit(solution)/shard_map/ppermute | solution.py:37
  134.6 67.6 %collective-permute-start.1 = (bf16[2048,256]{0,1:T(8,128)(2,1)S(1)}, bf16[2048,256]{0,1:T(8,128)(2,1)S(1)}, u32[]{:S(2)}, u32[]{:S(2)}) collective-permute-start(bf16[2048,256]{0,1:T(8,128)(2,1)S(1)} %copy-done.14), channel_id=1, source_target_pairs={{0,8},{4,12},{8,0},{12,4},{1,9},{5,13},{9,1},{13,5},{2,10},{6,14},... | collective-permute-start | bytes 3145736 | tf_op jit(solution)/shard_map/ppermute | solution.py:37
  157.5 45.5 %collective-permute-start = (bf16[2048,256]{0,1:T(8,128)(2,1)S(1)}, bf16[2048,256]{0,1:T(8,128)(2,1)S(1)}, u32[]{:S(2)}, u32[]{:S(2)}) collective-permute-start(bf16[2048,256]{0,1:T(8,128)(2,1)S(1)} %get-tuple-element.66), channel_id=1, source_target_pairs={{0,4},{4,0},{8,12},{12,8},{1,5},{5,1},{9,13},{13,9},{2,6},{6,2},{1... | collective-permute-start | bytes 3145736 | tf_op jit(solution)/shard_map/ppermute | solution.py:37
  179.6 36.9 %collective-permute-start.9 = (bf16[2048,256]{0,1:T(8,128)(2,1)}, bf16[2048,256]{0,1:T(8,128)(2,1)S(1)}, u32[]{:S(2)}, u32[]{:S(2)}) collective-permute-start(bf16[2048,256]{0,1:T(8,128)(2,1)} %get-tuple-element.60), channel_id=1, source_target_pairs={{0,4},{4,0},{8,12},{12,8},{1,5},{5,1},{9,13},{13,9},{2,6},{6,2},{1... | collective-permute-start | bytes 3145736 | tf_op jit(solution)/shard_map/ppermute | solution.py:37
  202.2 67.6 %collective-permute-start.17 = (bf16[2048,256]{0,1:T(8,128)(2,1)}, bf16[2048,256]{0,1:T(8,128)(2,1)}, u32[]{:S(2)}, u32[]{:S(2)}) collective-permute-start(bf16[2048,256]{0,1:T(8,128)(2,1)} %get-tuple-element.42), channel_id=1, source_target_pairs={{0,12},{4,8},{8,4},{12,0},{1,13},{5,9},{9,5},{13,1},{2,14},{6,10},... | collective-permute-start | bytes 3145736 | tf_op jit(solution)/shard_map/ppermute | solution.py:37
  202.9 67.3 %collective-permute-start.15 = (bf16[2048,256]{0,1:T(8,128)(2,1)}, bf16[2048,256]{0,1:T(8,128)(2,1)}, u32[]{:S(2)}, u32[]{:S(2)}) collective-permute-start(bf16[2048,256]{0,1:T(8,128)(2,1)} %get-tuple-element.43), channel_id=1, source_target_pairs={{0,8},{4,12},{8,0},{12,4},{1,9},{5,13},{9,1},{13,5},{2,10},{6,14},... | collective-permute-start | bytes 3145736 | tf_op jit(solution)/shard_map/ppermute | solution.py:37
  216.2 54.1 %collective-permute-start.13 = (bf16[2048,256]{0,1:T(8,128)(2,1)}, bf16[2048,256]{0,1:T(8,128)(2,1)}, u32[]{:S(2)}, u32[]{:S(2)}) collective-permute-start(bf16[2048,256]{0,1:T(8,128)(2,1)} %get-tuple-element.44), channel_id=1, source_target_pairs={{0,4},{4,0},{8,12},{12,8},{1,5},{5,1},{9,13},{13,9},{2,6},{6,2},{1... | collective-permute-start | bytes 3145736 | tf_op jit(solution)/shard_map/ppermute | solution.py:37
  244.2 13.4 %collective-permute-start.24 = (f32[64,4,256]{2,0,1:T(8,128)S(1)}, f32[64,4,256]{2,0,1:T(8,128)S(1)}, u32[]{:S(2)}, u32[]{:S(2)}) collective-permute-start(f32[64,4,256]{2,0,1:T(8,128)S(1)} %bitcast.127), channel_id=1, source_target_pairs={{0,1},{1,0},{2,3},{3,2},{4,5},{5,4},{6,7},{7,6},{8,9},{9,8},{10,11... | collective-permute-start | bytes 786440 | tf_op jit(solution)/shard_map/ppermute | solution.py:48
  246.6 21.0 %collective-permute-start.25 = (f32[64,4,256]{2,0,1:T(8,128)S(1)}, f32[64,4,256]{2,0,1:T(8,128)S(1)}, u32[]{:S(2)}, u32[]{:S(2)}) collective-permute-start(f32[64,4,256]{2,0,1:T(8,128)S(1)} %bitcast.126), channel_id=1, source_target_pairs={{0,2},{1,3},{2,0},{3,1},{4,6},{5,7},{6,4},{7,5},{8,10},{9,11},{10,... | collective-permute-start | bytes 786440 | tf_op jit(solution)/shard_map/ppermute | solution.py:48
  257.7 10.0 %collective-permute-start.26 = (f32[64,4,256]{2,0,1:T(8,128)S(1)}, f32[64,4,256]{2,0,1:T(8,128)S(1)}, u32[]{:S(2)}, u32[]{:S(2)}) collective-permute-start(f32[64,4,256]{2,0,1:T(8,128)S(1)} %bitcast.125), channel_id=1, source_target_pairs={{0,3},{1,2},{2,1},{3,0},{4,7},{5,6},{6,5},{7,4},{8,11},{9,10},{10,... | collective-permute-start | bytes 786440 | tf_op jit(solution)/shard_map/ppermute | solution.py:48
  267.6 25.5 %collective-permute-start.8 = (bf16[2048,256]{0,1:T(8,128)(2,1)S(1)}, bf16[2048,256]{0,1:T(8,128)(2,1)S(1)}, u32[]{:S(2)}, u32[]{:S(2)}) collective-permute-start(bf16[2048,256]{0,1:T(8,128)(2,1)S(1)} %copy-done.24), channel_id=1, source_target_pairs={{0,12},{4,8},{8,4},{12,0},{1,13},{5,9},{9,5},{13,1},{2,14},{6,10},... | collective-permute-start | bytes 3145736 | tf_op jit(solution)/shard_map/ppermute | solution.py:37
  267.6 47.8 %collective-permute-start.6 = (bf16[2048,256]{0,1:T(8,128)(2,1)S(1)}, bf16[2048,256]{0,1:T(8,128)(2,1)}, u32[]{:S(2)}, u32[]{:S(2)}) collective-permute-start(bf16[2048,256]{0,1:T(8,128)(2,1)S(1)} %copy-done.23), channel_id=1, source_target_pairs={{0,8},{4,12},{8,0},{12,4},{1,9},{5,13},{9,1},{13,5},{2,10},{6,14},... | collective-permute-start | bytes 3145736 | tf_op jit(solution)/shard_map/ppermute | solution.py:37
  269.8 45.6 %collective-permute-start.4 = (bf16[2048,256]{0,1:T(8,128)(2,1)S(1)}, bf16[2048,256]{0,1:T(8,128)(2,1)}, u32[]{:S(2)}, u32[]{:S(2)}) collective-permute-start(bf16[2048,256]{0,1:T(8,128)(2,1)S(1)} %copy-done.22), channel_id=1, source_target_pairs={{0,4},{4,0},{8,12},{12,8},{1,5},{5,1},{9,13},{13,9},{2,6},{6,2},{1... | collective-permute-start | bytes 3145736 | tf_op jit(solution)/shard_map/ppermute | solution.py:37
  287.7 59.4 %collective-permute-start.21 = (bf16[2048,256]{0,1:T(8,128)(2,1)}, bf16[2048,256]{0,1:T(8,128)(2,1)}, u32[]{:S(2)}, u32[]{:S(2)}) collective-permute-start(bf16[2048,256]{0,1:T(8,128)(2,1)} %get-tuple-element.28), channel_id=1, source_target_pairs={{0,4},{4,0},{8,12},{12,8},{1,5},{5,1},{9,13},{13,9},{2,6},{6,2},{1... | collective-permute-start | bytes 3145736 | tf_op jit(solution)/shard_map/ppermute | solution.py:37
  287.7 59.6 %collective-permute-start.22 = (bf16[2048,256]{0,1:T(8,128)(2,1)}, bf16[2048,256]{0,1:T(8,128)(2,1)}, u32[]{:S(2)}, u32[]{:S(2)}) collective-permute-start(bf16[2048,256]{0,1:T(8,128)(2,1)} %get-tuple-element.29), channel_id=1, source_target_pairs={{0,8},{4,12},{8,0},{12,4},{1,9},{5,13},{9,1},{13,5},{2,10},{6,14},... | collective-permute-start | bytes 3145736 | tf_op jit(solution)/shard_map/ppermute | solution.py:37
  293.1 67.5 %collective-permute-start.23 = (bf16[2048,256]{0,1:T(8,128)(2,1)}, bf16[2048,256]{0,1:T(8,128)(2,1)}, u32[]{:S(2)}, u32[]{:S(2)}) collective-permute-start(bf16[2048,256]{0,1:T(8,128)(2,1)} %get-tuple-element.30), channel_id=1, source_target_pairs={{0,12},{4,8},{8,4},{12,0},{1,13},{5,9},{9,5},{13,1},{2,14},{6,10},... | collective-permute-start | bytes 3145736 | tf_op jit(solution)/shard_map/ppermute | solution.py:37
  331.5 31.6 %collective-permute-start.18 = (bf16[2048,256]{0,1:T(8,128)(2,1)}, bf16[2048,256]{0,1:T(8,128)(2,1)S(1)}, u32[]{:S(2)}, u32[]{:S(2)}) collective-permute-start(bf16[2048,256]{0,1:T(8,128)(2,1)} %get-tuple-element.24), channel_id=1, source_target_pairs={{0,4},{4,0},{8,12},{12,8},{1,5},{5,1},{9,13},{13,9},{2,6},{6,2},{1... | collective-permute-start | bytes 3145736 | tf_op jit(solution)/shard_map/ppermute | solution.py:37
  331.9 50.8 %collective-permute-start.19 = (bf16[2048,256]{0,1:T(8,128)(2,1)}, bf16[2048,256]{0,1:T(8,128)(2,1)S(1)}, u32[]{:S(2)}, u32[]{:S(2)}) collective-permute-start(bf16[2048,256]{0,1:T(8,128)(2,1)} %get-tuple-element.25), channel_id=1, source_target_pairs={{0,8},{4,12},{8,0},{12,4},{1,9},{5,13},{9,1},{13,5},{2,10},{6,14},... | collective-permute-start | bytes 3145736 | tf_op jit(solution)/shard_map/ppermute | solution.py:37
  347.1 58.2 %collective-permute-start.20 = (bf16[2048,256]{0,1:T(8,128)(2,1)S(1)}, bf16[2048,256]{0,1:T(8,128)(2,1)S(1)}, u32[]{:S(2)}, u32[]{:S(2)}) collective-permute-start(bf16[2048,256]{0,1:T(8,128)(2,1)S(1)} %copy-done.19), channel_id=1, source_target_pairs={{0,12},{4,8},{8,4},{12,0},{1,13},{5,9},{9,5},{13,1},{2,14},{6,10},... | collective-permute-start | bytes 3145736 | tf_op jit(solution)/shard_map/ppermute | solution.py:37
  439.8 20.9 %collective-permute-start.27 = (f32[64,4,256]{2,0,1:T(8,128)S(1)}, f32[64,4,256]{2,0,1:T(8,128)S(1)}, u32[]{:S(2)}, u32[]{:S(2)}) collective-permute-start(f32[64,4,256]{2,0,1:T(8,128)S(1)} %bitcast.124), channel_id=1, source_target_pairs={{0,1},{1,0},{2,3},{3,2},{4,5},{5,4},{6,7},{7,6},{8,9},{9,8},{10,11... | collective-permute-start | bytes 786440 | tf_op jit(solution)/shard_map/ppermute | solution.py:48
  439.9 21.8 %collective-permute-start.28 = (f32[64,4,256]{2,0,1:T(8,128)S(1)}, f32[64,4,256]{2,0,1:T(8,128)S(1)}, u32[]{:S(2)}, u32[]{:S(2)}) collective-permute-start(f32[64,4,256]{2,0,1:T(8,128)S(1)} %bitcast.123), channel_id=1, source_target_pairs={{0,2},{1,3},{2,0},{3,1},{4,6},{5,7},{6,4},{7,5},{8,10},{9,11},{10,... | collective-permute-start | bytes 786440 | tf_op jit(solution)/shard_map/ppermute | solution.py:48
  443.3 18.4 %collective-permute-start.29 = (f32[64,4,256]{2,0,1:T(8,128)S(1)}, f32[64,4,256]{2,0,1:T(8,128)S(1)}, u32[]{:S(2)}, u32[]{:S(2)}) collective-permute-start(f32[64,4,256]{2,0,1:T(8,128)S(1)} %bitcast.122), channel_id=1, source_target_pairs={{0,3},{1,2},{2,1},{3,0},{4,7},{5,6},{6,5},{7,4},{8,11},{9,10},{10,... | collective-permute-start | bytes 786440 | tf_op jit(solution)/shard_map/ppermute | solution.py:48
  (32 other events, 529.2 us)

commit v12 on v7

--- a/solution.py
+++ b/solution.py
@@ -93,9 +93,13 @@
             x, returned, (((0,), (0,)), ((), ())), preferred_element_type=jnp.float32
         )
         pending.append((gt, gf, k * step))
+    gf_last = None
     for gt, gf, at in pending:
         grad_tokens = lax.dynamic_update_slice(grad_tokens, gt, (at, 0))
-        gf_acc = gf if gf_acc is None else gf_acc + gf
+        if at == (CHUNKS - 1) * step:
+            gf_last = gf
+        else:
+            gf_acc = gf if gf_acc is None else gf_acc + gf
 
     gs6 = gs_acc.reshape(n_dev, blk_local, blk_local, sub, blk_local, bs)
     gsd = jnp.sum(jnp.where(eye[None, :, None, None, :, None], gs6, 0.0), axis=4)
@@ -103,8 +107,11 @@
     second_term = gsd.transpose(3, 0, 2, 1, 4).reshape(bs, blk_local, bs) * grad_scale
     grad_second = lax.psum_scatter(second_term, "dp", scatter_dimension=0, tiled=True)
     gf_acc, grad_second = lax.optimization_barrier((gf_acc, grad_second))
-    gf6 = gf_acc.reshape(blk_local, bs, n_dev, blk_local, blk_local, sub)
-    gfd = jnp.sum(jnp.where(eye[:, None, None, None, :, None], gf6, 0.0), axis=4)
+    def diagonal_blocks(g):
+        g6 = g.reshape(blk_local, bs, n_dev, blk_local, blk_local, sub)
+        return jnp.sum(jnp.where(eye[:, None, None, None, :, None], g6, 0.0), axis=4)
+
+    gfd = diagonal_blocks(gf_acc) + diagonal_blocks(gf_last)
     gfd = jnp.take(gfd, order, axis=2)
     first_term = gfd.transpose(1, 0, 2, 3, 4).reshape(bs, blk_local, bs) * grad_scale
     grad_first = dp_reduce_scatter(first_term)

time: 457 us -> 462 us (1.011)
  waiting for transfers between devices: 153 us -> 146 us
    ppermute x24, waiting for transfers between devices: 151 us -> 145 us  [exchange(): lax.ppermute(pieces[m], 'tensor', [(i, i ^ m) for i in range(n_dev)])]
    reshape x1 -> x2, local copies, waits for them, and re-layouts: 5.71 us -> 11.4 us  [diagonal_blocks(): g6 = g.reshape(blk_local, bs, n_dev, blk_local, blk_local, sub)]
    unnamed x84 -> x64, local copies, waits for them, and re-layouts: 16.2 us -> 15.4 us
  transfers between devices with their start and end apart: 28 -> 28, of which waited for: 11 -> 12; matrix products, arithmetic and copies ran while one was open for 47% -> 49% of each run, Pallas kernels for 0% -> 0%
where the time goes in v12:
time: 462 us; the launch traced here: 455 us
  matrix products  169 us (37%)
  waiting for transfers between devices  146 us (32%)
  local copies, waits for them, and re-layouts  70.7 us (15%)
  other arithmetic  32.2 us (7%)
  starting transfers between devices  22.7 us (5%)
  between operations  15.5 us (3%)
    ppermute x24, waiting for transfers between devices, exchange(): lax.ppermute(pieces[m], 'tensor', [(i, i ^ m) for i in range(n_dev)])  145 us
    dot_general x4, matrix products, shards(): lax.dot_general(x, returned, (((0,), (0,)), ((), ())), preferred_element_...  36.9 us
    dot_general x4, matrix products, shards(): lax.dot_general(active, cot, (((0,), (0,)), ((), ())), preferred_element_...  35.9 us
    dot_general x4, matrix products, shards(): backed = jnp.dot(cot, w2p, preferred_element_type=jnp.float32)  33.8 us
    dot_general x4, matrix products, shards(): jnp.dot(returned, w1tp, preferred_element_type=jnp.float32)  31.1 us
    dot_general x4, matrix products, shards(): jnp.dot(x, w1p, preferred_element_type=jnp.float32).astype(jnp.bfloat16)  31.1 us
    ppermute x24, starting transfers between devices, exchange(): lax.ppermute(pieces[m], 'tensor', [(i, i ^ m) for i in range(n_dev)])  18 us
    slice x4, other arithmetic, shards(): hidden[:, m * part:(m + 1) * part]  15.5 us
  transfers between devices with their start and end apart: 28, of which 12 were waited for; matrix products, arithmetic and copies ran while one was open for 49% of the time, Pallas kernels for 0%

profile of v12, /device:TPU:0, one launch (start us, length us, event | category | flops | bytes accessed | tf_op | source)
XLA Modules:
  0.0 455.4 jit_solution(7945221373784589514)
XLA Ops:
  13.7 7.2 %convert_bitcast_fusion = bf16[2048,1024]{0,1:T(8,128)(2,1)S(1)} fusion(bf16[1024,1024]{0,1:T(8,128)(2,1)S(1)} %bitcast.103, bf16[8192,1024]{1,0:T(8,128)(2,1)} %param.4), kind=kOutput, calls=%fused_computation.49 | convolution fusion | flops 4297064448 | bytes 10485760 | tf_op jit(solution)/shard_map/dot_general | solution.py:74
  26.3 7.0 %convert_bitcast_fusion.2 = bf16[2048,1024]{0,1:T(8,128)(2,1)S(1)} fusion(bf16[1024,1024]{0,1:T(8,128)(2,1)S(1)} %bitcast.104, bf16[8192,1024]{1,0:T(8,128)(2,1)} %param.4), kind=kOutput, calls=%fused_computation.51 | convolution fusion | flops 4297064448 | bytes 10485760 | tf_op jit(solution)/shard_map/dot_general | solution.py:74
  37.2 9.2 %convolution_bitcast_fusion = bf16[2048,1024]{0,1:T(8,128)(2,1)} fusion(bf16[1024,1024]{0,1:T(8,128)(2,1)S(1)} %bitcast.99, bf16[8192,1024]{1,0:T(8,128)(2,1)} %param.5), kind=kOutput, calls=%fused_computation.4 | convolution fusion | flops 4294967296 | bytes 10485760 | tf_op jit(solution)/shard_map/dot_general | solution.py:75
  46.3 8.4 %convolution_bitcast_fusion.2 = bf16[2048,1024]{0,1:T(8,128)(2,1)} fusion(bf16[1024,1024]{0,1:T(8,128)(2,1)S(1)} %bitcast.100, bf16[8192,1024]{1,0:T(8,128)(2,1)} %param.5), kind=kOutput, calls=%fused_computation.6 | convolution fusion | flops 4294967296 | bytes 10485760 | tf_op jit(solution)/shard_map/dot_general | solution.py:75
  54.7 8.4 %convert_bitcast_fusion.3 = bf16[2048,1024]{0,1:T(8,128)(2,1)} fusion(bf16[1024,1024]{0,1:T(8,128)(2,1)S(1)} %bitcast.105, bf16[8192,1024]{1,0:T(8,128)(2,1)} %param.4), kind=kOutput, calls=%fused_computation.52 | convolution fusion | flops 4297064448 | bytes 10485760 | tf_op jit(solution)/shard_map/dot_general | solution.py:74
  63.1 8.7 %convolution_bitcast_fusion.3 = bf16[2048,1024]{0,1:T(8,128)(2,1)} fusion(bf16[1024,1024]{0,1:T(8,128)(2,1)S(1)} %bitcast.101, bf16[8192,1024]{1,0:T(8,128)(2,1)} %param.5), kind=kOutput, calls=%fused_computation.7 | convolution fusion | flops 4294967296 | bytes 10485760 | tf_op jit(solution)/shard_map/dot_general | solution.py:75
  71.9 8.4 %convert_bitcast_fusion.1 = bf16[2048,1024]{0,1:T(8,128)(2,1)} fusion(bf16[1024,1024]{0,1:T(8,128)(2,1)S(1)} %bitcast.106, bf16[8192,1024]{1,0:T(8,128)(2,1)} %param.4), kind=kOutput, calls=%fused_computation.50 | convolution fusion | flops 4297064448 | bytes 10485760 | tf_op jit(solution)/shard_map/dot_general | solution.py:74
  90.2 7.5 %convolution_bitcast_fusion.1 = bf16[2048,1024]{0,1:T(8,128)(2,1)S(1)} fusion(bf16[1024,1024]{0,1:T(8,128)(2,1)} %bitcast.102, bf16[8192,1024]{1,0:T(8,128)(2,1)} %param.5), kind=kOutput, calls=%fused_computation.5 | convolution fusion | flops 4294967296 | bytes 10485760 | tf_op jit(solution)/shard_map/dot_general | solution.py:75
  104.4 7.8 %fusion.7 = f32[1024,1024]{1,0:T(8,128)S(1)} fusion(bf16[2048,256]{0,1:T(8,128)(2,1)} %collective-permute-done.16, bf16[2048,256]{0,1:T(8,128)(2,1)} %collective-permute-done.14, bf16[2048,256]{0,1:T(8,128)(2,1)} %collective-permute-done.12, bf16[2048,256]{0,1:T(8,128)(2,1)S(1)} %get-tuple-element.48, bf16[8192,1024]{1,0:T(8,128)(2,1)} %param.5), kind=kOutput, calls=%fused_computation.19 | convolution fusion | flops 4315938816 | bytes 12582912 | tf_op jit(solution)/shard_map/dot_general | solution.py:82
  113.7 9.5 %collective-permute-done.7 = bf16[2048,256]{0,1:T(8,128)(2,1)S(1)} collective-permute-done((bf16[2048,256]{0,1:T(8,128)(2,1)S(1)}, bf16[2048,256]{0,1:T(8,128)(2,1)S(1)}, u32[]{:S(2)}, u32[]{:S(2)}) %collective-permute-start.7) | collective-permute-done | bytes 1048608 | tf_op jit(solution)/shard_map/ppermute | solution.py:37
  128.0 7.5 %fusion = f32[1024,1024]{1,0:T(8,128)S(1)} fusion(bf16[2048,256]{0,1:T(8,128)(2,1)S(1)} %collective-permute-done.7, bf16[2048,256]{0,1:T(8,128)(2,1)} %collective-permute-done.5, bf16[2048,256]{0,1:T(8,128)(2,1)} %collective-permute-done.3, bf16[2048,256]{0,1:T(8,128)(2,1)S(1)} %get-tuple-element.53, bf16[8192,1024]{1,0:T(8,128)(2,1)} %param.5), kind=kOutput, calls=%fused_computation.11 | convolution fusion | flops 4315938816 | bytes 12582912 | tf_op jit(solution)/shard_map/dot_general | solution.py:82
  136.2 9.7 %collective-permute-done.1 = bf16[2048,256]{0,1:T(8,128)(2,1)S(1)} collective-permute-done((bf16[2048,256]{0,1:T(8,128)(2,1)S(1)}, bf16[2048,256]{0,1:T(8,128)(2,1)S(1)}, u32[]{:S(2)}, u32[]{:S(2)}) %collective-permute-start.1) | collective-permute-done | bytes 1048608 | tf_op jit(solution)/shard_map/ppermute | solution.py:37
  145.9 22.2 %collective-permute-done.2 = bf16[2048,256]{0,1:T(8,128)(2,1)S(1)} collective-permute-done((bf16[2048,256]{0,1:T(8,128)(2,1)S(1)}, bf16[2048,256]{0,1:T(8,128)(2,1)S(1)}, u32[]{:S(2)}, u32[]{:S(2)}) %collective-permute-start.2) | collective-permute-done | bytes 1048608 | tf_op jit(solution)/shard_map/ppermute | solution.py:37
  172.9 8.7 %fusion.14 = f32[1024,1024]{1,0:T(8,128)} fusion(bf16[2048,256]{0,1:T(8,128)(2,1)S(1)} %collective-permute-done.2, bf16[2048,256]{0,1:T(8,128)(2,1)S(1)} %collective-permute-done.1, bf16[2048,256]{0,1:T(8,128)(2,1)S(1)} %collective-permute-done, bf16[2048,256]{0,1:T(8,128)(2,1)S(1)} %get-tuple-element.58, bf16[8192,1024]{1,0:T(8,128)(2,1)} %param.5), kind=kOutput, calls=%fused_computation.27 | convolution fusion | flops 4315938816 | bytes 12582912 | tf_op jit(solution)/shard_map/dot_general | solution.py:82
  181.6 9.2 %collective-permute-done.10 = bf16[2048,256]{0,1:T(8,128)(2,1)S(1)} collective-permute-done((bf16[2048,256]{0,1:T(8,128)(2,1)}, bf16[2048,256]{0,1:T(8,128)(2,1)S(1)}, u32[]{:S(2)}, u32[]{:S(2)}) %collective-permute-start.10) | collective-permute-done | bytes 1048608 | tf_op jit(solution)/shard_map/ppermute | solution.py:37
  191.4 21.6 %collective-permute-done.11 = bf16[2048,256]{0,1:T(8,128)(2,1)S(1)} collective-permute-done((bf16[2048,256]{0,1:T(8,128)(2,1)}, bf16[2048,256]{0,1:T(8,128)(2,1)S(1)}, u32[]{:S(2)}, u32[]{:S(2)}) %collective-permute-start.11) | collective-permute-done | bytes 1048608 | tf_op jit(solution)/shard_map/ppermute | solution.py:37
  216.7 11.9 %add_add_fusion = f32[1024,1024]{1,0:T(8,128)} fusion(f32[1024,1024]{1,0:T(8,128)} %fusion.14, f32[1024,1024]{1,0:T(8,128)S(1)} %fusion, f32[1024,1024]{1,0:T(8,128)S(1)} %fusion.7, bf16[8192,1024]{1,0:T(8,128)(2,1)} %param.5, bf16[2048,256]{0,1:T(8,128)(2,1)S(1)} %collective-permute-done.11, bf16[2048,256]{0,1:T(8,128)(2,1)S(1)} %collective-permute-done.10, ...), kind=kOutput, calls=%fused_computation.46 | convolution fusion | flops 4319084544 | bytes 25165824 | tf_op jit(solution)/shard_map/dot_general | solution.py:82
  228.7 6.0 %reshape.100 = f32[4,4,4,16,4,256]{5,4,3,2,1,0:T(4,128)} reshape(f32[1024,1024]{1,0:T(8,128)} %add_add_fusion) | data formatting | bytes 8388608 | tf_op jit(solution)/shard_map/reshape | solution.py:104
  244.4 13.6 %collective-permute-done.8 = bf16[2048,256]{0,1:T(8,128)(2,1)} collective-permute-done((bf16[2048,256]{0,1:T(8,128)(2,1)}, bf16[2048,256]{0,1:T(8,128)(2,1)}, u32[]{:S(2)}, u32[]{:S(2)}) %collective-permute-start.8) | collective-permute-done | bytes 1048608 | tf_op jit(solution)/shard_map/ppermute | solution.py:37
  258.1 9.2 %convolution_convert_fusion.1 = bf16[2048,1024]{1,0:T(8,128)(2,1)} fusion(bf16[1024,1024]{1,0:T(8,128)(2,1)} %bitcast.95, bf16[2048,256]{0,1:T(8,128)(2,1)} %collective-permute-done.8, bf16[2048,256]{0,1:T(8,128)(2,1)} %collective-permute-done.6, bf16[2048,256]{0,1:T(8,128)(2,1)} %collective-permute-done.4, bf16[2048,256]{0,1:T(8,128)(2,1)S(1)} %copy-done.17), kind=kOutput, calls=%fused_computation.54 | convolution fusion | flops 4313841664 | bytes 10485760 | tf_op jit(solution)/shard_map/dot_general | solution.py:91
  267.2 9.8 %fusion.48 = f32[1024,1024]{0,1:T(8,128)} fusion(bf16[8192,1024]{1,0:T(8,128)(2,1)} %param.4, bf16[2048,256]{0,1:T(8,128)(2,1)} %collective-permute-done.8, bf16[2048,256]{0,1:T(8,128)(2,1)} %collective-permute-done.6, bf16[2048,256]{0,1:T(8,128)(2,1)} %collective-permute-done.4, bf16[2048,256]{0,1:T(8,128)(2,1)S(1)} %copy-done.17), kind=kOutput, calls=%fused_computation.75 | convolution fusion | flops 4311744512 | bytes 12582912 | tf_op jit(solution)/shard_map/dot_general | solution.py:92
  280.7 22.2 %collective-permute-done.17 = bf16[2048,256]{0,1:T(8,128)(2,1)S(1)} collective-permute-done((bf16[2048,256]{0,1:T(8,128)(2,1)}, bf16[2048,256]{0,1:T(8,128)(2,1)S(1)}, u32[]{:S(2)}, u32[]{:S(2)}) %collective-permute-start.17) | collective-permute-done | bytes 1048608 | tf_op jit(solution)/shard_map/ppermute | solution.py:37
  302.9 9.0 %fusion.54 = f32[1024,1024]{0,1:T(8,128)} fusion(bf16[8192,1024]{1,0:T(8,128)(2,1)} %param.4, bf16[2048,256]{0,1:T(8,128)(2,1)S(1)} %collective-permute-done.17, bf16[2048,256]{0,1:T(8,128)(2,1)S(1)} %collective-permute-done.15, bf16[2048,256]{0,1:T(8,128)(2,1)S(1)} %collective-permute-done.13, bf16[2048,256]{0,1:T(8,128)(2,1)S(1)} %copy-done.15), kind=kOutput, calls=%fused_computation.77 | convolution fusion | flops 4311744512 | bytes 12582912 | tf_op jit(solution)/shard_map/dot_general | solution.py:92
  311.9 6.1 %convolution_convert_fusion = bf16[2048,1024]{1,0:T(8,128)(2,1)} fusion(bf16[1024,1024]{1,0:T(8,128)(2,1)S(1)} %bitcast.97, bf16[2048,256]{0,1:T(8,128)(2,1)S(1)} %collective-permute-done.17, bf16[2048,256]{0,1:T(8,128)(2,1)S(1)} %collective-permute-done.15, bf16[2048,256]{0,1:T(8,128)(2,1)S(1)} %collective-permute-done.13, bf16[2048,256]{0,1:T(8,128)(2,1)S(1)} %copy-done.15), kind=kOutput, calls=%fused_computation.53 | convolution fusion | flops 4313841664 | bytes 10485760 | tf_op jit(solution)/shard_map/dot_general | solution.py:91
  319.4 6.6 %broadcast_in_dim.157 = bf16[8192,1024]{1,0:T(8,128)(2,1)} broadcast(bf16[]{:T(256)} %constant.53.clone.1), dimensions={} | broadcast | bytes 16777218 | tf_op jit(solution)/shard_map/broadcast_in_dim | solution.py:69
  336.2 11.8 %collective-permute-done.20 = bf16[2048,256]{0,1:T(8,128)(2,1)} collective-permute-done((bf16[2048,256]{0,1:T(8,128)(2,1)}, bf16[2048,256]{0,1:T(8,128)(2,1)}, u32[]{:S(2)}, u32[]{:S(2)}) %collective-permute-start.20) | collective-permute-done | bytes 1048608 | tf_op jit(solution)/shard_map/ppermute | solution.py:37
  351.3 8.3 %bitcast_add_fusion = f32[1024,1024]{0,1:T(8,128)} fusion(f32[1024,1024]{0,1:T(8,128)S(1)} %copy-done.24, f32[1024,1024]{0,1:T(8,128)S(1)} %copy-done.25, bf16[2048,1024]{0,1:T(8,128)(2,1)S(1)} %constant_dynamic-update-slice_fusion, bf16[8192,1024]{1,0:T(8,128)(2,1)} %param.4), kind=kOutput, calls=%fused_computation.42 | convolution fusion | flops 4297064448 | bytes 20971520 | tf_op jit(solution)/shard_map/dot_general | solution.py:92
  373.0 19.8 %collective-permute-done.23 = bf16[2048,256]{0,1:T(8,128)(2,1)S(1)} collective-permute-done((bf16[2048,256]{0,1:T(8,128)(2,1)S(1)}, bf16[2048,256]{0,1:T(8,128)(2,1)S(1)}, u32[]{:S(2)}, u32[]{:S(2)}) %collective-permute-start.23) | collective-permute-done | bytes 1048608 | tf_op jit(solution)/shard_map/ppermute | solution.py:37
  393.9 9.9 %fusion.51 = f32[1024,1024]{0,1:T(8,128)} fusion(bf16[2048,1024]{0,1:T(8,128)(2,1)} %constant_dynamic-update-slice_fusion.4, bf16[8192,1024]{1,0:T(8,128)(2,1)} %param.4), kind=kOutput, calls=%fused_computation.76 | convolution fusion | flops 4294967296 | bytes 12582912 | tf_op jit(solution)/shard_map/dot_general | solution.py:92
  409.5 7.0 %select_reduce_fusion.1 = (f32[4,256,4,4,16]{1,0,4,3,2:T(4,128)S(1)}, f32[4,256,4,4,16]{1,0,4,3,2:T(4,128)S(1)}) fusion(f32[4,256,4,4,4,16]{1,0,5,4,3,2:T(4,128)} %reshape.101, pred[4,4]{0,1:T(4,128)(4,1)S(1)} %copy-done.22, f32[4,256,4,4,4,16]{1,0,5,4,3,2:T(4,128)} %reshape.102), kind=kLoop, calls=%fused_computation.44 | loop fusion | flops 3670016 | bytes 10485776 | tf_op jit(solution)/shard_map/reduce_sum | solution.py:112
  429.6 9.6 %convert_dynamic-update-slice_fusion.1 = bf16[8192,1024]{1,0:T(8,128)(2,1)} fusion(bf16[8192,1024]{1,0:T(8,128)(2,1)} %constant_dynamic-update-slice_fusion.8, bf16[2048,1024]{0,1:T(8,128)(2,1)} %copy-done.20, bf16[1024,1024]{1,0:T(8,128)(2,1)} %bitcast.96), kind=kOutput, calls=%fused_computation.48 | convolution fusion | flops 4297064448 | bytes 10485760 | tf_op jit(solution)/shard_map/dot_general | solution.py:91
  439.2 6.2 %convert_dynamic-update-slice_fusion = bf16[8192,1024]{1,0:T(8,128)(2,1)} fusion(bf16[8192,1024]{1,0:T(8,128)(2,1)} %convert_dynamic-update-slice_fusion.1, bf16[2048,1024]{0,1:T(8,128)(2,1)S(1)} %copy-done.19, bf16[1024,1024]{1,0:T(8,128)(2,1)S(1)} %bitcast.98), kind=kOutput, calls=%fused_computation.47 | convolution fusion | flops 4297064448 | bytes 10485760 | tf_op jit(solution)/shard_map/dot_general | solution.py:91
  (157 shorter events, 111.8 us)
Async XLA Ops:
  7.2 321.3 %all-reduce.3.cloned.1.call-start = ((), (), s32[]{:S(2)}) async-start(), calls=%async_computation | async-start | bytes 2097152
  7.3 73.0 %copy-start.21 = (pred[4,4]{0,1:T(4,128)(4,1)}, pred[4,4]{0,1:T(4,128)(4,1)S(1)}, u32[]{:S(2)}) copy-start(pred[4,4]{0,1:T(4,128)(4,1)S(1)} %iota_compare_fusion) | copy-start | bytes 52
  22.7 75.0 %collective-permute-start.12 = (bf16[2048,256]{0,1:T(8,128)(2,1)}, bf16[2048,256]{0,1:T(8,128)(2,1)}, u32[]{:S(2)}, u32[]{:S(2)}) collective-permute-start(bf16[2048,256]{0,1:T(8,128)(2,1)} %get-tuple-element.63), channel_id=1, source_target_pairs={{0,4},{4,0},{8,12},{12,8},{1,5},{5,1},{9,13},{13,9},{2,6},{6,2},{1... | collective-permute-start | bytes 3145736 | tf_op jit(solution)/shard_map/ppermute | solution.py:37
  23.2 75.2 %collective-permute-start.14 = (bf16[2048,256]{0,1:T(8,128)(2,1)}, bf16[2048,256]{0,1:T(8,128)(2,1)}, u32[]{:S(2)}, u32[]{:S(2)}) collective-permute-start(bf16[2048,256]{0,1:T(8,128)(2,1)} %get-tuple-element.65), channel_id=1, source_target_pairs={{0,8},{4,12},{8,0},{12,4},{1,9},{5,13},{9,1},{13,5},{2,10},{6,14},... | collective-permute-start | bytes 3145736 | tf_op jit(solution)/shard_map/ppermute | solution.py:37
  25.7 73.5 %collective-permute-start.16 = (bf16[2048,256]{0,1:T(8,128)(2,1)}, bf16[2048,256]{0,1:T(8,128)(2,1)}, u32[]{:S(2)}, u32[]{:S(2)}) collective-permute-start(bf16[2048,256]{0,1:T(8,128)(2,1)} %get-tuple-element.64), channel_id=1, source_target_pairs={{0,12},{4,8},{8,4},{12,0},{1,13},{5,9},{9,5},{13,1},{2,14},{6,10},... | collective-permute-start | bytes 3145736 | tf_op jit(solution)/shard_map/ppermute | solution.py:37
  35.1 77.0 %collective-permute-start.3 = (bf16[2048,256]{0,1:T(8,128)(2,1)}, bf16[2048,256]{0,1:T(8,128)(2,1)}, u32[]{:S(2)}, u32[]{:S(2)}) collective-permute-start(bf16[2048,256]{0,1:T(8,128)(2,1)} %get-tuple-element.69), channel_id=1, source_target_pairs={{0,4},{4,0},{8,12},{12,8},{1,5},{5,1},{9,13},{13,9},{2,6},{6,2},{1... | collective-permute-start | bytes 3145736 | tf_op jit(solution)/shard_map/ppermute | solution.py:37
  35.8 77.0 %collective-permute-start.5 = (bf16[2048,256]{0,1:T(8,128)(2,1)}, bf16[2048,256]{0,1:T(8,128)(2,1)}, u32[]{:S(2)}, u32[]{:S(2)}) collective-permute-start(bf16[2048,256]{0,1:T(8,128)(2,1)} %get-tuple-element.71), channel_id=1, source_target_pairs={{0,8},{4,12},{8,0},{12,4},{1,9},{5,13},{9,1},{13,5},{2,10},{6,14},... | collective-permute-start | bytes 3145736 | tf_op jit(solution)/shard_map/ppermute | solution.py:37
  37.1 26.0 %copy-start.11 = (bf16[128,8,4,256]{3,1,2,0:T(8,128)(2,1)}, bf16[128,8,4,256]{3,1,2,0:T(8,128)(2,1)S(1)}, u32[]{:S(2)}) copy-start(bf16[128,8,4,256]{3,1,2,0:T(8,128)(2,1)S(1)} %copy.48) | copy-start | bytes 6291460
  97.8 25.4 %collective-permute-start.7 = (bf16[2048,256]{0,1:T(8,128)(2,1)S(1)}, bf16[2048,256]{0,1:T(8,128)(2,1)S(1)}, u32[]{:S(2)}, u32[]{:S(2)}) collective-permute-start(bf16[2048,256]{0,1:T(8,128)(2,1)S(1)} %copy-done.14), channel_id=1, source_target_pairs={{0,12},{4,8},{8,4},{12,0},{1,13},{5,9},{9,5},{13,1},{2,14},{6,10},... | collective-permute-start | bytes 3145736 | tf_op jit(solution)/shard_map/ppermute | solution.py:37
  98.4 37.1 %collective-permute-start = (bf16[2048,256]{0,1:T(8,128)(2,1)S(1)}, bf16[2048,256]{0,1:T(8,128)(2,1)S(1)}, u32[]{:S(2)}, u32[]{:S(2)}) collective-permute-start(bf16[2048,256]{0,1:T(8,128)(2,1)S(1)} %copy-done.13), channel_id=1, source_target_pairs={{0,4},{4,0},{8,12},{12,8},{1,5},{5,1},{9,13},{13,9},{2,6},{6,2},{1... | collective-permute-start | bytes 3145736 | tf_op jit(solution)/shard_map/ppermute | solution.py:37
  99.2 46.7 %collective-permute-start.1 = (bf16[2048,256]{0,1:T(8,128)(2,1)S(1)}, bf16[2048,256]{0,1:T(8,128)(2,1)S(1)}, u32[]{:S(2)}, u32[]{:S(2)}) collective-permute-start(bf16[2048,256]{0,1:T(8,128)(2,1)S(1)} %copy-done.12), channel_id=1, source_target_pairs={{0,8},{4,12},{8,0},{12,4},{1,9},{5,13},{9,1},{13,5},{2,10},{6,14},... | collective-permute-start | bytes 3145736 | tf_op jit(solution)/shard_map/ppermute | solution.py:37
  112.1 55.9 %collective-permute-start.2 = (bf16[2048,256]{0,1:T(8,128)(2,1)S(1)}, bf16[2048,256]{0,1:T(8,128)(2,1)S(1)}, u32[]{:S(2)}, u32[]{:S(2)}) collective-permute-start(bf16[2048,256]{0,1:T(8,128)(2,1)S(1)} %get-tuple-element.72), channel_id=1, source_target_pairs={{0,12},{4,8},{8,4},{12,0},{1,13},{5,9},{9,5},{13,1},{2,14},{6,10},... | collective-permute-start | bytes 3145736 | tf_op jit(solution)/shard_map/ppermute | solution.py:37
  112.8 78.0 %collective-permute-start.10 = (bf16[2048,256]{0,1:T(8,128)(2,1)}, bf16[2048,256]{0,1:T(8,128)(2,1)S(1)}, u32[]{:S(2)}, u32[]{:S(2)}) collective-permute-start(bf16[2048,256]{0,1:T(8,128)(2,1)} %get-tuple-element.67), channel_id=1, source_target_pairs={{0,8},{4,12},{8,0},{12,4},{1,9},{5,13},{9,1},{13,5},{2,10},{6,14},... | collective-permute-start | bytes 3145736 | tf_op jit(solution)/shard_map/ppermute | solution.py:37
  123.1 89.9 %collective-permute-start.11 = (bf16[2048,256]{0,1:T(8,128)(2,1)}, bf16[2048,256]{0,1:T(8,128)(2,1)S(1)}, u32[]{:S(2)}, u32[]{:S(2)}) collective-permute-start(bf16[2048,256]{0,1:T(8,128)(2,1)} %get-tuple-element.66), channel_id=1, source_target_pairs={{0,12},{4,8},{8,4},{12,0},{1,13},{5,9},{9,5},{13,1},{2,14},{6,10},... | collective-permute-start | bytes 3145736 | tf_op jit(solution)/shard_map/ppermute | solution.py:37
  128.0 41.4 %copy-start = (bf16[2048,1024]{0,1:T(8,128)(2,1)S(1)}, bf16[2048,1024]{0,1:T(8,128)(2,1)}, u32[]{:S(2)}) copy-start(bf16[2048,1024]{0,1:T(8,128)(2,1)} %convolution_bitcast_fusion.3) | copy-start | bytes 12582916
  135.5 77.5 %collective-permute-start.9 = (bf16[2048,256]{0,1:T(8,128)(2,1)}, bf16[2048,256]{0,1:T(8,128)(2,1)S(1)}, u32[]{:S(2)}, u32[]{:S(2)}) collective-permute-start(bf16[2048,256]{0,1:T(8,128)(2,1)} %get-tuple-element.68), channel_id=1, source_target_pairs={{0,4},{4,0},{8,12},{12,8},{1,5},{5,1},{9,13},{13,9},{2,6},{6,2},{1... | collective-permute-start | bytes 3145736 | tf_op jit(solution)/shard_map/ppermute | solution.py:37
  145.9 98.1 %collective-permute-start.4 = (bf16[2048,256]{0,1:T(8,128)(2,1)}, bf16[2048,256]{0,1:T(8,128)(2,1)}, u32[]{:S(2)}, u32[]{:S(2)}) collective-permute-start(bf16[2048,256]{0,1:T(8,128)(2,1)} %get-tuple-element.57), channel_id=1, source_target_pairs={{0,4},{4,0},{8,12},{12,8},{1,5},{5,1},{9,13},{13,9},{2,6},{6,2},{1... | collective-permute-start | bytes 3145736 | tf_op jit(solution)/shard_map/ppermute | solution.py:37
  168.1 76.3 %collective-permute-start.6 = (bf16[2048,256]{0,1:T(8,128)(2,1)}, bf16[2048,256]{0,1:T(8,128)(2,1)}, u32[]{:S(2)}, u32[]{:S(2)}) collective-permute-start(bf16[2048,256]{0,1:T(8,128)(2,1)} %get-tuple-element.56), channel_id=1, source_target_pairs={{0,8},{4,12},{8,0},{12,4},{1,9},{5,13},{9,1},{13,5},{2,10},{6,14},... | collective-permute-start | bytes 3145736 | tf_op jit(solution)/shard_map/ppermute | solution.py:37
  190.8 67.3 %collective-permute-start.8 = (bf16[2048,256]{0,1:T(8,128)(2,1)}, bf16[2048,256]{0,1:T(8,128)(2,1)}, u32[]{:S(2)}, u32[]{:S(2)}) collective-permute-start(bf16[2048,256]{0,1:T(8,128)(2,1)} %get-tuple-element.55), channel_id=1, source_target_pairs={{0,12},{4,8},{8,4},{12,0},{1,13},{5,9},{9,5},{13,1},{2,14},{6,10},... | collective-permute-start | bytes 3145736 | tf_op jit(solution)/shard_map/ppermute | solution.py:37
  242.5 35.9 %collective-permute-start.13 = (bf16[2048,256]{0,1:T(8,128)(2,1)}, bf16[2048,256]{0,1:T(8,128)(2,1)S(1)}, u32[]{:S(2)}, u32[]{:S(2)}) collective-permute-start(bf16[2048,256]{0,1:T(8,128)(2,1)} %get-tuple-element.52), channel_id=1, source_target_pairs={{0,4},{4,0},{8,12},{12,8},{1,5},{5,1},{9,13},{13,9},{2,6},{6,2},{1... | collective-permute-start | bytes 3145736 | tf_op jit(solution)/shard_map/ppermute | solution.py:37
  242.7 38.0 %collective-permute-start.15 = (bf16[2048,256]{0,1:T(8,128)(2,1)}, bf16[2048,256]{0,1:T(8,128)(2,1)S(1)}, u32[]{:S(2)}, u32[]{:S(2)}) collective-permute-start(bf16[2048,256]{0,1:T(8,128)(2,1)} %get-tuple-element.51), channel_id=1, source_target_pairs={{0,8},{4,12},{8,0},{12,4},{1,9},{5,13},{9,1},{13,5},{2,10},{6,14},... | collective-permute-start | bytes 3145736 | tf_op jit(solution)/shard_map/ppermute | solution.py:37
  244.0 58.9 %collective-permute-start.17 = (bf16[2048,256]{0,1:T(8,128)(2,1)}, bf16[2048,256]{0,1:T(8,128)(2,1)S(1)}, u32[]{:S(2)}, u32[]{:S(2)}) collective-permute-start(bf16[2048,256]{0,1:T(8,128)(2,1)} %get-tuple-element.50), channel_id=1, source_target_pairs={{0,12},{4,8},{8,4},{12,0},{1,13},{5,9},{9,5},{13,1},{2,14},{6,10},... | collective-permute-start | bytes 3145736 | tf_op jit(solution)/shard_map/ppermute | solution.py:37
  267.2 35.7 %copy-start.15 = (bf16[2048,256]{0,1:T(8,128)(2,1)S(1)}, bf16[2048,256]{0,1:T(8,128)(2,1)}, u32[]{:S(2)}) copy-start(bf16[2048,256]{0,1:T(8,128)(2,1)} %get-tuple-element.49) | copy-start | bytes 3145732
  277.0 56.4 %collective-permute-start.18 = (bf16[2048,256]{0,1:T(8,128)(2,1)}, bf16[2048,256]{0,1:T(8,128)(2,1)}, u32[]{:S(2)}, u32[]{:S(2)}) collective-permute-start(bf16[2048,256]{0,1:T(8,128)(2,1)} %get-tuple-element.24), channel_id=1, source_target_pairs={{0,4},{4,0},{8,12},{12,8},{1,5},{5,1},{9,13},{13,9},{2,6},{6,2},{1... | collective-permute-start | bytes 3145736 | tf_op jit(solution)/shard_map/ppermute | solution.py:37
  277.3 58.8 %collective-permute-start.19 = (bf16[2048,256]{0,1:T(8,128)(2,1)}, bf16[2048,256]{0,1:T(8,128)(2,1)S(1)}, u32[]{:S(2)}, u32[]{:S(2)}) collective-permute-start(bf16[2048,256]{0,1:T(8,128)(2,1)} %get-tuple-element.25), channel_id=1, source_target_pairs={{0,8},{4,12},{8,0},{12,4},{1,9},{5,13},{9,1},{13,5},{2,10},{6,14},... | collective-permute-start | bytes 3145736 | tf_op jit(solution)/shard_map/ppermute | solution.py:37
  278.3 69.6 %collective-permute-start.20 = (bf16[2048,256]{0,1:T(8,128)(2,1)}, bf16[2048,256]{0,1:T(8,128)(2,1)}, u32[]{:S(2)}, u32[]{:S(2)}) collective-permute-start(bf16[2048,256]{0,1:T(8,128)(2,1)} %get-tuple-element.26), channel_id=1, source_target_pairs={{0,12},{4,8},{8,4},{12,0},{1,13},{5,9},{9,5},{13,1},{2,14},{6,10},... | collective-permute-start | bytes 3145736 | tf_op jit(solution)/shard_map/ppermute | solution.py:37
  318.0 47.3 %collective-permute-start.21 = (bf16[2048,256]{0,1:T(8,128)(2,1)}, bf16[2048,256]{0,1:T(8,128)(2,1)}, u32[]{:S(2)}, u32[]{:S(2)}) collective-permute-start(bf16[2048,256]{0,1:T(8,128)(2,1)} %get-tuple-element.28), channel_id=1, source_target_pairs={{0,4},{4,0},{8,12},{12,8},{1,5},{5,1},{9,13},{13,9},{2,6},{6,2},{1... | collective-permute-start | bytes 3145736 | tf_op jit(solution)/shard_map/ppermute | solution.py:37
  318.1 52.5 %collective-permute-start.22 = (bf16[2048,256]{0,1:T(8,128)(2,1)}, bf16[2048,256]{0,1:T(8,128)(2,1)}, u32[]{:S(2)}, u32[]{:S(2)}) collective-permute-start(bf16[2048,256]{0,1:T(8,128)(2,1)} %get-tuple-element.29), channel_id=1, source_target_pairs={{0,8},{4,12},{8,0},{12,4},{1,9},{5,13},{9,1},{13,5},{2,10},{6,14},... | collective-permute-start | bytes 3145736 | tf_op jit(solution)/shard_map/ppermute | solution.py:37
  333.4 59.3 %collective-permute-start.23 = (bf16[2048,256]{0,1:T(8,128)(2,1)S(1)}, bf16[2048,256]{0,1:T(8,128)(2,1)S(1)}, u32[]{:S(2)}, u32[]{:S(2)}) collective-permute-start(bf16[2048,256]{0,1:T(8,128)(2,1)S(1)} %copy-done.16), channel_id=1, source_target_pairs={{0,12},{4,8},{8,4},{12,0},{1,13},{5,9},{9,5},{13,1},{2,14},{6,10},... | collective-permute-start | bytes 3145736 | tf_op jit(solution)/shard_map/ppermute | solution.py:37
  423.3 23.3 %collective-permute-start.24 = (f32[64,4,256]{2,0,1:T(8,128)S(1)}, f32[64,4,256]{2,0,1:T(8,128)S(1)}, u32[]{:S(2)}, u32[]{:S(2)}) collective-permute-start(f32[64,4,256]{2,0,1:T(8,128)S(1)} %bitcast.108), channel_id=1, source_target_pairs={{0,1},{1,0},{2,3},{3,2},{4,5},{5,4},{6,7},{7,6},{8,9},{9,8},{10,11... | collective-permute-start | bytes 786440 | tf_op jit(solution)/shard_map/ppermute | solution.py:48
  426.1 21.4 %collective-permute-start.25 = (f32[64,4,256]{2,0,1:T(8,128)S(1)}, f32[64,4,256]{2,0,1:T(8,128)S(1)}, u32[]{:S(2)}, u32[]{:S(2)}) collective-permute-start(f32[64,4,256]{2,0,1:T(8,128)S(1)} %bitcast.109), channel_id=1, source_target_pairs={{0,2},{1,3},{2,0},{3,1},{4,6},{5,7},{6,4},{7,5},{8,10},{9,11},{10,... | collective-permute-start | bytes 786440 | tf_op jit(solution)/shard_map/ppermute | solution.py:48
  429.4 18.1 %collective-permute-start.26 = (f32[64,4,256]{2,0,1:T(8,128)S(1)}, f32[64,4,256]{2,0,1:T(8,128)S(1)}, u32[]{:S(2)}, u32[]{:S(2)}) collective-permute-start(f32[64,4,256]{2,0,1:T(8,128)S(1)} %bitcast.110), channel_id=1, source_target_pairs={{0,3},{1,2},{2,1},{3,0},{4,7},{5,6},{6,5},{7,4},{8,11},{9,10},{10,... | collective-permute-start | bytes 786440 | tf_op jit(solution)/shard_map/ppermute | solution.py:48
  (22 other events, 178.0 us)
Sparse Core Ops, SparseCore 0:
  242.6 52.9 all-reduce.2

commit v13 on v12

--- a/solution.py
+++ b/solution.py
@@ -89,9 +89,17 @@
             gf_acc = done[1] if gf_acc is None else gf_acc + done[1]
         returned = jnp.concatenate(exchange(masked, n_dev), axis=1)
         gt = jnp.dot(returned, w1tp, preferred_element_type=jnp.float32).astype(jnp.bfloat16)
-        gf = lax.dot_general(
-            x, returned, (((0,), (0,)), ((), ())), preferred_element_type=jnp.float32
-        )
+        if k + 1 < CHUNKS:
+            gf = lax.dot_general(
+                x, returned, (((0,), (0,)), ((), ())), preferred_element_type=jnp.float32
+            )
+        else:
+            gf = jnp.einsum(
+                "tmcbq,tbi->bimcq",
+                returned.reshape(step, n_dev, blk_local, blk_local, sub),
+                x.reshape(step, blk_local, bs),
+                preferred_element_type=jnp.float32,
+            )
         pending.append((gt, gf, k * step))
     gf_last = None
     for gt, gf, at in pending:
@@ -111,7 +119,7 @@
         g6 = g.reshape(blk_local, bs, n_dev, blk_local, blk_local, sub)
         return jnp.sum(jnp.where(eye[:, None, None, None, :, None], g6, 0.0), axis=4)
 
-    gfd = diagonal_blocks(gf_acc) + diagonal_blocks(gf_last)
+    gfd = diagonal_blocks(gf_acc) + gf_last
     gfd = jnp.take(gfd, order, axis=2)
     first_term = gfd.transpose(1, 0, 2, 3, 4).reshape(bs, blk_local, bs) * grad_scale
     grad_first = dp_reduce_scatter(first_term)

time: 462 us -> 444 us (0.961)
  waiting for transfers between devices: 146 us -> 133 us
  matrix products: 169 us -> 160 us
  local copies, waits for them, and re-layouts: 70.7 us -> 76.6 us
    ppermute x24, waiting for transfers between devices: 145 us -> 132 us  [exchange(): lax.ppermute(pieces[m], 'tensor', [(i, i ^ m) for i in range(n_dev)])]
    unnamed x64 -> x86, local copies, waits for them, and re-layouts: 15.4 us -> 28.2 us
    dot_general x4 -> x3, matrix products: 36.9 us -> 27.6 us  [shards(): lax.dot_general(x, returned, (((0,), (0,)), ((), ())), preferred_element_...]
    reshape x2 -> x1, local copies, waits for them, and re-layouts: 11.4 us -> 5.89 us  [diagonal_blocks(): g6 = g.reshape(blk_local, bs, n_dev, blk_local, blk_local, sub)]
  transfers between devices with their start and end apart: 28 -> 28, of which waited for: 12 -> 10; matrix products, arithmetic and copies ran while one was open for 49% -> 53% of each run, Pallas kernels for 0% -> 0%
where the time goes in v13:
time: 444 us; the launch traced here: 437 us
  matrix products  160 us (36%)
  waiting for transfers between devices  133 us (30%)
  local copies, waits for them, and re-layouts  76.6 us (17%)
  other arithmetic  28.7 us (6%)
  starting transfers between devices  22.7 us (5%)
  between operations  15.6 us (4%)
    ppermute x24, waiting for transfers between devices, exchange(): lax.ppermute(pieces[m], 'tensor', [(i, i ^ m) for i in range(n_dev)])  132 us
    dot_general x4, matrix products, shards(): lax.dot_general(active, cot, (((0,), (0,)), ((), ())), preferred_element_...  34.3 us
    dot_general x4, matrix products, shards(): jnp.dot(returned, w1tp, preferred_element_type=jnp.float32)  33.4 us
    dot_general x4, matrix products, shards(): jnp.dot(x, w1p, preferred_element_type=jnp.float32).astype(jnp.bfloat16)  30.9 us
    dot_general x4, matrix products, shards(): backed = jnp.dot(cot, w2p, preferred_element_type=jnp.float32)  30.7 us
    unnamed x86, local copies, waits for them, and re-layouts  28.2 us
    dot_general x3, matrix products, shards(): lax.dot_general(x, returned, (((0,), (0,)), ((), ())), preferred_element_...  27.6 us
    ppermute x24, starting transfers between devices, exchange(): lax.ppermute(pieces[m], 'tensor', [(i, i ^ m) for i in range(n_dev)])  18.2 us
  transfers between devices with their start and end apart: 28, of which 10 were waited for; matrix products, arithmetic and copies ran while one was open for 53% of the time, Pallas kernels for 0%

profile of v13, /device:TPU:0, one launch (start us, length us, event | category | flops | bytes accessed | tf_op | source)
XLA Modules:
  0.0 437.4 jit_solution(17977205728332719168)
XLA Ops:
  14.7 7.8 %convert_bitcast_fusion = bf16[2048,1024]{0,1:T(8,128)(2,1)S(1)} fusion(bf16[1024,1024]{0,1:T(8,128)(2,1)S(1)} %bitcast.110, bf16[8192,1024]{1,0:T(8,128)(2,1)} %param.4), kind=kOutput, calls=%fused_computation.50 | convolution fusion | flops 4297064448 | bytes 10485760 | tf_op jit(solution)/shard_map/dot_general | solution.py:74
  28.4 7.0 %convert_bitcast_fusion.1 = bf16[2048,1024]{0,1:T(8,128)(2,1)S(1)} fusion(bf16[1024,1024]{0,1:T(8,128)(2,1)S(1)} %bitcast.111, bf16[8192,1024]{1,0:T(8,128)(2,1)} %param.4), kind=kOutput, calls=%fused_computation.51 | convolution fusion | flops 4297064448 | bytes 10485760 | tf_op jit(solution)/shard_map/dot_general | solution.py:74
  40.5 7.5 %convert_bitcast_fusion.2 = bf16[2048,1024]{0,1:T(8,128)(2,1)S(1)} fusion(bf16[1024,1024]{0,1:T(8,128)(2,1)} %bitcast.112, bf16[8192,1024]{1,0:T(8,128)(2,1)} %param.4), kind=kOutput, calls=%fused_computation.52 | convolution fusion | flops 4297064448 | bytes 10485760 | tf_op jit(solution)/shard_map/dot_general | solution.py:74
  48.1 8.6 %convert_bitcast_fusion.3 = bf16[2048,1024]{0,1:T(8,128)(2,1)S(1)} fusion(bf16[1024,1024]{0,1:T(8,128)(2,1)S(1)} %bitcast.113, bf16[8192,1024]{1,0:T(8,128)(2,1)} %param.4), kind=kOutput, calls=%fused_computation.53 | convolution fusion | flops 4297064448 | bytes 10485760 | tf_op jit(solution)/shard_map/dot_general | solution.py:74
  57.2 11.2 %convolution_bitcast_fusion = bf16[2048,1024]{0,1:T(8,128)(2,1)} fusion(bf16[1024,1024]{0,1:T(8,128)(2,1)S(1)} %bitcast.106, bf16[8192,1024]{1,0:T(8,128)(2,1)} %param.5), kind=kOutput, calls=%fused_computation.4 | convolution fusion | flops 4294967296 | bytes 10485760 | tf_op jit(solution)/shard_map/dot_general | solution.py:75
  68.5 6.2 %convolution_bitcast_fusion.1 = bf16[2048,1024]{0,1:T(8,128)(2,1)} fusion(bf16[1024,1024]{0,1:T(8,128)(2,1)S(1)} %bitcast.107, bf16[8192,1024]{1,0:T(8,128)(2,1)S(1)} %bitcast.120), kind=kOutput, calls=%fused_computation.5 | convolution fusion | flops 4294967296 | bytes 10485760 | tf_op jit(solution)/shard_map/dot_general | solution.py:75
  74.6 6.2 %convolution_bitcast_fusion.2 = bf16[2048,1024]{0,1:T(8,128)(2,1)} fusion(bf16[1024,1024]{0,1:T(8,128)(2,1)S(1)} %bitcast.108, bf16[8192,1024]{1,0:T(8,128)(2,1)S(1)} %bitcast.120), kind=kOutput, calls=%fused_computation.6 | convolution fusion | flops 4294967296 | bytes 10485760 | tf_op jit(solution)/shard_map/dot_general | solution.py:75
  85.4 4.6 %slice.140 = bf16[2048,1024]{1,0:T(8,128)(2,1)} slice(bf16[8192,1024]{1,0:T(8,128)(2,1)} %param.4), slice={[6144:8192], [0:1024]} | slice | bytes 8388608
  91.8 6.6 %copy.59 = bf16[2048,1024]{0,1:T(8,128)(2,1)} copy(bf16[2048,1024]{1,0:T(8,128)(2,1)} %slice.140) | data formatting | bytes 8388608
  99.7 7.1 %convolution_bitcast_fusion.3 = bf16[2048,1024]{0,1:T(8,128)(2,1)S(1)} fusion(bf16[1024,1024]{0,1:T(8,128)(2,1)S(1)} %bitcast.109, bf16[8192,1024]{1,0:T(8,128)(2,1)} %param.5), kind=kOutput, calls=%fused_computation.7 | convolution fusion | flops 4294967296 | bytes 10485760 | tf_op jit(solution)/shard_map/dot_general | solution.py:75
  113.7 7.8 %fusion.7 = f32[1024,1024]{1,0:T(8,128)S(1)} fusion(bf16[2048,256]{0,1:T(8,128)(2,1)} %collective-permute-done.16, bf16[2048,256]{0,1:T(8,128)(2,1)} %collective-permute-done.14, bf16[2048,256]{0,1:T(8,128)(2,1)} %collective-permute-done.12, bf16[2048,256]{0,1:T(8,128)(2,1)S(1)} %get-tuple-element.46, bf16[8192,1024]{1,0:T(8,128)(2,1)} %param.5), kind=kOutput, calls=%fused_computation.19 | convolution fusion | flops 4315938816 | bytes 12582912 | tf_op jit(solution)/shard_map/dot_general | solution.py:82
  122.4 18.6 %collective-permute-done.7 = bf16[2048,256]{0,1:T(8,128)(2,1)S(1)} collective-permute-done((bf16[2048,256]{0,1:T(8,128)(2,1)S(1)}, bf16[2048,256]{0,1:T(8,128)(2,1)S(1)}, u32[]{:S(2)}, u32[]{:S(2)}) %collective-permute-start.7) | collective-permute-done | bytes 1048608 | tf_op jit(solution)/shard_map/ppermute | solution.py:37
  142.2 21.7 %collective-permute-done.5 = bf16[2048,256]{0,1:T(8,128)(2,1)S(1)} collective-permute-done((bf16[2048,256]{0,1:T(8,128)(2,1)S(1)}, bf16[2048,256]{0,1:T(8,128)(2,1)S(1)}, u32[]{:S(2)}, u32[]{:S(2)}) %collective-permute-start.5) | collective-permute-done | bytes 1048608 | tf_op jit(solution)/shard_map/ppermute | solution.py:37
  167.5 6.8 %fusion = f32[1024,1024]{1,0:T(8,128)S(1)} fusion(bf16[2048,256]{0,1:T(8,128)(2,1)S(1)} %collective-permute-done.7, bf16[2048,256]{0,1:T(8,128)(2,1)S(1)} %collective-permute-done.5, bf16[2048,256]{0,1:T(8,128)(2,1)S(1)} %collective-permute-done.3, bf16[2048,256]{0,1:T(8,128)(2,1)S(1)} %get-tuple-element.51, bf16[8192,1024]{1,0:T(8,128)(2,1)} %param.5), kind=kOutput, calls=%fused_computation.11 | convolution fusion | flops 4315938816 | bytes 12582912 | tf_op jit(solution)/shard_map/dot_general | solution.py:82
  174.3 11.7 %collective-permute-done.2 = bf16[2048,256]{0,1:T(8,128)(2,1)S(1)} collective-permute-done((bf16[2048,256]{0,1:T(8,128)(2,1)S(1)}, bf16[2048,256]{0,1:T(8,128)(2,1)S(1)}, u32[]{:S(2)}, u32[]{:S(2)}) %collective-permute-start.2) | collective-permute-done | bytes 1048608 | tf_op jit(solution)/shard_map/ppermute | solution.py:37
  186.1 22.5 %collective-permute-done.1 = bf16[2048,256]{0,1:T(8,128)(2,1)S(1)} collective-permute-done((bf16[2048,256]{0,1:T(8,128)(2,1)S(1)}, bf16[2048,256]{0,1:T(8,128)(2,1)S(1)}, u32[]{:S(2)}, u32[]{:S(2)}) %collective-permute-start.1) | collective-permute-done | bytes 1048608 | tf_op jit(solution)/shard_map/ppermute | solution.py:37
  213.8 8.8 %fusion.14 = f32[1024,1024]{1,0:T(8,128)} fusion(bf16[2048,256]{0,1:T(8,128)(2,1)S(1)} %collective-permute-done.2, bf16[2048,256]{0,1:T(8,128)(2,1)S(1)} %collective-permute-done.1, bf16[2048,256]{0,1:T(8,128)(2,1)S(1)} %collective-permute-done, bf16[2048,256]{0,1:T(8,128)(2,1)S(1)} %get-tuple-element.56, bf16[8192,1024]{1,0:T(8,128)(2,1)} %param.5), kind=kOutput, calls=%fused_computation.27 | convolution fusion | flops 4315938816 | bytes 12582912 | tf_op jit(solution)/shard_map/dot_general | solution.py:82
  228.8 10.9 %add_add_fusion = f32[1024,1024]{1,0:T(8,128)} fusion(f32[1024,1024]{1,0:T(8,128)} %fusion.14, f32[1024,1024]{1,0:T(8,128)S(1)} %fusion, f32[1024,1024]{1,0:T(8,128)S(1)} %fusion.7, bf16[8192,1024]{1,0:T(8,128)(2,1)} %param.5, bf16[2048,256]{0,1:T(8,128)(2,1)} %collective-permute-done.11, bf16[2048,256]{0,1:T(8,128)(2,1)} %collective-permute-done.10, ...), kind=kOutput, calls=%fused_computation.47 | convolution fusion | flops 4319084544 | bytes 25165824 | tf_op jit(solution)/shard_map/dot_general | solution.py:82
  239.7 6.1 %reshape.103 = f32[4,4,4,16,4,256]{5,4,3,2,1,0:T(4,128)} reshape(f32[1024,1024]{1,0:T(8,128)} %add_add_fusion) | data formatting | bytes 8388608 | tf_op jit(solution)/shard_map/reshape | solution.py:112
  245.8 5.3 %select_reduce_fusion.1 = f32[4,4,4,16,256]{4,3,2,1,0:T(8,128)S(1)} fusion(f32[4,4,4,16,4,256]{5,4,3,2,1,0:T(4,128)} %reshape.103, pred[4,4]{1,0:T(4,128)(4,1)S(1)} %copy.42), kind=kLoop, calls=%fused_computation.46 | loop fusion | flops 1835008 | bytes 5242896 | tf_op jit(solution)/shard_map/reduce_sum | solution.py:113
  257.0 9.2 %convolution_convert_fusion = bf16[2048,1024]{1,0:T(8,128)(2,1)} fusion(bf16[1024,1024]{1,0:T(8,128)(2,1)} %bitcast.102, bf16[2048,256]{0,1:T(8,128)(2,1)} %collective-permute-done.17, bf16[2048,256]{0,1:T(8,128)(2,1)} %collective-permute-done.15, bf16[2048,256]{0,1:T(8,128)(2,1)} %collective-permute-done.13, bf16[2048,256]{0,1:T(8,128)(2,1)S(1)} %copy-done.23), kind=kOutput, calls=%fused_computation.54 | convolution fusion | flops 4313841664 | bytes 10485760 | tf_op jit(solution)/shard_map/dot_general | solution.py:91
  266.2 9.8 %fusion.50 = f32[1024,1024]{0,1:T(8,128)} fusion(bf16[8192,1024]{1,0:T(8,128)(2,1)} %param.4, bf16[2048,256]{0,1:T(8,128)(2,1)} %collective-permute-done.17, bf16[2048,256]{0,1:T(8,128)(2,1)} %collective-permute-done.15, bf16[2048,256]{0,1:T(8,128)(2,1)} %collective-permute-done.13, bf16[2048,256]{0,1:T(8,128)(2,1)S(1)} %copy-done.23), kind=kOutput, calls=%fused_computation.74 | convolution fusion | flops 4311744512 | bytes 12582912 | tf_op jit(solution)/shard_map/dot_general | solution.py:93
  279.1 22.8 %collective-permute-done.6 = bf16[2048,256]{0,1:T(8,128)(2,1)} collective-permute-done((bf16[2048,256]{0,1:T(8,128)(2,1)}, bf16[2048,256]{0,1:T(8,128)(2,1)}, u32[]{:S(2)}, u32[]{:S(2)}) %collective-permute-start.6) | collective-permute-done | bytes 1048608 | tf_op jit(solution)/shard_map/ppermute | solution.py:37
  302.0 9.6 %fusion.47 = f32[1024,1024]{0,1:T(8,128)} fusion(bf16[8192,1024]{1,0:T(8,128)(2,1)} %param.4, bf16[2048,256]{0,1:T(8,128)(2,1)} %collective-permute-done.8, bf16[2048,256]{0,1:T(8,128)(2,1)} %collective-permute-done.6, bf16[2048,256]{0,1:T(8,128)(2,1)S(1)} %collective-permute-done.4, bf16[2048,256]{0,1:T(8,128)(2,1)S(1)} %copy-done.24), kind=kOutput, calls=%fused_computation.73 | convolution fusion | flops 4311744512 | bytes 12582912 | tf_op jit(solution)/shard_map/dot_general | solution.py:93
  311.5 8.1 %convolution_convert_fusion.1 = bf16[2048,1024]{1,0:T(8,128)(2,1)} fusion(bf16[1024,1024]{1,0:T(8,128)(2,1)S(1)} %bitcast.104, bf16[2048,256]{0,1:T(8,128)(2,1)} %collective-permute-done.8, bf16[2048,256]{0,1:T(8,128)(2,1)} %collective-permute-done.6, bf16[2048,256]{0,1:T(8,128)(2,1)S(1)} %collective-permute-done.4, bf16[2048,256]{0,1:T(8,128)(2,1)S(1)} %copy-done.24), kind=kOutput, calls=%fused_computation.55 | convolution fusion | flops 4313841664 | bytes 10485760 | tf_op jit(solution)/shard_map/dot_general | solution.py:91
  321.5 6.6 %broadcast_in_dim.150 = bf16[8192,1024]{1,0:T(8,128)(2,1)} broadcast(bf16[]{:T(256)} %constant.53.clone.1), dimensions={} | broadcast | bytes 16777218 | tf_op jit(solution)/shard_map/broadcast_in_dim | solution.py:69
  338.5 8.4 %collective-permute-done.19 = bf16[2048,256]{0,1:T(8,128)(2,1)} collective-permute-done((bf16[2048,256]{0,1:T(8,128)(2,1)}, bf16[2048,256]{0,1:T(8,128)(2,1)}, u32[]{:S(2)}, u32[]{:S(2)}) %collective-permute-start.19) | collective-permute-done | bytes 1048608 | tf_op jit(solution)/shard_map/ppermute | solution.py:37
  348.2 20.8 %collective-permute-done.20 = bf16[2048,256]{0,1:T(8,128)(2,1)} collective-permute-done((bf16[2048,256]{0,1:T(8,128)(2,1)}, bf16[2048,256]{0,1:T(8,128)(2,1)}, u32[]{:S(2)}, u32[]{:S(2)}) %collective-permute-start.20) | collective-permute-done | bytes 1048608 | tf_op jit(solution)/shard_map/ppermute | solution.py:37
  372.4 8.3 %bitcast_add_fusion = f32[1024,1024]{0,1:T(8,128)} fusion(f32[1024,1024]{0,1:T(8,128)S(1)} %copy-done.31, f32[1024,1024]{0,1:T(8,128)S(1)} %copy-done.30, bf16[2048,1024]{0,1:T(8,128)(2,1)S(1)} %constant_dynamic-update-slice_fusion, bf16[8192,1024]{1,0:T(8,128)(2,1)} %param.4), kind=kOutput, calls=%fused_computation.42 | convolution fusion | flops 4297064448 | bytes 20971520 | tf_op jit(solution)/shard_map/dot_general | solution.py:93
  380.6 5.9 %reshape.104 = f32[4,256,4,4,4,16]{1,0,5,4,3,2:T(4,128)} reshape(f32[1024,1024]{0,1:T(8,128)} %bitcast_add_fusion) | data formatting | bytes 8388608 | tf_op jit(solution)/shard_map/reshape | solution.py:119
  410.8 9.6 %convert_dynamic-update-slice_fusion.1 = bf16[8192,1024]{1,0:T(8,128)(2,1)} fusion(bf16[8192,1024]{1,0:T(8,128)(2,1)} %constant_dynamic-update-slice_fusion.8, bf16[2048,1024]{0,1:T(8,128)(2,1)} %copy-done.26, bf16[1024,1024]{1,0:T(8,128)(2,1)} %bitcast.103), kind=kOutput, calls=%fused_computation.49 | convolution fusion | flops 4297064448 | bytes 10485760 | tf_op jit(solution)/shard_map/dot_general | solution.py:91
  420.4 6.5 %convert_dynamic-update-slice_fusion = bf16[8192,1024]{1,0:T(8,128)(2,1)} fusion(bf16[8192,1024]{1,0:T(8,128)(2,1)} %convert_dynamic-update-slice_fusion.1, bf16[2048,1024]{0,1:T(8,128)(2,1)S(1)} %copy-done.25, bf16[1024,1024]{1,0:T(8,128)(2,1)S(1)} %bitcast.105), kind=kOutput, calls=%fused_computation.48 | convolution fusion | flops 4297064448 | bytes 10485760 | tf_op jit(solution)/shard_map/dot_general | solution.py:91
  (178 shorter events, 103.4 us)
Async XLA Ops:
  7.2 323.5 %all-reduce.3.cloned.1.call-start = ((), (), s32[]{:S(2)}) async-start(), calls=%async_computation | async-start | bytes 2097152
  24.3 82.5 %collective-permute-start.12 = (bf16[2048,256]{0,1:T(8,128)(2,1)}, bf16[2048,256]{0,1:T(8,128)(2,1)}, u32[]{:S(2)}, u32[]{:S(2)}) collective-permute-start(bf16[2048,256]{0,1:T(8,128)(2,1)} %get-tuple-element.61), channel_id=1, source_target_pairs={{0,4},{4,0},{8,12},{12,8},{1,5},{5,1},{9,13},{13,9},{2,6},{6,2},{1... | collective-permute-start | bytes 3145736 | tf_op jit(solution)/shard_map/ppermute | solution.py:37
  24.8 82.8 %collective-permute-start.16 = (bf16[2048,256]{0,1:T(8,128)(2,1)}, bf16[2048,256]{0,1:T(8,128)(2,1)}, u32[]{:S(2)}, u32[]{:S(2)}) collective-permute-start(bf16[2048,256]{0,1:T(8,128)(2,1)} %get-tuple-element.62), channel_id=1, source_target_pairs={{0,12},{4,8},{8,4},{12,0},{1,13},{5,9},{9,5},{13,1},{2,14},{6,10},... | collective-permute-start | bytes 3145736 | tf_op jit(solution)/shard_map/ppermute | solution.py:37
  27.4 80.9 %collective-permute-start.14 = (bf16[2048,256]{0,1:T(8,128)(2,1)}, bf16[2048,256]{0,1:T(8,128)(2,1)}, u32[]{:S(2)}, u32[]{:S(2)}) collective-permute-start(bf16[2048,256]{0,1:T(8,128)(2,1)} %get-tuple-element.63), channel_id=1, source_target_pairs={{0,8},{4,12},{8,0},{12,4},{1,9},{5,13},{9,1},{13,5},{2,10},{6,14},... | collective-permute-start | bytes 3145736 | tf_op jit(solution)/shard_map/ppermute | solution.py:37
  39.2 183.4 %collective-permute-start.11 = (bf16[2048,256]{0,1:T(8,128)(2,1)}, bf16[2048,256]{0,1:T(8,128)(2,1)}, u32[]{:S(2)}, u32[]{:S(2)}) collective-permute-start(bf16[2048,256]{0,1:T(8,128)(2,1)} %get-tuple-element.64), channel_id=1, source_target_pairs={{0,12},{4,8},{8,4},{12,0},{1,13},{5,9},{9,5},{13,1},{2,14},{6,10},... | collective-permute-start | bytes 3145736 | tf_op jit(solution)/shard_map/ppermute | solution.py:37
  39.6 183.3 %collective-permute-start.10 = (bf16[2048,256]{0,1:T(8,128)(2,1)}, bf16[2048,256]{0,1:T(8,128)(2,1)}, u32[]{:S(2)}, u32[]{:S(2)}) collective-permute-start(bf16[2048,256]{0,1:T(8,128)(2,1)} %get-tuple-element.65), channel_id=1, source_target_pairs={{0,8},{4,12},{8,0},{12,4},{1,9},{5,13},{9,1},{13,5},{2,10},{6,14},... | collective-permute-start | bytes 3145736 | tf_op jit(solution)/shard_map/ppermute | solution.py:37
  106.8 14.7 %collective-permute-start.3 = (bf16[2048,256]{0,1:T(8,128)(2,1)S(1)}, bf16[2048,256]{0,1:T(8,128)(2,1)S(1)}, u32[]{:S(2)}, u32[]{:S(2)}) collective-permute-start(bf16[2048,256]{0,1:T(8,128)(2,1)S(1)} %copy-done.22), channel_id=1, source_target_pairs={{0,4},{4,0},{8,12},{12,8},{1,5},{5,1},{9,13},{13,9},{2,6},{6,2},{1... | collective-permute-start | bytes 3145736 | tf_op jit(solution)/shard_map/ppermute | solution.py:37
  107.6 33.4 %collective-permute-start.7 = (bf16[2048,256]{0,1:T(8,128)(2,1)S(1)}, bf16[2048,256]{0,1:T(8,128)(2,1)S(1)}, u32[]{:S(2)}, u32[]{:S(2)}) collective-permute-start(bf16[2048,256]{0,1:T(8,128)(2,1)S(1)} %copy-done.21), channel_id=1, source_target_pairs={{0,12},{4,8},{8,4},{12,0},{1,13},{5,9},{9,5},{13,1},{2,14},{6,10},... | collective-permute-start | bytes 3145736 | tf_op jit(solution)/shard_map/ppermute | solution.py:37
  108.3 55.5 %collective-permute-start.5 = (bf16[2048,256]{0,1:T(8,128)(2,1)S(1)}, bf16[2048,256]{0,1:T(8,128)(2,1)S(1)}, u32[]{:S(2)}, u32[]{:S(2)}) collective-permute-start(bf16[2048,256]{0,1:T(8,128)(2,1)S(1)} %copy-done.20), channel_id=1, source_target_pairs={{0,8},{4,12},{8,0},{12,4},{1,9},{5,13},{9,1},{13,5},{2,10},{6,14},... | collective-permute-start | bytes 3145736 | tf_op jit(solution)/shard_map/ppermute | solution.py:37
  113.7 50.1 %copy-start.2 = (bf16[2048,1024]{0,1:T(8,128)(2,1)S(1)}, bf16[2048,1024]{0,1:T(8,128)(2,1)}, u32[]{:S(2)}) copy-start(bf16[2048,1024]{0,1:T(8,128)(2,1)} %convolution_bitcast_fusion.2) | copy-start | bytes 12582916
  121.5 64.4 %collective-permute-start.2 = (bf16[2048,256]{0,1:T(8,128)(2,1)S(1)}, bf16[2048,256]{0,1:T(8,128)(2,1)S(1)}, u32[]{:S(2)}, u32[]{:S(2)}) collective-permute-start(bf16[2048,256]{0,1:T(8,128)(2,1)S(1)} %copy-done.19), channel_id=1, source_target_pairs={{0,12},{4,8},{8,4},{12,0},{1,13},{5,9},{9,5},{13,1},{2,14},{6,10},... | collective-permute-start | bytes 3145736 | tf_op jit(solution)/shard_map/ppermute | solution.py:37
  141.0 67.6 %collective-permute-start.1 = (bf16[2048,256]{0,1:T(8,128)(2,1)S(1)}, bf16[2048,256]{0,1:T(8,128)(2,1)S(1)}, u32[]{:S(2)}, u32[]{:S(2)}) collective-permute-start(bf16[2048,256]{0,1:T(8,128)(2,1)S(1)} %copy-done.18), channel_id=1, source_target_pairs={{0,8},{4,12},{8,0},{12,4},{1,9},{5,13},{9,1},{13,5},{2,10},{6,14},... | collective-permute-start | bytes 3145736 | tf_op jit(solution)/shard_map/ppermute | solution.py:37
  163.8 45.5 %collective-permute-start = (bf16[2048,256]{0,1:T(8,128)(2,1)S(1)}, bf16[2048,256]{0,1:T(8,128)(2,1)S(1)}, u32[]{:S(2)}, u32[]{:S(2)}) collective-permute-start(bf16[2048,256]{0,1:T(8,128)(2,1)S(1)} %get-tuple-element.72), channel_id=1, source_target_pairs={{0,4},{4,0},{8,12},{12,8},{1,5},{5,1},{9,13},{13,9},{2,6},{6,2},{1... | collective-permute-start | bytes 3145736 | tf_op jit(solution)/shard_map/ppermute | solution.py:37
  185.9 38.2 %collective-permute-start.9 = (bf16[2048,256]{0,1:T(8,128)(2,1)S(1)}, bf16[2048,256]{0,1:T(8,128)(2,1)S(1)}, u32[]{:S(2)}, u32[]{:S(2)}) collective-permute-start(bf16[2048,256]{0,1:T(8,128)(2,1)S(1)} %copy-done.17), channel_id=1, source_target_pairs={{0,4},{4,0},{8,12},{12,8},{1,5},{5,1},{9,13},{13,9},{2,6},{6,2},{1... | collective-permute-start | bytes 3145736 | tf_op jit(solution)/shard_map/ppermute | solution.py:37
  208.6 45.1 %collective-permute-start.17 = (bf16[2048,256]{0,1:T(8,128)(2,1)}, bf16[2048,256]{0,1:T(8,128)(2,1)}, u32[]{:S(2)}, u32[]{:S(2)}) collective-permute-start(bf16[2048,256]{0,1:T(8,128)(2,1)} %get-tuple-element.48), channel_id=1, source_target_pairs={{0,12},{4,8},{8,4},{12,0},{1,13},{5,9},{9,5},{13,1},{2,14},{6,10},... | collective-permute-start | bytes 3145736 | tf_op jit(solution)/shard_map/ppermute | solution.py:37
  209.3 47.7 %collective-permute-start.15 = (bf16[2048,256]{0,1:T(8,128)(2,1)}, bf16[2048,256]{0,1:T(8,128)(2,1)}, u32[]{:S(2)}, u32[]{:S(2)}) collective-permute-start(bf16[2048,256]{0,1:T(8,128)(2,1)} %get-tuple-element.49), channel_id=1, source_target_pairs={{0,8},{4,12},{8,0},{12,4},{1,9},{5,13},{9,1},{13,5},{2,10},{6,14},... | collective-permute-start | bytes 3145736 | tf_op jit(solution)/shard_map/ppermute | solution.py:37
  222.6 34.4 %collective-permute-start.13 = (bf16[2048,256]{0,1:T(8,128)(2,1)}, bf16[2048,256]{0,1:T(8,128)(2,1)}, u32[]{:S(2)}, u32[]{:S(2)}) collective-permute-start(bf16[2048,256]{0,1:T(8,128)(2,1)} %get-tuple-element.50), channel_id=1, source_target_pairs={{0,4},{4,0},{8,12},{12,8},{1,5},{5,1},{9,13},{13,9},{2,6},{6,2},{1... | collective-permute-start | bytes 3145736 | tf_op jit(solution)/shard_map/ppermute | solution.py:37
  222.8 56.3 %collective-permute-start.8 = (bf16[2048,256]{0,1:T(8,128)(2,1)}, bf16[2048,256]{0,1:T(8,128)(2,1)}, u32[]{:S(2)}, u32[]{:S(2)}) collective-permute-start(bf16[2048,256]{0,1:T(8,128)(2,1)} %get-tuple-element.53), channel_id=1, source_target_pairs={{0,12},{4,8},{8,4},{12,0},{1,13},{5,9},{9,5},{13,1},{2,14},{6,10},... | collective-permute-start | bytes 3145736 | tf_op jit(solution)/shard_map/ppermute | solution.py:37
  224.2 77.8 %collective-permute-start.6 = (bf16[2048,256]{0,1:T(8,128)(2,1)}, bf16[2048,256]{0,1:T(8,128)(2,1)}, u32[]{:S(2)}, u32[]{:S(2)}) collective-permute-start(bf16[2048,256]{0,1:T(8,128)(2,1)} %get-tuple-element.54), channel_id=1, source_target_pairs={{0,8},{4,12},{8,0},{12,4},{1,9},{5,13},{9,1},{13,5},{2,10},{6,14},... | collective-permute-start | bytes 3145736 | tf_op jit(solution)/shard_map/ppermute | solution.py:37
  253.6 48.3 %collective-permute-start.4 = (bf16[2048,256]{0,1:T(8,128)(2,1)}, bf16[2048,256]{0,1:T(8,128)(2,1)S(1)}, u32[]{:S(2)}, u32[]{:S(2)}) collective-permute-start(bf16[2048,256]{0,1:T(8,128)(2,1)} %get-tuple-element.55), channel_id=1, source_target_pairs={{0,4},{4,0},{8,12},{12,8},{1,5},{5,1},{9,13},{13,9},{2,6},{6,2},{1... | collective-permute-start | bytes 3145736 | tf_op jit(solution)/shard_map/ppermute | solution.py:37
  266.2 35.8 %copy-start.24 = (bf16[2048,256]{0,1:T(8,128)(2,1)S(1)}, bf16[2048,256]{0,1:T(8,128)(2,1)}, u32[]{:S(2)}) copy-start(bf16[2048,256]{0,1:T(8,128)(2,1)} %get-tuple-element.52) | copy-start | bytes 3145732
  276.0 110.6 %collective-permute-start.21 = (bf16[2048,256]{0,1:T(8,128)(2,1)}, bf16[2048,256]{0,1:T(8,128)(2,1)}, u32[]{:S(2)}, u32[]{:S(2)}) collective-permute-start(bf16[2048,256]{0,1:T(8,128)(2,1)} %get-tuple-element.28), channel_id=1, source_target_pairs={{0,4},{4,0},{8,12},{12,8},{1,5},{5,1},{9,13},{13,9},{2,6},{6,2},{1... | collective-permute-start | bytes 3145736 | tf_op jit(solution)/shard_map/ppermute | solution.py:37
  276.0 112.9 %collective-permute-start.22 = (bf16[2048,256]{0,1:T(8,128)(2,1)}, bf16[2048,256]{0,1:T(8,128)(2,1)S(1)}, u32[]{:S(2)}, u32[]{:S(2)}) collective-permute-start(bf16[2048,256]{0,1:T(8,128)(2,1)} %get-tuple-element.29), channel_id=1, source_target_pairs={{0,8},{4,12},{8,0},{12,4},{1,9},{5,13},{9,1},{13,5},{2,10},{6,14},... | collective-permute-start | bytes 3145736 | tf_op jit(solution)/shard_map/ppermute | solution.py:37
  319.7 16.1 %collective-permute-start.18 = (bf16[2048,256]{0,1:T(8,128)(2,1)}, bf16[2048,256]{0,1:T(8,128)(2,1)}, u32[]{:S(2)}, u32[]{:S(2)}) collective-permute-start(bf16[2048,256]{0,1:T(8,128)(2,1)} %get-tuple-element.24), channel_id=1, source_target_pairs={{0,4},{4,0},{8,12},{12,8},{1,5},{5,1},{9,13},{13,9},{2,6},{6,2},{1... | collective-permute-start | bytes 3145736 | tf_op jit(solution)/shard_map/ppermute | solution.py:37
  319.7 27.2 %collective-permute-start.19 = (bf16[2048,256]{0,1:T(8,128)(2,1)}, bf16[2048,256]{0,1:T(8,128)(2,1)}, u32[]{:S(2)}, u32[]{:S(2)}) collective-permute-start(bf16[2048,256]{0,1:T(8,128)(2,1)} %get-tuple-element.25), channel_id=1, source_target_pairs={{0,8},{4,12},{8,0},{12,4},{1,9},{5,13},{9,1},{13,5},{2,10},{6,14},... | collective-permute-start | bytes 3145736 | tf_op jit(solution)/shard_map/ppermute | solution.py:37
  321.1 47.9 %collective-permute-start.20 = (bf16[2048,256]{0,1:T(8,128)(2,1)}, bf16[2048,256]{0,1:T(8,128)(2,1)}, u32[]{:S(2)}, u32[]{:S(2)}) collective-permute-start(bf16[2048,256]{0,1:T(8,128)(2,1)} %get-tuple-element.26), channel_id=1, source_target_pairs={{0,12},{4,8},{8,4},{12,0},{1,13},{5,9},{9,5},{13,1},{2,14},{6,10},... | collective-permute-start | bytes 3145736 | tf_op jit(solution)/shard_map/ppermute | solution.py:37
  333.2 39.2 %copy-start.31 = (f32[1024,1024]{0,1:T(8,128)S(1)}, f32[1024,1024]{0,1:T(8,128)}, u32[]{:S(2)}) copy-start(f32[1024,1024]{0,1:T(8,128)} %fusion.47) | copy-start | bytes 12582916
  335.8 36.6 %copy-start.30 = (f32[1024,1024]{0,1:T(8,128)S(1)}, f32[1024,1024]{0,1:T(8,128)}, u32[]{:S(2)}) copy-start(f32[1024,1024]{0,1:T(8,128)} %fusion.50) | copy-start | bytes 12582916
  335.8 58.0 %collective-permute-start.23 = (bf16[2048,256]{0,1:T(8,128)(2,1)}, bf16[2048,256]{0,1:T(8,128)(2,1)S(1)}, u32[]{:S(2)}, u32[]{:S(2)}) collective-permute-start(bf16[2048,256]{0,1:T(8,128)(2,1)} %get-tuple-element.30), channel_id=1, source_target_pairs={{0,12},{4,8},{8,4},{12,0},{1,13},{5,9},{9,5},{13,1},{2,14},{6,10},... | collective-permute-start | bytes 3145736 | tf_op jit(solution)/shard_map/ppermute | solution.py:37
  406.3 21.7 %collective-permute-start.24 = (f32[64,4,256]{2,0,1:T(8,128)S(1)}, f32[64,4,256]{2,0,1:T(8,128)S(1)}, u32[]{:S(2)}, u32[]{:S(2)}) collective-permute-start(f32[64,4,256]{2,0,1:T(8,128)S(1)} %bitcast.117), channel_id=1, source_target_pairs={{0,1},{1,0},{2,3},{3,2},{4,5},{5,4},{6,7},{7,6},{8,9},{9,8},{10,11... | collective-permute-start | bytes 786440 | tf_op jit(solution)/shard_map/ppermute | solution.py:48
  408.2 21.3 %collective-permute-start.25 = (f32[64,4,256]{2,0,1:T(8,128)S(1)}, f32[64,4,256]{2,0,1:T(8,128)S(1)}, u32[]{:S(2)}, u32[]{:S(2)}) collective-permute-start(f32[64,4,256]{2,0,1:T(8,128)S(1)} %bitcast.116), channel_id=1, source_target_pairs={{0,2},{1,3},{2,0},{3,1},{4,6},{5,7},{6,4},{7,5},{8,10},{9,11},{10,... | collective-permute-start | bytes 786440 | tf_op jit(solution)/shard_map/ppermute | solution.py:48
  410.8 18.7 %collective-permute-start.26 = (f32[64,4,256]{2,0,1:T(8,128)S(1)}, f32[64,4,256]{2,0,1:T(8,128)S(1)}, u32[]{:S(2)}, u32[]{:S(2)}) collective-permute-start(f32[64,4,256]{2,0,1:T(8,128)S(1)} %bitcast.115), channel_id=1, source_target_pairs={{0,3},{1,2},{2,1},{3,0},{4,7},{5,6},{6,5},{7,4},{8,11},{9,10},{10,... | collective-permute-start | bytes 786440 | tf_op jit(solution)/shard_map/ppermute | solution.py:48
  (32 other events, 353.3 us)
Sparse Core Ops, SparseCore 0:
  253.8 52.9 all-reduce.2

commit v14 on v13

--- a/solution.py
+++ b/solution.py
@@ -89,7 +89,7 @@
             gf_acc = done[1] if gf_acc is None else gf_acc + done[1]
         returned = jnp.concatenate(exchange(masked, n_dev), axis=1)
         gt = jnp.dot(returned, w1tp, preferred_element_type=jnp.float32).astype(jnp.bfloat16)
-        if k + 1 < CHUNKS:
+        if k + 2 < CHUNKS:
             gf = lax.dot_general(
                 x, returned, (((0,), (0,)), ((), ())), preferred_element_type=jnp.float32
             )
@@ -104,8 +104,8 @@
     gf_last = None
     for gt, gf, at in pending:
         grad_tokens = lax.dynamic_update_slice(grad_tokens, gt, (at, 0))
-        if at == (CHUNKS - 1) * step:
-            gf_last = gf
+        if at >= (CHUNKS - 2) * step:
+            gf_last = gf if gf_last is None else gf_last + gf
         else:
             gf_acc = gf if gf_acc is None else gf_acc + gf
 

time: 444 us -> 466 us (1.050)
  waiting for transfers between devices: 133 us -> 148 us
  other arithmetic: 28.7 us -> 35.6 us
    ppermute x24, waiting for transfers between devices: 132 us -> 145 us  [exchange(): lax.ppermute(pieces[m], 'tensor', [(i, i ^ m) for i in range(n_dev)])]
    dot_general x3 -> x2, matrix products: 27.6 us -> 19.4 us  [shards(): lax.dot_general(x, returned, (((0,), (0,)), ((), ())), preferred_element_...]
    add x0 -> x1, other arithmetic: none -> 6.85 us  [shards(): gf_acc = done[1] if gf_acc is None else gf_acc + done[1]]
    dot_general x4, matrix products: 30.7 us -> 35.4 us  [shards(): backed = jnp.dot(cot, w2p, preferred_element_type=jnp.float32)]
    unnamed x86 -> x99, local copies, waits for them, and re-layouts: 28.2 us -> 33 us
  transfers between devices with their start and end apart: 28 -> 28, of which waited for: 10 -> 11; matrix products, arithmetic and copies ran while one was open for 53% -> 52% of each run, Pallas kernels for 0% -> 0%
where the time goes in v14:
time: 466 us; the launch traced here: 458 us
  matrix products  157 us (34%)
  waiting for transfers between devices  148 us (32%)
  local copies, waits for them, and re-layouts  80.6 us (17%)
  other arithmetic  35.6 us (8%)
  starting transfers between devices  22 us (5%)
  between operations  15.5 us (3%)
    ppermute x24, waiting for transfers between devices, exchange(): lax.ppermute(pieces[m], 'tensor', [(i, i ^ m) for i in range(n_dev)])  145 us
    dot_general x4, matrix products, shards(): backed = jnp.dot(cot, w2p, preferred_element_type=jnp.float32)  35.4 us
    dot_general x4, matrix products, shards(): lax.dot_general(active, cot, (((0,), (0,)), ((), ())), preferred_element_...  34.3 us
    dot_general x4, matrix products, shards(): jnp.dot(returned, w1tp, preferred_element_type=jnp.float32)  34.2 us
    unnamed x99, local copies, waits for them, and re-layouts  33 us
    dot_general x4, matrix products, shards(): jnp.dot(x, w1p, preferred_element_type=jnp.float32).astype(jnp.bfloat16)  30.9 us
    dot_general x2, matrix products, shards(): lax.dot_general(x, returned, (((0,), (0,)), ((), ())), preferred_element_...  19.4 us
    ppermute x24, starting transfers between devices, exchange(): lax.ppermute(pieces[m], 'tensor', [(i, i ^ m) for i in range(n_dev)])  17.5 us
  transfers between devices with their start and end apart: 28, of which 11 were waited for; matrix products, arithmetic and copies ran while one was open for 52% of the time, Pallas kernels for 0%

profile of v14, /device:TPU:0, one launch (start us, length us, event | category | flops | bytes accessed | tf_op | source)
XLA Modules:
  0.0 458.5 jit_solution(5234561050982483381)
XLA Ops:
  14.7 7.8 %convert_bitcast_fusion = bf16[2048,1024]{0,1:T(8,128)(2,1)S(1)} fusion(bf16[1024,1024]{0,1:T(8,128)(2,1)S(1)} %bitcast.118, bf16[8192,1024]{1,0:T(8,128)(2,1)} %param.4), kind=kOutput, calls=%fused_computation.51 | convolution fusion | flops 4297064448 | bytes 10485760 | tf_op jit(solution)/shard_map/dot_general | solution.py:74
  28.6 7.0 %convert_bitcast_fusion.1 = bf16[2048,1024]{0,1:T(8,128)(2,1)S(1)} fusion(bf16[1024,1024]{0,1:T(8,128)(2,1)S(1)} %bitcast.119, bf16[8192,1024]{1,0:T(8,128)(2,1)} %param.4), kind=kOutput, calls=%fused_computation.52 | convolution fusion | flops 4297064448 | bytes 10485760 | tf_op jit(solution)/shard_map/dot_general | solution.py:74
  40.8 7.5 %convert_bitcast_fusion.2 = bf16[2048,1024]{0,1:T(8,128)(2,1)S(1)} fusion(bf16[1024,1024]{0,1:T(8,128)(2,1)} %bitcast.120, bf16[8192,1024]{1,0:T(8,128)(2,1)} %param.4), kind=kOutput, calls=%fused_computation.53 | convolution fusion | flops 4297064448 | bytes 10485760 | tf_op jit(solution)/shard_map/dot_general | solution.py:74
  48.3 8.6 %convert_bitcast_fusion.3 = bf16[2048,1024]{0,1:T(8,128)(2,1)S(1)} fusion(bf16[1024,1024]{0,1:T(8,128)(2,1)S(1)} %bitcast.121, bf16[8192,1024]{1,0:T(8,128)(2,1)} %param.4), kind=kOutput, calls=%fused_computation.54 | convolution fusion | flops 4297064448 | bytes 10485760 | tf_op jit(solution)/shard_map/dot_general | solution.py:74
  57.4 10.0 %convolution_bitcast_fusion = bf16[2048,1024]{0,1:T(8,128)(2,1)} fusion(bf16[1024,1024]{0,1:T(8,128)(2,1)S(1)} %bitcast.114, bf16[8192,1024]{1,0:T(8,128)(2,1)} %param.5), kind=kOutput, calls=%fused_computation.4 | convolution fusion | flops 4294967296 | bytes 10485760 | tf_op jit(solution)/shard_map/dot_general | solution.py:75
  67.4 8.5 %convolution_bitcast_fusion.1 = bf16[2048,1024]{0,1:T(8,128)(2,1)} fusion(bf16[1024,1024]{0,1:T(8,128)(2,1)S(1)} %bitcast.115, bf16[8192,1024]{1,0:T(8,128)(2,1)} %param.5), kind=kOutput, calls=%fused_computation.5 | convolution fusion | flops 4294967296 | bytes 10485760 | tf_op jit(solution)/shard_map/dot_general | solution.py:75
  75.9 9.6 %convolution_bitcast_fusion.2 = bf16[2048,1024]{0,1:T(8,128)(2,1)} fusion(bf16[1024,1024]{0,1:T(8,128)(2,1)} %bitcast.116, bf16[8192,1024]{1,0:T(8,128)(2,1)} %param.5), kind=kOutput, calls=%fused_computation.6 | convolution fusion | flops 4294967296 | bytes 10485760 | tf_op jit(solution)/shard_map/dot_general | solution.py:75
  95.8 6.5 %copy.72 = bf16[2048,1024]{0,1:T(8,128)(2,1)} copy(bf16[2048,1024]{1,0:T(8,128)(2,1)} %get-tuple-element.41) | data formatting | bytes 8388608
  102.3 6.7 %copy.73 = bf16[2048,1024]{0,1:T(8,128)(2,1)} copy(bf16[2048,1024]{1,0:T(8,128)(2,1)} %get-tuple-element.42) | data formatting | bytes 8388608
  110.2 7.3 %convolution_bitcast_fusion.3 = bf16[2048,1024]{0,1:T(8,128)(2,1)S(1)} fusion(bf16[1024,1024]{0,1:T(8,128)(2,1)S(1)} %bitcast.117, bf16[8192,1024]{1,0:T(8,128)(2,1)} %param.5), kind=kOutput, calls=%fused_computation.7 | convolution fusion | flops 4294967296 | bytes 10485760 | tf_op jit(solution)/shard_map/dot_general | solution.py:75
  124.2 7.8 %fusion.7 = f32[1024,1024]{1,0:T(8,128)S(1)} fusion(bf16[2048,256]{0,1:T(8,128)(2,1)} %collective-permute-done.16, bf16[2048,256]{0,1:T(8,128)(2,1)} %collective-permute-done.14, bf16[2048,256]{0,1:T(8,128)(2,1)} %collective-permute-done.12, bf16[2048,256]{0,1:T(8,128)(2,1)S(1)} %get-tuple-element.48, bf16[8192,1024]{1,0:T(8,128)(2,1)} %param.5), kind=kOutput, calls=%fused_computation.19 | convolution fusion | flops 4315938816 | bytes 12582912 | tf_op jit(solution)/shard_map/dot_general | solution.py:82
  132.8 10.7 %collective-permute-done.7 = bf16[2048,256]{0,1:T(8,128)(2,1)S(1)} collective-permute-done((bf16[2048,256]{0,1:T(8,128)(2,1)S(1)}, bf16[2048,256]{0,1:T(8,128)(2,1)S(1)}, u32[]{:S(2)}, u32[]{:S(2)}) %collective-permute-start.7) | collective-permute-done | bytes 1048608 | tf_op jit(solution)/shard_map/ppermute | solution.py:37
  144.5 22.0 %collective-permute-done.5 = bf16[2048,256]{0,1:T(8,128)(2,1)S(1)} collective-permute-done((bf16[2048,256]{0,1:T(8,128)(2,1)S(1)}, bf16[2048,256]{0,1:T(8,128)(2,1)S(1)}, u32[]{:S(2)}, u32[]{:S(2)}) %collective-permute-start.5) | collective-permute-done | bytes 1048608 | tf_op jit(solution)/shard_map/ppermute | solution.py:37
  170.2 6.8 %fusion = f32[1024,1024]{1,0:T(8,128)S(1)} fusion(bf16[2048,256]{0,1:T(8,128)(2,1)S(1)} %collective-permute-done.7, bf16[2048,256]{0,1:T(8,128)(2,1)S(1)} %collective-permute-done.5, bf16[2048,256]{0,1:T(8,128)(2,1)S(1)} %collective-permute-done.3, bf16[2048,256]{0,1:T(8,128)(2,1)S(1)} %get-tuple-element.53, bf16[8192,1024]{1,0:T(8,128)(2,1)} %param.5), kind=kOutput, calls=%fused_computation.11 | convolution fusion | flops 4315938816 | bytes 12582912 | tf_op jit(solution)/shard_map/dot_general | solution.py:82
  176.9 11.5 %collective-permute-done.2 = bf16[2048,256]{0,1:T(8,128)(2,1)S(1)} collective-permute-done((bf16[2048,256]{0,1:T(8,128)(2,1)S(1)}, bf16[2048,256]{0,1:T(8,128)(2,1)S(1)}, u32[]{:S(2)}, u32[]{:S(2)}) %collective-permute-start.2) | collective-permute-done | bytes 1048608 | tf_op jit(solution)/shard_map/ppermute | solution.py:37
  188.8 22.4 %collective-permute-done.1 = bf16[2048,256]{0,1:T(8,128)(2,1)S(1)} collective-permute-done((bf16[2048,256]{0,1:T(8,128)(2,1)S(1)}, bf16[2048,256]{0,1:T(8,128)(2,1)S(1)}, u32[]{:S(2)}, u32[]{:S(2)}) %collective-permute-start.1) | collective-permute-done | bytes 1048608 | tf_op jit(solution)/shard_map/ppermute | solution.py:37
  216.5 8.9 %fusion.14 = f32[1024,1024]{1,0:T(8,128)} fusion(bf16[2048,256]{0,1:T(8,128)(2,1)S(1)} %collective-permute-done.2, bf16[2048,256]{0,1:T(8,128)(2,1)S(1)} %collective-permute-done.1, bf16[2048,256]{0,1:T(8,128)(2,1)S(1)} %collective-permute-done, bf16[2048,256]{0,1:T(8,128)(2,1)S(1)} %get-tuple-element.58, bf16[8192,1024]{1,0:T(8,128)(2,1)} %param.5), kind=kOutput, calls=%fused_computation.27 | convolution fusion | flops 4315938816 | bytes 12582912 | tf_op jit(solution)/shard_map/dot_general | solution.py:82
  231.6 10.9 %add_add_fusion = f32[1024,1024]{1,0:T(8,128)} fusion(f32[1024,1024]{1,0:T(8,128)} %fusion.14, f32[1024,1024]{1,0:T(8,128)S(1)} %fusion, f32[1024,1024]{1,0:T(8,128)S(1)} %fusion.7, bf16[8192,1024]{1,0:T(8,128)(2,1)} %param.5, bf16[2048,256]{0,1:T(8,128)(2,1)} %collective-permute-done.11, bf16[2048,256]{0,1:T(8,128)(2,1)} %collective-permute-done.10, ...), kind=kOutput, calls=%fused_computation.48 | convolution fusion | flops 4319084544 | bytes 25165824 | tf_op jit(solution)/shard_map/dot_general | solution.py:82
  242.5 5.8 %reshape.109 = f32[4,4,4,16,4,256]{5,4,3,2,1,0:T(4,128)} reshape(f32[1024,1024]{1,0:T(8,128)} %add_add_fusion) | data formatting | bytes 8388608 | tf_op jit(solution)/shard_map/reshape | solution.py:112
  259.4 9.3 %convolution_convert_fusion = bf16[2048,1024]{1,0:T(8,128)(2,1)} fusion(bf16[1024,1024]{1,0:T(8,128)(2,1)} %bitcast.110, bf16[2048,256]{0,1:T(8,128)(2,1)} %collective-permute-done.17, bf16[2048,256]{0,1:T(8,128)(2,1)} %collective-permute-done.15, bf16[2048,256]{0,1:T(8,128)(2,1)} %collective-permute-done.13, bf16[2048,256]{0,1:T(8,128)(2,1)S(1)} %copy-done.27), kind=kOutput, calls=%fused_computation.55 | convolution fusion | flops 4313841664 | bytes 10485760 | tf_op jit(solution)/shard_map/dot_general | solution.py:91
  268.7 9.8 %fusion.49 = f32[1024,1024]{0,1:T(8,128)} fusion(bf16[8192,1024]{1,0:T(8,128)(2,1)} %param.4, bf16[2048,256]{0,1:T(8,128)(2,1)} %collective-permute-done.17, bf16[2048,256]{0,1:T(8,128)(2,1)} %collective-permute-done.15, bf16[2048,256]{0,1:T(8,128)(2,1)} %collective-permute-done.13, bf16[2048,256]{0,1:T(8,128)(2,1)S(1)} %copy-done.28), kind=kOutput, calls=%fused_computation.72 | convolution fusion | flops 4311744512 | bytes 12582912 | tf_op jit(solution)/shard_map/dot_general | solution.py:93
  281.9 22.5 %collective-permute-done.6 = bf16[2048,256]{0,1:T(8,128)(2,1)} collective-permute-done((bf16[2048,256]{0,1:T(8,128)(2,1)}, bf16[2048,256]{0,1:T(8,128)(2,1)}, u32[]{:S(2)}, u32[]{:S(2)}) %collective-permute-start.6) | collective-permute-done | bytes 1048608 | tf_op jit(solution)/shard_map/ppermute | solution.py:37
  304.4 9.1 %convolution_convert_fusion.1 = bf16[2048,1024]{1,0:T(8,128)(2,1)} fusion(bf16[1024,1024]{1,0:T(8,128)(2,1)S(1)} %bitcast.112, bf16[2048,256]{0,1:T(8,128)(2,1)} %collective-permute-done.8, bf16[2048,256]{0,1:T(8,128)(2,1)} %collective-permute-done.6, bf16[2048,256]{0,1:T(8,128)(2,1)} %collective-permute-done.4, bf16[2048,256]{0,1:T(8,128)(2,1)} %get-tuple-element.54), kind=kOutput, calls=%fused_computation.56 | convolution fusion | flops 4313841664 | bytes 10485760 | tf_op jit(solution)/shard_map/dot_general | solution.py:91
  313.4 9.7 %fusion.46 = f32[1024,1024]{0,1:T(8,128)} fusion(bf16[8192,1024]{1,0:T(8,128)(2,1)} %param.4, bf16[2048,256]{0,1:T(8,128)(2,1)} %collective-permute-done.8, bf16[2048,256]{0,1:T(8,128)(2,1)} %collective-permute-done.6, bf16[2048,256]{0,1:T(8,128)(2,1)} %collective-permute-done.4, bf16[2048,256]{0,1:T(8,128)(2,1)S(1)} %copy-done.29), kind=kOutput, calls=%fused_computation.71 | convolution fusion | flops 4311744512 | bytes 12582912 | tf_op jit(solution)/shard_map/dot_general | solution.py:93
  325.0 6.8 %add.76 = f32[1024,1024]{0,1:T(8,128)} add(f32[1024,1024]{0,1:T(8,128)} %fusion.46, f32[1024,1024]{0,1:T(8,128)} %fusion.49) | non-fusion elementwise | flops 1048576 | bytes 12582912 | tf_op jit(solution)/shard_map/add | solution.py:89
  332.8 5.6 %reshape.110 = f32[4,256,4,4,4,16]{1,0,5,4,3,2:T(4,128)} reshape(f32[1024,1024]{0,1:T(8,128)} %add.76) | data formatting | bytes 8388608 | tf_op jit(solution)/shard_map/reshape | solution.py:119
  342.6 7.0 %broadcast_in_dim.150 = bf16[8192,1024]{1,0:T(8,128)(2,1)} broadcast(bf16[]{:T(256)} %constant.53.clone.1), dimensions={} | broadcast | bytes 16777218 | tf_op jit(solution)/shard_map/broadcast_in_dim | solution.py:69
  361.1 9.9 %collective-permute-done.23 = bf16[2048,256]{0,1:T(8,128)(2,1)} collective-permute-done((bf16[2048,256]{0,1:T(8,128)(2,1)}, bf16[2048,256]{0,1:T(8,128)(2,1)}, u32[]{:S(2)}, u32[]{:S(2)}) %collective-permute-start.23) | collective-permute-done | bytes 1048608 | tf_op jit(solution)/shard_map/ppermute | solution.py:37
  374.4 19.9 %collective-permute-done.19 = bf16[2048,256]{0,1:T(8,128)(2,1)S(1)} collective-permute-done((bf16[2048,256]{0,1:T(8,128)(2,1)S(1)}, bf16[2048,256]{0,1:T(8,128)(2,1)S(1)}, u32[]{:S(2)}, u32[]{:S(2)}) %collective-permute-start.19) | collective-permute-done | bytes 1048608 | tf_op jit(solution)/shard_map/ppermute | solution.py:37
  395.7 20.1 %collective-permute-done.20 = bf16[2048,256]{0,1:T(8,128)(2,1)S(1)} collective-permute-done((bf16[2048,256]{0,1:T(8,128)(2,1)S(1)}, bf16[2048,256]{0,1:T(8,128)(2,1)S(1)}, u32[]{:S(2)}, u32[]{:S(2)}) %collective-permute-start.20) | collective-permute-done | bytes 1048608 | tf_op jit(solution)/shard_map/ppermute | solution.py:37
  432.1 9.6 %convert_dynamic-update-slice_fusion.1 = bf16[8192,1024]{1,0:T(8,128)(2,1)} fusion(bf16[8192,1024]{1,0:T(8,128)(2,1)} %constant_dynamic-update-slice_fusion.8, bf16[2048,1024]{0,1:T(8,128)(2,1)} %copy-done.1, bf16[1024,1024]{1,0:T(8,128)(2,1)} %bitcast.111), kind=kOutput, calls=%fused_computation.50 | convolution fusion | flops 4297064448 | bytes 10485760 | tf_op jit(solution)/shard_map/dot_general | solution.py:91
  441.7 6.2 %convert_dynamic-update-slice_fusion = bf16[8192,1024]{1,0:T(8,128)(2,1)} fusion(bf16[8192,1024]{1,0:T(8,128)(2,1)} %convert_dynamic-update-slice_fusion.1, bf16[2048,1024]{0,1:T(8,128)(2,1)S(1)} %copy-done.31, bf16[1024,1024]{1,0:T(8,128)(2,1)S(1)} %bitcast.113), kind=kOutput, calls=%fused_computation.49 | convolution fusion | flops 4297064448 | bytes 10485760 | tf_op jit(solution)/shard_map/dot_general | solution.py:91
  (192 shorter events, 111.2 us)
Async XLA Ops:
  7.2 324.7 %all-reduce.3.cloned.1.call-start = ((), (), s32[]{:S(2)}) async-start(), calls=%async_computation | async-start | bytes 2097152
  24.4 93.1 %collective-permute-start.12 = (bf16[2048,256]{0,1:T(8,128)(2,1)}, bf16[2048,256]{0,1:T(8,128)(2,1)}, u32[]{:S(2)}, u32[]{:S(2)}) collective-permute-start(bf16[2048,256]{0,1:T(8,128)(2,1)} %get-tuple-element.63), channel_id=1, source_target_pairs={{0,4},{4,0},{8,12},{12,8},{1,5},{5,1},{9,13},{13,9},{2,6},{6,2},{1... | collective-permute-start | bytes 3145736 | tf_op jit(solution)/shard_map/ppermute | solution.py:37
  24.9 93.4 %collective-permute-start.16 = (bf16[2048,256]{0,1:T(8,128)(2,1)}, bf16[2048,256]{0,1:T(8,128)(2,1)}, u32[]{:S(2)}, u32[]{:S(2)}) collective-permute-start(bf16[2048,256]{0,1:T(8,128)(2,1)} %get-tuple-element.64), channel_id=1, source_target_pairs={{0,12},{4,8},{8,4},{12,0},{1,13},{5,9},{9,5},{13,1},{2,14},{6,10},... | collective-permute-start | bytes 3145736 | tf_op jit(solution)/shard_map/ppermute | solution.py:37
  27.5 91.5 %collective-permute-start.14 = (bf16[2048,256]{0,1:T(8,128)(2,1)}, bf16[2048,256]{0,1:T(8,128)(2,1)}, u32[]{:S(2)}, u32[]{:S(2)}) collective-permute-start(bf16[2048,256]{0,1:T(8,128)(2,1)} %get-tuple-element.65), channel_id=1, source_target_pairs={{0,8},{4,12},{8,0},{12,4},{1,9},{5,13},{9,1},{13,5},{2,10},{6,14},... | collective-permute-start | bytes 3145736 | tf_op jit(solution)/shard_map/ppermute | solution.py:37
  39.5 185.9 %collective-permute-start.11 = (bf16[2048,256]{0,1:T(8,128)(2,1)}, bf16[2048,256]{0,1:T(8,128)(2,1)}, u32[]{:S(2)}, u32[]{:S(2)}) collective-permute-start(bf16[2048,256]{0,1:T(8,128)(2,1)} %get-tuple-element.66), channel_id=1, source_target_pairs={{0,12},{4,8},{8,4},{12,0},{1,13},{5,9},{9,5},{13,1},{2,14},{6,10},... | collective-permute-start | bytes 3145736 | tf_op jit(solution)/shard_map/ppermute | solution.py:37
  39.8 186.0 %collective-permute-start.10 = (bf16[2048,256]{0,1:T(8,128)(2,1)}, bf16[2048,256]{0,1:T(8,128)(2,1)}, u32[]{:S(2)}, u32[]{:S(2)}) collective-permute-start(bf16[2048,256]{0,1:T(8,128)(2,1)} %get-tuple-element.67), channel_id=1, source_target_pairs={{0,8},{4,12},{8,0},{12,4},{1,9},{5,13},{9,1},{13,5},{2,10},{6,14},... | collective-permute-start | bytes 3145736 | tf_op jit(solution)/shard_map/ppermute | solution.py:37
  48.3 43.2 %copy-start.10 = (bf16[2048,1024]{0,1:T(8,128)(2,1)}, bf16[2048,1024]{0,1:T(8,128)(2,1)S(1)}, u32[]{:S(2)}) copy-start(bf16[2048,1024]{0,1:T(8,128)(2,1)S(1)} %convert_bitcast_fusion.2) | copy-start | bytes 12582916
  117.6 14.5 %collective-permute-start.3 = (bf16[2048,256]{0,1:T(8,128)(2,1)S(1)}, bf16[2048,256]{0,1:T(8,128)(2,1)S(1)}, u32[]{:S(2)}, u32[]{:S(2)}) collective-permute-start(bf16[2048,256]{0,1:T(8,128)(2,1)S(1)} %copy-done.24), channel_id=1, source_target_pairs={{0,4},{4,0},{8,12},{12,8},{1,5},{5,1},{9,13},{13,9},{2,6},{6,2},{1... | collective-permute-start | bytes 3145736 | tf_op jit(solution)/shard_map/ppermute | solution.py:37
  118.3 25.2 %collective-permute-start.7 = (bf16[2048,256]{0,1:T(8,128)(2,1)S(1)}, bf16[2048,256]{0,1:T(8,128)(2,1)S(1)}, u32[]{:S(2)}, u32[]{:S(2)}) collective-permute-start(bf16[2048,256]{0,1:T(8,128)(2,1)S(1)} %copy-done.23), channel_id=1, source_target_pairs={{0,12},{4,8},{8,4},{12,0},{1,13},{5,9},{9,5},{13,1},{2,14},{6,10},... | collective-permute-start | bytes 3145736 | tf_op jit(solution)/shard_map/ppermute | solution.py:37
  119.0 47.5 %collective-permute-start.5 = (bf16[2048,256]{0,1:T(8,128)(2,1)S(1)}, bf16[2048,256]{0,1:T(8,128)(2,1)S(1)}, u32[]{:S(2)}, u32[]{:S(2)}) collective-permute-start(bf16[2048,256]{0,1:T(8,128)(2,1)S(1)} %copy-done.22), channel_id=1, source_target_pairs={{0,8},{4,12},{8,0},{12,4},{1,9},{5,13},{9,1},{13,5},{2,10},{6,14},... | collective-permute-start | bytes 3145736 | tf_op jit(solution)/shard_map/ppermute | solution.py:37
  124.2 42.3 %copy-start.4 = (bf16[2048,1024]{0,1:T(8,128)(2,1)S(1)}, bf16[2048,1024]{0,1:T(8,128)(2,1)}, u32[]{:S(2)}) copy-start(bf16[2048,1024]{0,1:T(8,128)(2,1)} %convolution_bitcast_fusion.2) | copy-start | bytes 12582916
  132.0 56.4 %collective-permute-start.2 = (bf16[2048,256]{0,1:T(8,128)(2,1)S(1)}, bf16[2048,256]{0,1:T(8,128)(2,1)S(1)}, u32[]{:S(2)}, u32[]{:S(2)}) collective-permute-start(bf16[2048,256]{0,1:T(8,128)(2,1)S(1)} %copy-done.21), channel_id=1, source_target_pairs={{0,12},{4,8},{8,4},{12,0},{1,13},{5,9},{9,5},{13,1},{2,14},{6,10},... | collective-permute-start | bytes 3145736 | tf_op jit(solution)/shard_map/ppermute | solution.py:37
  143.5 67.7 %collective-permute-start.1 = (bf16[2048,256]{0,1:T(8,128)(2,1)S(1)}, bf16[2048,256]{0,1:T(8,128)(2,1)S(1)}, u32[]{:S(2)}, u32[]{:S(2)}) collective-permute-start(bf16[2048,256]{0,1:T(8,128)(2,1)S(1)} %copy-done.20), channel_id=1, source_target_pairs={{0,8},{4,12},{8,0},{12,4},{1,9},{5,13},{9,1},{13,5},{2,10},{6,14},... | collective-permute-start | bytes 3145736 | tf_op jit(solution)/shard_map/ppermute | solution.py:37
  166.5 45.1 %collective-permute-start = (bf16[2048,256]{0,1:T(8,128)(2,1)S(1)}, bf16[2048,256]{0,1:T(8,128)(2,1)S(1)}, u32[]{:S(2)}, u32[]{:S(2)}) collective-permute-start(bf16[2048,256]{0,1:T(8,128)(2,1)S(1)} %get-tuple-element.74), channel_id=1, source_target_pairs={{0,4},{4,0},{8,12},{12,8},{1,5},{5,1},{9,13},{13,9},{2,6},{6,2},{1... | collective-permute-start | bytes 3145736 | tf_op jit(solution)/shard_map/ppermute | solution.py:37
  188.4 38.1 %collective-permute-start.9 = (bf16[2048,256]{0,1:T(8,128)(2,1)S(1)}, bf16[2048,256]{0,1:T(8,128)(2,1)S(1)}, u32[]{:S(2)}, u32[]{:S(2)}) collective-permute-start(bf16[2048,256]{0,1:T(8,128)(2,1)S(1)} %copy-done.19), channel_id=1, source_target_pairs={{0,4},{4,0},{8,12},{12,8},{1,5},{5,1},{9,13},{13,9},{2,6},{6,2},{1... | collective-permute-start | bytes 3145736 | tf_op jit(solution)/shard_map/ppermute | solution.py:37
  211.2 45.1 %collective-permute-start.17 = (bf16[2048,256]{0,1:T(8,128)(2,1)}, bf16[2048,256]{0,1:T(8,128)(2,1)}, u32[]{:S(2)}, u32[]{:S(2)}) collective-permute-start(bf16[2048,256]{0,1:T(8,128)(2,1)} %get-tuple-element.50), channel_id=1, source_target_pairs={{0,12},{4,8},{8,4},{12,0},{1,13},{5,9},{9,5},{13,1},{2,14},{6,10},... | collective-permute-start | bytes 3145736 | tf_op jit(solution)/shard_map/ppermute | solution.py:37
  211.6 47.9 %collective-permute-start.15 = (bf16[2048,256]{0,1:T(8,128)(2,1)}, bf16[2048,256]{0,1:T(8,128)(2,1)}, u32[]{:S(2)}, u32[]{:S(2)}) collective-permute-start(bf16[2048,256]{0,1:T(8,128)(2,1)} %get-tuple-element.51), channel_id=1, source_target_pairs={{0,8},{4,12},{8,0},{12,4},{1,9},{5,13},{9,1},{13,5},{2,10},{6,14},... | collective-permute-start | bytes 3145736 | tf_op jit(solution)/shard_map/ppermute | solution.py:37
  225.4 34.0 %collective-permute-start.13 = (bf16[2048,256]{0,1:T(8,128)(2,1)}, bf16[2048,256]{0,1:T(8,128)(2,1)}, u32[]{:S(2)}, u32[]{:S(2)}) collective-permute-start(bf16[2048,256]{0,1:T(8,128)(2,1)} %get-tuple-element.52), channel_id=1, source_target_pairs={{0,4},{4,0},{8,12},{12,8},{1,5},{5,1},{9,13},{13,9},{2,6},{6,2},{1... | collective-permute-start | bytes 3145736 | tf_op jit(solution)/shard_map/ppermute | solution.py:37
  225.8 56.1 %collective-permute-start.8 = (bf16[2048,256]{0,1:T(8,128)(2,1)}, bf16[2048,256]{0,1:T(8,128)(2,1)}, u32[]{:S(2)}, u32[]{:S(2)}) collective-permute-start(bf16[2048,256]{0,1:T(8,128)(2,1)} %get-tuple-element.55), channel_id=1, source_target_pairs={{0,12},{4,8},{8,4},{12,0},{1,13},{5,9},{9,5},{13,1},{2,14},{6,10},... | collective-permute-start | bytes 3145736 | tf_op jit(solution)/shard_map/ppermute | solution.py:37
  226.5 77.9 %collective-permute-start.6 = (bf16[2048,256]{0,1:T(8,128)(2,1)}, bf16[2048,256]{0,1:T(8,128)(2,1)}, u32[]{:S(2)}, u32[]{:S(2)}) collective-permute-start(bf16[2048,256]{0,1:T(8,128)(2,1)} %get-tuple-element.56), channel_id=1, source_target_pairs={{0,8},{4,12},{8,0},{12,4},{1,9},{5,13},{9,1},{13,5},{2,10},{6,14},... | collective-permute-start | bytes 3145736 | tf_op jit(solution)/shard_map/ppermute | solution.py:37
  256.3 48.0 %collective-permute-start.4 = (bf16[2048,256]{0,1:T(8,128)(2,1)}, bf16[2048,256]{0,1:T(8,128)(2,1)}, u32[]{:S(2)}, u32[]{:S(2)}) collective-permute-start(bf16[2048,256]{0,1:T(8,128)(2,1)} %get-tuple-element.57), channel_id=1, source_target_pairs={{0,4},{4,0},{8,12},{12,8},{1,5},{5,1},{9,13},{13,9},{2,6},{6,2},{1... | collective-permute-start | bytes 3145736 | tf_op jit(solution)/shard_map/ppermute | solution.py:37
  268.7 35.6 %copy-start.13 = (bf16[128,8,4,256]{3,1,2,0:T(8,128)(2,1)S(1)}, bf16[128,8,4,256]{3,1,2,0:T(8,128)(2,1)}, u32[]{:S(2)}) copy-start(bf16[128,8,4,256]{3,1,2,0:T(8,128)(2,1)} %copy.76) | copy-start | bytes 6291460
  323.1 34.7 %collective-permute-start.21 = (bf16[2048,256]{0,1:T(8,128)(2,1)}, bf16[2048,256]{0,1:T(8,128)(2,1)}, u32[]{:S(2)}, u32[]{:S(2)}) collective-permute-start(bf16[2048,256]{0,1:T(8,128)(2,1)} %get-tuple-element.28), channel_id=1, source_target_pairs={{0,4},{4,0},{8,12},{12,8},{1,5},{5,1},{9,13},{13,9},{2,6},{6,2},{1... | collective-permute-start | bytes 3145736 | tf_op jit(solution)/shard_map/ppermute | solution.py:37
  323.2 36.4 %collective-permute-start.22 = (bf16[2048,256]{0,1:T(8,128)(2,1)}, bf16[2048,256]{0,1:T(8,128)(2,1)}, u32[]{:S(2)}, u32[]{:S(2)}) collective-permute-start(bf16[2048,256]{0,1:T(8,128)(2,1)} %get-tuple-element.29), channel_id=1, source_target_pairs={{0,8},{4,12},{8,0},{12,4},{1,9},{5,13},{9,1},{13,5},{2,10},{6,14},... | collective-permute-start | bytes 3145736 | tf_op jit(solution)/shard_map/ppermute | solution.py:37
  324.1 46.8 %collective-permute-start.23 = (bf16[2048,256]{0,1:T(8,128)(2,1)}, bf16[2048,256]{0,1:T(8,128)(2,1)}, u32[]{:S(2)}, u32[]{:S(2)}) collective-permute-start(bf16[2048,256]{0,1:T(8,128)(2,1)} %get-tuple-element.30), channel_id=1, source_target_pairs={{0,12},{4,8},{8,4},{12,0},{1,13},{5,9},{9,5},{13,1},{2,14},{6,10},... | collective-permute-start | bytes 3145736 | tf_op jit(solution)/shard_map/ppermute | solution.py:37
  342.1 30.2 %collective-permute-start.18 = (bf16[2048,256]{0,1:T(8,128)(2,1)}, bf16[2048,256]{0,1:T(8,128)(2,1)}, u32[]{:S(2)}, u32[]{:S(2)}) collective-permute-start(bf16[2048,256]{0,1:T(8,128)(2,1)} %get-tuple-element.24), channel_id=1, source_target_pairs={{0,4},{4,0},{8,12},{12,8},{1,5},{5,1},{9,13},{13,9},{2,6},{6,2},{1... | collective-permute-start | bytes 3145736 | tf_op jit(solution)/shard_map/ppermute | solution.py:37
  355.9 38.4 %collective-permute-start.19 = (bf16[2048,256]{0,1:T(8,128)(2,1)S(1)}, bf16[2048,256]{0,1:T(8,128)(2,1)S(1)}, u32[]{:S(2)}, u32[]{:S(2)}) collective-permute-start(bf16[2048,256]{0,1:T(8,128)(2,1)S(1)} %copy-done.26), channel_id=1, source_target_pairs={{0,8},{4,12},{8,0},{12,4},{1,9},{5,13},{9,1},{13,5},{2,10},{6,14},... | collective-permute-start | bytes 3145736 | tf_op jit(solution)/shard_map/ppermute | solution.py:37
  357.8 58.1 %collective-permute-start.20 = (bf16[2048,256]{0,1:T(8,128)(2,1)S(1)}, bf16[2048,256]{0,1:T(8,128)(2,1)S(1)}, u32[]{:S(2)}, u32[]{:S(2)}) collective-permute-start(bf16[2048,256]{0,1:T(8,128)(2,1)S(1)} %copy-done.25), channel_id=1, source_target_pairs={{0,12},{4,8},{8,4},{12,0},{1,13},{5,9},{9,5},{13,1},{2,14},{6,10},... | collective-permute-start | bytes 3145736 | tf_op jit(solution)/shard_map/ppermute | solution.py:37
  359.6 34.8 %copy-start.2 = (bf16[2048,1024]{0,1:T(8,128)(2,1)S(1)}, bf16[2048,1024]{0,1:T(8,128)(2,1)}, u32[]{:S(2)}) copy-start(bf16[2048,1024]{0,1:T(8,128)(2,1)} %copy.73) | copy-start | bytes 12582916
  427.6 20.6 %collective-permute-start.24 = (f32[64,4,256]{2,0,1:T(8,128)S(1)}, f32[64,4,256]{2,0,1:T(8,128)S(1)}, u32[]{:S(2)}, u32[]{:S(2)}) collective-permute-start(f32[64,4,256]{2,0,1:T(8,128)S(1)} %bitcast.125), channel_id=1, source_target_pairs={{0,1},{1,0},{2,3},{3,2},{4,5},{5,4},{6,7},{7,6},{8,9},{9,8},{10,11... | collective-permute-start | bytes 786440 | tf_op jit(solution)/shard_map/ppermute | solution.py:48
  429.3 21.4 %collective-permute-start.25 = (f32[64,4,256]{2,0,1:T(8,128)S(1)}, f32[64,4,256]{2,0,1:T(8,128)S(1)}, u32[]{:S(2)}, u32[]{:S(2)}) collective-permute-start(f32[64,4,256]{2,0,1:T(8,128)S(1)} %bitcast.124), channel_id=1, source_target_pairs={{0,2},{1,3},{2,0},{3,1},{4,6},{5,7},{6,4},{7,5},{8,10},{9,11},{10,... | collective-permute-start | bytes 786440 | tf_op jit(solution)/shard_map/ppermute | solution.py:48
  431.9 18.8 %collective-permute-start.26 = (f32[64,4,256]{2,0,1:T(8,128)S(1)}, f32[64,4,256]{2,0,1:T(8,128)S(1)}, u32[]{:S(2)}, u32[]{:S(2)}) collective-permute-start(f32[64,4,256]{2,0,1:T(8,128)S(1)} %bitcast.123), channel_id=1, source_target_pairs={{0,3},{1,2},{2,1},{3,0},{4,7},{5,6},{6,5},{7,4},{8,11},{9,10},{10,... | collective-permute-start | bytes 786440 | tf_op jit(solution)/shard_map/ppermute | solution.py:48
  (38 other events, 394.7 us)
Sparse Core Ops, SparseCore 0:
  256.4 52.5 all-reduce.2

commit v15 on v13

--- a/solution.py
+++ b/solution.py
@@ -102,12 +102,13 @@
             )
         pending.append((gt, gf, k * step))
     gf_last = None
+    gf_mid = []
     for gt, gf, at in pending:
         grad_tokens = lax.dynamic_update_slice(grad_tokens, gt, (at, 0))
         if at == (CHUNKS - 1) * step:
             gf_last = gf
         else:
-            gf_acc = gf if gf_acc is None else gf_acc + gf
+            gf_mid.append(gf)
 
     gs6 = gs_acc.reshape(n_dev, blk_local, blk_local, sub, blk_local, bs)
     gsd = jnp.sum(jnp.where(eye[None, :, None, None, :, None], gs6, 0.0), axis=4)
@@ -119,7 +120,10 @@
         g6 = g.reshape(blk_local, bs, n_dev, blk_local, blk_local, sub)
         return jnp.sum(jnp.where(eye[:, None, None, None, :, None], g6, 0.0), axis=4)
 
-    gfd = diagonal_blocks(gf_acc) + gf_last
+    gfd = diagonal_blocks(gf_acc)
+    for gf in gf_mid:
+        gfd = gfd + diagonal_blocks(gf)
+    gfd = gfd + gf_last
     gfd = jnp.take(gfd, order, axis=2)
     first_term = gfd.transpose(1, 0, 2, 3, 4).reshape(bs, blk_local, bs) * grad_scale
     grad_first = dp_reduce_scatter(first_term)

time: 444 us -> 469 us (1.056)
  other arithmetic: 28.7 us -> 38.7 us
  waiting for transfers between devices: 133 us -> 142 us
  local copies, waits for them, and re-layouts: 76.6 us -> 83.6 us
    ppermute x24, waiting for transfers between devices: 132 us -> 139 us  [exchange(): lax.ppermute(pieces[m], 'tensor', [(i, i ^ m) for i in range(n_dev)])]
    add x0 -> x1, other arithmetic: none -> 6.85 us  [shards(): gf_acc = done[1] if gf_acc is None else gf_acc + done[1]]
    reshape x1 -> x2, local copies, waits for them, and re-layouts: 5.89 us -> 11.3 us  [diagonal_blocks(): g6 = g.reshape(blk_local, bs, n_dev, blk_local, blk_local, sub)]
    unnamed x86 -> x90, local copies, waits for them, and re-layouts: 28.2 us -> 30.6 us
  transfers between devices with their start and end apart: 28 -> 28, of which waited for: 10 -> 10; matrix products, arithmetic and copies ran while one was open for 53% -> 54% of each run, Pallas kernels for 0% -> 0%
where the time goes in v15:
time: 469 us; the launch traced here: 462 us
  matrix products  159 us (34%)
  waiting for transfers between devices  142 us (30%)
  local copies, waits for them, and re-layouts  83.6 us (18%)
  other arithmetic  38.7 us (8%)
  starting transfers between devices  22.3 us (5%)
  between operations  15.6 us (3%)
    ppermute x24, waiting for transfers between devices, exchange(): lax.ppermute(pieces[m], 'tensor', [(i, i ^ m) for i in range(n_dev)])  139 us
    dot_general x4, matrix products, shards(): lax.dot_general(active, cot, (((0,), (0,)), ((), ())), preferred_element_...  34.3 us
    dot_general x4, matrix products, shards(): jnp.dot(returned, w1tp, preferred_element_type=jnp.float32)  34 us
    dot_general x4, matrix products, shards(): jnp.dot(x, w1p, preferred_element_type=jnp.float32).astype(jnp.bfloat16)  30.9 us
    dot_general x4, matrix products, shards(): backed = jnp.dot(cot, w2p, preferred_element_type=jnp.float32)  30.7 us
    unnamed x90, local copies, waits for them, and re-layouts  30.6 us
    dot_general x3, matrix products, shards(): lax.dot_general(x, returned, (((0,), (0,)), ((), ())), preferred_element_...  28 us
    ppermute x24, starting transfers between devices, exchange(): lax.ppermute(pieces[m], 'tensor', [(i, i ^ m) for i in range(n_dev)])  17.8 us
  transfers between devices with their start and end apart: 28, of which 10 were waited for; matrix products, arithmetic and copies ran while one was open for 54% of the time, Pallas kernels for 0%

profile of v15, /device:TPU:0, one launch (start us, length us, event | category | flops | bytes accessed | tf_op | source)
XLA Modules:
  0.0 461.7 jit_solution(7388481740343591364)
XLA Ops:
  14.7 7.8 %convert_bitcast_fusion = bf16[2048,1024]{0,1:T(8,128)(2,1)S(1)} fusion(bf16[1024,1024]{0,1:T(8,128)(2,1)S(1)} %bitcast.112, bf16[8192,1024]{1,0:T(8,128)(2,1)} %param.4), kind=kOutput, calls=%fused_computation.50 | convolution fusion | flops 4297064448 | bytes 10485760 | tf_op jit(solution)/shard_map/dot_general | solution.py:74
  28.4 7.0 %convert_bitcast_fusion.1 = bf16[2048,1024]{0,1:T(8,128)(2,1)S(1)} fusion(bf16[1024,1024]{0,1:T(8,128)(2,1)S(1)} %bitcast.113, bf16[8192,1024]{1,0:T(8,128)(2,1)} %param.4), kind=kOutput, calls=%fused_computation.51 | convolution fusion | flops 4297064448 | bytes 10485760 | tf_op jit(solution)/shard_map/dot_general | solution.py:74
  40.5 7.5 %convert_bitcast_fusion.2 = bf16[2048,1024]{0,1:T(8,128)(2,1)S(1)} fusion(bf16[1024,1024]{0,1:T(8,128)(2,1)} %bitcast.114, bf16[8192,1024]{1,0:T(8,128)(2,1)} %param.4), kind=kOutput, calls=%fused_computation.52 | convolution fusion | flops 4297064448 | bytes 10485760 | tf_op jit(solution)/shard_map/dot_general | solution.py:74
  48.1 8.6 %convert_bitcast_fusion.3 = bf16[2048,1024]{0,1:T(8,128)(2,1)S(1)} fusion(bf16[1024,1024]{0,1:T(8,128)(2,1)S(1)} %bitcast.115, bf16[8192,1024]{1,0:T(8,128)(2,1)} %param.4), kind=kOutput, calls=%fused_computation.53 | convolution fusion | flops 4297064448 | bytes 10485760 | tf_op jit(solution)/shard_map/dot_general | solution.py:74
  57.2 11.2 %convolution_bitcast_fusion = bf16[2048,1024]{0,1:T(8,128)(2,1)} fusion(bf16[1024,1024]{0,1:T(8,128)(2,1)S(1)} %bitcast.108, bf16[8192,1024]{1,0:T(8,128)(2,1)} %param.5), kind=kOutput, calls=%fused_computation.4 | convolution fusion | flops 4294967296 | bytes 10485760 | tf_op jit(solution)/shard_map/dot_general | solution.py:75
  68.5 6.2 %convolution_bitcast_fusion.1 = bf16[2048,1024]{0,1:T(8,128)(2,1)} fusion(bf16[1024,1024]{0,1:T(8,128)(2,1)S(1)} %bitcast.109, bf16[8192,1024]{1,0:T(8,128)(2,1)S(1)} %bitcast.122), kind=kOutput, calls=%fused_computation.5 | convolution fusion | flops 4294967296 | bytes 10485760 | tf_op jit(solution)/shard_map/dot_general | solution.py:75
  74.6 6.2 %convolution_bitcast_fusion.2 = bf16[2048,1024]{0,1:T(8,128)(2,1)} fusion(bf16[1024,1024]{0,1:T(8,128)(2,1)S(1)} %bitcast.110, bf16[8192,1024]{1,0:T(8,128)(2,1)S(1)} %bitcast.122), kind=kOutput, calls=%fused_computation.6 | convolution fusion | flops 4294967296 | bytes 10485760 | tf_op jit(solution)/shard_map/dot_general | solution.py:75
  91.8 6.6 %copy.60 = bf16[2048,1024]{0,1:T(8,128)(2,1)} copy(bf16[2048,1024]{1,0:T(8,128)(2,1)} %slice.140) | data formatting | bytes 8388608
  99.7 7.1 %convolution_bitcast_fusion.3 = bf16[2048,1024]{0,1:T(8,128)(2,1)S(1)} fusion(bf16[1024,1024]{0,1:T(8,128)(2,1)S(1)} %bitcast.111, bf16[8192,1024]{1,0:T(8,128)(2,1)} %param.5), kind=kOutput, calls=%fused_computation.7 | convolution fusion | flops 4294967296 | bytes 10485760 | tf_op jit(solution)/shard_map/dot_general | solution.py:75
  113.7 7.8 %fusion.7 = f32[1024,1024]{1,0:T(8,128)S(1)} fusion(bf16[2048,256]{0,1:T(8,128)(2,1)} %collective-permute-done.16, bf16[2048,256]{0,1:T(8,128)(2,1)} %collective-permute-done.14, bf16[2048,256]{0,1:T(8,128)(2,1)} %collective-permute-done.12, bf16[2048,256]{0,1:T(8,128)(2,1)S(1)} %get-tuple-element.48, bf16[8192,1024]{1,0:T(8,128)(2,1)} %param.5), kind=kOutput, calls=%fused_computation.19 | convolution fusion | flops 4315938816 | bytes 12582912 | tf_op jit(solution)/shard_map/dot_general | solution.py:82
  122.3 18.7 %collective-permute-done.7 = bf16[2048,256]{0,1:T(8,128)(2,1)S(1)} collective-permute-done((bf16[2048,256]{0,1:T(8,128)(2,1)S(1)}, bf16[2048,256]{0,1:T(8,128)(2,1)S(1)}, u32[]{:S(2)}, u32[]{:S(2)}) %collective-permute-start.7) | collective-permute-done | bytes 1048608 | tf_op jit(solution)/shard_map/ppermute | solution.py:37
  142.2 21.7 %collective-permute-done.5 = bf16[2048,256]{0,1:T(8,128)(2,1)S(1)} collective-permute-done((bf16[2048,256]{0,1:T(8,128)(2,1)S(1)}, bf16[2048,256]{0,1:T(8,128)(2,1)S(1)}, u32[]{:S(2)}, u32[]{:S(2)}) %collective-permute-start.5) | collective-permute-done | bytes 1048608 | tf_op jit(solution)/shard_map/ppermute | solution.py:37
  167.5 6.8 %fusion = f32[1024,1024]{1,0:T(8,128)S(1)} fusion(bf16[2048,256]{0,1:T(8,128)(2,1)S(1)} %collective-permute-done.7, bf16[2048,256]{0,1:T(8,128)(2,1)S(1)} %collective-permute-done.5, bf16[2048,256]{0,1:T(8,128)(2,1)S(1)} %collective-permute-done.3, bf16[2048,256]{0,1:T(8,128)(2,1)S(1)} %get-tuple-element.53, bf16[8192,1024]{1,0:T(8,128)(2,1)} %param.5), kind=kOutput, calls=%fused_computation.11 | convolution fusion | flops 4315938816 | bytes 12582912 | tf_op jit(solution)/shard_map/dot_general | solution.py:82
  174.3 11.6 %collective-permute-done.2 = bf16[2048,256]{0,1:T(8,128)(2,1)S(1)} collective-permute-done((bf16[2048,256]{0,1:T(8,128)(2,1)S(1)}, bf16[2048,256]{0,1:T(8,128)(2,1)S(1)}, u32[]{:S(2)}, u32[]{:S(2)}) %collective-permute-start.2) | collective-permute-done | bytes 1048608 | tf_op jit(solution)/shard_map/ppermute | solution.py:37
  186.1 22.5 %collective-permute-done.1 = bf16[2048,256]{0,1:T(8,128)(2,1)S(1)} collective-permute-done((bf16[2048,256]{0,1:T(8,128)(2,1)S(1)}, bf16[2048,256]{0,1:T(8,128)(2,1)S(1)}, u32[]{:S(2)}, u32[]{:S(2)}) %collective-permute-start.1) | collective-permute-done | bytes 1048608 | tf_op jit(solution)/shard_map/ppermute | solution.py:37
  213.7 8.8 %fusion.14 = f32[1024,1024]{1,0:T(8,128)} fusion(bf16[2048,256]{0,1:T(8,128)(2,1)S(1)} %collective-permute-done.2, bf16[2048,256]{0,1:T(8,128)(2,1)S(1)} %collective-permute-done.1, bf16[2048,256]{0,1:T(8,128)(2,1)S(1)} %collective-permute-done, bf16[2048,256]{0,1:T(8,128)(2,1)S(1)} %get-tuple-element.58, bf16[8192,1024]{1,0:T(8,128)(2,1)} %param.5), kind=kOutput, calls=%fused_computation.27 | convolution fusion | flops 4315938816 | bytes 12582912 | tf_op jit(solution)/shard_map/dot_general | solution.py:82
  228.7 10.9 %add_add_fusion = f32[1024,1024]{1,0:T(8,128)} fusion(f32[1024,1024]{1,0:T(8,128)} %fusion.14, f32[1024,1024]{1,0:T(8,128)S(1)} %fusion, f32[1024,1024]{1,0:T(8,128)S(1)} %fusion.7, bf16[8192,1024]{1,0:T(8,128)(2,1)} %param.5, bf16[2048,256]{0,1:T(8,128)(2,1)} %collective-permute-done.11, bf16[2048,256]{0,1:T(8,128)(2,1)} %collective-permute-done.10, ...), kind=kOutput, calls=%fused_computation.47 | convolution fusion | flops 4319084544 | bytes 25165824 | tf_op jit(solution)/shard_map/dot_general | solution.py:82
  239.6 6.1 %reshape.106 = f32[4,4,4,16,4,256]{5,4,3,2,1,0:T(4,128)} reshape(f32[1024,1024]{1,0:T(8,128)} %add_add_fusion) | data formatting | bytes 8388608 | tf_op jit(solution)/shard_map/reshape | solution.py:113
  257.0 9.3 %convolution_convert_fusion = bf16[2048,1024]{1,0:T(8,128)(2,1)} fusion(bf16[1024,1024]{1,0:T(8,128)(2,1)} %bitcast.104, bf16[2048,256]{0,1:T(8,128)(2,1)} %collective-permute-done.17, bf16[2048,256]{0,1:T(8,128)(2,1)} %collective-permute-done.15, bf16[2048,256]{0,1:T(8,128)(2,1)} %collective-permute-done.13, bf16[2048,256]{0,1:T(8,128)(2,1)S(1)} %copy-done.24), kind=kOutput, calls=%fused_computation.54 | convolution fusion | flops 4313841664 | bytes 10485760 | tf_op jit(solution)/shard_map/dot_general | solution.py:91
  266.3 9.8 %fusion.53 = f32[1024,1024]{0,1:T(8,128)} fusion(bf16[8192,1024]{1,0:T(8,128)(2,1)} %param.4, bf16[2048,256]{0,1:T(8,128)(2,1)} %collective-permute-done.17, bf16[2048,256]{0,1:T(8,128)(2,1)} %collective-permute-done.15, bf16[2048,256]{0,1:T(8,128)(2,1)} %collective-permute-done.13, bf16[2048,256]{0,1:T(8,128)(2,1)S(1)} %copy-done.25), kind=kOutput, calls=%fused_computation.75 | convolution fusion | flops 4311744512 | bytes 12582912 | tf_op jit(solution)/shard_map/dot_general | solution.py:93
  279.1 22.7 %collective-permute-done.6 = bf16[2048,256]{0,1:T(8,128)(2,1)} collective-permute-done((bf16[2048,256]{0,1:T(8,128)(2,1)}, bf16[2048,256]{0,1:T(8,128)(2,1)}, u32[]{:S(2)}, u32[]{:S(2)}) %collective-permute-start.6) | collective-permute-done | bytes 1048608 | tf_op jit(solution)/shard_map/ppermute | solution.py:37
  301.8 9.0 %convolution_convert_fusion.1 = bf16[2048,1024]{1,0:T(8,128)(2,1)} fusion(bf16[1024,1024]{1,0:T(8,128)(2,1)S(1)} %bitcast.106, bf16[2048,256]{0,1:T(8,128)(2,1)} %collective-permute-done.8, bf16[2048,256]{0,1:T(8,128)(2,1)} %collective-permute-done.6, bf16[2048,256]{0,1:T(8,128)(2,1)} %collective-permute-done.4, bf16[2048,256]{0,1:T(8,128)(2,1)} %get-tuple-element.54), kind=kOutput, calls=%fused_computation.55 | convolution fusion | flops 4313841664 | bytes 10485760 | tf_op jit(solution)/shard_map/dot_general | solution.py:91
  310.7 9.7 %fusion.50 = f32[1024,1024]{0,1:T(8,128)} fusion(bf16[8192,1024]{1,0:T(8,128)(2,1)} %param.4, bf16[2048,256]{0,1:T(8,128)(2,1)} %collective-permute-done.8, bf16[2048,256]{0,1:T(8,128)(2,1)} %collective-permute-done.6, bf16[2048,256]{0,1:T(8,128)(2,1)} %collective-permute-done.4, bf16[2048,256]{0,1:T(8,128)(2,1)S(1)} %copy-done.26), kind=kOutput, calls=%fused_computation.74 | convolution fusion | flops 4311744512 | bytes 12582912 | tf_op jit(solution)/shard_map/dot_general | solution.py:93
  321.8 6.8 %add.73 = f32[1024,1024]{0,1:T(8,128)} add(f32[1024,1024]{0,1:T(8,128)} %fusion.50, f32[1024,1024]{0,1:T(8,128)} %fusion.53) | non-fusion elementwise | flops 1048576 | bytes 12582912 | tf_op jit(solution)/shard_map/add | solution.py:89
  329.6 5.7 %reshape.107 = f32[4,256,4,4,4,16]{1,0,5,4,3,2:T(4,128)} reshape(f32[1024,1024]{0,1:T(8,128)} %add.73) | data formatting | bytes 8388608 | tf_op jit(solution)/shard_map/reshape | solution.py:120
  337.9 6.6 %broadcast_in_dim.157 = bf16[8192,1024]{1,0:T(8,128)(2,1)} broadcast(bf16[]{:T(256)} %constant.53.clone.1), dimensions={} | broadcast | bytes 16777218 | tf_op jit(solution)/shard_map/broadcast_in_dim | solution.py:69
  353.5 15.7 %collective-permute-done.19 = bf16[2048,256]{0,1:T(8,128)(2,1)} collective-permute-done((bf16[2048,256]{0,1:T(8,128)(2,1)}, bf16[2048,256]{0,1:T(8,128)(2,1)}, u32[]{:S(2)}, u32[]{:S(2)}) %collective-permute-start.19) | collective-permute-done | bytes 1048608 | tf_op jit(solution)/shard_map/ppermute | solution.py:37
  370.4 20.4 %collective-permute-done.20 = bf16[2048,256]{0,1:T(8,128)(2,1)} collective-permute-done((bf16[2048,256]{0,1:T(8,128)(2,1)}, bf16[2048,256]{0,1:T(8,128)(2,1)}, u32[]{:S(2)}, u32[]{:S(2)}) %collective-permute-start.20) | collective-permute-done | bytes 1048608 | tf_op jit(solution)/shard_map/ppermute | solution.py:37
  394.2 8.5 %fusion.47 = f32[1024,1024]{0,1:T(8,128)} fusion(bf16[2048,1024]{0,1:T(8,128)(2,1)S(1)} %constant_dynamic-update-slice_fusion, bf16[8192,1024]{1,0:T(8,128)(2,1)} %param.4), kind=kOutput, calls=%fused_computation.73 | convolution fusion | flops 4294967296 | bytes 12582912 | tf_op jit(solution)/shard_map/dot_general | solution.py:93
  411.7 7.2 %select_reduce_fusion.1 = (f32[4,256,4,4,16]{1,0,4,3,2:T(4,128)S(1)}, f32[4,256,4,4,16]{1,0,4,3,2:T(4,128)S(1)}) fusion(f32[4,256,4,4,4,16]{1,0,5,4,3,2:T(4,128)} %reshape.107, pred[4,4]{0,1:T(4,128)(4,1)S(1)} %copy-done.32, f32[4,256,4,4,4,16]{1,0,5,4,3,2:T(4,128)} %reshape.108), kind=kLoop, calls=%fused_computation.45 | loop fusion | flops 3670016 | bytes 10485776 | tf_op jit(solution)/shard_map/reduce_sum | solution.py:121
  435.2 9.6 %convert_dynamic-update-slice_fusion.1 = bf16[8192,1024]{1,0:T(8,128)(2,1)} fusion(bf16[8192,1024]{1,0:T(8,128)(2,1)} %constant_dynamic-update-slice_fusion.8, bf16[2048,1024]{0,1:T(8,128)(2,1)} %copy-done.30, bf16[1024,1024]{1,0:T(8,128)(2,1)} %bitcast.105), kind=kOutput, calls=%fused_computation.49 | convolution fusion | flops 4297064448 | bytes 10485760 | tf_op jit(solution)/shard_map/dot_general | solution.py:91
  444.8 6.2 %convert_dynamic-update-slice_fusion = bf16[8192,1024]{1,0:T(8,128)(2,1)} fusion(bf16[8192,1024]{1,0:T(8,128)(2,1)} %convert_dynamic-update-slice_fusion.1, bf16[2048,1024]{0,1:T(8,128)(2,1)S(1)} %copy-done.29, bf16[1024,1024]{1,0:T(8,128)(2,1)S(1)} %bitcast.107), kind=kOutput, calls=%fused_computation.48 | convolution fusion | flops 4297064448 | bytes 10485760 | tf_op jit(solution)/shard_map/dot_general | solution.py:91
  (184 shorter events, 116.0 us)
Async XLA Ops:
  7.2 321.5 %all-reduce.3.cloned.1.call-start = ((), (), s32[]{:S(2)}) async-start(), calls=%async_computation | async-start | bytes 2097152
  7.3 33.2 %copy-start.31 = (pred[4,4]{0,1:T(4,128)(4,1)}, pred[4,4]{0,1:T(4,128)(4,1)S(1)}, u32[]{:S(2)}) copy-start(pred[4,4]{0,1:T(4,128)(4,1)S(1)} %iota_compare_fusion) | copy-start | bytes 52
  24.3 82.5 %collective-permute-start.12 = (bf16[2048,256]{0,1:T(8,128)(2,1)}, bf16[2048,256]{0,1:T(8,128)(2,1)}, u32[]{:S(2)}, u32[]{:S(2)}) collective-permute-start(bf16[2048,256]{0,1:T(8,128)(2,1)} %get-tuple-element.63), channel_id=1, source_target_pairs={{0,4},{4,0},{8,12},{12,8},{1,5},{5,1},{9,13},{13,9},{2,6},{6,2},{1... | collective-permute-start | bytes 3145736 | tf_op jit(solution)/shard_map/ppermute | solution.py:37
  24.8 82.8 %collective-permute-start.16 = (bf16[2048,256]{0,1:T(8,128)(2,1)}, bf16[2048,256]{0,1:T(8,128)(2,1)}, u32[]{:S(2)}, u32[]{:S(2)}) collective-permute-start(bf16[2048,256]{0,1:T(8,128)(2,1)} %get-tuple-element.64), channel_id=1, source_target_pairs={{0,12},{4,8},{8,4},{12,0},{1,13},{5,9},{9,5},{13,1},{2,14},{6,10},... | collective-permute-start | bytes 3145736 | tf_op jit(solution)/shard_map/ppermute | solution.py:37
  27.4 80.9 %collective-permute-start.14 = (bf16[2048,256]{0,1:T(8,128)(2,1)}, bf16[2048,256]{0,1:T(8,128)(2,1)}, u32[]{:S(2)}, u32[]{:S(2)}) collective-permute-start(bf16[2048,256]{0,1:T(8,128)(2,1)} %get-tuple-element.65), channel_id=1, source_target_pairs={{0,8},{4,12},{8,0},{12,4},{1,9},{5,13},{9,1},{13,5},{2,10},{6,14},... | collective-permute-start | bytes 3145736 | tf_op jit(solution)/shard_map/ppermute | solution.py:37
  39.2 183.3 %collective-permute-start.11 = (bf16[2048,256]{0,1:T(8,128)(2,1)}, bf16[2048,256]{0,1:T(8,128)(2,1)}, u32[]{:S(2)}, u32[]{:S(2)}) collective-permute-start(bf16[2048,256]{0,1:T(8,128)(2,1)} %get-tuple-element.66), channel_id=1, source_target_pairs={{0,12},{4,8},{8,4},{12,0},{1,13},{5,9},{9,5},{13,1},{2,14},{6,10},... | collective-permute-start | bytes 3145736 | tf_op jit(solution)/shard_map/ppermute | solution.py:37
  39.6 183.2 %collective-permute-start.10 = (bf16[2048,256]{0,1:T(8,128)(2,1)}, bf16[2048,256]{0,1:T(8,128)(2,1)}, u32[]{:S(2)}, u32[]{:S(2)}) collective-permute-start(bf16[2048,256]{0,1:T(8,128)(2,1)} %get-tuple-element.67), channel_id=1, source_target_pairs={{0,8},{4,12},{8,0},{12,4},{1,9},{5,13},{9,1},{13,5},{2,10},{6,14},... | collective-permute-start | bytes 3145736 | tf_op jit(solution)/shard_map/ppermute | solution.py:37
  48.1 34.8 %copy-start.8 = (bf16[2048,1024]{0,1:T(8,128)(2,1)}, bf16[2048,1024]{0,1:T(8,128)(2,1)S(1)}, u32[]{:S(2)}) copy-start(bf16[2048,1024]{0,1:T(8,128)(2,1)S(1)} %convert_bitcast_fusion.2) | copy-start | bytes 12582916
  106.8 14.6 %collective-permute-start.3 = (bf16[2048,256]{0,1:T(8,128)(2,1)S(1)}, bf16[2048,256]{0,1:T(8,128)(2,1)S(1)}, u32[]{:S(2)}, u32[]{:S(2)}) collective-permute-start(bf16[2048,256]{0,1:T(8,128)(2,1)S(1)} %copy-done.22), channel_id=1, source_target_pairs={{0,4},{4,0},{8,12},{12,8},{1,5},{5,1},{9,13},{13,9},{2,6},{6,2},{1... | collective-permute-start | bytes 3145736 | tf_op jit(solution)/shard_map/ppermute | solution.py:37
  107.6 33.4 %collective-permute-start.7 = (bf16[2048,256]{0,1:T(8,128)(2,1)S(1)}, bf16[2048,256]{0,1:T(8,128)(2,1)S(1)}, u32[]{:S(2)}, u32[]{:S(2)}) collective-permute-start(bf16[2048,256]{0,1:T(8,128)(2,1)S(1)} %copy-done.21), channel_id=1, source_target_pairs={{0,12},{4,8},{8,4},{12,0},{1,13},{5,9},{9,5},{13,1},{2,14},{6,10},... | collective-permute-start | bytes 3145736 | tf_op jit(solution)/shard_map/ppermute | solution.py:37
  108.3 55.5 %collective-permute-start.5 = (bf16[2048,256]{0,1:T(8,128)(2,1)S(1)}, bf16[2048,256]{0,1:T(8,128)(2,1)S(1)}, u32[]{:S(2)}, u32[]{:S(2)}) collective-permute-start(bf16[2048,256]{0,1:T(8,128)(2,1)S(1)} %copy-done.20), channel_id=1, source_target_pairs={{0,8},{4,12},{8,0},{12,4},{1,9},{5,13},{9,1},{13,5},{2,10},{6,14},... | collective-permute-start | bytes 3145736 | tf_op jit(solution)/shard_map/ppermute | solution.py:37
  113.6 50.2 %copy-start.2 = (bf16[2048,1024]{0,1:T(8,128)(2,1)S(1)}, bf16[2048,1024]{0,1:T(8,128)(2,1)}, u32[]{:S(2)}) copy-start(bf16[2048,1024]{0,1:T(8,128)(2,1)} %convolution_bitcast_fusion.2) | copy-start | bytes 12582916
  121.5 64.5 %collective-permute-start.2 = (bf16[2048,256]{0,1:T(8,128)(2,1)S(1)}, bf16[2048,256]{0,1:T(8,128)(2,1)S(1)}, u32[]{:S(2)}, u32[]{:S(2)}) collective-permute-start(bf16[2048,256]{0,1:T(8,128)(2,1)S(1)} %copy-done.19), channel_id=1, source_target_pairs={{0,12},{4,8},{8,4},{12,0},{1,13},{5,9},{9,5},{13,1},{2,14},{6,10},... | collective-permute-start | bytes 3145736 | tf_op jit(solution)/shard_map/ppermute | solution.py:37
  141.0 67.6 %collective-permute-start.1 = (bf16[2048,256]{0,1:T(8,128)(2,1)S(1)}, bf16[2048,256]{0,1:T(8,128)(2,1)S(1)}, u32[]{:S(2)}, u32[]{:S(2)}) collective-permute-start(bf16[2048,256]{0,1:T(8,128)(2,1)S(1)} %copy-done.18), channel_id=1, source_target_pairs={{0,8},{4,12},{8,0},{12,4},{1,9},{5,13},{9,1},{13,5},{2,10},{6,14},... | collective-permute-start | bytes 3145736 | tf_op jit(solution)/shard_map/ppermute | solution.py:37
  163.8 45.5 %collective-permute-start = (bf16[2048,256]{0,1:T(8,128)(2,1)S(1)}, bf16[2048,256]{0,1:T(8,128)(2,1)S(1)}, u32[]{:S(2)}, u32[]{:S(2)}) collective-permute-start(bf16[2048,256]{0,1:T(8,128)(2,1)S(1)} %get-tuple-element.74), channel_id=1, source_target_pairs={{0,4},{4,0},{8,12},{12,8},{1,5},{5,1},{9,13},{13,9},{2,6},{6,2},{1... | collective-permute-start | bytes 3145736 | tf_op jit(solution)/shard_map/ppermute | solution.py:37
  185.9 38.2 %collective-permute-start.9 = (bf16[2048,256]{0,1:T(8,128)(2,1)S(1)}, bf16[2048,256]{0,1:T(8,128)(2,1)S(1)}, u32[]{:S(2)}, u32[]{:S(2)}) collective-permute-start(bf16[2048,256]{0,1:T(8,128)(2,1)S(1)} %copy-done.17), channel_id=1, source_target_pairs={{0,4},{4,0},{8,12},{12,8},{1,5},{5,1},{9,13},{13,9},{2,6},{6,2},{1... | collective-permute-start | bytes 3145736 | tf_op jit(solution)/shard_map/ppermute | solution.py:37
  208.6 45.0 %collective-permute-start.17 = (bf16[2048,256]{0,1:T(8,128)(2,1)}, bf16[2048,256]{0,1:T(8,128)(2,1)}, u32[]{:S(2)}, u32[]{:S(2)}) collective-permute-start(bf16[2048,256]{0,1:T(8,128)(2,1)} %get-tuple-element.50), channel_id=1, source_target_pairs={{0,12},{4,8},{8,4},{12,0},{1,13},{5,9},{9,5},{13,1},{2,14},{6,10},... | collective-permute-start | bytes 3145736 | tf_op jit(solution)/shard_map/ppermute | solution.py:37
  209.3 47.7 %collective-permute-start.15 = (bf16[2048,256]{0,1:T(8,128)(2,1)}, bf16[2048,256]{0,1:T(8,128)(2,1)}, u32[]{:S(2)}, u32[]{:S(2)}) collective-permute-start(bf16[2048,256]{0,1:T(8,128)(2,1)} %get-tuple-element.51), channel_id=1, source_target_pairs={{0,8},{4,12},{8,0},{12,4},{1,9},{5,13},{9,1},{13,5},{2,10},{6,14},... | collective-permute-start | bytes 3145736 | tf_op jit(solution)/shard_map/ppermute | solution.py:37
  222.6 34.4 %collective-permute-start.13 = (bf16[2048,256]{0,1:T(8,128)(2,1)}, bf16[2048,256]{0,1:T(8,128)(2,1)}, u32[]{:S(2)}, u32[]{:S(2)}) collective-permute-start(bf16[2048,256]{0,1:T(8,128)(2,1)} %get-tuple-element.52), channel_id=1, source_target_pairs={{0,4},{4,0},{8,12},{12,8},{1,5},{5,1},{9,13},{13,9},{2,6},{6,2},{1... | collective-permute-start | bytes 3145736 | tf_op jit(solution)/shard_map/ppermute | solution.py:37
  222.8 56.3 %collective-permute-start.8 = (bf16[2048,256]{0,1:T(8,128)(2,1)}, bf16[2048,256]{0,1:T(8,128)(2,1)}, u32[]{:S(2)}, u32[]{:S(2)}) collective-permute-start(bf16[2048,256]{0,1:T(8,128)(2,1)} %get-tuple-element.55), channel_id=1, source_target_pairs={{0,12},{4,8},{8,4},{12,0},{1,13},{5,9},{9,5},{13,1},{2,14},{6,10},... | collective-permute-start | bytes 3145736 | tf_op jit(solution)/shard_map/ppermute | solution.py:37
  224.1 77.7 %collective-permute-start.6 = (bf16[2048,256]{0,1:T(8,128)(2,1)}, bf16[2048,256]{0,1:T(8,128)(2,1)}, u32[]{:S(2)}, u32[]{:S(2)}) collective-permute-start(bf16[2048,256]{0,1:T(8,128)(2,1)} %get-tuple-element.56), channel_id=1, source_target_pairs={{0,8},{4,12},{8,0},{12,4},{1,9},{5,13},{9,1},{13,5},{2,10},{6,14},... | collective-permute-start | bytes 3145736 | tf_op jit(solution)/shard_map/ppermute | solution.py:37
  253.6 48.1 %collective-permute-start.4 = (bf16[2048,256]{0,1:T(8,128)(2,1)}, bf16[2048,256]{0,1:T(8,128)(2,1)}, u32[]{:S(2)}, u32[]{:S(2)}) collective-permute-start(bf16[2048,256]{0,1:T(8,128)(2,1)} %get-tuple-element.57), channel_id=1, source_target_pairs={{0,4},{4,0},{8,12},{12,8},{1,5},{5,1},{9,13},{13,9},{2,6},{6,2},{1... | collective-permute-start | bytes 3145736 | tf_op jit(solution)/shard_map/ppermute | solution.py:37
  266.3 35.5 %copy-start.11 = (bf16[128,8,4,256]{3,1,2,0:T(8,128)(2,1)S(1)}, bf16[128,8,4,256]{3,1,2,0:T(8,128)(2,1)}, u32[]{:S(2)}) copy-start(bf16[128,8,4,256]{3,1,2,0:T(8,128)(2,1)} %copy.63) | copy-start | bytes 6291460
  320.4 87.9 %collective-permute-start.21 = (bf16[2048,256]{0,1:T(8,128)(2,1)}, bf16[2048,256]{0,1:T(8,128)(2,1)}, u32[]{:S(2)}, u32[]{:S(2)}) collective-permute-start(bf16[2048,256]{0,1:T(8,128)(2,1)} %get-tuple-element.28), channel_id=1, source_target_pairs={{0,4},{4,0},{8,12},{12,8},{1,5},{5,1},{9,13},{13,9},{2,6},{6,2},{1... | collective-permute-start | bytes 3145736 | tf_op jit(solution)/shard_map/ppermute | solution.py:37
  320.4 90.3 %collective-permute-start.22 = (bf16[2048,256]{0,1:T(8,128)(2,1)}, bf16[2048,256]{0,1:T(8,128)(2,1)S(1)}, u32[]{:S(2)}, u32[]{:S(2)}) collective-permute-start(bf16[2048,256]{0,1:T(8,128)(2,1)} %get-tuple-element.29), channel_id=1, source_target_pairs={{0,8},{4,12},{8,0},{12,4},{1,9},{5,13},{9,1},{13,5},{2,10},{6,14},... | collective-permute-start | bytes 3145736 | tf_op jit(solution)/shard_map/ppermute | solution.py:37
  336.1 15.4 %collective-permute-start.18 = (bf16[2048,256]{0,1:T(8,128)(2,1)}, bf16[2048,256]{0,1:T(8,128)(2,1)}, u32[]{:S(2)}, u32[]{:S(2)}) collective-permute-start(bf16[2048,256]{0,1:T(8,128)(2,1)} %get-tuple-element.24), channel_id=1, source_target_pairs={{0,4},{4,0},{8,12},{12,8},{1,5},{5,1},{9,13},{13,9},{2,6},{6,2},{1... | collective-permute-start | bytes 3145736 | tf_op jit(solution)/shard_map/ppermute | solution.py:37
  336.1 33.1 %collective-permute-start.19 = (bf16[2048,256]{0,1:T(8,128)(2,1)}, bf16[2048,256]{0,1:T(8,128)(2,1)}, u32[]{:S(2)}, u32[]{:S(2)}) collective-permute-start(bf16[2048,256]{0,1:T(8,128)(2,1)} %get-tuple-element.25), channel_id=1, source_target_pairs={{0,8},{4,12},{8,0},{12,4},{1,9},{5,13},{9,1},{13,5},{2,10},{6,14},... | collective-permute-start | bytes 3145736 | tf_op jit(solution)/shard_map/ppermute | solution.py:37
  336.9 53.9 %collective-permute-start.20 = (bf16[2048,256]{0,1:T(8,128)(2,1)}, bf16[2048,256]{0,1:T(8,128)(2,1)}, u32[]{:S(2)}, u32[]{:S(2)}) collective-permute-start(bf16[2048,256]{0,1:T(8,128)(2,1)} %get-tuple-element.26), channel_id=1, source_target_pairs={{0,12},{4,8},{8,4},{12,0},{1,13},{5,9},{9,5},{13,1},{2,14},{6,10},... | collective-permute-start | bytes 3145736 | tf_op jit(solution)/shard_map/ppermute | solution.py:37
  351.4 67.4 %collective-permute-start.23 = (bf16[2048,256]{0,1:T(8,128)(2,1)S(1)}, bf16[2048,256]{0,1:T(8,128)(2,1)S(1)}, u32[]{:S(2)}, u32[]{:S(2)}) collective-permute-start(bf16[2048,256]{0,1:T(8,128)(2,1)S(1)} %copy-done.23), channel_id=1, source_target_pairs={{0,12},{4,8},{8,4},{12,0},{1,13},{5,9},{9,5},{13,1},{2,14},{6,10},... | collective-permute-start | bytes 3145736 | tf_op jit(solution)/shard_map/ppermute | solution.py:37
  430.7 20.6 %collective-permute-start.24 = (f32[64,4,256]{2,0,1:T(8,128)S(1)}, f32[64,4,256]{2,0,1:T(8,128)S(1)}, u32[]{:S(2)}, u32[]{:S(2)}) collective-permute-start(f32[64,4,256]{2,0,1:T(8,128)S(1)} %bitcast.119), channel_id=1, source_target_pairs={{0,1},{1,0},{2,3},{3,2},{4,5},{5,4},{6,7},{7,6},{8,9},{9,8},{10,11... | collective-permute-start | bytes 786440 | tf_op jit(solution)/shard_map/ppermute | solution.py:48
  432.5 21.4 %collective-permute-start.25 = (f32[64,4,256]{2,0,1:T(8,128)S(1)}, f32[64,4,256]{2,0,1:T(8,128)S(1)}, u32[]{:S(2)}, u32[]{:S(2)}) collective-permute-start(f32[64,4,256]{2,0,1:T(8,128)S(1)} %bitcast.118), channel_id=1, source_target_pairs={{0,2},{1,3},{2,0},{3,1},{4,6},{5,7},{6,4},{7,5},{8,10},{9,11},{10,... | collective-permute-start | bytes 786440 | tf_op jit(solution)/shard_map/ppermute | solution.py:48
  435.0 18.8 %collective-permute-start.26 = (f32[64,4,256]{2,0,1:T(8,128)S(1)}, f32[64,4,256]{2,0,1:T(8,128)S(1)}, u32[]{:S(2)}, u32[]{:S(2)}) collective-permute-start(f32[64,4,256]{2,0,1:T(8,128)S(1)} %bitcast.117), channel_id=1, source_target_pairs={{0,3},{1,2},{2,1},{3,0},{4,7},{5,6},{6,5},{7,4},{8,11},{9,10},{10,... | collective-permute-start | bytes 786440 | tf_op jit(solution)/shard_map/ppermute | solution.py:48
  (34 other events, 311.3 us)
Sparse Core Ops, SparseCore 0:
  253.7 52.9 all-reduce.2

commit v16 on v13

--- a/solution.py
+++ b/solution.py
@@ -114,7 +114,6 @@
     gsd = jnp.take(gsd, order, axis=0)
     second_term = gsd.transpose(3, 0, 2, 1, 4).reshape(bs, blk_local, bs) * grad_scale
     grad_second = lax.psum_scatter(second_term, "dp", scatter_dimension=0, tiled=True)
-    gf_acc, grad_second = lax.optimization_barrier((gf_acc, grad_second))
     def diagonal_blocks(g):
         g6 = g.reshape(blk_local, bs, n_dev, blk_local, blk_local, sub)
         return jnp.sum(jnp.where(eye[:, None, None, None, :, None], g6, 0.0), axis=4)

time: 444 us -> 465 us (1.047)
  waiting for transfers between devices: 133 us -> 154 us
    ppermute x24, waiting for transfers between devices: 132 us -> 152 us  [exchange(): lax.ppermute(pieces[m], 'tensor', [(i, i ^ m) for i in range(n_dev)])]
    unnamed x86 -> x88, local copies, waits for them, and re-layouts: 28.2 us -> 27.8 us
  transfers between devices with their start and end apart: 28 -> 28, of which waited for: 10 -> 10; matrix products, arithmetic and copies ran while one was open for 53% -> 50% of each run, Pallas kernels for 0% -> 0%
where the time goes in v16:
time: 465 us; the launch traced here: 458 us
  matrix products  161 us (35%)
  waiting for transfers between devices  154 us (33%)
  local copies, waits for them, and re-layouts  76.1 us (16%)
  other arithmetic  28.6 us (6%)
  starting transfers between devices  22.3 us (5%)
  between operations  15.6 us (3%)
    ppermute x24, waiting for transfers between devices, exchange(): lax.ppermute(pieces[m], 'tensor', [(i, i ^ m) for i in range(n_dev)])  152 us
    dot_general x4, matrix products, shards(): jnp.dot(returned, w1tp, preferred_element_type=jnp.float32)  34.3 us
    dot_general x4, matrix products, shards(): lax.dot_general(active, cot, (((0,), (0,)), ((), ())), preferred_element_...  34.3 us
    dot_general x4, matrix products, shards(): jnp.dot(x, w1p, preferred_element_type=jnp.float32).astype(jnp.bfloat16)  30.9 us
    dot_general x4, matrix products, shards(): backed = jnp.dot(cot, w2p, preferred_element_type=jnp.float32)  30.7 us
    unnamed x88, local copies, waits for them, and re-layouts  27.8 us
    dot_general x3, matrix products, shards(): lax.dot_general(x, returned, (((0,), (0,)), ((), ())), preferred_element_...  27.7 us
    ppermute x24, starting transfers between devices, exchange(): lax.ppermute(pieces[m], 'tensor', [(i, i ^ m) for i in range(n_dev)])  17.8 us
  transfers between devices with their start and end apart: 28, of which 10 were waited for; matrix products, arithmetic and copies ran while one was open for 50% of the time, Pallas kernels for 0%

profile of v16, /device:TPU:0, one launch (start us, length us, event | category | flops | bytes accessed | tf_op | source)
XLA Modules:
  0.0 457.8 jit_solution(4574036620645100346)
XLA Ops:
  14.7 7.8 %convert_bitcast_fusion = bf16[2048,1024]{0,1:T(8,128)(2,1)S(1)} fusion(bf16[1024,1024]{0,1:T(8,128)(2,1)S(1)} %bitcast.109, bf16[8192,1024]{1,0:T(8,128)(2,1)} %param.4), kind=kOutput, calls=%fused_computation.50 | convolution fusion | flops 4297064448 | bytes 10485760 | tf_op jit(solution)/shard_map/dot_general | solution.py:74
  28.4 7.0 %convert_bitcast_fusion.1 = bf16[2048,1024]{0,1:T(8,128)(2,1)S(1)} fusion(bf16[1024,1024]{0,1:T(8,128)(2,1)S(1)} %bitcast.110, bf16[8192,1024]{1,0:T(8,128)(2,1)} %param.4), kind=kOutput, calls=%fused_computation.51 | convolution fusion | flops 4297064448 | bytes 10485760 | tf_op jit(solution)/shard_map/dot_general | solution.py:74
  40.5 7.5 %convert_bitcast_fusion.2 = bf16[2048,1024]{0,1:T(8,128)(2,1)S(1)} fusion(bf16[1024,1024]{0,1:T(8,128)(2,1)} %bitcast.111, bf16[8192,1024]{1,0:T(8,128)(2,1)} %param.4), kind=kOutput, calls=%fused_computation.52 | convolution fusion | flops 4297064448 | bytes 10485760 | tf_op jit(solution)/shard_map/dot_general | solution.py:74
  48.1 8.6 %convert_bitcast_fusion.3 = bf16[2048,1024]{0,1:T(8,128)(2,1)S(1)} fusion(bf16[1024,1024]{0,1:T(8,128)(2,1)S(1)} %bitcast.112, bf16[8192,1024]{1,0:T(8,128)(2,1)} %param.4), kind=kOutput, calls=%fused_computation.53 | convolution fusion | flops 4297064448 | bytes 10485760 | tf_op jit(solution)/shard_map/dot_general | solution.py:74
  57.2 11.2 %convolution_bitcast_fusion = bf16[2048,1024]{0,1:T(8,128)(2,1)} fusion(bf16[1024,1024]{0,1:T(8,128)(2,1)S(1)} %bitcast.105, bf16[8192,1024]{1,0:T(8,128)(2,1)} %param.5), kind=kOutput, calls=%fused_computation.4 | convolution fusion | flops 4294967296 | bytes 10485760 | tf_op jit(solution)/shard_map/dot_general | solution.py:75
  68.5 6.2 %convolution_bitcast_fusion.1 = bf16[2048,1024]{0,1:T(8,128)(2,1)} fusion(bf16[1024,1024]{0,1:T(8,128)(2,1)S(1)} %bitcast.106, bf16[8192,1024]{1,0:T(8,128)(2,1)S(1)} %bitcast.118), kind=kOutput, calls=%fused_computation.5 | convolution fusion | flops 4294967296 | bytes 10485760 | tf_op jit(solution)/shard_map/dot_general | solution.py:75
  74.6 6.1 %convolution_bitcast_fusion.2 = bf16[2048,1024]{0,1:T(8,128)(2,1)} fusion(bf16[1024,1024]{0,1:T(8,128)(2,1)S(1)} %bitcast.107, bf16[8192,1024]{1,0:T(8,128)(2,1)S(1)} %bitcast.118), kind=kOutput, calls=%fused_computation.6 | convolution fusion | flops 4294967296 | bytes 10485760 | tf_op jit(solution)/shard_map/dot_general | solution.py:75
  85.4 4.6 slice.140
  91.8 6.6 %copy.59 = bf16[2048,1024]{0,1:T(8,128)(2,1)} copy(bf16[2048,1024]{1,0:T(8,128)(2,1)} %slice.140) | data formatting | bytes 8388608
  99.7 7.1 %convolution_bitcast_fusion.3 = bf16[2048,1024]{0,1:T(8,128)(2,1)S(1)} fusion(bf16[1024,1024]{0,1:T(8,128)(2,1)S(1)} %bitcast.108, bf16[8192,1024]{1,0:T(8,128)(2,1)} %param.5), kind=kOutput, calls=%fused_computation.7 | convolution fusion | flops 4294967296 | bytes 10485760 | tf_op jit(solution)/shard_map/dot_general | solution.py:75
  113.6 7.8 %fusion.7 = f32[1024,1024]{1,0:T(8,128)S(1)} fusion(bf16[2048,256]{0,1:T(8,128)(2,1)} %collective-permute-done.16, bf16[2048,256]{0,1:T(8,128)(2,1)} %collective-permute-done.14, bf16[2048,256]{0,1:T(8,128)(2,1)} %collective-permute-done.12, bf16[2048,256]{0,1:T(8,128)(2,1)S(1)} %get-tuple-element.42, bf16[8192,1024]{1,0:T(8,128)(2,1)} %param.5), kind=kOutput, calls=%fused_computation.19 | convolution fusion | flops 4315938816 | bytes 12582912 | tf_op jit(solution)/shard_map/dot_general | solution.py:82
  122.2 18.7 %collective-permute-done.7 = bf16[2048,256]{0,1:T(8,128)(2,1)S(1)} collective-permute-done((bf16[2048,256]{0,1:T(8,128)(2,1)S(1)}, bf16[2048,256]{0,1:T(8,128)(2,1)S(1)}, u32[]{:S(2)}, u32[]{:S(2)}) %collective-permute-start.7) | collective-permute-done | bytes 1048608 | tf_op jit(solution)/shard_map/ppermute | solution.py:37
  142.1 21.7 %collective-permute-done.5 = bf16[2048,256]{0,1:T(8,128)(2,1)S(1)} collective-permute-done((bf16[2048,256]{0,1:T(8,128)(2,1)S(1)}, bf16[2048,256]{0,1:T(8,128)(2,1)S(1)}, u32[]{:S(2)}, u32[]{:S(2)}) %collective-permute-start.5) | collective-permute-done | bytes 1048608 | tf_op jit(solution)/shard_map/ppermute | solution.py:37
  167.5 6.8 %fusion = f32[1024,1024]{1,0:T(8,128)S(1)} fusion(bf16[2048,256]{0,1:T(8,128)(2,1)S(1)} %collective-permute-done.7, bf16[2048,256]{0,1:T(8,128)(2,1)S(1)} %collective-permute-done.5, bf16[2048,256]{0,1:T(8,128)(2,1)S(1)} %collective-permute-done.3, bf16[2048,256]{0,1:T(8,128)(2,1)S(1)} %get-tuple-element.47, bf16[8192,1024]{1,0:T(8,128)(2,1)} %param.5), kind=kOutput, calls=%fused_computation.11 | convolution fusion | flops 4315938816 | bytes 12582912 | tf_op jit(solution)/shard_map/dot_general | solution.py:82
  174.3 11.6 %collective-permute-done.2 = bf16[2048,256]{0,1:T(8,128)(2,1)S(1)} collective-permute-done((bf16[2048,256]{0,1:T(8,128)(2,1)S(1)}, bf16[2048,256]{0,1:T(8,128)(2,1)S(1)}, u32[]{:S(2)}, u32[]{:S(2)}) %collective-permute-start.2) | collective-permute-done | bytes 1048608 | tf_op jit(solution)/shard_map/ppermute | solution.py:37
  186.1 22.5 %collective-permute-done.1 = bf16[2048,256]{0,1:T(8,128)(2,1)S(1)} collective-permute-done((bf16[2048,256]{0,1:T(8,128)(2,1)S(1)}, bf16[2048,256]{0,1:T(8,128)(2,1)S(1)}, u32[]{:S(2)}, u32[]{:S(2)}) %collective-permute-start.1) | collective-permute-done | bytes 1048608 | tf_op jit(solution)/shard_map/ppermute | solution.py:37
  213.8 8.8 %fusion.14 = f32[1024,1024]{1,0:T(8,128)} fusion(bf16[2048,256]{0,1:T(8,128)(2,1)S(1)} %collective-permute-done.2, bf16[2048,256]{0,1:T(8,128)(2,1)S(1)} %collective-permute-done.1, bf16[2048,256]{0,1:T(8,128)(2,1)S(1)} %collective-permute-done, bf16[2048,256]{0,1:T(8,128)(2,1)S(1)} %get-tuple-element.52, bf16[8192,1024]{1,0:T(8,128)(2,1)} %param.5), kind=kOutput, calls=%fused_computation.27 | convolution fusion | flops 4315938816 | bytes 12582912 | tf_op jit(solution)/shard_map/dot_general | solution.py:82
  228.8 10.9 %add_add_fusion = f32[1024,1024]{1,0:T(8,128)} fusion(f32[1024,1024]{1,0:T(8,128)} %fusion.14, f32[1024,1024]{1,0:T(8,128)S(1)} %fusion, f32[1024,1024]{1,0:T(8,128)S(1)} %fusion.7, bf16[8192,1024]{1,0:T(8,128)(2,1)} %param.5, bf16[2048,256]{0,1:T(8,128)(2,1)} %collective-permute-done.11, bf16[2048,256]{0,1:T(8,128)(2,1)} %collective-permute-done.10, ...), kind=kOutput, calls=%fused_computation.46 | convolution fusion | flops 4319084544 | bytes 25165824 | tf_op jit(solution)/shard_map/dot_general | solution.py:82
  239.7 6.1 %reshape.106 = f32[4,4,4,16,4,256]{5,4,3,2,1,0:T(4,128)} reshape(f32[1024,1024]{1,0:T(8,128)} %add_add_fusion) | data formatting | bytes 8388608 | tf_op jit(solution)/shard_map/reshape | solution.py:112
  245.8 5.3 %select_reduce_fusion = f32[4,4,4,16,256]{4,3,2,1,0:T(8,128)S(1)} fusion(f32[4,4,4,16,4,256]{5,4,3,2,1,0:T(4,128)} %reshape.106, pred[4,4]{1,0:T(4,128)(4,1)S(1)} %copy.42), kind=kLoop, calls=%fused_computation.45 | loop fusion | flops 1835008 | bytes 5242896 | tf_op jit(solution)/shard_map/reduce_sum | solution.py:113
  257.0 9.3 %convolution_convert_fusion = bf16[2048,1024]{1,0:T(8,128)(2,1)} fusion(bf16[1024,1024]{1,0:T(8,128)(2,1)} %bitcast.101, bf16[2048,256]{0,1:T(8,128)(2,1)} %collective-permute-done.17, bf16[2048,256]{0,1:T(8,128)(2,1)} %collective-permute-done.15, bf16[2048,256]{0,1:T(8,128)(2,1)} %collective-permute-done.13, bf16[2048,256]{0,1:T(8,128)(2,1)S(1)} %copy-done.23), kind=kOutput, calls=%fused_computation.54 | convolution fusion | flops 4313841664 | bytes 10485760 | tf_op jit(solution)/shard_map/dot_general | solution.py:91
  266.3 9.8 %fusion.50 = f32[1024,1024]{0,1:T(8,128)} fusion(bf16[8192,1024]{1,0:T(8,128)(2,1)} %param.4, bf16[2048,256]{0,1:T(8,128)(2,1)} %collective-permute-done.17, bf16[2048,256]{0,1:T(8,128)(2,1)} %collective-permute-done.15, bf16[2048,256]{0,1:T(8,128)(2,1)} %collective-permute-done.13, bf16[2048,256]{0,1:T(8,128)(2,1)S(1)} %copy-done.24), kind=kOutput, calls=%fused_computation.74 | convolution fusion | flops 4311744512 | bytes 12582912 | tf_op jit(solution)/shard_map/dot_general | solution.py:93
  279.1 22.7 %collective-permute-done.6 = bf16[2048,256]{0,1:T(8,128)(2,1)} collective-permute-done((bf16[2048,256]{0,1:T(8,128)(2,1)}, bf16[2048,256]{0,1:T(8,128)(2,1)}, u32[]{:S(2)}, u32[]{:S(2)}) %collective-permute-start.6) | collective-permute-done | bytes 1048608 | tf_op jit(solution)/shard_map/ppermute | solution.py:37
  301.8 9.0 %convolution_convert_fusion.1 = bf16[2048,1024]{1,0:T(8,128)(2,1)} fusion(bf16[1024,1024]{1,0:T(8,128)(2,1)S(1)} %bitcast.103, bf16[2048,256]{0,1:T(8,128)(2,1)} %collective-permute-done.8, bf16[2048,256]{0,1:T(8,128)(2,1)} %collective-permute-done.6, bf16[2048,256]{0,1:T(8,128)(2,1)} %collective-permute-done.4, bf16[2048,256]{0,1:T(8,128)(2,1)} %get-tuple-element.48), kind=kOutput, calls=%fused_computation.55 | convolution fusion | flops 4313841664 | bytes 10485760 | tf_op jit(solution)/shard_map/dot_general | solution.py:91
  310.8 9.6 %fusion.47 = f32[1024,1024]{0,1:T(8,128)} fusion(bf16[8192,1024]{1,0:T(8,128)(2,1)} %param.4, bf16[2048,256]{0,1:T(8,128)(2,1)} %collective-permute-done.8, bf16[2048,256]{0,1:T(8,128)(2,1)} %collective-permute-done.6, bf16[2048,256]{0,1:T(8,128)(2,1)} %collective-permute-done.4, bf16[2048,256]{0,1:T(8,128)(2,1)S(1)} %copy-done.25), kind=kOutput, calls=%fused_computation.73 | convolution fusion | flops 4311744512 | bytes 12582912 | tf_op jit(solution)/shard_map/dot_general | solution.py:93
  325.3 6.6 %broadcast_in_dim.150 = bf16[8192,1024]{1,0:T(8,128)(2,1)} broadcast(bf16[]{:T(256)} %constant.53.clone.1), dimensions={} | broadcast | bytes 16777218 | tf_op jit(solution)/shard_map/broadcast_in_dim | solution.py:69
  341.5 27.6 %collective-permute-done.19 = bf16[2048,256]{0,1:T(8,128)(2,1)} collective-permute-done((bf16[2048,256]{0,1:T(8,128)(2,1)}, bf16[2048,256]{0,1:T(8,128)(2,1)}, u32[]{:S(2)}, u32[]{:S(2)}) %collective-permute-start.19) | collective-permute-done | bytes 1048608 | tf_op jit(solution)/shard_map/ppermute | solution.py:37
  370.4 20.4 %collective-permute-done.20 = bf16[2048,256]{0,1:T(8,128)(2,1)} collective-permute-done((bf16[2048,256]{0,1:T(8,128)(2,1)}, bf16[2048,256]{0,1:T(8,128)(2,1)}, u32[]{:S(2)}, u32[]{:S(2)}) %collective-permute-start.20) | collective-permute-done | bytes 1048608 | tf_op jit(solution)/shard_map/ppermute | solution.py:37
  394.2 8.3 %bitcast_add_fusion = f32[1024,1024]{0,1:T(8,128)} fusion(f32[1024,1024]{0,1:T(8,128)S(1)} %copy-done.32, f32[1024,1024]{0,1:T(8,128)S(1)} %copy-done.31, bf16[2048,1024]{0,1:T(8,128)(2,1)S(1)} %constant_dynamic-update-slice_fusion, bf16[8192,1024]{1,0:T(8,128)(2,1)} %param.4), kind=kOutput, calls=%fused_computation.42 | convolution fusion | flops 4297064448 | bytes 20971520 | tf_op jit(solution)/shard_map/dot_general | solution.py:93
  402.4 5.9 %reshape.103 = f32[4,256,4,4,4,16]{1,0,5,4,3,2:T(4,128)} reshape(f32[1024,1024]{0,1:T(8,128)} %bitcast_add_fusion) | data formatting | bytes 8388608 | tf_op jit(solution)/shard_map/reshape | solution.py:118
  431.3 9.6 %convert_dynamic-update-slice_fusion.1 = bf16[8192,1024]{1,0:T(8,128)(2,1)} fusion(bf16[8192,1024]{1,0:T(8,128)(2,1)} %constant_dynamic-update-slice_fusion.8, bf16[2048,1024]{0,1:T(8,128)(2,1)} %copy-done.27, bf16[1024,1024]{1,0:T(8,128)(2,1)} %bitcast.102), kind=kOutput, calls=%fused_computation.49 | convolution fusion | flops 4297064448 | bytes 10485760 | tf_op jit(solution)/shard_map/dot_general | solution.py:91
  440.9 6.5 %convert_dynamic-update-slice_fusion = bf16[8192,1024]{1,0:T(8,128)(2,1)} fusion(bf16[8192,1024]{1,0:T(8,128)(2,1)} %convert_dynamic-update-slice_fusion.1, bf16[2048,1024]{0,1:T(8,128)(2,1)S(1)} %copy-done.26, bf16[1024,1024]{1,0:T(8,128)(2,1)S(1)} %bitcast.104), kind=kOutput, calls=%fused_computation.48 | convolution fusion | flops 4297064448 | bytes 10485760 | tf_op jit(solution)/shard_map/dot_general | solution.py:91
  (180 shorter events, 104.1 us)
Async XLA Ops:
  7.2 314.6 %all-reduce.3.cloned.1.call-start = ((), (), s32[]{:S(2)}) async-start(), calls=%async_computation | async-start | bytes 2097152
  24.3 82.5 %collective-permute-start.12 = (bf16[2048,256]{0,1:T(8,128)(2,1)}, bf16[2048,256]{0,1:T(8,128)(2,1)}, u32[]{:S(2)}, u32[]{:S(2)}) collective-permute-start(bf16[2048,256]{0,1:T(8,128)(2,1)} %get-tuple-element.57), channel_id=1, source_target_pairs={{0,4},{4,0},{8,12},{12,8},{1,5},{5,1},{9,13},{13,9},{2,6},{6,2},{1... | collective-permute-start | bytes 3145736 | tf_op jit(solution)/shard_map/ppermute | solution.py:37
  24.7 82.8 %collective-permute-start.16 = (bf16[2048,256]{0,1:T(8,128)(2,1)}, bf16[2048,256]{0,1:T(8,128)(2,1)}, u32[]{:S(2)}, u32[]{:S(2)}) collective-permute-start(bf16[2048,256]{0,1:T(8,128)(2,1)} %get-tuple-element.58), channel_id=1, source_target_pairs={{0,12},{4,8},{8,4},{12,0},{1,13},{5,9},{9,5},{13,1},{2,14},{6,10},... | collective-permute-start | bytes 3145736 | tf_op jit(solution)/shard_map/ppermute | solution.py:37
  27.3 80.9 %collective-permute-start.14 = (bf16[2048,256]{0,1:T(8,128)(2,1)}, bf16[2048,256]{0,1:T(8,128)(2,1)}, u32[]{:S(2)}, u32[]{:S(2)}) collective-permute-start(bf16[2048,256]{0,1:T(8,128)(2,1)} %get-tuple-element.59), channel_id=1, source_target_pairs={{0,8},{4,12},{8,0},{12,4},{1,9},{5,13},{9,1},{13,5},{2,10},{6,14},... | collective-permute-start | bytes 3145736 | tf_op jit(solution)/shard_map/ppermute | solution.py:37
  39.2 183.4 %collective-permute-start.11 = (bf16[2048,256]{0,1:T(8,128)(2,1)}, bf16[2048,256]{0,1:T(8,128)(2,1)}, u32[]{:S(2)}, u32[]{:S(2)}) collective-permute-start(bf16[2048,256]{0,1:T(8,128)(2,1)} %get-tuple-element.60), channel_id=1, source_target_pairs={{0,12},{4,8},{8,4},{12,0},{1,13},{5,9},{9,5},{13,1},{2,14},{6,10},... | collective-permute-start | bytes 3145736 | tf_op jit(solution)/shard_map/ppermute | solution.py:37
  39.5 183.3 %collective-permute-start.10 = (bf16[2048,256]{0,1:T(8,128)(2,1)}, bf16[2048,256]{0,1:T(8,128)(2,1)}, u32[]{:S(2)}, u32[]{:S(2)}) collective-permute-start(bf16[2048,256]{0,1:T(8,128)(2,1)} %get-tuple-element.61), channel_id=1, source_target_pairs={{0,8},{4,12},{8,0},{12,4},{1,9},{5,13},{9,1},{13,5},{2,10},{6,14},... | collective-permute-start | bytes 3145736 | tf_op jit(solution)/shard_map/ppermute | solution.py:37
  106.8 14.6 %collective-permute-start.3 = (bf16[2048,256]{0,1:T(8,128)(2,1)S(1)}, bf16[2048,256]{0,1:T(8,128)(2,1)S(1)}, u32[]{:S(2)}, u32[]{:S(2)}) collective-permute-start(bf16[2048,256]{0,1:T(8,128)(2,1)S(1)} %copy-done.22), channel_id=1, source_target_pairs={{0,4},{4,0},{8,12},{12,8},{1,5},{5,1},{9,13},{13,9},{2,6},{6,2},{1... | collective-permute-start | bytes 3145736 | tf_op jit(solution)/shard_map/ppermute | solution.py:37
  107.5 33.4 %collective-permute-start.7 = (bf16[2048,256]{0,1:T(8,128)(2,1)S(1)}, bf16[2048,256]{0,1:T(8,128)(2,1)S(1)}, u32[]{:S(2)}, u32[]{:S(2)}) collective-permute-start(bf16[2048,256]{0,1:T(8,128)(2,1)S(1)} %copy-done.21), channel_id=1, source_target_pairs={{0,12},{4,8},{8,4},{12,0},{1,13},{5,9},{9,5},{13,1},{2,14},{6,10},... | collective-permute-start | bytes 3145736 | tf_op jit(solution)/shard_map/ppermute | solution.py:37
  108.2 55.6 %collective-permute-start.5 = (bf16[2048,256]{0,1:T(8,128)(2,1)S(1)}, bf16[2048,256]{0,1:T(8,128)(2,1)S(1)}, u32[]{:S(2)}, u32[]{:S(2)}) collective-permute-start(bf16[2048,256]{0,1:T(8,128)(2,1)S(1)} %copy-done.20), channel_id=1, source_target_pairs={{0,8},{4,12},{8,0},{12,4},{1,9},{5,13},{9,1},{13,5},{2,10},{6,14},... | collective-permute-start | bytes 3145736 | tf_op jit(solution)/shard_map/ppermute | solution.py:37
  113.6 50.2 %copy-start.2 = (bf16[2048,1024]{0,1:T(8,128)(2,1)S(1)}, bf16[2048,1024]{0,1:T(8,128)(2,1)}, u32[]{:S(2)}) copy-start(bf16[2048,1024]{0,1:T(8,128)(2,1)} %convolution_bitcast_fusion.2) | copy-start | bytes 12582916
  121.4 64.5 %collective-permute-start.2 = (bf16[2048,256]{0,1:T(8,128)(2,1)S(1)}, bf16[2048,256]{0,1:T(8,128)(2,1)S(1)}, u32[]{:S(2)}, u32[]{:S(2)}) collective-permute-start(bf16[2048,256]{0,1:T(8,128)(2,1)S(1)} %copy-done.19), channel_id=1, source_target_pairs={{0,12},{4,8},{8,4},{12,0},{1,13},{5,9},{9,5},{13,1},{2,14},{6,10},... | collective-permute-start | bytes 3145736 | tf_op jit(solution)/shard_map/ppermute | solution.py:37
  141.0 67.6 %collective-permute-start.1 = (bf16[2048,256]{0,1:T(8,128)(2,1)S(1)}, bf16[2048,256]{0,1:T(8,128)(2,1)S(1)}, u32[]{:S(2)}, u32[]{:S(2)}) collective-permute-start(bf16[2048,256]{0,1:T(8,128)(2,1)S(1)} %copy-done.18), channel_id=1, source_target_pairs={{0,8},{4,12},{8,0},{12,4},{1,9},{5,13},{9,1},{13,5},{2,10},{6,14},... | collective-permute-start | bytes 3145736 | tf_op jit(solution)/shard_map/ppermute | solution.py:37
  163.8 45.5 %collective-permute-start = (bf16[2048,256]{0,1:T(8,128)(2,1)S(1)}, bf16[2048,256]{0,1:T(8,128)(2,1)S(1)}, u32[]{:S(2)}, u32[]{:S(2)}) collective-permute-start(bf16[2048,256]{0,1:T(8,128)(2,1)S(1)} %get-tuple-element.68), channel_id=1, source_target_pairs={{0,4},{4,0},{8,12},{12,8},{1,5},{5,1},{9,13},{13,9},{2,6},{6,2},{1... | collective-permute-start | bytes 3145736 | tf_op jit(solution)/shard_map/ppermute | solution.py:37
  185.9 38.2 %collective-permute-start.9 = (bf16[2048,256]{0,1:T(8,128)(2,1)S(1)}, bf16[2048,256]{0,1:T(8,128)(2,1)S(1)}, u32[]{:S(2)}, u32[]{:S(2)}) collective-permute-start(bf16[2048,256]{0,1:T(8,128)(2,1)S(1)} %copy-done.17), channel_id=1, source_target_pairs={{0,4},{4,0},{8,12},{12,8},{1,5},{5,1},{9,13},{13,9},{2,6},{6,2},{1... | collective-permute-start | bytes 3145736 | tf_op jit(solution)/shard_map/ppermute | solution.py:37
  208.6 45.0 %collective-permute-start.17 = (bf16[2048,256]{0,1:T(8,128)(2,1)}, bf16[2048,256]{0,1:T(8,128)(2,1)}, u32[]{:S(2)}, u32[]{:S(2)}) collective-permute-start(bf16[2048,256]{0,1:T(8,128)(2,1)} %get-tuple-element.44), channel_id=1, source_target_pairs={{0,12},{4,8},{8,4},{12,0},{1,13},{5,9},{9,5},{13,1},{2,14},{6,10},... | collective-permute-start | bytes 3145736 | tf_op jit(solution)/shard_map/ppermute | solution.py:37
  209.3 47.7 %collective-permute-start.15 = (bf16[2048,256]{0,1:T(8,128)(2,1)}, bf16[2048,256]{0,1:T(8,128)(2,1)}, u32[]{:S(2)}, u32[]{:S(2)}) collective-permute-start(bf16[2048,256]{0,1:T(8,128)(2,1)} %get-tuple-element.45), channel_id=1, source_target_pairs={{0,8},{4,12},{8,0},{12,4},{1,9},{5,13},{9,1},{13,5},{2,10},{6,14},... | collective-permute-start | bytes 3145736 | tf_op jit(solution)/shard_map/ppermute | solution.py:37
  222.6 34.4 %collective-permute-start.13 = (bf16[2048,256]{0,1:T(8,128)(2,1)}, bf16[2048,256]{0,1:T(8,128)(2,1)}, u32[]{:S(2)}, u32[]{:S(2)}) collective-permute-start(bf16[2048,256]{0,1:T(8,128)(2,1)} %get-tuple-element.46), channel_id=1, source_target_pairs={{0,4},{4,0},{8,12},{12,8},{1,5},{5,1},{9,13},{13,9},{2,6},{6,2},{1... | collective-permute-start | bytes 3145736 | tf_op jit(solution)/shard_map/ppermute | solution.py:37
  222.8 56.3 %collective-permute-start.8 = (bf16[2048,256]{0,1:T(8,128)(2,1)}, bf16[2048,256]{0,1:T(8,128)(2,1)}, u32[]{:S(2)}, u32[]{:S(2)}) collective-permute-start(bf16[2048,256]{0,1:T(8,128)(2,1)} %get-tuple-element.49), channel_id=1, source_target_pairs={{0,12},{4,8},{8,4},{12,0},{1,13},{5,9},{9,5},{13,1},{2,14},{6,10},... | collective-permute-start | bytes 3145736 | tf_op jit(solution)/shard_map/ppermute | solution.py:37
  224.1 77.6 %collective-permute-start.6 = (bf16[2048,256]{0,1:T(8,128)(2,1)}, bf16[2048,256]{0,1:T(8,128)(2,1)}, u32[]{:S(2)}, u32[]{:S(2)}) collective-permute-start(bf16[2048,256]{0,1:T(8,128)(2,1)} %get-tuple-element.50), channel_id=1, source_target_pairs={{0,8},{4,12},{8,0},{12,4},{1,9},{5,13},{9,1},{13,5},{2,10},{6,14},... | collective-permute-start | bytes 3145736 | tf_op jit(solution)/shard_map/ppermute | solution.py:37
  253.6 48.2 %collective-permute-start.4 = (bf16[2048,256]{0,1:T(8,128)(2,1)}, bf16[2048,256]{0,1:T(8,128)(2,1)}, u32[]{:S(2)}, u32[]{:S(2)}) collective-permute-start(bf16[2048,256]{0,1:T(8,128)(2,1)} %get-tuple-element.51), channel_id=1, source_target_pairs={{0,4},{4,0},{8,12},{12,8},{1,5},{5,1},{9,13},{13,9},{2,6},{6,2},{1... | collective-permute-start | bytes 3145736 | tf_op jit(solution)/shard_map/ppermute | solution.py:37
  266.3 35.5 %copy-start.11 = (bf16[128,8,4,256]{3,1,2,0:T(8,128)(2,1)S(1)}, bf16[128,8,4,256]{3,1,2,0:T(8,128)(2,1)}, u32[]{:S(2)}) copy-start(bf16[128,8,4,256]{3,1,2,0:T(8,128)(2,1)} %copy.62) | copy-start | bytes 6291460
  320.4 88.0 %collective-permute-start.21 = (bf16[2048,256]{0,1:T(8,128)(2,1)}, bf16[2048,256]{0,1:T(8,128)(2,1)S(1)}, u32[]{:S(2)}, u32[]{:S(2)}) collective-permute-start(bf16[2048,256]{0,1:T(8,128)(2,1)} %get-tuple-element.26), channel_id=1, source_target_pairs={{0,4},{4,0},{8,12},{12,8},{1,5},{5,1},{9,13},{13,9},{2,6},{6,2},{1... | collective-permute-start | bytes 3145736 | tf_op jit(solution)/shard_map/ppermute | solution.py:37
  320.4 89.0 %collective-permute-start.22 = (bf16[2048,256]{0,1:T(8,128)(2,1)}, bf16[2048,256]{0,1:T(8,128)(2,1)S(1)}, u32[]{:S(2)}, u32[]{:S(2)}) collective-permute-start(bf16[2048,256]{0,1:T(8,128)(2,1)} %get-tuple-element.27), channel_id=1, source_target_pairs={{0,8},{4,12},{8,0},{12,4},{1,9},{5,13},{9,1},{13,5},{2,10},{6,14},... | collective-permute-start | bytes 3145736 | tf_op jit(solution)/shard_map/ppermute | solution.py:37
  323.5 15.5 %collective-permute-start.18 = (bf16[2048,256]{0,1:T(8,128)(2,1)}, bf16[2048,256]{0,1:T(8,128)(2,1)}, u32[]{:S(2)}, u32[]{:S(2)}) collective-permute-start(bf16[2048,256]{0,1:T(8,128)(2,1)} %get-tuple-element.22), channel_id=1, source_target_pairs={{0,4},{4,0},{8,12},{12,8},{1,5},{5,1},{9,13},{13,9},{2,6},{6,2},{1... | collective-permute-start | bytes 3145736 | tf_op jit(solution)/shard_map/ppermute | solution.py:37
  323.5 45.6 %collective-permute-start.19 = (bf16[2048,256]{0,1:T(8,128)(2,1)}, bf16[2048,256]{0,1:T(8,128)(2,1)}, u32[]{:S(2)}, u32[]{:S(2)}) collective-permute-start(bf16[2048,256]{0,1:T(8,128)(2,1)} %get-tuple-element.23), channel_id=1, source_target_pairs={{0,8},{4,12},{8,0},{12,4},{1,9},{5,13},{9,1},{13,5},{2,10},{6,14},... | collective-permute-start | bytes 3145736 | tf_op jit(solution)/shard_map/ppermute | solution.py:37
  324.3 66.5 %collective-permute-start.20 = (bf16[2048,256]{0,1:T(8,128)(2,1)}, bf16[2048,256]{0,1:T(8,128)(2,1)}, u32[]{:S(2)}, u32[]{:S(2)}) collective-permute-start(bf16[2048,256]{0,1:T(8,128)(2,1)} %get-tuple-element.24), channel_id=1, source_target_pairs={{0,12},{4,8},{8,4},{12,0},{1,13},{5,9},{9,5},{13,1},{2,14},{6,10},... | collective-permute-start | bytes 3145736 | tf_op jit(solution)/shard_map/ppermute | solution.py:37
  336.4 57.8 %copy-start.32 = (f32[1024,1024]{0,1:T(8,128)S(1)}, f32[1024,1024]{0,1:T(8,128)}, u32[]{:S(2)}) copy-start(f32[1024,1024]{0,1:T(8,128)} %fusion.47) | copy-start | bytes 12582916
  339.0 55.2 %copy-start.31 = (f32[1024,1024]{0,1:T(8,128)S(1)}, f32[1024,1024]{0,1:T(8,128)}, u32[]{:S(2)}) copy-start(f32[1024,1024]{0,1:T(8,128)} %fusion.50) | copy-start | bytes 12582916
  339.0 75.4 %collective-permute-start.23 = (bf16[2048,256]{0,1:T(8,128)(2,1)}, bf16[2048,256]{0,1:T(8,128)(2,1)S(1)}, u32[]{:S(2)}, u32[]{:S(2)}) collective-permute-start(bf16[2048,256]{0,1:T(8,128)(2,1)} %get-tuple-element.28), channel_id=1, source_target_pairs={{0,12},{4,8},{8,4},{12,0},{1,13},{5,9},{9,5},{13,1},{2,14},{6,10},... | collective-permute-start | bytes 3145736 | tf_op jit(solution)/shard_map/ppermute | solution.py:37
  426.8 20.8 %collective-permute-start.24 = (f32[64,4,256]{2,0,1:T(8,128)S(1)}, f32[64,4,256]{2,0,1:T(8,128)S(1)}, u32[]{:S(2)}, u32[]{:S(2)}) collective-permute-start(f32[64,4,256]{2,0,1:T(8,128)S(1)} %bitcast.115), channel_id=1, source_target_pairs={{0,1},{1,0},{2,3},{3,2},{4,5},{5,4},{6,7},{7,6},{8,9},{9,8},{10,11... | collective-permute-start | bytes 786440 | tf_op jit(solution)/shard_map/ppermute | solution.py:48
  428.5 21.4 %collective-permute-start.25 = (f32[64,4,256]{2,0,1:T(8,128)S(1)}, f32[64,4,256]{2,0,1:T(8,128)S(1)}, u32[]{:S(2)}, u32[]{:S(2)}) collective-permute-start(f32[64,4,256]{2,0,1:T(8,128)S(1)} %bitcast.114), channel_id=1, source_target_pairs={{0,2},{1,3},{2,0},{3,1},{4,6},{5,7},{6,4},{7,5},{8,10},{9,11},{10,... | collective-permute-start | bytes 786440 | tf_op jit(solution)/shard_map/ppermute | solution.py:48
  431.1 18.8 %collective-permute-start.26 = (f32[64,4,256]{2,0,1:T(8,128)S(1)}, f32[64,4,256]{2,0,1:T(8,128)S(1)}, u32[]{:S(2)}, u32[]{:S(2)}) collective-permute-start(f32[64,4,256]{2,0,1:T(8,128)S(1)} %bitcast.113), channel_id=1, source_target_pairs={{0,3},{1,2},{2,1},{3,0},{4,7},{5,6},{6,5},{7,4},{8,11},{9,10},{10,... | collective-permute-start | bytes 786440 | tf_op jit(solution)/shard_map/ppermute | solution.py:48
  (33 other events, 361.9 us)
Sparse Core Ops, SparseCore 0:
  253.7 52.9 all-reduce.2
